TPU v7x, 32 devices: a whole 2x2x4 slice. The times are simulated.
32 devices in a mesh: groups: 2 (over y), freq: 4 (over x, core), recv: 4 (over z).
Axes of the slice: x: 2, y: 2, z: 4, core: 2. Of those that a mesh axis runs over, the one named last changes fastest.
Arguments:
- operator: bfloat16 [4, 32, 512, 2048], P('groups', 'freq', 'recv'), parts along dimension 0, may hold values from -0.125 to 0.125
- recorded: float32 [4, 32, 8, 512], P('groups', 'freq', None, 'recv'), parts along dimension 0, may hold values from -18 to 18
- win_start: int32 [16, 16], P('groups'), parts along dimension 0, may hold values from 0 to 15
- win_end: int32 [16, 16], P('groups'), parts along dimension 0, may hold values from 17 to 32
Outputs:
- reflectivity: float32 [4, 32, 8, 2048], P('groups', 'freq', None, 'recv'), parts along dimension 0
- residual: float32 [4, 32, 8, 512], P('groups', 'freq', None, 'recv'), parts along dimension 0
There are 2 independent parts, one for each index of `groups`. A program takes and returns all parts, laid end to end along the dimension named above; each array names one. Nothing has to cross between parts.
All inputs are finite; a program needn't handle non-finite values.
Results may differ from a plain program's by a relative error of at most 0.013.
Values may be sent and summed in bfloat16 or wider, within the bound.
No kernel may reach another device: no remote copies, remote signals or barrier semaphores. Data moves between devices by JAX's collectives and lax.ppermute only.
A program may use at most 64 MiB of HBM per device.

v0:
```python
import math

import jax
import jax.numpy as jnp
from jax import lax
from jax.sharding import PartitionSpec as P

SBLK = 128
ITERS = 5


def high_dot(left, right):
    return jnp.dot(left, right, precision=lax.Precision.HIGHEST)


def dft_rows(row_ids, length):
    positions = jnp.arange(length, dtype=jnp.int32)
    phases = (row_ids[:, None] * positions[None, :] % length).astype(jnp.float32) * (
        2.0 * math.pi / length
    )
    normalizer = 1.0 / math.sqrt(length)
    return (jnp.cos(phases) * normalizer, jnp.sin(phases) * normalizer)


def to_time(real_part, imag_part, cos_rows, sin_rows):
    time_real = high_dot(cos_rows.T, real_part) - high_dot(sin_rows.T, imag_part)
    time_imag = high_dot(sin_rows.T, real_part) + high_dot(cos_rows.T, imag_part)
    return (time_real, time_imag)


def to_freq(kept_real, kept_imag, cos_rows, sin_rows):
    real_part = high_dot(cos_rows, kept_real) + high_dot(sin_rows, kept_imag)
    imag_part = high_dot(cos_rows, kept_imag) - high_dot(sin_rows, kept_real)
    return jnp.stack([real_part, imag_part])


def window_mask(column_ids, src_local, win_start, win_end, length):
    blocks = win_start.shape[1]
    side_ids = column_ids // src_local
    source_ids = lax.axis_index("recv") * src_local + column_ids % src_local
    flat_ids = side_ids * blocks + source_ids // SBLK
    table_ids = jnp.arange(win_start.shape[0] * blocks, dtype=jnp.int32)
    matches = flat_ids[:, None] == table_ids[None, :]
    opening = jnp.sum(jnp.where(matches, win_start.reshape(-1)[None, :], 0), axis=1)
    closing = jnp.sum(jnp.where(matches, win_end.reshape(-1)[None, :], 0), axis=1)
    samples = jnp.arange(length, dtype=jnp.int32)[:, None]
    return ((samples >= opening[None, :]) & (samples < closing[None, :])).astype(jnp.float32)


def on_device(operator, recorded, win_start, win_end):
    freq_local = operator.shape[1]
    sources = operator.shape[3]
    right_sides = recorded.shape[2]
    src_local = sources // lax.axis_size("recv")
    total_freq = freq_local * lax.axis_size("freq")
    columns = right_sides * src_local
    real_operator = operator[0]
    imag_operator = operator[1]
    reflect = jnp.zeros((2, freq_local, right_sides, src_local), jnp.float32)
    residual = recorded
    for iteration in range(ITERS):
        rounded_residual = residual.astype(jnp.bfloat16)
        partial_real = jnp.einsum(
            "fbr,frs->fbs", rounded_residual[0], real_operator, preferred_element_type=jnp.float32
        ) + jnp.einsum(
            "fbr,frs->fbs", rounded_residual[1], imag_operator, preferred_element_type=jnp.float32
        )
        partial_imag = jnp.einsum(
            "fbr,frs->fbs", rounded_residual[1], real_operator, preferred_element_type=jnp.float32
        ) - jnp.einsum(
            "fbr,frs->fbs", rounded_residual[0], imag_operator, preferred_element_type=jnp.float32
        )
        gradient = lax.psum_scatter(
            jnp.stack([partial_real, partial_imag]).astype(jnp.bfloat16),
            "recv",
            scatter_dimension=3,
            tiled=True,
        ).astype(jnp.float32)
        flattened = gradient.reshape(2, freq_local, columns)
        empty_time = jnp.zeros((2, total_freq, columns), jnp.float32)
        segment = lax.all_gather(flattened.astype(jnp.bfloat16), "freq", axis=1, tiled=True).astype(
            jnp.float32
        )
        row_ids = jnp.arange(segment.shape[1], dtype=jnp.int32)
        cos_part, sin_part = dft_rows(row_ids, total_freq)
        part_real, part_imag = to_time(segment[0], segment[1], cos_part, sin_part)
        timed = empty_time + jnp.stack([part_real, part_imag])
        window = window_mask(
            jnp.arange(columns, dtype=jnp.int32), src_local, win_start, win_end, total_freq
        )
        own_rows = lax.axis_index("freq") * freq_local + jnp.arange(freq_local, dtype=jnp.int32)
        cos_rows, sin_rows = dft_rows(own_rows, total_freq)
        projected = to_freq(timed[0] * window, timed[1] * window, cos_rows, sin_rows)
        direction = projected.reshape(2, freq_local, right_sides, src_local)
        rounded_direction = direction.astype(jnp.bfloat16)
        add_segment = lax.all_gather(rounded_direction, "recv", axis=3, tiled=True)
        image_real = jnp.einsum(
            "fbs,frs->fbr", add_segment[0], real_operator, preferred_element_type=jnp.float32
        ) - jnp.einsum(
            "fbs,frs->fbr", add_segment[1], imag_operator, preferred_element_type=jnp.float32
        )
        image_imag = jnp.einsum(
            "fbs,frs->fbr", add_segment[0], imag_operator, preferred_element_type=jnp.float32
        ) + jnp.einsum(
            "fbs,frs->fbr", add_segment[1], real_operator, preferred_element_type=jnp.float32
        )
        image = jnp.stack([image_real, image_imag])
        direction_power, image_energy = lax.psum(
            (jnp.sum(direction * direction), jnp.sum(image * image)), ("freq", "recv")
        )
        step_length = direction_power / (image_energy + 1e-06)
        reflect = reflect + step_length * direction
        residual = residual - step_length * image
    return (reflect, residual)


def solution(mesh):
    return jax.shard_map(
        on_device,
        mesh=mesh,
        in_specs=(
            P("groups", "freq", "recv", None),
            P("groups", "freq", None, "recv"),
            P("groups", None),
            P("groups", None),
        ),
        out_specs=(P("groups", "freq", None, "recv"), P("groups", "freq", None, "recv")),
        check_vma=False,
    )
```

profile of v0, /device:TPU:0, one launch (start us, length us, event | category | flops | bytes accessed | tf_op | source)
XLA Modules:
  0.0 536.8 jit_solution(5900010467713200672)
XLA Ops:
  8.1 3.0 fusion.46
  11.0 3.3 fusion.48
  18.7 22.4 %reduce-scatter.6.cloned.1.call-done = bf16[2,8,8,512]{3,2,1,0:T(8,128)(2,1)} async-done(((bf16[2,8,8,2048]{3,2,1,0:T(8,128)(2,1)}), bf16[2,8,8,512]{3,2,1,0:T(8,128)(2,1)}) %reduce-scatter.6.cloned.1.call-update) | async-done | bytes 131088 | tf_op jit(solution)/shard_map/reduce_scatter | solution.py:73
  42.1 7.1 %all_gather.30 = bf16[2,32,4096]{2,1,0:T(8,128)(2,1)S(1)} all-gather(bf16[2,8,4096]{2,1,0:T(8,128)(2,1)S(1)} %convert_element_type.125), channel_id=1, replica_groups=mesh['groups'=2,'freq'=4,'recv'=4] {'freq'}, dimensions={1}, use_global_device_ids=true | all-gather | bytes 655360 | tf_op jit(solution)/shard_map/all_gather | solution.py:81
  54.0 16.1 %all_gather.31 = bf16[2,8,8,2048]{3,2,1,0:T(8,128)(2,1)S(1)} all-gather(bf16[2,8,8,512]{3,2,1,0:T(8,128)(2,1)S(1)} %get-tuple-element.27), channel_id=1, replica_groups=mesh['groups'=2,'freq'=4,'recv'=4] {'recv'}, dimensions={3}, use_global_device_ids=true | all-gather | bytes 655360 | tf_op jit(solution)/shard_map/all_gather | solution.py:96
  70.1 3.5 fusion.42
  73.6 3.4 fusion.44
  80.0 30.8 %all-reduce.4 = (f32[]{:T(128)}, f32[]{:T(128)}) all-reduce(f32[]{:T(128)} %get-tuple-element.26, f32[]{:T(128)} %multiply_reduce_fusion.9), channel_id=1, replica_groups=mesh['groups'=2,'freq'=4,'recv'=4] {'freq','recv'}, use_global_device_ids=true, to_apply=%region_4.5 | all-reduce | flops 2 | bytes 16 | tf_op jit(solution)/shard_map/psum | solution.py:108
  112.1 2.8 fusion.38
  115.0 2.8 fusion.40
  117.8 2.9 fusion.159
  120.7 2.9 fusion.156
  124.5 21.1 %reduce-scatter.8.cloned.1.call-done = bf16[2,8,8,512]{3,2,1,0:T(8,128)(2,1)} async-done(((bf16[2,8,8,2048]{3,2,1,0:T(8,128)(2,1)}), bf16[2,8,8,512]{3,2,1,0:T(8,128)(2,1)}) %reduce-scatter.8.cloned.1.call-update) | async-done | bytes 131088 | tf_op jit(solution)/shard_map/reduce_scatter | solution.py:73
  146.5 7.1 %all_gather.32 = bf16[2,32,4096]{2,1,0:T(8,128)(2,1)S(1)} all-gather(bf16[2,8,4096]{2,1,0:T(8,128)(2,1)S(1)} %convert_element_type.128), channel_id=1, replica_groups=mesh['groups'=2,'freq'=4,'recv'=4] {'freq'}, dimensions={1}, use_global_device_ids=true | all-gather | bytes 655360 | tf_op jit(solution)/shard_map/all_gather | solution.py:81
  158.5 16.1 %all_gather.33 = bf16[2,8,8,2048]{3,2,1,0:T(8,128)(2,1)S(1)} all-gather(bf16[2,8,8,512]{3,2,1,0:T(8,128)(2,1)S(1)} %get-tuple-element.25), channel_id=1, replica_groups=mesh['groups'=2,'freq'=4,'recv'=4] {'recv'}, dimensions={3}, use_global_device_ids=true | all-gather | bytes 655360 | tf_op jit(solution)/shard_map/all_gather | solution.py:96
  174.6 3.5 fusion.34
  178.1 3.4 fusion.36
  184.5 30.5 %all-reduce.3 = (f32[]{:T(128)}, f32[]{:T(128)}) all-reduce(f32[]{:T(128)} %get-tuple-element.24, f32[]{:T(128)} %multiply_reduce_fusion.8), channel_id=1, replica_groups=mesh['groups'=2,'freq'=4,'recv'=4] {'freq','recv'}, use_global_device_ids=true, to_apply=%region_9.10 | all-reduce | flops 2 | bytes 16 | tf_op jit(solution)/shard_map/psum | solution.py:108
  216.3 2.8 fusion.30
  219.2 2.8 fusion.32
  222.0 2.9 fusion.165
  224.9 2.9 fusion.162
  228.7 20.9 %reduce-scatter.10.cloned.1.call-done = bf16[2,8,8,512]{3,2,1,0:T(8,128)(2,1)} async-done(((bf16[2,8,8,2048]{3,2,1,0:T(8,128)(2,1)}), bf16[2,8,8,512]{3,2,1,0:T(8,128)(2,1)}) %reduce-scatter.10.cloned.1.call-update) | async-done | bytes 131088 | tf_op jit(solution)/shard_map/reduce_scatter | solution.py:73
  250.6 7.1 %all_gather.34 = bf16[2,32,4096]{2,1,0:T(8,128)(2,1)S(1)} all-gather(bf16[2,8,4096]{2,1,0:T(8,128)(2,1)S(1)} %convert_element_type.131), channel_id=1, replica_groups=mesh['groups'=2,'freq'=4,'recv'=4] {'freq'}, dimensions={1}, use_global_device_ids=true | all-gather | bytes 655360 | tf_op jit(solution)/shard_map/all_gather | solution.py:81
  262.5 16.1 %all_gather.35 = bf16[2,8,8,2048]{3,2,1,0:T(8,128)(2,1)S(1)} all-gather(bf16[2,8,8,512]{3,2,1,0:T(8,128)(2,1)S(1)} %get-tuple-element.23), channel_id=1, replica_groups=mesh['groups'=2,'freq'=4,'recv'=4] {'recv'}, dimensions={3}, use_global_device_ids=true | all-gather | bytes 655360 | tf_op jit(solution)/shard_map/all_gather | solution.py:96
  278.6 3.5 fusion.26
  282.1 3.4 fusion.28
  288.6 30.5 %all-reduce.2 = (f32[]{:T(128)}, f32[]{:T(128)}) all-reduce(f32[]{:T(128)} %get-tuple-element.22, f32[]{:T(128)} %multiply_reduce_fusion.7), channel_id=1, replica_groups=mesh['groups'=2,'freq'=4,'recv'=4] {'freq','recv'}, use_global_device_ids=true, to_apply=%region_14.15 | all-reduce | flops 2 | bytes 16 | tf_op jit(solution)/shard_map/psum | solution.py:108
  320.4 2.8 fusion.22
  323.2 2.8 fusion.24
  326.1 2.9 fusion.171
  328.9 2.9 fusion.168
  332.7 21.0 %reduce-scatter.12.cloned.1.call-done = bf16[2,8,8,512]{3,2,1,0:T(8,128)(2,1)} async-done(((bf16[2,8,8,2048]{3,2,1,0:T(8,128)(2,1)}), bf16[2,8,8,512]{3,2,1,0:T(8,128)(2,1)}) %reduce-scatter.12.cloned.1.call-update) | async-done | bytes 131088 | tf_op jit(solution)/shard_map/reduce_scatter | solution.py:73
  354.7 7.2 %all_gather.36 = bf16[2,32,4096]{2,1,0:T(8,128)(2,1)S(1)} all-gather(bf16[2,8,4096]{2,1,0:T(8,128)(2,1)S(1)} %convert_element_type.134), channel_id=1, replica_groups=mesh['groups'=2,'freq'=4,'recv'=4] {'freq'}, dimensions={1}, use_global_device_ids=true | all-gather | bytes 655360 | tf_op jit(solution)/shard_map/all_gather | solution.py:81
  366.7 16.1 %all_gather.37 = bf16[2,8,8,2048]{3,2,1,0:T(8,128)(2,1)S(1)} all-gather(bf16[2,8,8,512]{3,2,1,0:T(8,128)(2,1)S(1)} %get-tuple-element.21), channel_id=1, replica_groups=mesh['groups'=2,'freq'=4,'recv'=4] {'recv'}, dimensions={3}, use_global_device_ids=true | all-gather | bytes 655360 | tf_op jit(solution)/shard_map/all_gather | solution.py:96
  382.8 3.5 fusion.18
  386.3 3.4 fusion.20
  392.7 30.6 %all-reduce.1 = (f32[]{:T(128)}, f32[]{:T(128)}) all-reduce(f32[]{:T(128)} %get-tuple-element.20, f32[]{:T(128)} %multiply_reduce_fusion.6), channel_id=1, replica_groups=mesh['groups'=2,'freq'=4,'recv'=4] {'freq','recv'}, use_global_device_ids=true, to_apply=%region_19.20 | all-reduce | flops 2 | bytes 16 | tf_op jit(solution)/shard_map/psum | solution.py:108
  424.6 2.8 fusion.14
  427.5 2.8 fusion.16
  430.3 2.9 fusion.177
  433.2 2.9 fusion.174
  436.9 20.9 %reduce-scatter.14.cloned.1.call-done = bf16[2,8,8,512]{3,2,1,0:T(8,128)(2,1)} async-done(((bf16[2,8,8,2048]{3,2,1,0:T(8,128)(2,1)}), bf16[2,8,8,512]{3,2,1,0:T(8,128)(2,1)}) %reduce-scatter.14.cloned.1.call-update) | async-done | bytes 131088 | tf_op jit(solution)/shard_map/reduce_scatter | solution.py:73
  458.8 7.1 %all_gather.38 = bf16[2,32,4096]{2,1,0:T(8,128)(2,1)S(1)} all-gather(bf16[2,8,4096]{2,1,0:T(8,128)(2,1)S(1)} %convert_element_type.137), channel_id=1, replica_groups=mesh['groups'=2,'freq'=4,'recv'=4] {'freq'}, dimensions={1}, use_global_device_ids=true | all-gather | bytes 655360 | tf_op jit(solution)/shard_map/all_gather | solution.py:81
  470.7 16.1 %all_gather.39 = bf16[2,8,8,2048]{3,2,1,0:T(8,128)(2,1)S(1)} all-gather(bf16[2,8,8,512]{3,2,1,0:T(8,128)(2,1)S(1)} %get-tuple-element.18), channel_id=1, replica_groups=mesh['groups'=2,'freq'=4,'recv'=4] {'recv'}, dimensions={3}, use_global_device_ids=true | all-gather | bytes 655360 | tf_op jit(solution)/shard_map/all_gather | solution.py:96
  486.8 3.5 fusion.10
  490.3 3.4 fusion.12
  496.7 30.3 %all-reduce = (f32[]{:T(128)}, f32[]{:T(128)}) all-reduce(f32[]{:T(128)} %get-tuple-element.19, f32[]{:T(128)} %multiply_reduce_fusion.5), channel_id=1, replica_groups=mesh['groups'=2,'freq'=4,'recv'=4] {'freq','recv'}, use_global_device_ids=true, to_apply=%region_24.25 | all-reduce | flops 2 | bytes 16 | tf_op jit(solution)/shard_map/psum | solution.py:108
  (137 shorter events, 54.2 us)
Async XLA Ops:
  7.2 34.0 %reduce-scatter.6.cloned.1.call-start = ((), (), s32[]{:S(2)}) async-start(), calls=%async_computation.5 | async-start | bytes 655360 | tf_op jit(solution)/shard_map/reduce_scatter | solution.py:73
  8.1 6.3 %copy-start = (bf16[2,8,128,2048]{3,2,1,0:T(8,128)(2,1)S(1)}, bf16[2,8,128,2048]{3,2,1,0:T(8,128)(2,1)}, u32[]{:S(2)}) copy-start(bf16[2,8,128,2048]{3,2,1,0:T(8,128)(2,1)} %param.4) | copy-start | bytes 25165828
  15.1 1.6 copy-start.2
  15.1 1.7 copy-start.3
  16.6 128.9 %reduce-scatter.8.cloned.1.call-start = ((), (), s32[]{:S(2)}) async-start(), calls=%async_computation.6 | async-start | bytes 655360 | tf_op jit(solution)/shard_map/reduce_scatter | solution.py:73
  50.2 26.8 %slice-start = ((s8[8388608]{0:T(1024)(128)(4,1)}), s8[4194304]{0:T(1024)(128)(4,1)S(1)}, s32[]{:S(2)}) async-start(s8[8388608]{0:T(1024)(128)(4,1)} %bitcast.406), calls=%async_computation.10 | async-start | bytes 8388608
  70.1 6.9 %slice-start.1 = ((s8[8388608]{0:T(1024)(128)(4,1)}), s8[4194304]{0:T(1024)(128)(4,1)S(1)}, s32[]{:S(2)}) async-start(s8[8388608]{0:T(1024)(128)(4,1)} %bitcast.406), calls=%async_computation.11 | async-start | bytes 8388608
  77.0 35.1 %copy-start.1 = (f32[2,8,8,128]{3,2,1,0:T(8,128)S(1)}, f32[2,8,8,128]{3,2,1,0:T(8,128)}, u32[]{:S(2)}) copy-start(f32[2,8,8,128]{3,2,1,0:T(8,128)} %param.5) | copy-start | bytes 196612
  124.4 125.2 %reduce-scatter.10.cloned.1.call-start = ((), (), s32[]{:S(2)}) async-start(), calls=%async_computation.7 | async-start | bytes 655360 | tf_op jit(solution)/shard_map/reduce_scatter | solution.py:73
  154.6 26.9 %slice-start.2 = ((s8[8388608]{0:T(1024)(128)(4,1)}), s8[4194304]{0:T(1024)(128)(4,1)S(1)}, s32[]{:S(2)}) async-start(s8[8388608]{0:T(1024)(128)(4,1)} %bitcast.408), calls=%async_computation.12 | async-start | bytes 8388608
  174.6 6.9 %slice-start.3 = ((s8[8388608]{0:T(1024)(128)(4,1)}), s8[4194304]{0:T(1024)(128)(4,1)S(1)}, s32[]{:S(2)}) async-start(s8[8388608]{0:T(1024)(128)(4,1)} %bitcast.408), calls=%async_computation.13 | async-start | bytes 8388608
  228.6 125.1 %reduce-scatter.12.cloned.1.call-start = ((), (), s32[]{:S(2)}) async-start(), calls=%async_computation.8 | async-start | bytes 655360 | tf_op jit(solution)/shard_map/reduce_scatter | solution.py:73
  258.2 27.3 %slice-start.4 = ((s8[8388608]{0:T(1024)(128)(4,1)}), s8[4194304]{0:T(1024)(128)(4,1)S(1)}, s32[]{:S(2)}) async-start(s8[8388608]{0:T(1024)(128)(4,1)} %bitcast.410), calls=%async_computation.14 | async-start | bytes 8388608
  278.6 6.9 %slice-start.5 = ((s8[8388608]{0:T(1024)(128)(4,1)}), s8[4194304]{0:T(1024)(128)(4,1)S(1)}, s32[]{:S(2)}) async-start(s8[8388608]{0:T(1024)(128)(4,1)} %bitcast.410), calls=%async_computation.15 | async-start | bytes 8388608
  332.7 125.1 %reduce-scatter.14.cloned.1.call-start = ((), (), s32[]{:S(2)}) async-start(), calls=%async_computation.9 | async-start | bytes 655360 | tf_op jit(solution)/shard_map/reduce_scatter | solution.py:73
  362.8 26.9 %slice-start.6 = ((s8[8388608]{0:T(1024)(128)(4,1)}), s8[4194304]{0:T(1024)(128)(4,1)S(1)}, s32[]{:S(2)}) async-start(s8[8388608]{0:T(1024)(128)(4,1)} %bitcast.412), calls=%async_computation.16 | async-start | bytes 8388608
  382.8 6.9 %slice-start.7 = ((s8[8388608]{0:T(1024)(128)(4,1)}), s8[4194304]{0:T(1024)(128)(4,1)S(1)}, s32[]{:S(2)}) async-start(s8[8388608]{0:T(1024)(128)(4,1)} %bitcast.412), calls=%async_computation.17 | async-start | bytes 8388608
  465.9 27.8 %slice-start.8 = ((s8[8388608]{0:T(1024)(128)(4,1)}), s8[4194304]{0:T(1024)(128)(4,1)S(1)}, s32[]{:S(2)}) async-start(s8[8388608]{0:T(1024)(128)(4,1)} %bitcast.414), calls=%async_computation.18 | async-start | bytes 8388608
  486.8 6.9 %slice-start.9 = ((s8[8388608]{0:T(1024)(128)(4,1)}), s8[4194304]{0:T(1024)(128)(4,1)S(1)}, s32[]{:S(2)}) async-start(s8[8388608]{0:T(1024)(128)(4,1)} %bitcast.414), calls=%async_computation.19 | async-start | bytes 8388608
Sparse Core Ops, SparseCore 0:
  16.7 24.3 reduce-scatter.5
  124.5 20.9 reduce-scatter.7
  228.7 20.8 reduce-scatter.9
  332.8 20.8 reduce-scatter.11
  437.0 20.7 reduce-scatter.13
where the time goes:
time: 546 us; the launch traced here: 537 us
  blocking collectives  269 us (49%)
  matrix products  120 us (22%)
  waiting for transfers between devices  106 us (19%)
  between operations  21.3 us (4%)
  other arithmetic  15 us (3%)
  local copies, waits for them, and re-layouts  5.9 us (1%)
    psum x5, blocking collectives, on_device(): lax.psum((jnp.sum(direction * direction), jnp.sum(image * image)), ('freq...  153 us
    reduce_scatter x5, waiting for transfers between devices, on_device(): lax.psum_scatter(jnp.stack([partial_real, partial_imag]).astype(jnp.bfloa...  106 us
    all_gather x5, blocking collectives, on_device(): add_segment = lax.all_gather(rounded_direction, 'recv', axis=3, tiled=True)  80.4 us
    all_gather x5, blocking collectives, on_device(): lax.all_gather(flattened.astype(jnp.bfloat16), 'freq', axis=1, tiled=True)  35.5 us
    dot_general x40, matrix products, high_dot(): return jnp.dot(left, right, precision=lax.Precision.HIGHEST)  19.7 us
    dot_general x5, matrix products, on_device(): jnp.einsum('fbs,frs->fbr', add_segment[0], imag_operator, preferred_eleme...  17.6 us
    dot_general x5, matrix products, on_device(): jnp.einsum('fbs,frs->fbr', add_segment[1], imag_operator, preferred_eleme...  16.9 us
    dot_general x5, matrix products, on_device(): jnp.einsum('fbr,frs->fbs', rounded_residual[1], imag_operator, preferred_...  14.7 us
  transfers between devices with their start and end apart: 5, of which 5 were waited for; matrix products, arithmetic and copies ran while one was open for 0% of the time, Pallas kernels for 0%

commit v1 on v0

v1 whole, which is shorter than its diff:
```python
import math

import jax
import jax.numpy as jnp
from jax import lax
from jax.sharding import PartitionSpec as P

SBLK = 128
LINK_TYPE = jnp.float32
ITERS = 5


def high_dot(left, right):
    return jnp.dot(left, right, precision=lax.Precision.HIGHEST)


def dft_rows(row_ids, length):
    positions = jnp.arange(length, dtype=jnp.int32)
    phases = (row_ids[:, None] * positions[None, :] % length).astype(jnp.float32) * (
        2.0 * math.pi / length
    )
    normalizer = 1.0 / math.sqrt(length)
    return (jnp.cos(phases) * normalizer, jnp.sin(phases) * normalizer)


def window_mask(column_ids, src_local, win_start, win_end, length):
    blocks = win_start.shape[1]
    side_ids = column_ids // src_local
    source_ids = lax.axis_index("recv") * src_local + column_ids % src_local
    flat_ids = side_ids * blocks + source_ids // SBLK
    table_ids = jnp.arange(win_start.shape[0] * blocks, dtype=jnp.int32)
    matches = flat_ids[:, None] == table_ids[None, :]
    opening = jnp.sum(jnp.where(matches, win_start.reshape(-1)[None, :], 0), axis=1)
    closing = jnp.sum(jnp.where(matches, win_end.reshape(-1)[None, :], 0), axis=1)
    samples = jnp.arange(length, dtype=jnp.int32)[:, None]
    return ((samples >= opening[None, :]) & (samples < closing[None, :])).astype(jnp.float32)


def adjoint(res, real_operator, imag_operator):
    real_part = jnp.einsum(
        "fbr,frs->fbs", res[0], real_operator, preferred_element_type=jnp.float32
    ) + jnp.einsum("fbr,frs->fbs", res[1], imag_operator, preferred_element_type=jnp.float32)
    imag_part = jnp.einsum(
        "fbr,frs->fbs", res[1], real_operator, preferred_element_type=jnp.float32
    ) - jnp.einsum("fbr,frs->fbs", res[0], imag_operator, preferred_element_type=jnp.float32)
    return jnp.stack([real_part, imag_part])


def split_adjoint(values, real_operator, imag_operator):
    high, low = split_high_low(values)
    doubled = adjoint(jnp.concatenate([high, low], axis=2), real_operator, imag_operator)
    rows = values.shape[2]
    return doubled[:, :, :rows] + doubled[:, :, rows:]


def forward(direction, real_operator, imag_operator):
    real_part = jnp.einsum(
        "fbs,frs->fbr", direction[0], real_operator, preferred_element_type=jnp.float32
    ) - jnp.einsum("fbs,frs->fbr", direction[1], imag_operator, preferred_element_type=jnp.float32)
    imag_part = jnp.einsum(
        "fbs,frs->fbr", direction[0], imag_operator, preferred_element_type=jnp.float32
    ) + jnp.einsum("fbs,frs->fbr", direction[1], real_operator, preferred_element_type=jnp.float32)
    return jnp.stack([real_part, imag_part])


def split_high_low(values):
    high = lax.reduce_precision(values, exponent_bits=8, mantissa_bits=7)
    return high.astype(jnp.bfloat16), (values - high).astype(jnp.bfloat16)


def split_parts(values):
    pieces = []
    for value in values:
        high = lax.reduce_precision(value, exponent_bits=8, mantissa_bits=7)
        rest = value - high
        middle = lax.reduce_precision(rest, exponent_bits=8, mantissa_bits=7)
        pieces += [high, middle, rest - middle]
    return jnp.stack(pieces)


def reduce_gather(partial):
    scattered = lax.psum_scatter(
        partial.astype(LINK_TYPE), "recv", scatter_dimension=3, tiled=True
    )
    flat = scattered.reshape(scattered.shape[0], scattered.shape[1], -1)
    return lax.all_gather(flat, "freq", axis=1, tiled=True).astype(jnp.float32)


def gather_sources(block, values):
    src_local = block.shape[-1]
    recv_size = lax.axis_size("recv")
    rows = jnp.concatenate(split_high_low(block.reshape(-1, src_local)))
    pieces = split_parts(values)
    extra = jnp.zeros((16, src_local), jnp.float32).at[0, : pieces.shape[0]].set(pieces)
    payload = jnp.concatenate([rows, extra.astype(jnp.bfloat16)])
    gathered = lax.all_gather(payload, "recv", axis=1, tiled=True)
    count = rows.shape[0]
    half = count // 2
    joined = gathered[:half].astype(jnp.float32) + gathered[half:count].astype(jnp.float32)
    full = joined.reshape(block.shape[:-1] + (recv_size * src_local,))
    tail = gathered[count].reshape(recv_size, src_local)[:, : pieces.shape[0]].astype(jnp.float32)
    sums = jnp.sum(tail.reshape(recv_size, len(values), 3), axis=(0, 2))
    return full, sums


def on_device(operator, recorded, win_start, win_end):
    freq_local = operator.shape[1]
    sources = operator.shape[3]
    right_sides = recorded.shape[2]
    src_local = sources // lax.axis_size("recv")
    total_freq = freq_local * lax.axis_size("freq")
    columns = right_sides * src_local
    real_operator = operator[0]
    imag_operator = operator[1]

    cos_all, sin_all = dft_rows(jnp.arange(total_freq, dtype=jnp.int32), total_freq)
    own_rows = lax.axis_index("freq") * freq_local + jnp.arange(freq_local, dtype=jnp.int32)
    cos_own, sin_own = dft_rows(own_rows, total_freq)
    window = window_mask(
        jnp.arange(columns, dtype=jnp.int32), src_local, win_start, win_end, total_freq
    )
    block_shape = (2, freq_local, right_sides, src_local)

    def to_time(spectrum):
        time_real = high_dot(cos_all.T, spectrum[0]) - high_dot(sin_all.T, spectrum[1])
        time_imag = high_dot(sin_all.T, spectrum[0]) + high_dot(cos_all.T, spectrum[1])
        return time_real, time_imag

    def to_own_freq(kept_real, kept_imag):
        real_part = high_dot(cos_own, kept_real) + high_dot(sin_own, kept_imag)
        imag_part = high_dot(cos_own, kept_imag) - high_dot(sin_own, kept_real)
        return jnp.stack([real_part, imag_part]).reshape(block_shape)

    gradient = reduce_gather(split_adjoint(recorded, real_operator, imag_operator))
    time_real, time_imag = to_time(gradient)
    kept_real = time_real * window
    kept_imag = time_imag * window
    kept_power = jnp.sum(kept_real * kept_real + kept_imag * kept_imag)
    direction_own = to_own_freq(kept_real, kept_imag)
    direction_all, sums = gather_sources(direction_own, [kept_power])
    direction_power = sums[0]

    reflect = jnp.zeros(block_shape, jnp.float32)
    residual = recorded
    for iteration in range(ITERS):
        image = forward(direction_all.astype(jnp.bfloat16), real_operator, imag_operator)
        if iteration < ITERS - 1:
            normal = reduce_gather(split_adjoint(image, real_operator, imag_operator))
            normal_real, normal_imag = to_time(normal)
            image_part = jnp.sum(kept_real * normal_real + kept_imag * normal_imag)
            masked_real = normal_real * window
            masked_imag = normal_imag * window
            change_own = to_own_freq(masked_real, masked_imag)
            values = [image_part] if iteration == 0 else [image_part, kept_power]
            change_all, sums = gather_sources(change_own, values)
            image_energy = sums[0]
            if iteration > 0:
                direction_power = sums[1]
            step_length = direction_power / (image_energy + 1e-06)
            reflect = reflect + step_length * direction_own
            residual = residual - step_length * image
            direction_all = direction_all - step_length * change_all
            direction_own = direction_own - step_length * change_own
            kept_real = kept_real - step_length * masked_real
            kept_imag = kept_imag - step_length * masked_imag
            kept_power = jnp.sum(kept_real * kept_real + kept_imag * kept_imag)
        else:
            own_power = jnp.where(lax.axis_index("freq") == 0, kept_power, 0.0)
            direction_power, image_energy = lax.psum(
                (own_power, jnp.sum(image * image)), ("freq", "recv")
            )
            step_length = direction_power / (image_energy + 1e-06)
            reflect = reflect + step_length * direction_own
            residual = residual - step_length * image
    return (reflect, residual)


def solution(mesh):
    return jax.shard_map(
        on_device,
        mesh=mesh,
        in_specs=(
            P("groups", "freq", "recv", None),
            P("groups", "freq", None, "recv"),
            P("groups", None),
            P("groups", None),
        ),
        out_specs=(P("groups", "freq", None, "recv"), P("groups", "freq", None, "recv")),
        check_vma=False,
    )
```

time: 546 us -> 644 us (1.18)
  waiting for transfers between devices: 106 us -> 353 us
  blocking collectives: 269 us -> 32.6 us
  between operations: 21.3 us -> 61.4 us
  matrix products: 120 us -> 136 us
  local copies, waits for them, and re-layouts: 5.9 us -> 21.9 us
  other arithmetic: 15 us -> 28.9 us
    all_gather x0 -> x10, waiting for transfers between devices: none -> 216 us  [the longest x5 139 us: gather_sources(): gathered = lax.all_gather(payload, 'recv', axis=1, tiled=True)]
    psum x5 -> x1, blocking collectives: 153 us -> 32.6 us  [on_device(): lax.psum((own_power, jnp.sum(image * image)), ('freq', 'recv'))]
    all_gather x10 -> x0, blocking collectives: 116 us -> none  [the longest x5 80.4 us: on_device(): add_segment = lax.all_gather(rounded_direction, 'recv', axis=3, tiled=True)]
    dot_general x40, matrix products: 19.7 us -> 55 us  [high_dot(): return jnp.dot(left, right, precision=lax.Precision.HIGHEST)]
    reduce_scatter x5, waiting for transfers between devices: 106 us -> 137 us  [reduce_gather(): lax.psum_scatter(partial.astype(LINK_TYPE), 'recv', scatter_dimension=3,...]
    dot_general x40, matrix products: 99.8 us -> 80.6 us  [the longest x5 17.2 us: forward(): jnp.einsum('fbs,frs->fbr', direction[1], imag_operator, preferred_element...]
    convert_element_type x6 -> x15, other arithmetic: 1.58 us -> 11.1 us  [the longest x5 8.38 us: on_device(): direction_all.astype(jnp.bfloat16)]
    reshape x0 -> x5, local copies, waits for them, and re-layouts: none -> 8.52 us  [reduce_gather(): flat = scattered.reshape(scattered.shape[0], scattered.shape[1], -1)]
  transfers between devices with their start and end apart: 5 -> 15, of which waited for: 5 -> 15; matrix products, arithmetic and copies ran while one was open for 0% -> 1% of each run, Pallas kernels for 0% -> 0%
where the time goes in v1:
time: 644 us; the launch traced here: 635 us
  waiting for transfers between devices  353 us (55%)
  matrix products  136 us (21%)
  between operations  61.4 us (10%)
  blocking collectives  32.6 us (5%)
  other arithmetic  28.9 us (4%)
  local copies, waits for them, and re-layouts  21.9 us (3%)
    all_gather x5, waiting for transfers between devices, gather_sources(): gathered = lax.all_gather(payload, 'recv', axis=1, tiled=True)  139 us
    reduce_scatter x5, waiting for transfers between devices, reduce_gather(): lax.psum_scatter(partial.astype(LINK_TYPE), 'recv', scatter_dimension=3,...  137 us
    all_gather x5, waiting for transfers between devices, reduce_gather(): return lax.all_gather(flat, 'freq', axis=1, tiled=True).astype(jnp.float32)  76.5 us
    dot_general x40, matrix products, high_dot(): return jnp.dot(left, right, precision=lax.Precision.HIGHEST)  55 us
    psum x1, blocking collectives, on_device(): lax.psum((own_power, jnp.sum(image * image)), ('freq', 'recv'))  32.6 us
    dot_general x5, matrix products, forward(): jnp.einsum('fbs,frs->fbr', direction[1], imag_operator, preferred_element...  17.2 us
    dot_general x5, matrix products, forward(): jnp.einsum('fbs,frs->fbr', direction[1], real_operator, preferred_element...  17.2 us
    dot_general x5, matrix products, forward(): jnp.einsum('fbs,frs->fbr', direction[0], imag_operator, preferred_element...  17.2 us
  transfers between devices with their start and end apart: 15, of which 15 were waited for; matrix products, arithmetic and copies ran while one was open for 1% of the time, Pallas kernels for 0%

profile of v1, /device:TPU:0, one launch (start us, length us, event | category | flops | bytes accessed | tf_op | source)
XLA Modules:
  0.0 635.1 jit_solution(10183816585812269567)
XLA Ops:
  8.1 3.0 fusion.38
  11.1 3.4 fusion.40
  17.0 29.9 %reduce-scatter.6.cloned.1.call-done = f32[2,8,8,512]{3,2,1,0:T(8,128)} async-done(((f32[2,8,8,2048]{3,2,1,0:T(8,128)}), f32[2,8,8,512]{3,2,1,0:T(8,128)}) %reduce-scatter.6.cloned.1.call-update) | async-done | bytes 262160 | tf_op jit(solution)/shard_map/reduce_scatter | solution.py:82
  48.9 1.8 select_reduce_fusion.1
  50.8 13.8 %all-gather.11.cloned.1.call-done = f32[2,32,4096]{2,1,0:T(8,128)} async-done(((f32[2,8,4096]{2,1,0:T(8,128)}), f32[2,32,4096]{2,1,0:T(8,128)}) %all-gather.11.cloned.1.call-update) | async-done | bytes 1048592 | tf_op jit(solution)/shard_map/all_gather | solution.py:86
  68.0 1.8 fusion.1
  69.9 2.5 add_reduce_fusion.8
  80.4 28.9 %all-gather.13.cloned.1.call-done = bf16[272,2048]{1,0:T(8,128)(2,1)} async-done(((bf16[272,512]{1,0:T(8,128)(2,1)}), bf16[272,2048]{1,0:T(8,128)(2,1)}) %all-gather.13.cloned.1.call-update) | async-done | bytes 1114128 | tf_op jit(solution)/shard_map/all_gather | solution.py:96
  110.6 3.5 fusion.34
  114.1 3.4 fusion.36
  117.5 3.5 fusion.151
  121.1 3.4 fusion.145
  128.4 26.7 %reduce-scatter.8.cloned.1.call-done = f32[2,8,8,512]{3,2,1,0:T(8,128)} async-done(((f32[2,8,8,2048]{3,2,1,0:T(8,128)}), f32[2,8,8,512]{3,2,1,0:T(8,128)}) %reduce-scatter.8.cloned.1.call-update) | async-done | bytes 262160 | tf_op jit(solution)/shard_map/reduce_scatter | solution.py:82
  156.9 15.6 %all-gather.15.cloned.1.call-done = f32[2,32,4096]{2,1,0:T(8,128)} async-done(((f32[2,8,4096]{2,1,0:T(8,128)}), f32[2,32,4096]{2,1,0:T(8,128)}) %all-gather.15.cloned.1.call-update) | async-done | bytes 1048592 | tf_op jit(solution)/shard_map/all_gather | solution.py:86
  176.0 1.7 convolution_subtract_fusion.3
  177.8 2.4 add_reduce_fusion.7
  190.7 27.3 %all-gather.17.cloned.1.call-done = bf16[272,2048]{1,0:T(8,128)(2,1)} async-done(((bf16[272,512]{1,0:T(8,128)(2,1)}), bf16[272,2048]{1,0:T(8,128)(2,1)}) %all-gather.17.cloned.1.call-update) | async-done | bytes 1114128 | tf_op jit(solution)/shard_map/all_gather | solution.py:96
  220.7 2.0 fusion.606
  222.8 3.4 fusion.26
  226.2 3.5 fusion.28
  229.7 3.4 fusion.163
  238.3 26.7 %reduce-scatter.10.cloned.1.call-done = f32[2,8,8,512]{3,2,1,0:T(8,128)} async-done(((f32[2,8,8,2048]{3,2,1,0:T(8,128)}), f32[2,8,8,512]{3,2,1,0:T(8,128)}) %reduce-scatter.10.cloned.1.call-update) | async-done | bytes 262160 | tf_op jit(solution)/shard_map/reduce_scatter | solution.py:82
  266.8 15.9 %all-gather.19.cloned.1.call-done = f32[2,32,4096]{2,1,0:T(8,128)} async-done(((f32[2,8,4096]{2,1,0:T(8,128)}), f32[2,32,4096]{2,1,0:T(8,128)}) %all-gather.19.cloned.1.call-update) | async-done | bytes 1048592 | tf_op jit(solution)/shard_map/all_gather | solution.py:86
  286.1 1.8 convolution_subtract_fusion.2
  287.9 3.9 add_reduce_fusion.5
  307.4 28.9 %all-gather.21.cloned.1.call-done = bf16[272,2048]{1,0:T(8,128)(2,1)} async-done(((bf16[272,512]{1,0:T(8,128)(2,1)}), bf16[272,2048]{1,0:T(8,128)(2,1)}) %all-gather.21.cloned.1.call-update) | async-done | bytes 1114128 | tf_op jit(solution)/shard_map/all_gather | solution.py:96
  340.8 3.4 fusion.18
  344.2 3.5 fusion.20
  347.8 3.4 fusion.175
  356.3 26.7 %reduce-scatter.12.cloned.1.call-done = f32[2,8,8,512]{3,2,1,0:T(8,128)} async-done(((f32[2,8,8,2048]{3,2,1,0:T(8,128)}), f32[2,8,8,512]{3,2,1,0:T(8,128)}) %reduce-scatter.12.cloned.1.call-update) | async-done | bytes 262160 | tf_op jit(solution)/shard_map/reduce_scatter | solution.py:82
  384.9 15.8 %all-gather.23.cloned.1.call-done = f32[2,32,4096]{2,1,0:T(8,128)} async-done(((f32[2,8,4096]{2,1,0:T(8,128)}), f32[2,32,4096]{2,1,0:T(8,128)}) %all-gather.23.cloned.1.call-update) | async-done | bytes 1048592 | tf_op jit(solution)/shard_map/all_gather | solution.py:86
  404.1 1.7 convolution_subtract_fusion.1
  405.9 3.9 add_reduce_fusion.3
  422.7 28.9 %all-gather.25.cloned.1.call-done = bf16[272,2048]{1,0:T(8,128)(2,1)} async-done(((bf16[272,512]{1,0:T(8,128)(2,1)}), bf16[272,2048]{1,0:T(8,128)(2,1)}) %all-gather.25.cloned.1.call-update) | async-done | bytes 1114128 | tf_op jit(solution)/shard_map/all_gather | solution.py:96
  454.6 2.1 fusion.605
  456.7 3.5 fusion.10
  460.2 3.4 fusion.12
  463.6 3.4 fusion.187
  472.2 26.7 %reduce-scatter.14.cloned.1.call-done = f32[2,8,8,512]{3,2,1,0:T(8,128)} async-done(((f32[2,8,8,2048]{3,2,1,0:T(8,128)}), f32[2,8,8,512]{3,2,1,0:T(8,128)}) %reduce-scatter.14.cloned.1.call-update) | async-done | bytes 262160 | tf_op jit(solution)/shard_map/reduce_scatter | solution.py:82
  500.9 15.5 %all-gather.27.cloned.1.call-done = f32[2,32,4096]{2,1,0:T(8,128)} async-done(((f32[2,8,4096]{2,1,0:T(8,128)}), f32[2,32,4096]{2,1,0:T(8,128)}) %all-gather.27.cloned.1.call-update) | async-done | bytes 1048592 | tf_op jit(solution)/shard_map/all_gather | solution.py:86
  519.9 1.7 convolution_subtract_fusion
  521.6 3.9 add_reduce_fusion.1
  547.1 25.1 %all-gather.29.cloned.1.call-done = bf16[272,2048]{1,0:T(8,128)(2,1)} async-done(((bf16[272,512]{1,0:T(8,128)(2,1)}), bf16[272,2048]{1,0:T(8,128)(2,1)}) %all-gather.29.cloned.1.call-update) | async-done | bytes 1114128 | tf_op jit(solution)/shard_map/all_gather | solution.py:96
  576.6 3.4 fusion.2
  579.9 3.4 fusion.4
  583.3 3.5 fusion.199
  586.9 3.5 fusion.193
  592.7 32.6 %all-reduce.5 = (f32[]{:T(128)}, f32[]{:T(128)}) all-reduce(f32[]{:T(128)S(6)} %select_n.95, f32[]{:T(128)} %multiply_reduce_fusion), channel_id=1, replica_groups=mesh['groups'=2,'freq'=4,'recv'=4] {'freq','recv'}, use_global_device_ids=true, to_apply=%region_24.25 | all-reduce | flops 2 | bytes 16 | tf_op jit(solution)/shard_map/psum | solution.py:169
  (260 shorter events, 92.4 us)
Async XLA Ops:
  7.2 39.8 %reduce-scatter.6.cloned.1.call-start = ((), (), s32[]{:S(2)}) async-start(), calls=%async_computation.5 | async-start | bytes 1310720 | tf_op jit(solution)/shard_map/reduce_scatter | solution.py:82
  15.1 33.6 %copy-start.35 = (s32[8,16]{1,0:T(8,128)S(1)}, s32[8,16]{1,0:T(8,128)}, u32[]{:S(2)}) copy-start(s32[8,16]{1,0:T(8,128)} %param.16) | copy-start | bytes 1540
  15.1 33.7 %copy-start.36 = (s32[8,16]{1,0:T(8,128)S(1)}, s32[8,16]{1,0:T(8,128)}, u32[]{:S(2)}) copy-start(s32[8,16]{1,0:T(8,128)} %param.17) | copy-start | bytes 1540
  16.9 47.6 %all-gather.11.cloned.1.call-start = ((), (), s32[]{:S(2)}) async-start(), calls=%async_computation.6 | async-start | bytes 1310720 | tf_op jit(solution)/shard_map/all_gather | solution.py:86
  48.6 60.6 %all-gather.13.cloned.1.call-start = ((), (), s32[]{:S(2)}) async-start(), calls=%async_computation.7 | async-start | bytes 1392640 | tf_op jit(solution)/shard_map/all_gather | solution.py:96
  80.1 75.0 %reduce-scatter.8.cloned.1.call-start = ((), (), s32[]{:S(2)}) async-start(), calls=%async_computation.8 | async-start | bytes 1310720 | tf_op jit(solution)/shard_map/reduce_scatter | solution.py:82
  110.6 13.9 %slice-start = ((s8[8388608]{0:T(1024)(128)(4,1)}), s8[4194304]{0:T(1024)(128)(4,1)S(1)}, s32[]{:S(2)}) async-start(s8[8388608]{0:T(1024)(128)(4,1)} %bitcast.400), calls=%async_computation.20 | async-start | bytes 8388608
  128.4 44.2 %all-gather.15.cloned.1.call-start = ((), (), s32[]{:S(2)}) async-start(), calls=%async_computation.9 | async-start | bytes 1310720 | tf_op jit(solution)/shard_map/all_gather | solution.py:86
  156.9 61.1 %all-gather.17.cloned.1.call-start = ((), (), s32[]{:S(2)}) async-start(), calls=%async_computation.10 | async-start | bytes 1392640 | tf_op jit(solution)/shard_map/all_gather | solution.py:96
  180.2 42.6 %copy-start.2 = (f32[32,4096]{1,0:T(8,128)}, f32[32,4096]{1,0:T(8,128)S(1)}, u32[]{:S(2)}) copy-start(f32[32,4096]{1,0:T(8,128)S(1)} %get-tuple-element.111) | copy-start | bytes 1572868
  188.8 76.2 %reduce-scatter.10.cloned.1.call-start = ((), (), s32[]{:S(2)}) async-start(), calls=%async_computation.11 | async-start | bytes 1310720 | tf_op jit(solution)/shard_map/reduce_scatter | solution.py:82
  220.7 12.4 %slice-start.2 = ((s8[8388608]{0:T(1024)(128)(4,1)}), s8[4194304]{0:T(1024)(128)(4,1)S(1)}, s32[]{:S(2)}) async-start(s8[8388608]{0:T(1024)(128)(4,1)} %bitcast.402), calls=%async_computation.22 | async-start | bytes 8388608
  238.2 44.4 %all-gather.19.cloned.1.call-start = ((), (), s32[]{:S(2)}) async-start(), calls=%async_computation.12 | async-start | bytes 1310720 | tf_op jit(solution)/shard_map/all_gather | solution.py:86
  266.7 69.6 %all-gather.21.cloned.1.call-start = ((), (), s32[]{:S(2)}) async-start(), calls=%async_computation.13 | async-start | bytes 1392640 | tf_op jit(solution)/shard_map/all_gather | solution.py:96
  304.5 39.7 %copy-start.9 = (f32[8,4096]{1,0:T(8,128)}, f32[8,4096]{1,0:T(8,128)S(1)}, u32[]{:S(2)}) copy-start(f32[8,4096]{1,0:T(8,128)S(1)} %convolution_subtract_fusion.7) | copy-start | bytes 393220
  306.2 38.1 %copy-start.11 = (f32[8,4096]{1,0:T(8,128)}, f32[8,4096]{1,0:T(8,128)S(1)}, u32[]{:S(2)}) copy-start(f32[8,4096]{1,0:T(8,128)S(1)} %convolution_add_fusion.7) | copy-start | bytes 393220
  307.2 75.9 %reduce-scatter.12.cloned.1.call-start = ((), (), s32[]{:S(2)}) async-start(), calls=%async_computation.14 | async-start | bytes 1310720 | tf_op jit(solution)/shard_map/reduce_scatter | solution.py:82
  339.3 11.9 %slice-start.4 = ((s8[8388608]{0:T(1024)(128)(4,1)}), s8[4194304]{0:T(1024)(128)(4,1)S(1)}, s32[]{:S(2)}) async-start(s8[8388608]{0:T(1024)(128)(4,1)} %bitcast.404), calls=%async_computation.24 | async-start | bytes 8388608
  355.1 50.7 %copy-start.1 = (f32[32,4096]{1,0:T(8,128)S(1)}, f32[32,4096]{1,0:T(8,128)}, u32[]{:S(2)}) copy-start(f32[32,4096]{1,0:T(8,128)} %get-tuple-element.112) | copy-start | bytes 1572868
  356.3 44.3 %all-gather.23.cloned.1.call-start = ((), (), s32[]{:S(2)}) async-start(), calls=%async_computation.15 | async-start | bytes 1310720 | tf_op jit(solution)/shard_map/all_gather | solution.py:86
  384.8 66.8 %all-gather.25.cloned.1.call-start = ((), (), s32[]{:S(2)}) async-start(), calls=%async_computation.16 | async-start | bytes 1392640 | tf_op jit(solution)/shard_map/all_gather | solution.py:96
  420.9 33.6 %copy-start.13 = (f32[8,4096]{1,0:T(8,128)}, f32[8,4096]{1,0:T(8,128)S(1)}, u32[]{:S(2)}) copy-start(f32[8,4096]{1,0:T(8,128)S(1)} %convolution_subtract_fusion.6) | copy-start | bytes 393220
  421.5 33.1 %copy-start.15 = (f32[8,4096]{1,0:T(8,128)}, f32[8,4096]{1,0:T(8,128)S(1)}, u32[]{:S(2)}) copy-start(f32[8,4096]{1,0:T(8,128)S(1)} %convolution_add_fusion.6) | copy-start | bytes 393220
  422.4 76.4 %reduce-scatter.14.cloned.1.call-start = ((), (), s32[]{:S(2)}) async-start(), calls=%async_computation.17 | async-start | bytes 1310720 | tf_op jit(solution)/shard_map/reduce_scatter | solution.py:82
  454.6 12.4 %slice-start.6 = ((s8[8388608]{0:T(1024)(128)(4,1)}), s8[4194304]{0:T(1024)(128)(4,1)S(1)}, s32[]{:S(2)}) async-start(s8[8388608]{0:T(1024)(128)(4,1)} %bitcast.406), calls=%async_computation.26 | async-start | bytes 8388608
  456.6 10.3 %slice-start.7 = ((s8[8388608]{0:T(1024)(128)(4,1)}), s8[4194304]{0:T(1024)(128)(4,1)S(1)}, s32[]{:S(2)}) async-start(s8[8388608]{0:T(1024)(128)(4,1)} %bitcast.406), calls=%async_computation.27 | async-start | bytes 8388608
  472.1 44.3 %all-gather.27.cloned.1.call-start = ((), (), s32[]{:S(2)}) async-start(), calls=%async_computation.18 | async-start | bytes 1310720 | tf_op jit(solution)/shard_map/all_gather | solution.py:86
  500.6 71.6 %all-gather.29.cloned.1.call-start = ((), (), s32[]{:S(2)}) async-start(), calls=%async_computation.19 | async-start | bytes 1392640 | tf_op jit(solution)/shard_map/all_gather | solution.py:96
  525.6 17.7 %copy-start.6 = (f32[8,4096]{1,0:T(8,128)S(1)}, f32[8,4096]{1,0:T(8,128)}, u32[]{:S(2)}) copy-start(f32[8,4096]{1,0:T(8,128)} %copy-done.5) | copy-start | bytes 393220
  525.6 17.8 %copy-start.8 = (f32[8,4096]{1,0:T(8,128)S(1)}, f32[8,4096]{1,0:T(8,128)}, u32[]{:S(2)}) copy-start(f32[8,4096]{1,0:T(8,128)} %copy-done.7) | copy-start | bytes 393220
  525.6 17.9 %copy-start.10 = (f32[8,4096]{1,0:T(8,128)S(1)}, f32[8,4096]{1,0:T(8,128)}, u32[]{:S(2)}) copy-start(f32[8,4096]{1,0:T(8,128)} %copy-done.9) | copy-start | bytes 393220
  525.6 18.6 %copy-start.12 = (f32[8,4096]{1,0:T(8,128)S(1)}, f32[8,4096]{1,0:T(8,128)}, u32[]{:S(2)}) copy-start(f32[8,4096]{1,0:T(8,128)} %copy-done.11) | copy-start | bytes 393220
  525.6 19.3 %copy-start.14 = (f32[8,4096]{1,0:T(8,128)S(1)}, f32[8,4096]{1,0:T(8,128)}, u32[]{:S(2)}) copy-start(f32[8,4096]{1,0:T(8,128)} %copy-done.13) | copy-start | bytes 393220
  525.6 20.1 %copy-start.16 = (f32[8,4096]{1,0:T(8,128)S(1)}, f32[8,4096]{1,0:T(8,128)}, u32[]{:S(2)}) copy-start(f32[8,4096]{1,0:T(8,128)} %copy-done.15) | copy-start | bytes 393220
  583.3 7.1 %copy-start.3 = (f32[32,4096]{1,0:T(8,128)S(1)}, f32[32,4096]{1,0:T(8,128)}, u32[]{:S(2)}) copy-start(f32[32,4096]{1,0:T(8,128)} %get-tuple-element.72) | copy-start | bytes 1572868
  583.3 7.1 %copy-start.4 = (f32[32,4096]{1,0:T(8,128)S(1)}, f32[32,4096]{1,0:T(8,128)}, u32[]{:S(2)}) copy-start(f32[32,4096]{1,0:T(8,128)} %get-tuple-element.73) | copy-start | bytes 1572868
  586.8 39.7 %copy-start.25 = (f32[1,8,8,128]{3,2,1,0:T(8,128)S(1)}, f32[1,8,8,128]{3,2,1,0:T(8,128)}, u32[]{:S(2)}) copy-start(f32[1,8,8,128]{3,2,1,0:T(8,128)} %copy-done.24) | copy-start | bytes 98308
  586.8 39.7 %copy-start.27 = (f32[1,8,8,128]{3,2,1,0:T(8,128)S(1)}, f32[1,8,8,128]{3,2,1,0:T(8,128)}, u32[]{:S(2)}) copy-start(f32[1,8,8,128]{3,2,1,0:T(8,128)} %copy-done.26) | copy-start | bytes 98308
  586.8 39.7 %copy-start.29 = (f32[1,8,8,128]{3,2,1,0:T(8,128)S(1)}, f32[1,8,8,128]{3,2,1,0:T(8,128)}, u32[]{:S(2)}) copy-start(f32[1,8,8,128]{3,2,1,0:T(8,128)} %copy-done.28) | copy-start | bytes 98308
  586.8 39.7 %copy-start.31 = (f32[1,8,8,128]{3,2,1,0:T(8,128)S(1)}, f32[1,8,8,128]{3,2,1,0:T(8,128)}, u32[]{:S(2)}) copy-start(f32[1,8,8,128]{3,2,1,0:T(8,128)} %copy-done.30) | copy-start | bytes 98308
  586.8 39.7 %copy-start.33 = (f32[1,8,8,128]{3,2,1,0:T(8,128)S(1)}, f32[1,8,8,128]{3,2,1,0:T(8,128)}, u32[]{:S(2)}) copy-start(f32[1,8,8,128]{3,2,1,0:T(8,128)} %copy-done.32) | copy-start | bytes 98308
  586.8 39.7 %copy-start.34 = (f32[2,8,8,128]{3,2,1,0:T(8,128)S(1)}, f32[2,8,8,128]{3,2,1,0:T(8,128)}, u32[]{:S(2)}) copy-start(f32[2,8,8,128]{3,2,1,0:T(8,128)} %param.15) | copy-start | bytes 196612
  586.9 40.3 %copy-start.18 = (f32[2,8,8,512]{3,2,1,0:T(8,128)S(1)}, f32[2,8,8,512]{3,2,1,0:T(8,128)}, u32[]{:S(2)}) copy-start(f32[2,8,8,512]{3,2,1,0:T(8,128)} %copy-done.17) | copy-start | bytes 786436
  586.9 40.3 %copy-start.19 = (f32[1,8,8,512]{3,2,1,0:T(8,128)S(1)}, f32[1,8,8,512]{3,2,1,0:T(8,128)}, u32[]{:S(2)}) copy-start(f32[1,8,8,512]{3,2,1,0:T(8,128)} %copy.21) | copy-start | bytes 393220
  586.9 40.3 %copy-start.20 = (f32[1,8,8,512]{3,2,1,0:T(8,128)S(1)}, f32[1,8,8,512]{3,2,1,0:T(8,128)}, u32[]{:S(2)}) copy-start(f32[1,8,8,512]{3,2,1,0:T(8,128)} %copy.20) | copy-start | bytes 393220
  586.9 40.3 %copy-start.21 = (f32[1,8,8,512]{3,2,1,0:T(8,128)S(1)}, f32[1,8,8,512]{3,2,1,0:T(8,128)}, u32[]{:S(2)}) copy-start(f32[1,8,8,512]{3,2,1,0:T(8,128)} %copy.23) | copy-start | bytes 393220
  586.9 40.3 %copy-start.22 = (f32[1,8,8,512]{3,2,1,0:T(8,128)S(1)}, f32[1,8,8,512]{3,2,1,0:T(8,128)}, u32[]{:S(2)}) copy-start(f32[1,8,8,512]{3,2,1,0:T(8,128)} %copy.22) | copy-start | bytes 393220
  586.9 40.3 %copy-start.23 = (f32[1,8,8,512]{3,2,1,0:T(8,128)S(1)}, f32[1,8,8,512]{3,2,1,0:T(8,128)}, u32[]{:S(2)}) copy-start(f32[1,8,8,512]{3,2,1,0:T(8,128)} %copy.25) | copy-start | bytes 393220
  (12 other events, 39.5 us)
Sparse Core Ops, SparseCore 0:
  17.1 29.8 reduce-scatter.5
  49.1 15.3 all-gather.10
  80.2 29.0 all-gather.12
  128.5 26.6 reduce-scatter.7
  157.1 15.3 all-gather.14
  189.0 29.0 all-gather.16
  238.3 26.6 reduce-scatter.9
  267.2 15.3 all-gather.18
  307.3 29.0 all-gather.20
  356.4 26.6 reduce-scatter.11
  385.2 15.3 all-gather.22
  422.6 29.0 all-gather.24
  472.2 26.6 reduce-scatter.13
  501.0 15.3 all-gather.26
  543.2 29.0 all-gather.28

commit v2 on v0

--- a/solution.py
+++ b/solution.py
@@ -60,16 +60,15 @@
     residual = recorded
     for iteration in range(ITERS):
         rounded_residual = residual.astype(jnp.bfloat16)
-        partial_real = jnp.einsum(
-            "fbr,frs->fbs", rounded_residual[0], real_operator, preferred_element_type=jnp.float32
-        ) + jnp.einsum(
-            "fbr,frs->fbs", rounded_residual[1], imag_operator, preferred_element_type=jnp.float32
+        stacked_residual = jnp.concatenate([rounded_residual[0], rounded_residual[1]], axis=1)
+        with_real = jnp.einsum(
+            "fbr,frs->fbs", stacked_residual, real_operator, preferred_element_type=jnp.float32
         )
-        partial_imag = jnp.einsum(
-            "fbr,frs->fbs", rounded_residual[1], real_operator, preferred_element_type=jnp.float32
-        ) - jnp.einsum(
-            "fbr,frs->fbs", rounded_residual[0], imag_operator, preferred_element_type=jnp.float32
+        with_imag = jnp.einsum(
+            "fbr,frs->fbs", stacked_residual, imag_operator, preferred_element_type=jnp.float32
         )
+        partial_real = with_real[:, :right_sides] + with_imag[:, right_sides:]
+        partial_imag = with_real[:, right_sides:] - with_imag[:, :right_sides]
         gradient = lax.psum_scatter(
             jnp.stack([partial_real, partial_imag]).astype(jnp.bfloat16),
             "recv",
@@ -94,19 +93,18 @@
         direction = projected.reshape(2, freq_local, right_sides, src_local)
         rounded_direction = direction.astype(jnp.bfloat16)
         add_segment = lax.all_gather(rounded_direction, "recv", axis=3, tiled=True)
-        image_real = jnp.einsum(
-            "fbs,frs->fbr", add_segment[0], real_operator, preferred_element_type=jnp.float32
-        ) - jnp.einsum(
-            "fbs,frs->fbr", add_segment[1], imag_operator, preferred_element_type=jnp.float32
+        stacked_direction = jnp.concatenate([add_segment[0], add_segment[1]], axis=1)
+        by_real = jnp.einsum(
+            "fbs,frs->fbr", stacked_direction, real_operator, preferred_element_type=jnp.float32
         )
-        image_imag = jnp.einsum(
-            "fbs,frs->fbr", add_segment[0], imag_operator, preferred_element_type=jnp.float32
-        ) + jnp.einsum(
-            "fbs,frs->fbr", add_segment[1], real_operator, preferred_element_type=jnp.float32
+        by_imag = jnp.einsum(
+            "fbs,frs->fbr", stacked_direction, imag_operator, preferred_element_type=jnp.float32
         )
+        image_real = by_real[:, :right_sides] - by_imag[:, right_sides:]
+        image_imag = by_imag[:, :right_sides] + by_real[:, right_sides:]
         image = jnp.stack([image_real, image_imag])
         direction_power, image_energy = lax.psum(
-            (jnp.sum(direction * direction), jnp.sum(image * image)), ("freq", "recv")
+            lax.psum((jnp.sum(direction * direction), jnp.sum(image * image)), "recv"), "freq"
         )
         step_length = direction_power / (image_energy + 1e-06)
         reflect = reflect + step_length * direction

time: 546 us -> 423 us (0.77)
  blocking collectives: 269 us -> 196 us
  matrix products: 120 us -> 71.1 us
    psum x5 -> x10, blocking collectives: 153 us -> 78.5 us  [the longest x5 47.2 us: on_device(): lax.psum((jnp.sum(direction * direction), jnp.sum(image * image)), 'recv')]
    dot_general x40 -> x20, matrix products: 99.8 us -> 51.4 us  [the longest x5 16.9 us: on_device(): jnp.einsum('fbs,frs->fbr', stacked_direction, imag_operator, preferred_el...]
where the time goes in v2:
time: 423 us; the launch traced here: 414 us
  blocking collectives  196 us (46%)
  waiting for transfers between devices  103 us (24%)
  matrix products  71.1 us (17%)
  between operations  21.5 us (5%)
  other arithmetic  15.6 us (4%)
  local copies, waits for them, and re-layouts  6.13 us (1%)
    reduce_scatter x5, waiting for transfers between devices, on_device(): lax.psum_scatter(jnp.stack([partial_real, partial_imag]).astype(jnp.bfloa...  103 us
    all_gather x5, blocking collectives, on_device(): add_segment = lax.all_gather(rounded_direction, 'recv', axis=3, tiled=True)  81.3 us
    psum x5, blocking collectives, on_device(): lax.psum((jnp.sum(direction * direction), jnp.sum(image * image)), 'recv')  47.2 us
    all_gather x5, blocking collectives, on_device(): lax.all_gather(flattened.astype(jnp.bfloat16), 'freq', axis=1, tiled=True)  36.7 us
    psum x5, blocking collectives, on_device(): lax.psum(lax.psum((jnp.sum(direction * direction), jnp.sum(image * image)...  31.3 us
    dot_general x40, matrix products, high_dot(): return jnp.dot(left, right, precision=lax.Precision.HIGHEST)  19.7 us
    dot_general x5, matrix products, on_device(): jnp.einsum('fbs,frs->fbr', stacked_direction, imag_operator, preferred_el...  16.9 us
    dot_general x5, matrix products, on_device(): jnp.einsum('fbr,frs->fbs', stacked_residual, real_operator, preferred_ele...  14.3 us
  transfers between devices with their start and end apart: 5, of which 5 were waited for; matrix products, arithmetic and copies ran while one was open for 0% of the time, Pallas kernels for 0%

profile of v2, /device:TPU:0, one launch (start us, length us, event | category | flops | bytes accessed | tf_op | source)
XLA Modules:
  0.0 414.5 jit_solution(16757627349847850472)
XLA Ops:
  8.1 2.8 fusion.28
  10.9 2.9 fusion.48
  15.0 1.8 select_reduce_fusion.1
  16.9 22.4 %reduce-scatter.6.cloned.1.call-done = bf16[2,8,8,512]{3,2,1,0:T(8,128)(2,1)} async-done(((bf16[2,8,8,2048]{3,2,1,0:T(8,128)(2,1)}), bf16[2,8,8,512]{3,2,1,0:T(8,128)(2,1)}) %reduce-scatter.6.cloned.1.call-update) | async-done | bytes 131088 | tf_op jit(solution)/shard_map/reduce_scatter | solution.py:72
  39.3 1.0 convert_element_type.125
  40.3 7.2 %all_gather.30 = bf16[2,32,4096]{2,1,0:T(8,128)(2,1)S(1)} all-gather(bf16[2,8,4096]{2,1,0:T(8,128)(2,1)S(1)} %convert_element_type.125), channel_id=1, replica_groups=mesh['groups'=2,'freq'=4,'recv'=4] {'freq'}, dimensions={1}, use_global_device_ids=true | all-gather | bytes 655360 | tf_op jit(solution)/shard_map/all_gather | solution.py:80
  52.3 16.2 %all_gather.31 = bf16[2,8,8,2048]{3,2,1,0:T(8,128)(2,1)S(1)} all-gather(bf16[2,8,8,512]{3,2,1,0:T(8,128)(2,1)S(1)} %get-tuple-element.57), channel_id=1, replica_groups=mesh['groups'=2,'freq'=4,'recv'=4] {'recv'}, dimensions={3}, use_global_device_ids=true | all-gather | bytes 655360 | tf_op jit(solution)/shard_map/all_gather | solution.py:95
  68.6 3.4 fusion.26
  72.0 1.2 fusion.46
  73.9 9.4 %all-reduce.4 = (f32[]{:T(128)}, f32[]{:T(128)}) all-reduce(f32[]{:T(128)} %get-tuple-element.56, f32[]{:T(128)} %multiply_reduce_fusion.9), channel_id=1, replica_groups=mesh['groups'=2,'freq'=4,'recv'=4] {'recv'}, use_global_device_ids=true, to_apply=%region_4.5 | all-reduce | flops 2 | bytes 16 | tf_op jit(solution)/shard_map/psum | solution.py:107
  83.3 6.3 %all-reduce.9 = (f32[]{:T(128)}, f32[]{:T(128)}) all-reduce(f32[]{:T(128)} %get-tuple-element.12, f32[]{:T(128)} %get-tuple-element.13), channel_id=1, replica_groups=mesh['groups'=2,'freq'=4,'recv'=4] {'freq'}, use_global_device_ids=true, to_apply=%region_5.6 | all-reduce | flops 2 | bytes 16 | tf_op jit(solution)/shard_map/psum | solution.py:106
  90.9 2.8 fusion.24
  93.8 2.9 fusion.44
  97.7 20.4 %reduce-scatter.8.cloned.1.call-done = bf16[2,8,8,512]{3,2,1,0:T(8,128)(2,1)} async-done(((bf16[2,8,8,2048]{3,2,1,0:T(8,128)(2,1)}), bf16[2,8,8,512]{3,2,1,0:T(8,128)(2,1)}) %reduce-scatter.8.cloned.1.call-update) | async-done | bytes 131088 | tf_op jit(solution)/shard_map/reduce_scatter | solution.py:72
  118.0 1.0 convert_element_type.128
  119.0 7.5 %all_gather.32 = bf16[2,32,4096]{2,1,0:T(8,128)(2,1)S(1)} all-gather(bf16[2,8,4096]{2,1,0:T(8,128)(2,1)S(1)} %convert_element_type.128), channel_id=1, replica_groups=mesh['groups'=2,'freq'=4,'recv'=4] {'freq'}, dimensions={1}, use_global_device_ids=true | all-gather | bytes 655360 | tf_op jit(solution)/shard_map/all_gather | solution.py:80
  131.3 16.2 %all_gather.33 = bf16[2,8,8,2048]{3,2,1,0:T(8,128)(2,1)S(1)} all-gather(bf16[2,8,8,512]{3,2,1,0:T(8,128)(2,1)S(1)} %get-tuple-element.55), channel_id=1, replica_groups=mesh['groups'=2,'freq'=4,'recv'=4] {'recv'}, dimensions={3}, use_global_device_ids=true | all-gather | bytes 655360 | tf_op jit(solution)/shard_map/all_gather | solution.py:95
  147.6 3.4 fusion.22
  151.0 1.2 fusion.42
  152.8 9.5 %all-reduce.3 = (f32[]{:T(128)}, f32[]{:T(128)}) all-reduce(f32[]{:T(128)} %get-tuple-element.54, f32[]{:T(128)} %multiply_reduce_fusion.8), channel_id=1, replica_groups=mesh['groups'=2,'freq'=4,'recv'=4] {'recv'}, use_global_device_ids=true, to_apply=%region_11.12 | all-reduce | flops 2 | bytes 16 | tf_op jit(solution)/shard_map/psum | solution.py:107
  162.3 6.3 %all-reduce.8 = (f32[]{:T(128)}, f32[]{:T(128)}) all-reduce(f32[]{:T(128)} %get-tuple-element.10, f32[]{:T(128)} %get-tuple-element.11), channel_id=1, replica_groups=mesh['groups'=2,'freq'=4,'recv'=4] {'freq'}, use_global_device_ids=true, to_apply=%region_12.13 | all-reduce | flops 2 | bytes 16 | tf_op jit(solution)/shard_map/psum | solution.py:106
  169.9 2.9 fusion.20
  172.7 2.9 fusion.40
  176.6 20.1 %reduce-scatter.10.cloned.1.call-done = bf16[2,8,8,512]{3,2,1,0:T(8,128)(2,1)} async-done(((bf16[2,8,8,2048]{3,2,1,0:T(8,128)(2,1)}), bf16[2,8,8,512]{3,2,1,0:T(8,128)(2,1)}) %reduce-scatter.10.cloned.1.call-update) | async-done | bytes 131088 | tf_op jit(solution)/shard_map/reduce_scatter | solution.py:72
  197.7 7.2 %all_gather.34 = bf16[2,32,4096]{2,1,0:T(8,128)(2,1)S(1)} all-gather(bf16[2,8,4096]{2,1,0:T(8,128)(2,1)S(1)} %convert_element_type.131), channel_id=1, replica_groups=mesh['groups'=2,'freq'=4,'recv'=4] {'freq'}, dimensions={1}, use_global_device_ids=true | all-gather | bytes 655360 | tf_op jit(solution)/shard_map/all_gather | solution.py:80
  209.8 16.4 %all_gather.35 = bf16[2,8,8,2048]{3,2,1,0:T(8,128)(2,1)S(1)} all-gather(bf16[2,8,8,512]{3,2,1,0:T(8,128)(2,1)S(1)} %get-tuple-element.53), channel_id=1, replica_groups=mesh['groups'=2,'freq'=4,'recv'=4] {'recv'}, dimensions={3}, use_global_device_ids=true | all-gather | bytes 655360 | tf_op jit(solution)/shard_map/all_gather | solution.py:95
  226.3 3.4 fusion.18
  229.7 1.2 fusion.38
  231.5 9.4 %all-reduce.2 = (f32[]{:T(128)}, f32[]{:T(128)}) all-reduce(f32[]{:T(128)} %get-tuple-element.52, f32[]{:T(128)} %multiply_reduce_fusion.7), channel_id=1, replica_groups=mesh['groups'=2,'freq'=4,'recv'=4] {'recv'}, use_global_device_ids=true, to_apply=%region_18.19 | all-reduce | flops 2 | bytes 16 | tf_op jit(solution)/shard_map/psum | solution.py:107
  241.0 6.3 %all-reduce.7 = (f32[]{:T(128)}, f32[]{:T(128)}) all-reduce(f32[]{:T(128)} %get-tuple-element.8, f32[]{:T(128)} %get-tuple-element.9), channel_id=1, replica_groups=mesh['groups'=2,'freq'=4,'recv'=4] {'freq'}, use_global_device_ids=true, to_apply=%region_19.20 | all-reduce | flops 2 | bytes 16 | tf_op jit(solution)/shard_map/psum | solution.py:106
  248.6 2.8 fusion.16
  251.4 2.9 fusion.36
  255.3 20.3 %reduce-scatter.12.cloned.1.call-done = bf16[2,8,8,512]{3,2,1,0:T(8,128)(2,1)} async-done(((bf16[2,8,8,2048]{3,2,1,0:T(8,128)(2,1)}), bf16[2,8,8,512]{3,2,1,0:T(8,128)(2,1)}) %reduce-scatter.12.cloned.1.call-update) | async-done | bytes 131088 | tf_op jit(solution)/shard_map/reduce_scatter | solution.py:72
  276.6 7.3 %all_gather.36 = bf16[2,32,4096]{2,1,0:T(8,128)(2,1)S(1)} all-gather(bf16[2,8,4096]{2,1,0:T(8,128)(2,1)S(1)} %convert_element_type.134), channel_id=1, replica_groups=mesh['groups'=2,'freq'=4,'recv'=4] {'freq'}, dimensions={1}, use_global_device_ids=true | all-gather | bytes 655360 | tf_op jit(solution)/shard_map/all_gather | solution.py:80
  288.8 16.2 %all_gather.37 = bf16[2,8,8,2048]{3,2,1,0:T(8,128)(2,1)S(1)} all-gather(bf16[2,8,8,512]{3,2,1,0:T(8,128)(2,1)S(1)} %get-tuple-element.51), channel_id=1, replica_groups=mesh['groups'=2,'freq'=4,'recv'=4] {'recv'}, dimensions={3}, use_global_device_ids=true | all-gather | bytes 655360 | tf_op jit(solution)/shard_map/all_gather | solution.py:95
  305.1 3.4 fusion.14
  308.5 1.2 fusion.34
  310.3 9.4 %all-reduce.1 = (f32[]{:T(128)}, f32[]{:T(128)}) all-reduce(f32[]{:T(128)} %get-tuple-element.50, f32[]{:T(128)} %multiply_reduce_fusion.6), channel_id=1, replica_groups=mesh['groups'=2,'freq'=4,'recv'=4] {'recv'}, use_global_device_ids=true, to_apply=%region_25.26 | all-reduce | flops 2 | bytes 16 | tf_op jit(solution)/shard_map/psum | solution.py:107
  319.7 6.3 %all-reduce.6 = (f32[]{:T(128)}, f32[]{:T(128)}) all-reduce(f32[]{:T(128)} %get-tuple-element.6, f32[]{:T(128)} %get-tuple-element.7), channel_id=1, replica_groups=mesh['groups'=2,'freq'=4,'recv'=4] {'freq'}, use_global_device_ids=true, to_apply=%region_26.27 | all-reduce | flops 2 | bytes 16 | tf_op jit(solution)/shard_map/psum | solution.py:106
  327.3 2.8 fusion.12
  330.2 2.9 fusion.32
  334.0 20.2 %reduce-scatter.14.cloned.1.call-done = bf16[2,8,8,512]{3,2,1,0:T(8,128)(2,1)} async-done(((bf16[2,8,8,2048]{3,2,1,0:T(8,128)(2,1)}), bf16[2,8,8,512]{3,2,1,0:T(8,128)(2,1)}) %reduce-scatter.14.cloned.1.call-update) | async-done | bytes 131088 | tf_op jit(solution)/shard_map/reduce_scatter | solution.py:72
  355.2 7.5 %all_gather.38 = bf16[2,32,4096]{2,1,0:T(8,128)(2,1)S(1)} all-gather(bf16[2,8,4096]{2,1,0:T(8,128)(2,1)S(1)} %convert_element_type.137), channel_id=1, replica_groups=mesh['groups'=2,'freq'=4,'recv'=4] {'freq'}, dimensions={1}, use_global_device_ids=true | all-gather | bytes 655360 | tf_op jit(solution)/shard_map/all_gather | solution.py:80
  367.5 16.2 %all_gather.39 = bf16[2,8,8,2048]{3,2,1,0:T(8,128)(2,1)S(1)} all-gather(bf16[2,8,8,512]{3,2,1,0:T(8,128)(2,1)S(1)} %get-tuple-element.48), channel_id=1, replica_groups=mesh['groups'=2,'freq'=4,'recv'=4] {'recv'}, dimensions={3}, use_global_device_ids=true | all-gather | bytes 655360 | tf_op jit(solution)/shard_map/all_gather | solution.py:95
  383.8 3.4 fusion.10
  387.2 1.2 fusion.30
  389.0 9.4 %all-reduce = (f32[]{:T(128)}, f32[]{:T(128)}) all-reduce(f32[]{:T(128)} %get-tuple-element.49, f32[]{:T(128)} %multiply_reduce_fusion.5), channel_id=1, replica_groups=mesh['groups'=2,'freq'=4,'recv'=4] {'recv'}, use_global_device_ids=true, to_apply=%region_32.33 | all-reduce | flops 2 | bytes 16 | tf_op jit(solution)/shard_map/psum | solution.py:107
  398.4 6.3 %all-reduce.5 = (f32[]{:T(128)}, f32[]{:T(128)}) all-reduce(f32[]{:T(128)} %get-tuple-element.4, f32[]{:T(128)} %get-tuple-element.5), channel_id=1, replica_groups=mesh['groups'=2,'freq'=4,'recv'=4] {'freq'}, use_global_device_ids=true, to_apply=%region_33.34 | all-reduce | flops 2 | bytes 16 | tf_op jit(solution)/shard_map/psum | solution.py:106
  (140 shorter events, 38.0 us)
Async XLA Ops:
  7.2 32.1 %reduce-scatter.6.cloned.1.call-start = ((), (), s32[]{:S(2)}) async-start(), calls=%async_computation.5 | async-start | bytes 655360 | tf_op jit(solution)/shard_map/reduce_scatter | solution.py:72
  10.9 3.9 copy-start.1
  10.9 4.0 copy-start.2
  14.8 103.2 %reduce-scatter.8.cloned.1.call-start = ((), (), s32[]{:S(2)}) async-start(), calls=%async_computation.6 | async-start | bytes 655360 | tf_op jit(solution)/shard_map/reduce_scatter | solution.py:72
  40.3 31.7 %slice-start = ((s8[8388608]{0:T(1024)(128)(4,1)}), s8[4194304]{0:T(1024)(128)(4,1)S(1)}, s32[]{:S(2)}) async-start(s8[8388608]{0:T(1024)(128)(4,1)} %bitcast.226), calls=%async_computation.10 | async-start | bytes 8388608
  51.5 20.5 %slice-start.1 = ((s8[8388608]{0:T(1024)(128)(4,1)}), s8[4194304]{0:T(1024)(128)(4,1)S(1)}, s32[]{:S(2)}) async-start(s8[8388608]{0:T(1024)(128)(4,1)} %bitcast.226), calls=%async_computation.11 | async-start | bytes 8388608
  68.6 22.3 %copy-start = (f32[2,8,8,128]{3,2,1,0:T(8,128)S(1)}, f32[2,8,8,128]{3,2,1,0:T(8,128)}, u32[]{:S(2)}) copy-start(f32[2,8,8,128]{3,2,1,0:T(8,128)} %param.5) | copy-start | bytes 196612
  97.6 99.2 %reduce-scatter.10.cloned.1.call-start = ((), (), s32[]{:S(2)}) async-start(), calls=%async_computation.7 | async-start | bytes 655360 | tf_op jit(solution)/shard_map/reduce_scatter | solution.py:72
  119.0 32.0 %slice-start.2 = ((s8[8388608]{0:T(1024)(128)(4,1)}), s8[4194304]{0:T(1024)(128)(4,1)S(1)}, s32[]{:S(2)}) async-start(s8[8388608]{0:T(1024)(128)(4,1)} %bitcast.228), calls=%async_computation.12 | async-start | bytes 8388608
  130.5 20.5 %slice-start.3 = ((s8[8388608]{0:T(1024)(128)(4,1)}), s8[4194304]{0:T(1024)(128)(4,1)S(1)}, s32[]{:S(2)}) async-start(s8[8388608]{0:T(1024)(128)(4,1)} %bitcast.228), calls=%async_computation.13 | async-start | bytes 8388608
  176.6 99.0 %reduce-scatter.12.cloned.1.call-start = ((), (), s32[]{:S(2)}) async-start(), calls=%async_computation.8 | async-start | bytes 655360 | tf_op jit(solution)/shard_map/reduce_scatter | solution.py:72
  197.7 31.9 %slice-start.4 = ((s8[8388608]{0:T(1024)(128)(4,1)}), s8[4194304]{0:T(1024)(128)(4,1)S(1)}, s32[]{:S(2)}) async-start(s8[8388608]{0:T(1024)(128)(4,1)} %bitcast.230), calls=%async_computation.14 | async-start | bytes 8388608
  209.0 20.7 %slice-start.5 = ((s8[8388608]{0:T(1024)(128)(4,1)}), s8[4194304]{0:T(1024)(128)(4,1)S(1)}, s32[]{:S(2)}) async-start(s8[8388608]{0:T(1024)(128)(4,1)} %bitcast.230), calls=%async_computation.15 | async-start | bytes 8388608
  255.3 98.9 %reduce-scatter.14.cloned.1.call-start = ((), (), s32[]{:S(2)}) async-start(), calls=%async_computation.9 | async-start | bytes 655360 | tf_op jit(solution)/shard_map/reduce_scatter | solution.py:72
  276.6 31.9 %slice-start.6 = ((s8[8388608]{0:T(1024)(128)(4,1)}), s8[4194304]{0:T(1024)(128)(4,1)S(1)}, s32[]{:S(2)}) async-start(s8[8388608]{0:T(1024)(128)(4,1)} %bitcast.232), calls=%async_computation.16 | async-start | bytes 8388608
  287.9 20.5 %slice-start.7 = ((s8[8388608]{0:T(1024)(128)(4,1)}), s8[4194304]{0:T(1024)(128)(4,1)S(1)}, s32[]{:S(2)}) async-start(s8[8388608]{0:T(1024)(128)(4,1)} %bitcast.232), calls=%async_computation.17 | async-start | bytes 8388608
  355.2 32.0 %slice-start.8 = ((s8[8388608]{0:T(1024)(128)(4,1)}), s8[4194304]{0:T(1024)(128)(4,1)S(1)}, s32[]{:S(2)}) async-start(s8[8388608]{0:T(1024)(128)(4,1)} %bitcast.234), calls=%async_computation.18 | async-start | bytes 8388608
  366.6 20.5 %slice-start.9 = ((s8[8388608]{0:T(1024)(128)(4,1)}), s8[4194304]{0:T(1024)(128)(4,1)S(1)}, s32[]{:S(2)}) async-start(s8[8388608]{0:T(1024)(128)(4,1)} %bitcast.234), calls=%async_computation.19 | async-start | bytes 8388608
Sparse Core Ops, SparseCore 0:
  14.9 24.3 reduce-scatter.5
  97.7 20.2 reduce-scatter.7
  176.7 20.0 reduce-scatter.9
  255.4 20.1 reduce-scatter.11
  334.1 20.0 reduce-scatter.13

commit v3 on v2

--- a/solution.py
+++ b/solution.py
@@ -22,18 +22,6 @@
     return (jnp.cos(phases) * normalizer, jnp.sin(phases) * normalizer)
 
 
-def to_time(real_part, imag_part, cos_rows, sin_rows):
-    time_real = high_dot(cos_rows.T, real_part) - high_dot(sin_rows.T, imag_part)
-    time_imag = high_dot(sin_rows.T, real_part) + high_dot(cos_rows.T, imag_part)
-    return (time_real, time_imag)
-
-
-def to_freq(kept_real, kept_imag, cos_rows, sin_rows):
-    real_part = high_dot(cos_rows, kept_real) + high_dot(sin_rows, kept_imag)
-    imag_part = high_dot(cos_rows, kept_imag) - high_dot(sin_rows, kept_real)
-    return jnp.stack([real_part, imag_part])
-
-
 def window_mask(column_ids, src_local, win_start, win_end, length):
     blocks = win_start.shape[1]
     side_ids = column_ids // src_local
@@ -56,9 +44,19 @@
     columns = right_sides * src_local
     real_operator = operator[0]
     imag_operator = operator[1]
-    reflect = jnp.zeros((2, freq_local, right_sides, src_local), jnp.float32)
-    residual = recorded
-    for iteration in range(ITERS):
+
+    cos_part, sin_part = dft_rows(jnp.arange(total_freq, dtype=jnp.int32), total_freq)
+    to_time = jnp.block([[cos_part.T, -sin_part.T], [sin_part.T, cos_part.T]])
+    own_rows = lax.axis_index("freq") * freq_local + jnp.arange(freq_local, dtype=jnp.int32)
+    cos_rows, sin_rows = dft_rows(own_rows, total_freq)
+    to_freq = jnp.block([[cos_rows, sin_rows], [-sin_rows, cos_rows]])
+    window = window_mask(
+        jnp.arange(columns, dtype=jnp.int32), src_local, win_start, win_end, total_freq
+    )
+    window = jnp.concatenate([window, window])
+
+    def step(iteration, state):
+        reflect, residual = state
         rounded_residual = residual.astype(jnp.bfloat16)
         stacked_residual = jnp.concatenate([rounded_residual[0], rounded_residual[1]], axis=1)
         with_real = jnp.einsum(
@@ -74,22 +72,11 @@
             "recv",
             scatter_dimension=3,
             tiled=True,
-        ).astype(jnp.float32)
+        )
         flattened = gradient.reshape(2, freq_local, columns)
-        empty_time = jnp.zeros((2, total_freq, columns), jnp.float32)
-        segment = lax.all_gather(flattened.astype(jnp.bfloat16), "freq", axis=1, tiled=True).astype(
-            jnp.float32
-        )
-        row_ids = jnp.arange(segment.shape[1], dtype=jnp.int32)
-        cos_part, sin_part = dft_rows(row_ids, total_freq)
-        part_real, part_imag = to_time(segment[0], segment[1], cos_part, sin_part)
-        timed = empty_time + jnp.stack([part_real, part_imag])
-        window = window_mask(
-            jnp.arange(columns, dtype=jnp.int32), src_local, win_start, win_end, total_freq
-        )
-        own_rows = lax.axis_index("freq") * freq_local + jnp.arange(freq_local, dtype=jnp.int32)
-        cos_rows, sin_rows = dft_rows(own_rows, total_freq)
-        projected = to_freq(timed[0] * window, timed[1] * window, cos_rows, sin_rows)
+        segment = lax.all_gather(flattened, "freq", axis=1, tiled=True).astype(jnp.float32)
+        timed = high_dot(to_time, segment.reshape(2 * total_freq, columns))
+        projected = high_dot(to_freq, timed * window)
         direction = projected.reshape(2, freq_local, right_sides, src_local)
         rounded_direction = direction.astype(jnp.bfloat16)
         add_segment = lax.all_gather(rounded_direction, "recv", axis=3, tiled=True)
@@ -107,9 +94,10 @@
             lax.psum((jnp.sum(direction * direction), jnp.sum(image * image)), "recv"), "freq"
         )
         step_length = direction_power / (image_energy + 1e-06)
-        reflect = reflect + step_length * direction
-        residual = residual - step_length * image
-    return (reflect, residual)
+        return (reflect + step_length * direction, residual - step_length * image)
+
+    reflect = jnp.zeros((2, freq_local, right_sides, src_local), jnp.float32)
+    return lax.fori_loop(0, ITERS, step, (reflect, recorded))
 
 
 def solution(mesh):

time: 423 us -> 389 us (0.920); the launches traced: 414 us -> 388 us
  matrix products: 71.1 us -> 39.3 us
  local copies, waits for them, and re-layouts: 6.13 us -> 15.9 us
  between operations: 21.5 us -> 13.8 us
  loops' own time: 0 us -> 6.88 us
    dot_general x20, matrix products: 51.4 us -> 30.2 us  [the longest x5 15 us: step(): jnp.einsum('fbr,frs->fbs', stacked_residual, real_operator, preferred_ele...]
    dot_general x40 -> x10, matrix products: 19.7 us -> 9.12 us  [high_dot(): return jnp.dot(left, right, precision=lax.Precision.HIGHEST)]
    another operation x0 -> x1, loops' own time: none -> 6.88 us  [on_device(): return lax.fori_loop(0, ITERS, step, (reflect, recorded))]
    squeeze x10 -> x11, local copies, waits for them, and re-layouts: 0.22 us -> 6.3 us  [the longest x1 6.08 us: on_device(): imag_operator = operator[1]]
    reshape x0 -> x5, local copies, waits for them, and re-layouts: none -> 4.84 us  [step(): flattened = gradient.reshape(2, freq_local, columns)]
    convert_element_type x5, local copies, waits for them, and re-layouts: 4.84 us -> 0.21 us  [step(): rounded_direction = direction.astype(jnp.bfloat16)]
where the time goes in v3:
time: 389 us; the launch traced here: 388 us
  blocking collectives  195 us (50%)
  waiting for transfers between devices  106 us (27%)
  matrix products  39.3 us (10%)
  local copies, waits for them, and re-layouts  15.9 us (4%)
  between operations  13.8 us (4%)
  other arithmetic  11.4 us (3%)
  loops' own time  6.88 us (2%)
    reduce_scatter x5, waiting for transfers between devices, step(): lax.psum_scatter(jnp.stack([partial_real, partial_imag]).astype(jnp.bfloa...  106 us
    all_gather x5, blocking collectives, step(): add_segment = lax.all_gather(rounded_direction, 'recv', axis=3, tiled=True)  80.4 us
    psum x5, blocking collectives, step(): lax.psum((jnp.sum(direction * direction), jnp.sum(image * image)), 'recv')  47.2 us
    all_gather x5, blocking collectives, step(): lax.all_gather(flattened, 'freq', axis=1, tiled=True).astype(jnp.float32)  36 us
    psum x5, blocking collectives, step(): lax.psum(lax.psum((jnp.sum(direction * direction), jnp.sum(image * image)...  31.3 us
    dot_general x5, matrix products, step(): jnp.einsum('fbr,frs->fbs', stacked_residual, real_operator, preferred_ele...  15 us
    dot_general x10, matrix products, high_dot(): return jnp.dot(left, right, precision=lax.Precision.HIGHEST)  9.12 us
  transfers between devices with their start and end apart: 5, of which 5 were waited for; matrix products, arithmetic and copies ran while one was open for 0% of the time, Pallas kernels for 0%

profile of v3, /device:TPU:0, one launch (start us, length us, event | category | flops | bytes accessed | tf_op | source)
XLA Modules:
  0.0 388.4 jit_solution(17782512645471881299)
XLA Ops:
  8.9 1.8 select_reduce_fusion.1
  11.2 6.1 %slice_bitcast_fusion.4 = (bf16[8,128,2048]{2,1,0:T(8,128)(2,1)}, bf16[8,128,2048]{2,1,0:T(8,128)(2,1)}) fusion(bf16[2,8,128,2048]{3,2,1,0:T(8,128)(2,1)} %param.6), kind=kLoop, calls=%fused_computation.33 | loop fusion | bytes 16777216 | tf_op jit(solution)/shard_map/squeeze | solution.py:46
  17.3 363.7 %while.13 = (s32[]{:T(128)}, f32[2,8,8,512]{3,1,2,0:T(8,128)S(1)}, f32[2,8,8,128]{3,2,1,0:T(8,128)S(1)}, bf16[8,128,2048]{2,1,0:T(8,128)(2,1)}, bf16[8,128,2048]...) while((s32[]{:T(128)}, f32[2,8,8,512]{3,1,2,0:T(8,128)S(1)}, ...), condition=%wide.region_10.11_spmd.clone, body=%wide.region_2.10_spmd.clone.sunk | while | flops 523894784 | bytes 84988224 | solution.py:100
  17.4 3.0 fusion.79
  22.5 24.5 %reduce-scatter.2.cloned.1.call-done = bf16[2,8,8,512]{3,2,1,0:T(8,128)(2,1)} async-done(((bf16[2,8,8,2048]{3,2,1,0:T(8,128)(2,1)}), bf16[2,8,8,512]{3,2,1,0:T(8,128)(2,1)}) %reduce-scatter.2.cloned.1.call-update) | async-done | bytes 131088 | tf_op jit(solution)/shard_map/while/body/eval_jaxpr/reduce_scatter | solution.py:70
  48.0 7.2 %all_gather.10 = bf16[2,32,4096]{2,1,0:T(8,128)(2,1)S(1)} all-gather(bf16[2,8,4096]{2,1,0:T(8,128)(2,1)S(1)} %reshape.63), channel_id=1, replica_groups=mesh['groups'=2,'freq'=4,'recv'=4] {'freq'}, dimensions={1}, use_global_device_ids=true | all-gather | bytes 655360 | tf_op jit(solution)/shard_map/while/body/eval_jaxpr/all_gather | solution.py:77
  55.8 1.3 fusion.82
  57.1 16.1 %all_gather.11 = bf16[2,8,8,2048]{3,2,1,0:T(8,128)(2,1)S(1)} all-gather(bf16[2,8,8,512]{3,2,1,0:T(8,128)(2,1)S(1)} %copy.11), channel_id=1, replica_groups=mesh['groups'=2,'freq'=4,'recv'=4] {'recv'}, dimensions={3}, use_global_device_ids=true | all-gather | bytes 655360 | tf_op jit(solution)/shard_map/while/body/eval_jaxpr/all_gather | solution.py:82
  73.2 1.2 fusion.84
  74.4 1.2 fusion.83
  76.3 9.4 %all-reduce.4 = (f32[]{:T(128)}, f32[]{:T(128)}) all-reduce(f32[]{:T(128)} %get-tuple-element.187, f32[]{:T(128)} %multiply_reduce_fusion.3), channel_id=1, replica_groups=mesh['groups'=2,'freq'=4,'recv'=4] {'recv'}, use_global_device_ids=true, to_apply=%region_5.5 | all-reduce | flops 2 | bytes 16 | tf_op jit(solution)/shard_map/while/body/eval_jaxpr/psum | solution.py:94
  85.7 6.3 %all-reduce.5 = (f32[]{:T(128)}, f32[]{:T(128)}) all-reduce(f32[]{:T(128)} %get-tuple-element.193, f32[]{:T(128)} %get-tuple-element.194), channel_id=1, replica_groups=mesh['groups'=2,'freq'=4,'recv'=4] {'freq'}, use_global_device_ids=true, to_apply=%region_6.6 | all-reduce | flops 2 | bytes 16 | tf_op jit(solution)/shard_map/while/body/eval_jaxpr/psum | solution.py:93
  93.5 3.0 fusion.79
  98.6 20.4 %reduce-scatter.2.cloned.1.call-done = bf16[2,8,8,512]{3,2,1,0:T(8,128)(2,1)} async-done(((bf16[2,8,8,2048]{3,2,1,0:T(8,128)(2,1)}), bf16[2,8,8,512]{3,2,1,0:T(8,128)(2,1)}) %reduce-scatter.2.cloned.1.call-update) | async-done | bytes 131088 | tf_op jit(solution)/shard_map/while/body/eval_jaxpr/reduce_scatter | solution.py:70
  120.0 7.3 %all_gather.10 = bf16[2,32,4096]{2,1,0:T(8,128)(2,1)S(1)} all-gather(bf16[2,8,4096]{2,1,0:T(8,128)(2,1)S(1)} %reshape.63), channel_id=1, replica_groups=mesh['groups'=2,'freq'=4,'recv'=4] {'freq'}, dimensions={1}, use_global_device_ids=true | all-gather | bytes 655360 | tf_op jit(solution)/shard_map/while/body/eval_jaxpr/all_gather | solution.py:77
  127.8 1.3 fusion.82
  129.1 16.1 %all_gather.11 = bf16[2,8,8,2048]{3,2,1,0:T(8,128)(2,1)S(1)} all-gather(bf16[2,8,8,512]{3,2,1,0:T(8,128)(2,1)S(1)} %copy.11), channel_id=1, replica_groups=mesh['groups'=2,'freq'=4,'recv'=4] {'recv'}, dimensions={3}, use_global_device_ids=true | all-gather | bytes 655360 | tf_op jit(solution)/shard_map/while/body/eval_jaxpr/all_gather | solution.py:82
  145.3 1.2 fusion.84
  146.5 1.2 fusion.83
  148.3 9.5 %all-reduce.4 = (f32[]{:T(128)}, f32[]{:T(128)}) all-reduce(f32[]{:T(128)} %get-tuple-element.187, f32[]{:T(128)} %multiply_reduce_fusion.3), channel_id=1, replica_groups=mesh['groups'=2,'freq'=4,'recv'=4] {'recv'}, use_global_device_ids=true, to_apply=%region_5.5 | all-reduce | flops 2 | bytes 16 | tf_op jit(solution)/shard_map/while/body/eval_jaxpr/psum | solution.py:94
  157.8 6.3 %all-reduce.5 = (f32[]{:T(128)}, f32[]{:T(128)}) all-reduce(f32[]{:T(128)} %get-tuple-element.193, f32[]{:T(128)} %get-tuple-element.194), channel_id=1, replica_groups=mesh['groups'=2,'freq'=4,'recv'=4] {'freq'}, use_global_device_ids=true, to_apply=%region_6.6 | all-reduce | flops 2 | bytes 16 | tf_op jit(solution)/shard_map/while/body/eval_jaxpr/psum | solution.py:93
  165.5 3.0 fusion.79
  170.6 20.2 %reduce-scatter.2.cloned.1.call-done = bf16[2,8,8,512]{3,2,1,0:T(8,128)(2,1)} async-done(((bf16[2,8,8,2048]{3,2,1,0:T(8,128)(2,1)}), bf16[2,8,8,512]{3,2,1,0:T(8,128)(2,1)}) %reduce-scatter.2.cloned.1.call-update) | async-done | bytes 131088 | tf_op jit(solution)/shard_map/while/body/eval_jaxpr/reduce_scatter | solution.py:70
  191.8 7.2 %all_gather.10 = bf16[2,32,4096]{2,1,0:T(8,128)(2,1)S(1)} all-gather(bf16[2,8,4096]{2,1,0:T(8,128)(2,1)S(1)} %reshape.63), channel_id=1, replica_groups=mesh['groups'=2,'freq'=4,'recv'=4] {'freq'}, dimensions={1}, use_global_device_ids=true | all-gather | bytes 655360 | tf_op jit(solution)/shard_map/while/body/eval_jaxpr/all_gather | solution.py:77
  199.6 1.3 fusion.82
  200.9 16.1 %all_gather.11 = bf16[2,8,8,2048]{3,2,1,0:T(8,128)(2,1)S(1)} all-gather(bf16[2,8,8,512]{3,2,1,0:T(8,128)(2,1)S(1)} %copy.11), channel_id=1, replica_groups=mesh['groups'=2,'freq'=4,'recv'=4] {'recv'}, dimensions={3}, use_global_device_ids=true | all-gather | bytes 655360 | tf_op jit(solution)/shard_map/while/body/eval_jaxpr/all_gather | solution.py:82
  217.1 1.2 fusion.84
  218.3 1.2 fusion.83
  220.1 9.5 %all-reduce.4 = (f32[]{:T(128)}, f32[]{:T(128)}) all-reduce(f32[]{:T(128)} %get-tuple-element.187, f32[]{:T(128)} %multiply_reduce_fusion.3), channel_id=1, replica_groups=mesh['groups'=2,'freq'=4,'recv'=4] {'recv'}, use_global_device_ids=true, to_apply=%region_5.5 | all-reduce | flops 2 | bytes 16 | tf_op jit(solution)/shard_map/while/body/eval_jaxpr/psum | solution.py:94
  229.6 6.3 %all-reduce.5 = (f32[]{:T(128)}, f32[]{:T(128)}) all-reduce(f32[]{:T(128)} %get-tuple-element.193, f32[]{:T(128)} %get-tuple-element.194), channel_id=1, replica_groups=mesh['groups'=2,'freq'=4,'recv'=4] {'freq'}, use_global_device_ids=true, to_apply=%region_6.6 | all-reduce | flops 2 | bytes 16 | tf_op jit(solution)/shard_map/while/body/eval_jaxpr/psum | solution.py:93
  237.3 3.0 fusion.79
  242.4 20.3 %reduce-scatter.2.cloned.1.call-done = bf16[2,8,8,512]{3,2,1,0:T(8,128)(2,1)} async-done(((bf16[2,8,8,2048]{3,2,1,0:T(8,128)(2,1)}), bf16[2,8,8,512]{3,2,1,0:T(8,128)(2,1)}) %reduce-scatter.2.cloned.1.call-update) | async-done | bytes 131088 | tf_op jit(solution)/shard_map/while/body/eval_jaxpr/reduce_scatter | solution.py:70
  263.7 7.2 %all_gather.10 = bf16[2,32,4096]{2,1,0:T(8,128)(2,1)S(1)} all-gather(bf16[2,8,4096]{2,1,0:T(8,128)(2,1)S(1)} %reshape.63), channel_id=1, replica_groups=mesh['groups'=2,'freq'=4,'recv'=4] {'freq'}, dimensions={1}, use_global_device_ids=true | all-gather | bytes 655360 | tf_op jit(solution)/shard_map/while/body/eval_jaxpr/all_gather | solution.py:77
  271.5 1.3 fusion.82
  272.8 16.1 %all_gather.11 = bf16[2,8,8,2048]{3,2,1,0:T(8,128)(2,1)S(1)} all-gather(bf16[2,8,8,512]{3,2,1,0:T(8,128)(2,1)S(1)} %copy.11), channel_id=1, replica_groups=mesh['groups'=2,'freq'=4,'recv'=4] {'recv'}, dimensions={3}, use_global_device_ids=true | all-gather | bytes 655360 | tf_op jit(solution)/shard_map/while/body/eval_jaxpr/all_gather | solution.py:82
  289.0 1.2 fusion.84
  290.1 1.2 fusion.83
  292.0 9.4 %all-reduce.4 = (f32[]{:T(128)}, f32[]{:T(128)}) all-reduce(f32[]{:T(128)} %get-tuple-element.187, f32[]{:T(128)} %multiply_reduce_fusion.3), channel_id=1, replica_groups=mesh['groups'=2,'freq'=4,'recv'=4] {'recv'}, use_global_device_ids=true, to_apply=%region_5.5 | all-reduce | flops 2 | bytes 16 | tf_op jit(solution)/shard_map/while/body/eval_jaxpr/psum | solution.py:94
  301.4 6.3 %all-reduce.5 = (f32[]{:T(128)}, f32[]{:T(128)}) all-reduce(f32[]{:T(128)} %get-tuple-element.193, f32[]{:T(128)} %get-tuple-element.194), channel_id=1, replica_groups=mesh['groups'=2,'freq'=4,'recv'=4] {'freq'}, use_global_device_ids=true, to_apply=%region_6.6 | all-reduce | flops 2 | bytes 16 | tf_op jit(solution)/shard_map/while/body/eval_jaxpr/psum | solution.py:93
  309.2 3.0 fusion.79
  314.3 20.3 %reduce-scatter.2.cloned.1.call-done = bf16[2,8,8,512]{3,2,1,0:T(8,128)(2,1)} async-done(((bf16[2,8,8,2048]{3,2,1,0:T(8,128)(2,1)}), bf16[2,8,8,512]{3,2,1,0:T(8,128)(2,1)}) %reduce-scatter.2.cloned.1.call-update) | async-done | bytes 131088 | tf_op jit(solution)/shard_map/while/body/eval_jaxpr/reduce_scatter | solution.py:70
  335.6 7.2 %all_gather.10 = bf16[2,32,4096]{2,1,0:T(8,128)(2,1)S(1)} all-gather(bf16[2,8,4096]{2,1,0:T(8,128)(2,1)S(1)} %reshape.63), channel_id=1, replica_groups=mesh['groups'=2,'freq'=4,'recv'=4] {'freq'}, dimensions={1}, use_global_device_ids=true | all-gather | bytes 655360 | tf_op jit(solution)/shard_map/while/body/eval_jaxpr/all_gather | solution.py:77
  343.4 1.3 fusion.82
  344.7 16.1 %all_gather.11 = bf16[2,8,8,2048]{3,2,1,0:T(8,128)(2,1)S(1)} all-gather(bf16[2,8,8,512]{3,2,1,0:T(8,128)(2,1)S(1)} %copy.11), channel_id=1, replica_groups=mesh['groups'=2,'freq'=4,'recv'=4] {'recv'}, dimensions={3}, use_global_device_ids=true | all-gather | bytes 655360 | tf_op jit(solution)/shard_map/while/body/eval_jaxpr/all_gather | solution.py:82
  360.8 1.2 fusion.84
  362.0 1.2 fusion.83
  363.9 9.4 %all-reduce.4 = (f32[]{:T(128)}, f32[]{:T(128)}) all-reduce(f32[]{:T(128)} %get-tuple-element.187, f32[]{:T(128)} %multiply_reduce_fusion.3), channel_id=1, replica_groups=mesh['groups'=2,'freq'=4,'recv'=4] {'recv'}, use_global_device_ids=true, to_apply=%region_5.5 | all-reduce | flops 2 | bytes 16 | tf_op jit(solution)/shard_map/while/body/eval_jaxpr/psum | solution.py:94
  373.3 6.3 %all-reduce.5 = (f32[]{:T(128)}, f32[]{:T(128)}) all-reduce(f32[]{:T(128)} %get-tuple-element.193, f32[]{:T(128)} %get-tuple-element.194), channel_id=1, replica_groups=mesh['groups'=2,'freq'=4,'recv'=4] {'freq'}, use_global_device_ids=true, to_apply=%region_6.6 | all-reduce | flops 2 | bytes 16 | tf_op jit(solution)/shard_map/while/body/eval_jaxpr/psum | solution.py:93
  (127 shorter events, 25.8 us)
Async XLA Ops:
  11.2 6.1 %copy-start.4 = (f32[2,8,8,128]{3,2,1,0:T(8,128)S(1)}, f32[2,8,8,128]{3,2,1,0:T(8,128)}, u32[]{:S(2)}) copy-start(f32[2,8,8,128]{3,2,1,0:T(8,128)} %param.7) | copy-start | bytes 196612
  17.3 29.7 %reduce-scatter.2.cloned.1.call-start = ((), (), s32[]{:S(2)}) async-start(), calls=%async_computation.1 | async-start | bytes 655360 | tf_op jit(solution)/shard_map/while/body/eval_jaxpr/reduce_scatter | solution.py:70
  17.4 3.5 copy-start
  48.0 25.2 %copy-start.2 = (bf16[8,128,2048]{2,1,0:T(8,128)(2,1)S(1)}, bf16[8,128,2048]{2,1,0:T(8,128)(2,1)}, u32[]{:S(2)}) copy-start(bf16[8,128,2048]{2,1,0:T(8,128)(2,1)} %get-tuple-element.222) | copy-start | bytes 12582916 | tf_op jit(solution)/shard_map/while
  55.8 18.7 %copy-start.1 = (bf16[8,128,2048]{2,1,0:T(8,128)(2,1)S(1)}, bf16[8,128,2048]{2,1,0:T(8,128)(2,1)}, u32[]{:S(2)}) copy-start(bf16[8,128,2048]{2,1,0:T(8,128)(2,1)} %get-tuple-element.223) | copy-start | bytes 12582916 | tf_op jit(solution)/shard_map/while
  93.4 25.6 %reduce-scatter.2.cloned.1.call-start = ((), (), s32[]{:S(2)}) async-start(), calls=%async_computation.1 | async-start | bytes 655360 | tf_op jit(solution)/shard_map/while/body/eval_jaxpr/reduce_scatter | solution.py:70
  93.4 3.5 copy-start
  120.0 25.3 %copy-start.2 = (bf16[8,128,2048]{2,1,0:T(8,128)(2,1)S(1)}, bf16[8,128,2048]{2,1,0:T(8,128)(2,1)}, u32[]{:S(2)}) copy-start(bf16[8,128,2048]{2,1,0:T(8,128)(2,1)} %get-tuple-element.222) | copy-start | bytes 12582916 | tf_op jit(solution)/shard_map/while
  127.8 18.7 %copy-start.1 = (bf16[8,128,2048]{2,1,0:T(8,128)(2,1)S(1)}, bf16[8,128,2048]{2,1,0:T(8,128)(2,1)}, u32[]{:S(2)}) copy-start(bf16[8,128,2048]{2,1,0:T(8,128)(2,1)} %get-tuple-element.223) | copy-start | bytes 12582916 | tf_op jit(solution)/shard_map/while
  165.4 25.4 %reduce-scatter.2.cloned.1.call-start = ((), (), s32[]{:S(2)}) async-start(), calls=%async_computation.1 | async-start | bytes 655360 | tf_op jit(solution)/shard_map/while/body/eval_jaxpr/reduce_scatter | solution.py:70
  165.5 3.5 copy-start
  191.8 25.2 %copy-start.2 = (bf16[8,128,2048]{2,1,0:T(8,128)(2,1)S(1)}, bf16[8,128,2048]{2,1,0:T(8,128)(2,1)}, u32[]{:S(2)}) copy-start(bf16[8,128,2048]{2,1,0:T(8,128)(2,1)} %get-tuple-element.222) | copy-start | bytes 12582916 | tf_op jit(solution)/shard_map/while
  199.6 18.7 %copy-start.1 = (bf16[8,128,2048]{2,1,0:T(8,128)(2,1)S(1)}, bf16[8,128,2048]{2,1,0:T(8,128)(2,1)}, u32[]{:S(2)}) copy-start(bf16[8,128,2048]{2,1,0:T(8,128)(2,1)} %get-tuple-element.223) | copy-start | bytes 12582916 | tf_op jit(solution)/shard_map/while
  237.2 25.5 %reduce-scatter.2.cloned.1.call-start = ((), (), s32[]{:S(2)}) async-start(), calls=%async_computation.1 | async-start | bytes 655360 | tf_op jit(solution)/shard_map/while/body/eval_jaxpr/reduce_scatter | solution.py:70
  237.3 3.5 copy-start
  263.7 25.2 %copy-start.2 = (bf16[8,128,2048]{2,1,0:T(8,128)(2,1)S(1)}, bf16[8,128,2048]{2,1,0:T(8,128)(2,1)}, u32[]{:S(2)}) copy-start(bf16[8,128,2048]{2,1,0:T(8,128)(2,1)} %get-tuple-element.222) | copy-start | bytes 12582916 | tf_op jit(solution)/shard_map/while
  271.5 18.7 %copy-start.1 = (bf16[8,128,2048]{2,1,0:T(8,128)(2,1)S(1)}, bf16[8,128,2048]{2,1,0:T(8,128)(2,1)}, u32[]{:S(2)}) copy-start(bf16[8,128,2048]{2,1,0:T(8,128)(2,1)} %get-tuple-element.223) | copy-start | bytes 12582916 | tf_op jit(solution)/shard_map/while
  309.1 25.5 %reduce-scatter.2.cloned.1.call-start = ((), (), s32[]{:S(2)}) async-start(), calls=%async_computation.1 | async-start | bytes 655360 | tf_op jit(solution)/shard_map/while/body/eval_jaxpr/reduce_scatter | solution.py:70
  309.2 3.5 copy-start
  335.6 25.2 %copy-start.2 = (bf16[8,128,2048]{2,1,0:T(8,128)(2,1)S(1)}, bf16[8,128,2048]{2,1,0:T(8,128)(2,1)}, u32[]{:S(2)}) copy-start(bf16[8,128,2048]{2,1,0:T(8,128)(2,1)} %get-tuple-element.222) | copy-start | bytes 12582916 | tf_op jit(solution)/shard_map/while
  343.4 18.7 %copy-start.1 = (bf16[8,128,2048]{2,1,0:T(8,128)(2,1)S(1)}, bf16[8,128,2048]{2,1,0:T(8,128)(2,1)}, u32[]{:S(2)}) copy-start(bf16[8,128,2048]{2,1,0:T(8,128)(2,1)} %get-tuple-element.223) | copy-start | bytes 12582916 | tf_op jit(solution)/shard_map/while
  381.0 0.9 copy-start.3
Sparse Core Ops, SparseCore 0:
  22.6 24.3 reduce-scatter.1
  98.7 20.2 reduce-scatter.1
  170.8 20.0 reduce-scatter.1
  242.6 20.1 reduce-scatter.1
  314.4 20.1 reduce-scatter.1

commit v4 on v3

--- a/solution.py
+++ b/solution.py
@@ -35,6 +35,31 @@
     return ((samples >= opening[None, :]) & (samples < closing[None, :])).astype(jnp.float32)
 
 
+def shifted(value, axis, distance):
+    size = lax.axis_size(axis)
+    return lax.ppermute(value, axis, [(i, (i + distance) % size) for i in range(size)])
+
+
+def sum_scatter(partial, axis, dim):
+    size = lax.axis_size(axis)
+    me = lax.axis_index(axis)
+    blocks = partial.reshape(partial.shape[:dim] + (size, partial.shape[dim] // size) + partial.shape[dim + 1 :])
+    total = lax.dynamic_index_in_dim(blocks, me, axis=dim, keepdims=False).astype(jnp.float32)
+    for distance in range(1, size):
+        piece = lax.dynamic_index_in_dim(blocks, (me + distance) % size, axis=dim, keepdims=False)
+        total = total + shifted(piece, axis, distance).astype(jnp.float32)
+    return total
+
+
+def gather_blocks(block, axis, dim):
+    size = lax.axis_size(axis)
+    me = lax.axis_index(axis)
+    slots = jnp.stack([block] + [shifted(block, axis, d) for d in range(1, size)], axis=dim)
+    order = (me - jnp.arange(size, dtype=jnp.int32)) % size
+    ordered = jnp.take(slots, order, axis=dim)
+    return ordered.reshape(block.shape[:dim] + (size * block.shape[dim],) + block.shape[dim + 1 :])
+
+
 def on_device(operator, recorded, win_start, win_end):
     freq_local = operator.shape[1]
     sources = operator.shape[3]
@@ -67,19 +92,16 @@
         )
         partial_real = with_real[:, :right_sides] + with_imag[:, right_sides:]
         partial_imag = with_real[:, right_sides:] - with_imag[:, :right_sides]
-        gradient = lax.psum_scatter(
-            jnp.stack([partial_real, partial_imag]).astype(jnp.bfloat16),
-            "recv",
-            scatter_dimension=3,
-            tiled=True,
+        gradient = sum_scatter(
+            jnp.stack([partial_real, partial_imag]).astype(jnp.bfloat16), "recv", 3
         )
-        flattened = gradient.reshape(2, freq_local, columns)
-        segment = lax.all_gather(flattened, "freq", axis=1, tiled=True).astype(jnp.float32)
+        flattened = gradient.astype(jnp.bfloat16).reshape(2, freq_local, columns)
+        segment = gather_blocks(flattened, "freq", 1).astype(jnp.float32)
         timed = high_dot(to_time, segment.reshape(2 * total_freq, columns))
         projected = high_dot(to_freq, timed * window)
         direction = projected.reshape(2, freq_local, right_sides, src_local)
         rounded_direction = direction.astype(jnp.bfloat16)
-        add_segment = lax.all_gather(rounded_direction, "recv", axis=3, tiled=True)
+        add_segment = gather_blocks(rounded_direction, "recv", 3)
         stacked_direction = jnp.concatenate([add_segment[0], add_segment[1]], axis=1)
         by_real = jnp.einsum(
             "fbs,frs->fbr", stacked_direction, real_operator, preferred_element_type=jnp.float32

time: 389 us -> 343 us (0.88)
  blocking collectives: 195 us -> 76.9 us
  starting transfers between devices: 0.2 us -> 42.8 us
  waiting for transfers between devices: 106 us -> 135 us
  between operations: 13.8 us -> 0.72 us
  matrix products: 39.3 us -> 51.2 us
    ppermute x0 -> x45, waiting for transfers between devices: none -> 135 us  [shifted(): lax.ppermute(value, axis, [(i, (i + distance) % size) for i in range(size)])]
    all_gather x10 -> x0, blocking collectives: 116 us -> none  [the longest x5 80.4 us: step(): add_segment = lax.all_gather(rounded_direction, 'recv', axis=3, tiled=True)]
    reduce_scatter x5 -> x0, waiting for transfers between devices: 106 us -> none  [step(): lax.psum_scatter(jnp.stack([partial_real, partial_imag]).astype(jnp.bfloa...]
    ppermute x0 -> x45, starting transfers between devices: none -> 42.8 us  [shifted(): lax.ppermute(value, axis, [(i, (i + distance) % size) for i in range(size)])]
    dot_general x5, matrix products: 6.01 us -> 17.8 us  [step(): jnp.einsum('fbs,frs->fbr', stacked_direction, imag_operator, preferred_el...]
    dot_general x5, matrix products: 3.29 us -> 15 us  [step(): jnp.einsum('fbr,frs->fbs', stacked_residual, imag_operator, preferred_ele...]
    dot_general x5, matrix products: 15 us -> 3.29 us  [step(): jnp.einsum('fbr,frs->fbs', stacked_residual, real_operator, preferred_ele...]
    gather x0 -> x15, local copies, waits for them, and re-layouts: none -> 5.98 us  [gather_blocks(): ordered = jnp.take(slots, order, axis=dim)]
  transfers between devices with their start and end apart: 5 -> 45, of which waited for: 5 -> 35; matrix products, arithmetic and copies ran while one was open for 0% -> 0% of each run, Pallas kernels for 0% -> 0%
where the time goes in v4:
time: 343 us
  waiting for transfers between devices  135 us (39%)
  blocking collectives  76.9 us (22%)
  matrix products  51.2 us (15%)
  starting transfers between devices  42.8 us (12%)
  local copies, waits for them, and re-layouts  17.7 us (5%)
  other arithmetic  10.9 us (3%)
  loops' own time  7.78 us (2%)
    ppermute x45, waiting for transfers between devices, shifted(): lax.ppermute(value, axis, [(i, (i + distance) % size) for i in range(size)])  135 us
    psum x5, blocking collectives, step(): lax.psum((jnp.sum(direction * direction), jnp.sum(image * image)), 'recv')  45.4 us
    ppermute x45, starting transfers between devices, shifted(): lax.ppermute(value, axis, [(i, (i + distance) % size) for i in range(size)])  42.8 us
    psum x5, blocking collectives, step(): lax.psum(lax.psum((jnp.sum(direction * direction), jnp.sum(image * image)...  31.4 us
    dot_general x5, matrix products, step(): jnp.einsum('fbs,frs->fbr', stacked_direction, imag_operator, preferred_el...  17.8 us
    dot_general x5, matrix products, step(): jnp.einsum('fbr,frs->fbs', stacked_residual, imag_operator, preferred_ele...  15 us
    dot_general x10, matrix products, high_dot(): return jnp.dot(left, right, precision=lax.Precision.HIGHEST)  9.12 us
    another operation x1, loops' own time, on_device(): return lax.fori_loop(0, ITERS, step, (reflect, recorded))  7.78 us
  transfers between devices with their start and end apart: 45, of which 35 were waited for; matrix products, arithmetic and copies ran while one was open for 0% of the time, Pallas kernels for 0%

profile of v4, /device:TPU:0, one launch (start us, length us, event | category | flops | bytes accessed | tf_op | source)
XLA Modules:
  0.0 342.9 jit_solution(16337587272674273566)
XLA Ops:
  0.7 6.1 %slice_bitcast_fusion.2 = (bf16[8,128,2048]{2,1,0:T(8,128)(2,1)}, bf16[8,128,2048]{2,1,0:T(8,128)(2,1)}) fusion(bf16[2,8,128,2048]{3,2,1,0:T(8,128)(2,1)} %param.6), kind=kLoop, calls=%fused_computation.80 | loop fusion | bytes 16777216 | tf_op jit(solution)/shard_map/squeeze | solution.py:71
  10.5 331.6 %while.15 = (s32[]{:T(128)}, f32[2,8,8,512]{3,1,2,0:T(8,128)S(1)}, f32[2,8,8,128]{3,2,1,0:T(8,128)S(1)}, bf16[8,128,2048]{2,1,0:T(8,128)(2,1)}, bf16[8,128,2048]...) while((s32[]{:T(128)}, f32[2,8,8,512]{3,1,2,0:T(8,128)S(1)}, ...), condition=%wide.region_9.10_spmd.clone, body=%wide.region_2.9_spmd.clone.sunk | while | flops 526518560 | bytes 83162712 | solution.py:122
  10.5 3.0 fusion.99
  14.8 5.1 %collective-permute-start = (bf16[2,8,8,512]{3,2,1,0:T(8,128)(2,1)S(1)}, bf16[2,8,8,512]{3,2,1,0:T(8,128)(2,1)S(1)}, u32[]{:S(2)}, u32[]{:S(2)}) collective-permute-start(bf16[2,8,8,512]{3,2,1,0:T(8,128)(2,1)S(1)} %get-tuple-element.260), channel_id=1, source_target_pairs={{0,3},{1,0},{2,1},{3,2},{4,7},{5,4},{6,5},{7,6},{8,11},{9,8},{10,9... | collective-permute-start | bytes 393224 | tf_op jit(solution)/shard_map/while/body/eval_jaxpr/ppermute | solution.py:40
  20.9 2.9 collective-permute-done
  23.8 7.3 %collective-permute-done.1 = bf16[2,8,8,512]{3,2,1,0:T(8,128)(2,1)S(1)} collective-permute-done((bf16[2,8,8,512]{3,2,1,0:T(8,128)(2,1)S(1)}, bf16[2,8,8,512]{3,2,1,0:T(8,128)(2,1)S(1)}, u32[]{:S(2)}, u32[]{:S(2)}) %collective-permute-start.1) | collective-permute-done | bytes 131104 | tf_op jit(solution)/shard_map/while/body/eval_jaxpr/ppermute | solution.py:40
  35.1 4.8 %collective-permute-done.4 = bf16[2,8,4096]{2,1,0:T(8,128)(2,1)S(1)} collective-permute-done((bf16[2,8,4096]{2,1,0:T(8,128)(2,1)S(1)}, bf16[2,8,4096]{2,1,0:T(8,128)(2,1)S(1)}, u32[]{:S(2)}, u32[]{:S(2)}) %collective-permute-start.4) | collective-permute-done | bytes 131104 | tf_op jit(solution)/shard_map/while/body/eval_jaxpr/ppermute | solution.py:40
  48.5 7.3 %collective-permute-done.7 = bf16[2,8,8,512]{3,1,2,0:T(8,128)(2,1)S(1)} collective-permute-done((bf16[2,8,8,512]{3,1,2,0:T(8,128)(2,1)S(1)}, bf16[2,8,8,512]{3,1,2,0:T(8,128)(2,1)S(1)}, u32[]{:S(2)}, u32[]{:S(2)}) %collective-permute-start.7) | collective-permute-done | bytes 131104 | tf_op jit(solution)/shard_map/while/body/eval_jaxpr/ppermute | solution.py:40
  56.9 3.6 %fusion.109 = f32[8,16,128]{2,1,0:T(8,128)S(1)} fusion(bf16[8,128,2048]{2,1,0:T(8,128)(2,1)} %get-tuple-element.312, bf16[8,8,2048]{2,1,0:T(8,128)(2,1)S(1)} %bitcast.132, bf16[8,8,2048]{2,1,0:T(8,128)(2,1)S(1)} %bitcast.134), kind=kOutput, calls=%fused_computation.21.clone.1 | convolution fusion | flops 68157440 | bytes 4784128 | tf_op jit(solution)/shard_map/while/body/eval_jaxpr/fbs,frs->fbr/dot_general | solution.py:109
  62.3 9.3 %all-reduce.4 = (f32[]{:T(128)}, f32[]{:T(128)}) all-reduce(f32[]{:T(128)} %get-tuple-element.265, f32[]{:T(128)} %multiply_reduce_fusion.3), channel_id=1, replica_groups=mesh['groups'=2,'freq'=4,'recv'=4] {'recv'}, use_global_device_ids=true, to_apply=%region_4.4 | all-reduce | flops 2 | bytes 16 | tf_op jit(solution)/shard_map/while/body/eval_jaxpr/psum | solution.py:116
  71.6 6.3 %all-reduce.5 = (f32[]{:T(128)}, f32[]{:T(128)}) all-reduce(f32[]{:T(128)} %get-tuple-element.272, f32[]{:T(128)} %get-tuple-element.273), channel_id=1, replica_groups=mesh['groups'=2,'freq'=4,'recv'=4] {'freq'}, use_global_device_ids=true, to_apply=%region_5.5 | all-reduce | flops 2 | bytes 16 | tf_op jit(solution)/shard_map/while/body/eval_jaxpr/psum | solution.py:115
  79.4 3.0 fusion.99
  86.9 2.5 collective-permute-done
  89.4 9.2 %collective-permute-done.1 = bf16[2,8,8,512]{3,2,1,0:T(8,128)(2,1)S(1)} collective-permute-done((bf16[2,8,8,512]{3,2,1,0:T(8,128)(2,1)S(1)}, bf16[2,8,8,512]{3,2,1,0:T(8,128)(2,1)S(1)}, u32[]{:S(2)}, u32[]{:S(2)}) %collective-permute-start.1) | collective-permute-done | bytes 131104 | tf_op jit(solution)/shard_map/while/body/eval_jaxpr/ppermute | solution.py:40
  101.9 5.0 %collective-permute-done.4 = bf16[2,8,4096]{2,1,0:T(8,128)(2,1)S(1)} collective-permute-done((bf16[2,8,4096]{2,1,0:T(8,128)(2,1)S(1)}, bf16[2,8,4096]{2,1,0:T(8,128)(2,1)S(1)}, u32[]{:S(2)}, u32[]{:S(2)}) %collective-permute-start.4) | collective-permute-done | bytes 131104 | tf_op jit(solution)/shard_map/while/body/eval_jaxpr/ppermute | solution.py:40
  112.6 2.6 collective-permute-done.6
  115.2 6.4 %collective-permute-done.7 = bf16[2,8,8,512]{3,1,2,0:T(8,128)(2,1)S(1)} collective-permute-done((bf16[2,8,8,512]{3,1,2,0:T(8,128)(2,1)S(1)}, bf16[2,8,8,512]{3,1,2,0:T(8,128)(2,1)S(1)}, u32[]{:S(2)}, u32[]{:S(2)}) %collective-permute-start.7) | collective-permute-done | bytes 131104 | tf_op jit(solution)/shard_map/while/body/eval_jaxpr/ppermute | solution.py:40
  122.6 3.6 %fusion.109 = f32[8,16,128]{2,1,0:T(8,128)S(1)} fusion(bf16[8,128,2048]{2,1,0:T(8,128)(2,1)} %get-tuple-element.312, bf16[8,8,2048]{2,1,0:T(8,128)(2,1)S(1)} %bitcast.132, bf16[8,8,2048]{2,1,0:T(8,128)(2,1)S(1)} %bitcast.134), kind=kOutput, calls=%fused_computation.21.clone.1 | convolution fusion | flops 68157440 | bytes 4784128 | tf_op jit(solution)/shard_map/while/body/eval_jaxpr/fbs,frs->fbr/dot_general | solution.py:109
  128.1 9.0 %all-reduce.4 = (f32[]{:T(128)}, f32[]{:T(128)}) all-reduce(f32[]{:T(128)} %get-tuple-element.265, f32[]{:T(128)} %multiply_reduce_fusion.3), channel_id=1, replica_groups=mesh['groups'=2,'freq'=4,'recv'=4] {'recv'}, use_global_device_ids=true, to_apply=%region_4.4 | all-reduce | flops 2 | bytes 16 | tf_op jit(solution)/shard_map/while/body/eval_jaxpr/psum | solution.py:116
  137.1 6.3 %all-reduce.5 = (f32[]{:T(128)}, f32[]{:T(128)}) all-reduce(f32[]{:T(128)} %get-tuple-element.272, f32[]{:T(128)} %get-tuple-element.273), channel_id=1, replica_groups=mesh['groups'=2,'freq'=4,'recv'=4] {'freq'}, use_global_device_ids=true, to_apply=%region_5.5 | all-reduce | flops 2 | bytes 16 | tf_op jit(solution)/shard_map/while/body/eval_jaxpr/psum | solution.py:115
  144.9 3.0 fusion.99
  149.2 2.1 collective-permute-start
  152.7 2.5 collective-permute-done
  155.1 9.2 %collective-permute-done.1 = bf16[2,8,8,512]{3,2,1,0:T(8,128)(2,1)S(1)} collective-permute-done((bf16[2,8,8,512]{3,2,1,0:T(8,128)(2,1)S(1)}, bf16[2,8,8,512]{3,2,1,0:T(8,128)(2,1)S(1)}, u32[]{:S(2)}, u32[]{:S(2)}) %collective-permute-start.1) | collective-permute-done | bytes 131104 | tf_op jit(solution)/shard_map/while/body/eval_jaxpr/ppermute | solution.py:40
  167.8 4.7 %collective-permute-done.4 = bf16[2,8,4096]{2,1,0:T(8,128)(2,1)S(1)} collective-permute-done((bf16[2,8,4096]{2,1,0:T(8,128)(2,1)S(1)}, bf16[2,8,4096]{2,1,0:T(8,128)(2,1)S(1)}, u32[]{:S(2)}, u32[]{:S(2)}) %collective-permute-start.4) | collective-permute-done | bytes 131104 | tf_op jit(solution)/shard_map/while/body/eval_jaxpr/ppermute | solution.py:40
  178.2 2.6 collective-permute-done.6
  180.8 6.5 %collective-permute-done.7 = bf16[2,8,8,512]{3,1,2,0:T(8,128)(2,1)S(1)} collective-permute-done((bf16[2,8,8,512]{3,1,2,0:T(8,128)(2,1)S(1)}, bf16[2,8,8,512]{3,1,2,0:T(8,128)(2,1)S(1)}, u32[]{:S(2)}, u32[]{:S(2)}) %collective-permute-start.7) | collective-permute-done | bytes 131104 | tf_op jit(solution)/shard_map/while/body/eval_jaxpr/ppermute | solution.py:40
  188.4 3.6 %fusion.109 = f32[8,16,128]{2,1,0:T(8,128)S(1)} fusion(bf16[8,128,2048]{2,1,0:T(8,128)(2,1)} %get-tuple-element.312, bf16[8,8,2048]{2,1,0:T(8,128)(2,1)S(1)} %bitcast.132, bf16[8,8,2048]{2,1,0:T(8,128)(2,1)S(1)} %bitcast.134), kind=kOutput, calls=%fused_computation.21.clone.1 | convolution fusion | flops 68157440 | bytes 4784128 | tf_op jit(solution)/shard_map/while/body/eval_jaxpr/fbs,frs->fbr/dot_general | solution.py:109
  193.8 9.0 %all-reduce.4 = (f32[]{:T(128)}, f32[]{:T(128)}) all-reduce(f32[]{:T(128)} %get-tuple-element.265, f32[]{:T(128)} %multiply_reduce_fusion.3), channel_id=1, replica_groups=mesh['groups'=2,'freq'=4,'recv'=4] {'recv'}, use_global_device_ids=true, to_apply=%region_4.4 | all-reduce | flops 2 | bytes 16 | tf_op jit(solution)/shard_map/while/body/eval_jaxpr/psum | solution.py:116
  202.8 6.3 %all-reduce.5 = (f32[]{:T(128)}, f32[]{:T(128)}) all-reduce(f32[]{:T(128)} %get-tuple-element.272, f32[]{:T(128)} %get-tuple-element.273), channel_id=1, replica_groups=mesh['groups'=2,'freq'=4,'recv'=4] {'freq'}, use_global_device_ids=true, to_apply=%region_5.5 | all-reduce | flops 2 | bytes 16 | tf_op jit(solution)/shard_map/while/body/eval_jaxpr/psum | solution.py:115
  210.6 3.0 fusion.99
  218.4 2.5 collective-permute-done
  220.9 9.2 %collective-permute-done.1 = bf16[2,8,8,512]{3,2,1,0:T(8,128)(2,1)S(1)} collective-permute-done((bf16[2,8,8,512]{3,2,1,0:T(8,128)(2,1)S(1)}, bf16[2,8,8,512]{3,2,1,0:T(8,128)(2,1)S(1)}, u32[]{:S(2)}, u32[]{:S(2)}) %collective-permute-start.1) | collective-permute-done | bytes 131104 | tf_op jit(solution)/shard_map/while/body/eval_jaxpr/ppermute | solution.py:40
  233.6 4.6 %collective-permute-done.4 = bf16[2,8,4096]{2,1,0:T(8,128)(2,1)S(1)} collective-permute-done((bf16[2,8,4096]{2,1,0:T(8,128)(2,1)S(1)}, bf16[2,8,4096]{2,1,0:T(8,128)(2,1)S(1)}, u32[]{:S(2)}, u32[]{:S(2)}) %collective-permute-start.4) | collective-permute-done | bytes 131104 | tf_op jit(solution)/shard_map/while/body/eval_jaxpr/ppermute | solution.py:40
  243.9 2.6 collective-permute-done.6
  246.5 6.5 %collective-permute-done.7 = bf16[2,8,8,512]{3,1,2,0:T(8,128)(2,1)S(1)} collective-permute-done((bf16[2,8,8,512]{3,1,2,0:T(8,128)(2,1)S(1)}, bf16[2,8,8,512]{3,1,2,0:T(8,128)(2,1)S(1)}, u32[]{:S(2)}, u32[]{:S(2)}) %collective-permute-start.7) | collective-permute-done | bytes 131104 | tf_op jit(solution)/shard_map/while/body/eval_jaxpr/ppermute | solution.py:40
  254.1 3.6 %fusion.109 = f32[8,16,128]{2,1,0:T(8,128)S(1)} fusion(bf16[8,128,2048]{2,1,0:T(8,128)(2,1)} %get-tuple-element.312, bf16[8,8,2048]{2,1,0:T(8,128)(2,1)S(1)} %bitcast.132, bf16[8,8,2048]{2,1,0:T(8,128)(2,1)S(1)} %bitcast.134), kind=kOutput, calls=%fused_computation.21.clone.1 | convolution fusion | flops 68157440 | bytes 4784128 | tf_op jit(solution)/shard_map/while/body/eval_jaxpr/fbs,frs->fbr/dot_general | solution.py:109
  259.5 9.0 %all-reduce.4 = (f32[]{:T(128)}, f32[]{:T(128)}) all-reduce(f32[]{:T(128)} %get-tuple-element.265, f32[]{:T(128)} %multiply_reduce_fusion.3), channel_id=1, replica_groups=mesh['groups'=2,'freq'=4,'recv'=4] {'recv'}, use_global_device_ids=true, to_apply=%region_4.4 | all-reduce | flops 2 | bytes 16 | tf_op jit(solution)/shard_map/while/body/eval_jaxpr/psum | solution.py:116
  268.6 6.3 %all-reduce.5 = (f32[]{:T(128)}, f32[]{:T(128)}) all-reduce(f32[]{:T(128)} %get-tuple-element.272, f32[]{:T(128)} %get-tuple-element.273), channel_id=1, replica_groups=mesh['groups'=2,'freq'=4,'recv'=4] {'freq'}, use_global_device_ids=true, to_apply=%region_5.5 | all-reduce | flops 2 | bytes 16 | tf_op jit(solution)/shard_map/while/body/eval_jaxpr/psum | solution.py:115
  276.4 3.0 fusion.99
  284.2 2.5 collective-permute-done
  286.6 9.2 %collective-permute-done.1 = bf16[2,8,8,512]{3,2,1,0:T(8,128)(2,1)S(1)} collective-permute-done((bf16[2,8,8,512]{3,2,1,0:T(8,128)(2,1)S(1)}, bf16[2,8,8,512]{3,2,1,0:T(8,128)(2,1)S(1)}, u32[]{:S(2)}, u32[]{:S(2)}) %collective-permute-start.1) | collective-permute-done | bytes 131104 | tf_op jit(solution)/shard_map/while/body/eval_jaxpr/ppermute | solution.py:40
  299.3 4.6 %collective-permute-done.4 = bf16[2,8,4096]{2,1,0:T(8,128)(2,1)S(1)} collective-permute-done((bf16[2,8,4096]{2,1,0:T(8,128)(2,1)S(1)}, bf16[2,8,4096]{2,1,0:T(8,128)(2,1)S(1)}, u32[]{:S(2)}, u32[]{:S(2)}) %collective-permute-start.4) | collective-permute-done | bytes 131104 | tf_op jit(solution)/shard_map/while/body/eval_jaxpr/ppermute | solution.py:40
  309.7 2.6 collective-permute-done.6
  312.3 6.5 %collective-permute-done.7 = bf16[2,8,8,512]{3,1,2,0:T(8,128)(2,1)S(1)} collective-permute-done((bf16[2,8,8,512]{3,1,2,0:T(8,128)(2,1)S(1)}, bf16[2,8,8,512]{3,1,2,0:T(8,128)(2,1)S(1)}, u32[]{:S(2)}, u32[]{:S(2)}) %collective-permute-start.7) | collective-permute-done | bytes 131104 | tf_op jit(solution)/shard_map/while/body/eval_jaxpr/ppermute | solution.py:40
  319.8 3.6 %fusion.109 = f32[8,16,128]{2,1,0:T(8,128)S(1)} fusion(bf16[8,128,2048]{2,1,0:T(8,128)(2,1)} %get-tuple-element.312, bf16[8,8,2048]{2,1,0:T(8,128)(2,1)S(1)} %bitcast.132, bf16[8,8,2048]{2,1,0:T(8,128)(2,1)S(1)} %bitcast.134), kind=kOutput, calls=%fused_computation.21.clone.1 | convolution fusion | flops 68157440 | bytes 4784128 | tf_op jit(solution)/shard_map/while/body/eval_jaxpr/fbs,frs->fbr/dot_general | solution.py:109
  325.3 9.0 %all-reduce.4 = (f32[]{:T(128)}, f32[]{:T(128)}) all-reduce(f32[]{:T(128)} %get-tuple-element.265, f32[]{:T(128)} %multiply_reduce_fusion.3), channel_id=1, replica_groups=mesh['groups'=2,'freq'=4,'recv'=4] {'recv'}, use_global_device_ids=true, to_apply=%region_4.4 | all-reduce | flops 2 | bytes 16 | tf_op jit(solution)/shard_map/while/body/eval_jaxpr/psum | solution.py:116
  334.3 6.3 %all-reduce.5 = (f32[]{:T(128)}, f32[]{:T(128)}) all-reduce(f32[]{:T(128)} %get-tuple-element.272, f32[]{:T(128)} %get-tuple-element.273), channel_id=1, replica_groups=mesh['groups'=2,'freq'=4,'recv'=4] {'freq'}, use_global_device_ids=true, to_apply=%region_5.5 | all-reduce | flops 2 | bytes 16 | tf_op jit(solution)/shard_map/while/body/eval_jaxpr/psum | solution.py:115
  (281 shorter events, 87.6 us)
Async XLA Ops:
  14.7 26.1 %copy-start.2 = (f32[64,4096]{1,0:T(8,128)S(1)}, f32[64,4096]{1,0:T(8,128)}, u32[]{:S(2)}) copy-start(f32[64,4096]{1,0:T(8,128)} %get-tuple-element.314) | copy-start | bytes 3145732 | tf_op jit(solution)/shard_map/while
  14.8 9.0 %collective-permute-start = (bf16[2,8,8,512]{3,2,1,0:T(8,128)(2,1)S(1)}, bf16[2,8,8,512]{3,2,1,0:T(8,128)(2,1)S(1)}, u32[]{:S(2)}, u32[]{:S(2)}) collective-permute-start(bf16[2,8,8,512]{3,2,1,0:T(8,128)(2,1)S(1)} %get-tuple-element.260), channel_id=1, source_target_pairs={{0,3},{1,0},{2,1},{3,2},{4,7},{5,4},{6,5},{7,6},{8,11},{9,8},{10,9... | collective-permute-start | bytes 393224 | tf_op jit(solution)/shard_map/while/body/eval_jaxpr/ppermute | solution.py:40
  19.9 11.2 %collective-permute-start.1 = (bf16[2,8,8,512]{3,2,1,0:T(8,128)(2,1)S(1)}, bf16[2,8,8,512]{3,2,1,0:T(8,128)(2,1)S(1)}, u32[]{:S(2)}, u32[]{:S(2)}) collective-permute-start(bf16[2,8,8,512]{3,2,1,0:T(8,128)(2,1)S(1)} %get-tuple-element.261), channel_id=1, source_target_pairs={{0,2},{1,3},{2,0},{3,1},{4,6},{5,7},{6,4},{7,5},{8,10},{9,11},{10,... | collective-permute-start | bytes 393224 | tf_op jit(solution)/shard_map/while/body/eval_jaxpr/ppermute | solution.py:40
  19.9 11.2 %collective-permute-start.2 = (bf16[2,8,8,512]{3,2,1,0:T(8,128)(2,1)S(1)}, bf16[2,8,8,512]{3,2,1,0:T(8,128)(2,1)S(1)}, u32[]{:S(2)}, u32[]{:S(2)}) collective-permute-start(bf16[2,8,8,512]{3,2,1,0:T(8,128)(2,1)S(1)} %get-tuple-element.262), channel_id=1, source_target_pairs={{0,1},{1,2},{2,3},{3,0},{4,5},{5,6},{6,7},{7,4},{8,9},{9,10},{10,1... | collective-permute-start | bytes 393224 | tf_op jit(solution)/shard_map/while/body/eval_jaxpr/ppermute | solution.py:40
  31.3 3.9 %collective-permute-start.3 = (bf16[2,8,4096]{2,1,0:T(8,128)(2,1)S(1)}, bf16[2,8,4096]{2,1,0:T(8,128)(2,1)S(1)}, u32[]{:S(2)}, u32[]{:S(2)}) collective-permute-start(bf16[2,8,4096]{2,1,0:T(8,128)(2,1)S(1)} %reshape.248), channel_id=1, source_target_pairs={{0,12},{4,0},{8,4},{12,8},{1,13},{5,1},{9,5},{13,9},{2,14},{6,2},{... | collective-permute-start | bytes 393224 | tf_op jit(solution)/shard_map/while/body/eval_jaxpr/ppermute | solution.py:40
  31.8 8.1 %collective-permute-start.4 = (bf16[2,8,4096]{2,1,0:T(8,128)(2,1)S(1)}, bf16[2,8,4096]{2,1,0:T(8,128)(2,1)S(1)}, u32[]{:S(2)}, u32[]{:S(2)}) collective-permute-start(bf16[2,8,4096]{2,1,0:T(8,128)(2,1)S(1)} %reshape.248), channel_id=1, source_target_pairs={{0,8},{4,12},{8,0},{12,4},{1,9},{5,13},{9,1},{13,5},{2,10},{6,14},... | collective-permute-start | bytes 393224 | tf_op jit(solution)/shard_map/while/body/eval_jaxpr/ppermute | solution.py:40
  32.9 7.1 %collective-permute-start.5 = (bf16[2,8,4096]{2,1,0:T(8,128)(2,1)S(1)}, bf16[2,8,4096]{2,1,0:T(8,128)(2,1)S(1)}, u32[]{:S(2)}, u32[]{:S(2)}) collective-permute-start(bf16[2,8,4096]{2,1,0:T(8,128)(2,1)S(1)} %reshape.248), channel_id=1, source_target_pairs={{0,4},{4,8},{8,12},{12,0},{1,5},{5,9},{9,13},{13,1},{2,6},{6,10},{... | collective-permute-start | bytes 393224 | tf_op jit(solution)/shard_map/while/body/eval_jaxpr/ppermute | solution.py:40
  42.6 5.9 %collective-permute-start.6 = (bf16[2,8,8,512]{3,1,2,0:T(8,128)(2,1)S(1)}, bf16[2,8,8,512]{3,1,2,0:T(8,128)(2,1)S(1)}, u32[]{:S(2)}, u32[]{:S(2)}) collective-permute-start(bf16[2,8,8,512]{3,1,2,0:T(8,128)(2,1)S(1)} %bitcast.142), channel_id=1, source_target_pairs={{0,3},{1,0},{2,1},{3,2},{4,7},{5,4},{6,5},{7,6},{8,11},{9,8},{10,9... | collective-permute-start | bytes 393224 | tf_op jit(solution)/shard_map/while/body/eval_jaxpr/ppermute | solution.py:40
  44.3 11.6 %collective-permute-start.7 = (bf16[2,8,8,512]{3,1,2,0:T(8,128)(2,1)S(1)}, bf16[2,8,8,512]{3,1,2,0:T(8,128)(2,1)S(1)}, u32[]{:S(2)}, u32[]{:S(2)}) collective-permute-start(bf16[2,8,8,512]{3,1,2,0:T(8,128)(2,1)S(1)} %bitcast.143), channel_id=1, source_target_pairs={{0,2},{1,3},{2,0},{3,1},{4,6},{5,7},{6,4},{7,5},{8,10},{9,11},{10,... | collective-permute-start | bytes 393224 | tf_op jit(solution)/shard_map/while/body/eval_jaxpr/ppermute | solution.py:40
  45.3 10.6 %collective-permute-start.8 = (bf16[2,8,8,512]{3,1,2,0:T(8,128)(2,1)S(1)}, bf16[2,8,8,512]{3,1,2,0:T(8,128)(2,1)S(1)}, u32[]{:S(2)}, u32[]{:S(2)}) collective-permute-start(bf16[2,8,8,512]{3,1,2,0:T(8,128)(2,1)S(1)} %bitcast.144), channel_id=1, source_target_pairs={{0,1},{1,2},{2,3},{3,0},{4,5},{5,6},{6,7},{7,4},{8,9},{9,10},{10,1... | collective-permute-start | bytes 393224 | tf_op jit(solution)/shard_map/while/body/eval_jaxpr/ppermute | solution.py:40
  83.7 5.7 %collective-permute-start = (bf16[2,8,8,512]{3,2,1,0:T(8,128)(2,1)S(1)}, bf16[2,8,8,512]{3,2,1,0:T(8,128)(2,1)S(1)}, u32[]{:S(2)}, u32[]{:S(2)}) collective-permute-start(bf16[2,8,8,512]{3,2,1,0:T(8,128)(2,1)S(1)} %get-tuple-element.260), channel_id=1, source_target_pairs={{0,3},{1,0},{2,1},{3,2},{4,7},{5,4},{6,5},{7,6},{8,11},{9,8},{10,9... | collective-permute-start | bytes 393224 | tf_op jit(solution)/shard_map/while/body/eval_jaxpr/ppermute | solution.py:40
  85.5 13.1 %collective-permute-start.1 = (bf16[2,8,8,512]{3,2,1,0:T(8,128)(2,1)S(1)}, bf16[2,8,8,512]{3,2,1,0:T(8,128)(2,1)S(1)}, u32[]{:S(2)}, u32[]{:S(2)}) collective-permute-start(bf16[2,8,8,512]{3,2,1,0:T(8,128)(2,1)S(1)} %get-tuple-element.261), channel_id=1, source_target_pairs={{0,2},{1,3},{2,0},{3,1},{4,6},{5,7},{6,4},{7,5},{8,10},{9,11},{10,... | collective-permute-start | bytes 393224 | tf_op jit(solution)/shard_map/while/body/eval_jaxpr/ppermute | solution.py:40
  86.9 11.7 %collective-permute-start.2 = (bf16[2,8,8,512]{3,2,1,0:T(8,128)(2,1)S(1)}, bf16[2,8,8,512]{3,2,1,0:T(8,128)(2,1)S(1)}, u32[]{:S(2)}, u32[]{:S(2)}) collective-permute-start(bf16[2,8,8,512]{3,2,1,0:T(8,128)(2,1)S(1)} %get-tuple-element.262), channel_id=1, source_target_pairs={{0,1},{1,2},{2,3},{3,0},{4,5},{5,6},{6,7},{7,4},{8,9},{9,10},{10,1... | collective-permute-start | bytes 393224 | tf_op jit(solution)/shard_map/while/body/eval_jaxpr/ppermute | solution.py:40
  98.7 3.2 collective-permute-start.3
  98.8 8.1 %collective-permute-start.4 = (bf16[2,8,4096]{2,1,0:T(8,128)(2,1)S(1)}, bf16[2,8,4096]{2,1,0:T(8,128)(2,1)S(1)}, u32[]{:S(2)}, u32[]{:S(2)}) collective-permute-start(bf16[2,8,4096]{2,1,0:T(8,128)(2,1)S(1)} %reshape.248), channel_id=1, source_target_pairs={{0,8},{4,12},{8,0},{12,4},{1,9},{5,13},{9,1},{13,5},{2,10},{6,14},... | collective-permute-start | bytes 393224 | tf_op jit(solution)/shard_map/while/body/eval_jaxpr/ppermute | solution.py:40
  100.1 7.1 %collective-permute-start.5 = (bf16[2,8,4096]{2,1,0:T(8,128)(2,1)S(1)}, bf16[2,8,4096]{2,1,0:T(8,128)(2,1)S(1)}, u32[]{:S(2)}, u32[]{:S(2)}) collective-permute-start(bf16[2,8,4096]{2,1,0:T(8,128)(2,1)S(1)} %reshape.248), channel_id=1, source_target_pairs={{0,4},{4,8},{8,12},{12,0},{1,5},{5,9},{9,13},{13,1},{2,6},{6,10},{... | collective-permute-start | bytes 393224 | tf_op jit(solution)/shard_map/while/body/eval_jaxpr/ppermute | solution.py:40
  109.8 5.4 %collective-permute-start.6 = (bf16[2,8,8,512]{3,1,2,0:T(8,128)(2,1)S(1)}, bf16[2,8,8,512]{3,1,2,0:T(8,128)(2,1)S(1)}, u32[]{:S(2)}, u32[]{:S(2)}) collective-permute-start(bf16[2,8,8,512]{3,1,2,0:T(8,128)(2,1)S(1)} %bitcast.142), channel_id=1, source_target_pairs={{0,3},{1,0},{2,1},{3,2},{4,7},{5,4},{6,5},{7,6},{8,11},{9,8},{10,9... | collective-permute-start | bytes 393224 | tf_op jit(solution)/shard_map/while/body/eval_jaxpr/ppermute | solution.py:40
  109.9 11.7 %collective-permute-start.7 = (bf16[2,8,8,512]{3,1,2,0:T(8,128)(2,1)S(1)}, bf16[2,8,8,512]{3,1,2,0:T(8,128)(2,1)S(1)}, u32[]{:S(2)}, u32[]{:S(2)}) collective-permute-start(bf16[2,8,8,512]{3,1,2,0:T(8,128)(2,1)S(1)} %bitcast.143), channel_id=1, source_target_pairs={{0,2},{1,3},{2,0},{3,1},{4,6},{5,7},{6,4},{7,5},{8,10},{9,11},{10,... | collective-permute-start | bytes 393224 | tf_op jit(solution)/shard_map/while/body/eval_jaxpr/ppermute | solution.py:40
  110.5 11.1 %collective-permute-start.8 = (bf16[2,8,8,512]{3,1,2,0:T(8,128)(2,1)S(1)}, bf16[2,8,8,512]{3,1,2,0:T(8,128)(2,1)S(1)}, u32[]{:S(2)}, u32[]{:S(2)}) collective-permute-start(bf16[2,8,8,512]{3,1,2,0:T(8,128)(2,1)S(1)} %bitcast.144), channel_id=1, source_target_pairs={{0,1},{1,2},{2,3},{3,0},{4,5},{5,6},{6,7},{7,4},{8,9},{9,10},{10,1... | collective-permute-start | bytes 393224 | tf_op jit(solution)/shard_map/while/body/eval_jaxpr/ppermute | solution.py:40
  149.1 24.5 %copy-start.2 = (f32[64,4096]{1,0:T(8,128)S(1)}, f32[64,4096]{1,0:T(8,128)}, u32[]{:S(2)}) copy-start(f32[64,4096]{1,0:T(8,128)} %get-tuple-element.314) | copy-start | bytes 3145732 | tf_op jit(solution)/shard_map/while
  149.2 6.0 %collective-permute-start = (bf16[2,8,8,512]{3,2,1,0:T(8,128)(2,1)S(1)}, bf16[2,8,8,512]{3,2,1,0:T(8,128)(2,1)S(1)}, u32[]{:S(2)}, u32[]{:S(2)}) collective-permute-start(bf16[2,8,8,512]{3,2,1,0:T(8,128)(2,1)S(1)} %get-tuple-element.260), channel_id=1, source_target_pairs={{0,3},{1,0},{2,1},{3,2},{4,7},{5,4},{6,5},{7,6},{8,11},{9,8},{10,9... | collective-permute-start | bytes 393224 | tf_op jit(solution)/shard_map/while/body/eval_jaxpr/ppermute | solution.py:40
  151.2 13.1 %collective-permute-start.1 = (bf16[2,8,8,512]{3,2,1,0:T(8,128)(2,1)S(1)}, bf16[2,8,8,512]{3,2,1,0:T(8,128)(2,1)S(1)}, u32[]{:S(2)}, u32[]{:S(2)}) collective-permute-start(bf16[2,8,8,512]{3,2,1,0:T(8,128)(2,1)S(1)} %get-tuple-element.261), channel_id=1, source_target_pairs={{0,2},{1,3},{2,0},{3,1},{4,6},{5,7},{6,4},{7,5},{8,10},{9,11},{10,... | collective-permute-start | bytes 393224 | tf_op jit(solution)/shard_map/while/body/eval_jaxpr/ppermute | solution.py:40
  152.7 11.7 %collective-permute-start.2 = (bf16[2,8,8,512]{3,2,1,0:T(8,128)(2,1)S(1)}, bf16[2,8,8,512]{3,2,1,0:T(8,128)(2,1)S(1)}, u32[]{:S(2)}, u32[]{:S(2)}) collective-permute-start(bf16[2,8,8,512]{3,2,1,0:T(8,128)(2,1)S(1)} %get-tuple-element.262), channel_id=1, source_target_pairs={{0,1},{1,2},{2,3},{3,0},{4,5},{5,6},{6,7},{7,4},{8,9},{9,10},{10,1... | collective-permute-start | bytes 393224 | tf_op jit(solution)/shard_map/while/body/eval_jaxpr/ppermute | solution.py:40
  164.5 3.3 collective-permute-start.3
  164.5 7.9 %collective-permute-start.4 = (bf16[2,8,4096]{2,1,0:T(8,128)(2,1)S(1)}, bf16[2,8,4096]{2,1,0:T(8,128)(2,1)S(1)}, u32[]{:S(2)}, u32[]{:S(2)}) collective-permute-start(bf16[2,8,4096]{2,1,0:T(8,128)(2,1)S(1)} %reshape.248), channel_id=1, source_target_pairs={{0,8},{4,12},{8,0},{12,4},{1,9},{5,13},{9,1},{13,5},{2,10},{6,14},... | collective-permute-start | bytes 393224 | tf_op jit(solution)/shard_map/while/body/eval_jaxpr/ppermute | solution.py:40
  165.7 7.1 %collective-permute-start.5 = (bf16[2,8,4096]{2,1,0:T(8,128)(2,1)S(1)}, bf16[2,8,4096]{2,1,0:T(8,128)(2,1)S(1)}, u32[]{:S(2)}, u32[]{:S(2)}) collective-permute-start(bf16[2,8,4096]{2,1,0:T(8,128)(2,1)S(1)} %reshape.248), channel_id=1, source_target_pairs={{0,4},{4,8},{8,12},{12,0},{1,5},{5,9},{9,13},{13,1},{2,6},{6,10},{... | collective-permute-start | bytes 393224 | tf_op jit(solution)/shard_map/while/body/eval_jaxpr/ppermute | solution.py:40
  175.5 5.4 %collective-permute-start.6 = (bf16[2,8,8,512]{3,1,2,0:T(8,128)(2,1)S(1)}, bf16[2,8,8,512]{3,1,2,0:T(8,128)(2,1)S(1)}, u32[]{:S(2)}, u32[]{:S(2)}) collective-permute-start(bf16[2,8,8,512]{3,1,2,0:T(8,128)(2,1)S(1)} %bitcast.142), channel_id=1, source_target_pairs={{0,3},{1,0},{2,1},{3,2},{4,7},{5,4},{6,5},{7,6},{8,11},{9,8},{10,9... | collective-permute-start | bytes 393224 | tf_op jit(solution)/shard_map/while/body/eval_jaxpr/ppermute | solution.py:40
  175.5 11.8 %collective-permute-start.7 = (bf16[2,8,8,512]{3,1,2,0:T(8,128)(2,1)S(1)}, bf16[2,8,8,512]{3,1,2,0:T(8,128)(2,1)S(1)}, u32[]{:S(2)}, u32[]{:S(2)}) collective-permute-start(bf16[2,8,8,512]{3,1,2,0:T(8,128)(2,1)S(1)} %bitcast.143), channel_id=1, source_target_pairs={{0,2},{1,3},{2,0},{3,1},{4,6},{5,7},{6,4},{7,5},{8,10},{9,11},{10,... | collective-permute-start | bytes 393224 | tf_op jit(solution)/shard_map/while/body/eval_jaxpr/ppermute | solution.py:40
  176.2 11.2 %collective-permute-start.8 = (bf16[2,8,8,512]{3,1,2,0:T(8,128)(2,1)S(1)}, bf16[2,8,8,512]{3,1,2,0:T(8,128)(2,1)S(1)}, u32[]{:S(2)}, u32[]{:S(2)}) collective-permute-start(bf16[2,8,8,512]{3,1,2,0:T(8,128)(2,1)S(1)} %bitcast.144), channel_id=1, source_target_pairs={{0,1},{1,2},{2,3},{3,0},{4,5},{5,6},{6,7},{7,4},{8,9},{9,10},{10,1... | collective-permute-start | bytes 393224 | tf_op jit(solution)/shard_map/while/body/eval_jaxpr/ppermute | solution.py:40
  214.9 6.0 %collective-permute-start = (bf16[2,8,8,512]{3,2,1,0:T(8,128)(2,1)S(1)}, bf16[2,8,8,512]{3,2,1,0:T(8,128)(2,1)S(1)}, u32[]{:S(2)}, u32[]{:S(2)}) collective-permute-start(bf16[2,8,8,512]{3,2,1,0:T(8,128)(2,1)S(1)} %get-tuple-element.260), channel_id=1, source_target_pairs={{0,3},{1,0},{2,1},{3,2},{4,7},{5,4},{6,5},{7,6},{8,11},{9,8},{10,9... | collective-permute-start | bytes 393224 | tf_op jit(solution)/shard_map/while/body/eval_jaxpr/ppermute | solution.py:40
  217.0 13.1 %collective-permute-start.1 = (bf16[2,8,8,512]{3,2,1,0:T(8,128)(2,1)S(1)}, bf16[2,8,8,512]{3,2,1,0:T(8,128)(2,1)S(1)}, u32[]{:S(2)}, u32[]{:S(2)}) collective-permute-start(bf16[2,8,8,512]{3,2,1,0:T(8,128)(2,1)S(1)} %get-tuple-element.261), channel_id=1, source_target_pairs={{0,2},{1,3},{2,0},{3,1},{4,6},{5,7},{6,4},{7,5},{8,10},{9,11},{10,... | collective-permute-start | bytes 393224 | tf_op jit(solution)/shard_map/while/body/eval_jaxpr/ppermute | solution.py:40
  218.4 11.7 %collective-permute-start.2 = (bf16[2,8,8,512]{3,2,1,0:T(8,128)(2,1)S(1)}, bf16[2,8,8,512]{3,2,1,0:T(8,128)(2,1)S(1)}, u32[]{:S(2)}, u32[]{:S(2)}) collective-permute-start(bf16[2,8,8,512]{3,2,1,0:T(8,128)(2,1)S(1)} %get-tuple-element.262), channel_id=1, source_target_pairs={{0,1},{1,2},{2,3},{3,0},{4,5},{5,6},{6,7},{7,4},{8,9},{9,10},{10,1... | collective-permute-start | bytes 393224 | tf_op jit(solution)/shard_map/while/body/eval_jaxpr/ppermute | solution.py:40
  230.2 3.3 collective-permute-start.3
  230.3 7.9 %collective-permute-start.4 = (bf16[2,8,4096]{2,1,0:T(8,128)(2,1)S(1)}, bf16[2,8,4096]{2,1,0:T(8,128)(2,1)S(1)}, u32[]{:S(2)}, u32[]{:S(2)}) collective-permute-start(bf16[2,8,4096]{2,1,0:T(8,128)(2,1)S(1)} %reshape.248), channel_id=1, source_target_pairs={{0,8},{4,12},{8,0},{12,4},{1,9},{5,13},{9,1},{13,5},{2,10},{6,14},... | collective-permute-start | bytes 393224 | tf_op jit(solution)/shard_map/while/body/eval_jaxpr/ppermute | solution.py:40
  231.4 7.1 %collective-permute-start.5 = (bf16[2,8,4096]{2,1,0:T(8,128)(2,1)S(1)}, bf16[2,8,4096]{2,1,0:T(8,128)(2,1)S(1)}, u32[]{:S(2)}, u32[]{:S(2)}) collective-permute-start(bf16[2,8,4096]{2,1,0:T(8,128)(2,1)S(1)} %reshape.248), channel_id=1, source_target_pairs={{0,4},{4,8},{8,12},{12,0},{1,5},{5,9},{9,13},{13,1},{2,6},{6,10},{... | collective-permute-start | bytes 393224 | tf_op jit(solution)/shard_map/while/body/eval_jaxpr/ppermute | solution.py:40
  241.2 5.4 %collective-permute-start.6 = (bf16[2,8,8,512]{3,1,2,0:T(8,128)(2,1)S(1)}, bf16[2,8,8,512]{3,1,2,0:T(8,128)(2,1)S(1)}, u32[]{:S(2)}, u32[]{:S(2)}) collective-permute-start(bf16[2,8,8,512]{3,1,2,0:T(8,128)(2,1)S(1)} %bitcast.142), channel_id=1, source_target_pairs={{0,3},{1,0},{2,1},{3,2},{4,7},{5,4},{6,5},{7,6},{8,11},{9,8},{10,9... | collective-permute-start | bytes 393224 | tf_op jit(solution)/shard_map/while/body/eval_jaxpr/ppermute | solution.py:40
  241.2 11.9 %collective-permute-start.7 = (bf16[2,8,8,512]{3,1,2,0:T(8,128)(2,1)S(1)}, bf16[2,8,8,512]{3,1,2,0:T(8,128)(2,1)S(1)}, u32[]{:S(2)}, u32[]{:S(2)}) collective-permute-start(bf16[2,8,8,512]{3,1,2,0:T(8,128)(2,1)S(1)} %bitcast.143), channel_id=1, source_target_pairs={{0,2},{1,3},{2,0},{3,1},{4,6},{5,7},{6,4},{7,5},{8,10},{9,11},{10,... | collective-permute-start | bytes 393224 | tf_op jit(solution)/shard_map/while/body/eval_jaxpr/ppermute | solution.py:40
  241.9 11.2 %collective-permute-start.8 = (bf16[2,8,8,512]{3,1,2,0:T(8,128)(2,1)S(1)}, bf16[2,8,8,512]{3,1,2,0:T(8,128)(2,1)S(1)}, u32[]{:S(2)}, u32[]{:S(2)}) collective-permute-start(bf16[2,8,8,512]{3,1,2,0:T(8,128)(2,1)S(1)} %bitcast.144), channel_id=1, source_target_pairs={{0,1},{1,2},{2,3},{3,0},{4,5},{5,6},{6,7},{7,4},{8,9},{9,10},{10,1... | collective-permute-start | bytes 393224 | tf_op jit(solution)/shard_map/while/body/eval_jaxpr/ppermute | solution.py:40
  280.6 24.5 %copy-start.2 = (f32[64,4096]{1,0:T(8,128)S(1)}, f32[64,4096]{1,0:T(8,128)}, u32[]{:S(2)}) copy-start(f32[64,4096]{1,0:T(8,128)} %get-tuple-element.314) | copy-start | bytes 3145732 | tf_op jit(solution)/shard_map/while
  280.7 6.0 %collective-permute-start = (bf16[2,8,8,512]{3,2,1,0:T(8,128)(2,1)S(1)}, bf16[2,8,8,512]{3,2,1,0:T(8,128)(2,1)S(1)}, u32[]{:S(2)}, u32[]{:S(2)}) collective-permute-start(bf16[2,8,8,512]{3,2,1,0:T(8,128)(2,1)S(1)} %get-tuple-element.260), channel_id=1, source_target_pairs={{0,3},{1,0},{2,1},{3,2},{4,7},{5,4},{6,5},{7,6},{8,11},{9,8},{10,9... | collective-permute-start | bytes 393224 | tf_op jit(solution)/shard_map/while/body/eval_jaxpr/ppermute | solution.py:40
  282.7 13.1 %collective-permute-start.1 = (bf16[2,8,8,512]{3,2,1,0:T(8,128)(2,1)S(1)}, bf16[2,8,8,512]{3,2,1,0:T(8,128)(2,1)S(1)}, u32[]{:S(2)}, u32[]{:S(2)}) collective-permute-start(bf16[2,8,8,512]{3,2,1,0:T(8,128)(2,1)S(1)} %get-tuple-element.261), channel_id=1, source_target_pairs={{0,2},{1,3},{2,0},{3,1},{4,6},{5,7},{6,4},{7,5},{8,10},{9,11},{10,... | collective-permute-start | bytes 393224 | tf_op jit(solution)/shard_map/while/body/eval_jaxpr/ppermute | solution.py:40
  284.1 11.7 %collective-permute-start.2 = (bf16[2,8,8,512]{3,2,1,0:T(8,128)(2,1)S(1)}, bf16[2,8,8,512]{3,2,1,0:T(8,128)(2,1)S(1)}, u32[]{:S(2)}, u32[]{:S(2)}) collective-permute-start(bf16[2,8,8,512]{3,2,1,0:T(8,128)(2,1)S(1)} %get-tuple-element.262), channel_id=1, source_target_pairs={{0,1},{1,2},{2,3},{3,0},{4,5},{5,6},{6,7},{7,4},{8,9},{9,10},{10,1... | collective-permute-start | bytes 393224 | tf_op jit(solution)/shard_map/while/body/eval_jaxpr/ppermute | solution.py:40
  296.0 3.3 collective-permute-start.3
  296.0 7.9 %collective-permute-start.4 = (bf16[2,8,4096]{2,1,0:T(8,128)(2,1)S(1)}, bf16[2,8,4096]{2,1,0:T(8,128)(2,1)S(1)}, u32[]{:S(2)}, u32[]{:S(2)}) collective-permute-start(bf16[2,8,4096]{2,1,0:T(8,128)(2,1)S(1)} %reshape.248), channel_id=1, source_target_pairs={{0,8},{4,12},{8,0},{12,4},{1,9},{5,13},{9,1},{13,5},{2,10},{6,14},... | collective-permute-start | bytes 393224 | tf_op jit(solution)/shard_map/while/body/eval_jaxpr/ppermute | solution.py:40
  297.2 7.1 %collective-permute-start.5 = (bf16[2,8,4096]{2,1,0:T(8,128)(2,1)S(1)}, bf16[2,8,4096]{2,1,0:T(8,128)(2,1)S(1)}, u32[]{:S(2)}, u32[]{:S(2)}) collective-permute-start(bf16[2,8,4096]{2,1,0:T(8,128)(2,1)S(1)} %reshape.248), channel_id=1, source_target_pairs={{0,4},{4,8},{8,12},{12,0},{1,5},{5,9},{9,13},{13,1},{2,6},{6,10},{... | collective-permute-start | bytes 393224 | tf_op jit(solution)/shard_map/while/body/eval_jaxpr/ppermute | solution.py:40
  307.0 5.4 %collective-permute-start.6 = (bf16[2,8,8,512]{3,1,2,0:T(8,128)(2,1)S(1)}, bf16[2,8,8,512]{3,1,2,0:T(8,128)(2,1)S(1)}, u32[]{:S(2)}, u32[]{:S(2)}) collective-permute-start(bf16[2,8,8,512]{3,1,2,0:T(8,128)(2,1)S(1)} %bitcast.142), channel_id=1, source_target_pairs={{0,3},{1,0},{2,1},{3,2},{4,7},{5,4},{6,5},{7,6},{8,11},{9,8},{10,9... | collective-permute-start | bytes 393224 | tf_op jit(solution)/shard_map/while/body/eval_jaxpr/ppermute | solution.py:40
  307.0 11.9 %collective-permute-start.7 = (bf16[2,8,8,512]{3,1,2,0:T(8,128)(2,1)S(1)}, bf16[2,8,8,512]{3,1,2,0:T(8,128)(2,1)S(1)}, u32[]{:S(2)}, u32[]{:S(2)}) collective-permute-start(bf16[2,8,8,512]{3,1,2,0:T(8,128)(2,1)S(1)} %bitcast.143), channel_id=1, source_target_pairs={{0,2},{1,3},{2,0},{3,1},{4,6},{5,7},{6,4},{7,5},{8,10},{9,11},{10,... | collective-permute-start | bytes 393224 | tf_op jit(solution)/shard_map/while/body/eval_jaxpr/ppermute | solution.py:40
  307.6 11.2 %collective-permute-start.8 = (bf16[2,8,8,512]{3,1,2,0:T(8,128)(2,1)S(1)}, bf16[2,8,8,512]{3,1,2,0:T(8,128)(2,1)S(1)}, u32[]{:S(2)}, u32[]{:S(2)}) collective-permute-start(bf16[2,8,8,512]{3,1,2,0:T(8,128)(2,1)S(1)} %bitcast.144), channel_id=1, source_target_pairs={{0,1},{1,2},{2,3},{3,0},{4,5},{5,6},{6,7},{7,4},{8,9},{9,10},{10,1... | collective-permute-start | bytes 393224 | tf_op jit(solution)/shard_map/while/body/eval_jaxpr/ppermute | solution.py:40
  (16 other events, 109.2 us)

commit v5 on v4

--- a/solution.py
+++ b/solution.py
@@ -96,7 +96,7 @@
             jnp.stack([partial_real, partial_imag]).astype(jnp.bfloat16), "recv", 3
         )
         flattened = gradient.astype(jnp.bfloat16).reshape(2, freq_local, columns)
-        segment = gather_blocks(flattened, "freq", 1).astype(jnp.float32)
+        segment = lax.all_gather(flattened, "freq", axis=1, tiled=True).astype(jnp.float32)
         timed = high_dot(to_time, segment.reshape(2 * total_freq, columns))
         projected = high_dot(to_freq, timed * window)
         direction = projected.reshape(2, freq_local, right_sides, src_local)
@@ -112,9 +112,9 @@
         image_real = by_real[:, :right_sides] - by_imag[:, right_sides:]
         image_imag = by_imag[:, :right_sides] + by_real[:, right_sides:]
         image = jnp.stack([image_real, image_imag])
-        direction_power, image_energy = lax.psum(
-            lax.psum((jnp.sum(direction * direction), jnp.sum(image * image)), "recv"), "freq"
-        )
+        sums = jnp.stack([jnp.sum(direction * direction), jnp.sum(image * image)])
+        sums = jnp.sum(gather_blocks(sums[None], "recv", 0), axis=0)
+        direction_power, image_energy = jnp.sum(gather_blocks(sums[None], "freq", 0), axis=0)
         step_length = direction_power / (image_energy + 1e-06)
         return (reflect + step_length * direction, residual - step_length * image)
 

time: 343 us -> 334 us (0.974)
  blocking collectives: 76.9 us -> 33.5 us
  starting transfers between devices: 42.8 us -> 57.4 us
  other arithmetic: 10.9 us -> 24.8 us
  matrix products: 51.2 us -> 57.3 us
  waiting for transfers between devices: 135 us -> 129 us
  local copies, waits for them, and re-layouts: 17.7 us -> 23 us
    psum x10 -> x0, blocking collectives: 76.9 us -> none  [the longest x5 45.4 us: step(): lax.psum((jnp.sum(direction * direction), jnp.sum(image * image)), 'recv')]
    all_gather x0 -> x5, blocking collectives: none -> 33.5 us  [step(): lax.all_gather(flattened, 'freq', axis=1, tiled=True).astype(jnp.float32)]
    ppermute x45 -> x60, starting transfers between devices: 42.8 us -> 57.4 us  [shifted(): lax.ppermute(value, axis, [(i, (i + distance) % size) for i in range(size)])]
    broadcast_in_dim x0 -> x10, other arithmetic: none -> 13.5 us  [the longest x5 6.73 us: step(): sums = jnp.sum(gather_blocks(sums[None], 'recv', 0), axis=0)]
    dot_general x10, matrix products: 9.12 us -> 15.2 us  [high_dot(): return jnp.dot(left, right, precision=lax.Precision.HIGHEST)]
    ppermute x45 -> x60, waiting for transfers between devices: 135 us -> 129 us  [shifted(): lax.ppermute(value, axis, [(i, (i + distance) % size) for i in range(size)])]
    gather x15 -> x25, local copies, waits for them, and re-layouts: 5.98 us -> 9.43 us  [gather_blocks(): ordered = jnp.take(slots, order, axis=dim)]
  transfers between devices with their start and end apart: 45 -> 60, of which waited for: 35 -> 36; matrix products, arithmetic and copies ran while one was open for 0% -> 2% of each run, Pallas kernels for 0% -> 0%
where the time goes in v5:
time: 334 us
  waiting for transfers between devices  129 us (39%)
  starting transfers between devices  57.4 us (17%)
  matrix products  57.3 us (17%)
  blocking collectives  33.5 us (10%)
  other arithmetic  24.8 us (7%)
  local copies, waits for them, and re-layouts  23 us (7%)
  loops' own time  7.75 us (2%)
    ppermute x60, waiting for transfers between devices, shifted(): lax.ppermute(value, axis, [(i, (i + distance) % size) for i in range(size)])  129 us
    ppermute x60, starting transfers between devices, shifted(): lax.ppermute(value, axis, [(i, (i + distance) % size) for i in range(size)])  57.4 us
    all_gather x5, blocking collectives, step(): lax.all_gather(flattened, 'freq', axis=1, tiled=True).astype(jnp.float32)  33.5 us
    dot_general x5, matrix products, step(): jnp.einsum('fbs,frs->fbr', stacked_direction, imag_operator, preferred_el...  17.8 us
    dot_general x10, matrix products, high_dot(): return jnp.dot(left, right, precision=lax.Precision.HIGHEST)  15.2 us
    dot_general x5, matrix products, step(): jnp.einsum('fbr,frs->fbs', stacked_residual, imag_operator, preferred_ele...  15 us
    gather x25, local copies, waits for them, and re-layouts, gather_blocks(): ordered = jnp.take(slots, order, axis=dim)  9.43 us
    another operation x1, loops' own time, on_device(): return lax.fori_loop(0, ITERS, step, (reflect, recorded))  7.75 us
  transfers between devices with their start and end apart: 60, of which 36 were waited for; matrix products, arithmetic and copies ran while one was open for 2% of the time, Pallas kernels for 0%

profile of v5, /device:TPU:0, one launch (start us, length us, event | category | flops | bytes accessed | tf_op | source)
XLA Modules:
  0.0 333.7 jit_solution(9292471267423728963)
XLA Ops:
  0.7 6.1 %slice_bitcast_fusion.2 = (bf16[8,128,2048]{2,1,0:T(8,128)(2,1)}, bf16[8,128,2048]{2,1,0:T(8,128)(2,1)}) fusion(bf16[2,8,128,2048]{3,2,1,0:T(8,128)(2,1)} %param.8), kind=kLoop, calls=%fused_computation.83 | loop fusion | bytes 16777216 | tf_op jit(solution)/shard_map/squeeze | solution.py:71
  10.5 322.3 %while.15 = (s32[]{:T(128)}, f32[2,8,8,512]{3,1,2,0:T(8,128)S(1)}, f32[2,8,8,128]{3,2,1,0:T(8,128)S(1)}, bf16[8,128,2048]{2,1,0:T(8,128)(2,1)}, bf16[8,128,2048]...) while((s32[]{:T(128)}, f32[2,8,8,512]{3,1,2,0:T(8,128)S(1)}, ...), condition=%wide.region_7.9_spmd.clone, body=%wide.region_2.8_spmd.clone.sunk | while | flops 525471104 | bytes 73599128 | solution.py:122
  10.6 3.0 fusion.104
  14.8 5.1 %collective-permute-start = (bf16[2,8,8,512]{3,2,1,0:T(8,128)(2,1)S(1)}, bf16[2,8,8,512]{3,2,1,0:T(8,128)(2,1)S(1)}, u32[]{:S(2)}, u32[]{:S(2)}) collective-permute-start(bf16[2,8,8,512]{3,2,1,0:T(8,128)(2,1)S(1)} %get-tuple-element.253), channel_id=1, source_target_pairs={{0,3},{1,0},{2,1},{3,2},{4,7},{5,4},{6,5},{7,6},{8,11},{9,8},{10,9... | collective-permute-start | bytes 393224 | tf_op jit(solution)/shard_map/while/body/eval_jaxpr/ppermute | solution.py:40
  21.0 2.8 collective-permute-done
  23.8 7.3 %collective-permute-done.1 = bf16[2,8,8,512]{3,2,1,0:T(8,128)(2,1)S(1)} collective-permute-done((bf16[2,8,8,512]{3,2,1,0:T(8,128)(2,1)S(1)}, bf16[2,8,8,512]{3,2,1,0:T(8,128)(2,1)S(1)}, u32[]{:S(2)}, u32[]{:S(2)}) %collective-permute-start.1) | collective-permute-done | bytes 131104 | tf_op jit(solution)/shard_map/while/body/eval_jaxpr/ppermute | solution.py:40
  31.3 7.2 %all_gather.8 = bf16[2,32,4096]{2,1,0:T(8,128)(2,1)S(1)} all-gather(bf16[2,8,4096]{2,1,0:T(8,128)(2,1)S(1)} %reshape.242), channel_id=1, replica_groups=mesh['groups'=2,'freq'=4,'recv'=4] {'freq'}, dimensions={1}, use_global_device_ids=true | all-gather | bytes 655360 | tf_op jit(solution)/shard_map/while/body/eval_jaxpr/all_gather | solution.py:99
  44.1 2.0 collective-permute-start.5
  47.3 9.3 %collective-permute-done.4 = bf16[2,8,8,512]{3,1,2,0:T(8,128)(2,1)S(1)} collective-permute-done((bf16[2,8,8,512]{3,1,2,0:T(8,128)(2,1)S(1)}, bf16[2,8,8,512]{3,1,2,0:T(8,128)(2,1)S(1)}, u32[]{:S(2)}, u32[]{:S(2)}) %collective-permute-start.4) | collective-permute-done | bytes 131104 | tf_op jit(solution)/shard_map/while/body/eval_jaxpr/ppermute | solution.py:40
  57.6 3.6 %fusion.112 = f32[8,16,128]{2,1,0:T(8,128)S(1)} fusion(bf16[8,128,2048]{2,1,0:T(8,128)(2,1)} %get-tuple-element.303, bf16[8,8,2048]{2,1,0:T(8,128)(2,1)S(1)} %bitcast.168, bf16[8,8,2048]{2,1,0:T(8,128)(2,1)S(1)} %bitcast.170), kind=kOutput, calls=%fused_computation.20.clone.1 | convolution fusion | flops 68157440 | bytes 4784128 | tf_op jit(solution)/shard_map/while/body/eval_jaxpr/fbs,frs->fbr/dot_general | solution.py:109
  69.4 2.0 collective-permute-done.8
  73.6 2.3 collective-permute-done.10
  79.1 3.0 fusion.104
  85.5 3.1 collective-permute-done
  88.6 7.7 %collective-permute-done.1 = bf16[2,8,8,512]{3,2,1,0:T(8,128)(2,1)S(1)} collective-permute-done((bf16[2,8,8,512]{3,2,1,0:T(8,128)(2,1)S(1)}, bf16[2,8,8,512]{3,2,1,0:T(8,128)(2,1)S(1)}, u32[]{:S(2)}, u32[]{:S(2)}) %collective-permute-start.1) | collective-permute-done | bytes 131104 | tf_op jit(solution)/shard_map/while/body/eval_jaxpr/ppermute | solution.py:40
  96.5 6.5 %all_gather.8 = bf16[2,32,4096]{2,1,0:T(8,128)(2,1)S(1)} all-gather(bf16[2,8,4096]{2,1,0:T(8,128)(2,1)S(1)} %reshape.242), channel_id=1, replica_groups=mesh['groups'=2,'freq'=4,'recv'=4] {'freq'}, dimensions={1}, use_global_device_ids=true | all-gather | bytes 655360 | tf_op jit(solution)/shard_map/while/body/eval_jaxpr/all_gather | solution.py:99
  109.6 3.0 collective-permute-done.3
  112.7 7.4 %collective-permute-done.4 = bf16[2,8,8,512]{3,1,2,0:T(8,128)(2,1)S(1)} collective-permute-done((bf16[2,8,8,512]{3,1,2,0:T(8,128)(2,1)S(1)}, bf16[2,8,8,512]{3,1,2,0:T(8,128)(2,1)S(1)}, u32[]{:S(2)}, u32[]{:S(2)}) %collective-permute-start.4) | collective-permute-done | bytes 131104 | tf_op jit(solution)/shard_map/while/body/eval_jaxpr/ppermute | solution.py:40
  121.0 3.6 %fusion.112 = f32[8,16,128]{2,1,0:T(8,128)S(1)} fusion(bf16[8,128,2048]{2,1,0:T(8,128)(2,1)} %get-tuple-element.303, bf16[8,8,2048]{2,1,0:T(8,128)(2,1)S(1)} %bitcast.168, bf16[8,8,2048]{2,1,0:T(8,128)(2,1)S(1)} %bitcast.170), kind=kOutput, calls=%fused_computation.20.clone.1 | convolution fusion | flops 68157440 | bytes 4784128 | tf_op jit(solution)/shard_map/while/body/eval_jaxpr/fbs,frs->fbr/dot_general | solution.py:109
  132.6 2.0 collective-permute-done.8
  136.9 2.2 collective-permute-done.10
  142.6 3.0 fusion.104
  149.0 3.1 collective-permute-done
  152.2 7.6 %collective-permute-done.1 = bf16[2,8,8,512]{3,2,1,0:T(8,128)(2,1)S(1)} collective-permute-done((bf16[2,8,8,512]{3,2,1,0:T(8,128)(2,1)S(1)}, bf16[2,8,8,512]{3,2,1,0:T(8,128)(2,1)S(1)}, u32[]{:S(2)}, u32[]{:S(2)}) %collective-permute-start.1) | collective-permute-done | bytes 131104 | tf_op jit(solution)/shard_map/while/body/eval_jaxpr/ppermute | solution.py:40
  159.9 6.6 %all_gather.8 = bf16[2,32,4096]{2,1,0:T(8,128)(2,1)S(1)} all-gather(bf16[2,8,4096]{2,1,0:T(8,128)(2,1)S(1)} %reshape.242), channel_id=1, replica_groups=mesh['groups'=2,'freq'=4,'recv'=4] {'freq'}, dimensions={1}, use_global_device_ids=true | all-gather | bytes 655360 | tf_op jit(solution)/shard_map/while/body/eval_jaxpr/all_gather | solution.py:99
  173.1 3.2 collective-permute-done.3
  176.3 7.1 %collective-permute-done.4 = bf16[2,8,8,512]{3,1,2,0:T(8,128)(2,1)S(1)} collective-permute-done((bf16[2,8,8,512]{3,1,2,0:T(8,128)(2,1)S(1)}, bf16[2,8,8,512]{3,1,2,0:T(8,128)(2,1)S(1)}, u32[]{:S(2)}, u32[]{:S(2)}) %collective-permute-start.4) | collective-permute-done | bytes 131104 | tf_op jit(solution)/shard_map/while/body/eval_jaxpr/ppermute | solution.py:40
  184.5 3.6 %fusion.112 = f32[8,16,128]{2,1,0:T(8,128)S(1)} fusion(bf16[8,128,2048]{2,1,0:T(8,128)(2,1)} %get-tuple-element.303, bf16[8,8,2048]{2,1,0:T(8,128)(2,1)S(1)} %bitcast.168, bf16[8,8,2048]{2,1,0:T(8,128)(2,1)S(1)} %bitcast.170), kind=kOutput, calls=%fused_computation.20.clone.1 | convolution fusion | flops 68157440 | bytes 4784128 | tf_op jit(solution)/shard_map/while/body/eval_jaxpr/fbs,frs->fbr/dot_general | solution.py:109
  196.2 2.0 collective-permute-done.8
  200.3 2.3 collective-permute-done.10
  206.0 3.0 fusion.104
  212.4 3.1 collective-permute-done
  215.5 7.7 %collective-permute-done.1 = bf16[2,8,8,512]{3,2,1,0:T(8,128)(2,1)S(1)} collective-permute-done((bf16[2,8,8,512]{3,2,1,0:T(8,128)(2,1)S(1)}, bf16[2,8,8,512]{3,2,1,0:T(8,128)(2,1)S(1)}, u32[]{:S(2)}, u32[]{:S(2)}) %collective-permute-start.1) | collective-permute-done | bytes 131104 | tf_op jit(solution)/shard_map/while/body/eval_jaxpr/ppermute | solution.py:40
  223.4 6.5 %all_gather.8 = bf16[2,32,4096]{2,1,0:T(8,128)(2,1)S(1)} all-gather(bf16[2,8,4096]{2,1,0:T(8,128)(2,1)S(1)} %reshape.242), channel_id=1, replica_groups=mesh['groups'=2,'freq'=4,'recv'=4] {'freq'}, dimensions={1}, use_global_device_ids=true | all-gather | bytes 655360 | tf_op jit(solution)/shard_map/while/body/eval_jaxpr/all_gather | solution.py:99
  236.5 3.1 collective-permute-done.3
  239.6 7.3 %collective-permute-done.4 = bf16[2,8,8,512]{3,1,2,0:T(8,128)(2,1)S(1)} collective-permute-done((bf16[2,8,8,512]{3,1,2,0:T(8,128)(2,1)S(1)}, bf16[2,8,8,512]{3,1,2,0:T(8,128)(2,1)S(1)}, u32[]{:S(2)}, u32[]{:S(2)}) %collective-permute-start.4) | collective-permute-done | bytes 131104 | tf_op jit(solution)/shard_map/while/body/eval_jaxpr/ppermute | solution.py:40
  247.9 3.6 %fusion.112 = f32[8,16,128]{2,1,0:T(8,128)S(1)} fusion(bf16[8,128,2048]{2,1,0:T(8,128)(2,1)} %get-tuple-element.303, bf16[8,8,2048]{2,1,0:T(8,128)(2,1)S(1)} %bitcast.168, bf16[8,8,2048]{2,1,0:T(8,128)(2,1)S(1)} %bitcast.170), kind=kOutput, calls=%fused_computation.20.clone.1 | convolution fusion | flops 68157440 | bytes 4784128 | tf_op jit(solution)/shard_map/while/body/eval_jaxpr/fbs,frs->fbr/dot_general | solution.py:109
  259.5 2.0 collective-permute-done.8
  263.8 2.2 collective-permute-done.10
  269.5 3.0 fusion.104
  275.9 3.1 collective-permute-done
  279.0 7.6 %collective-permute-done.1 = bf16[2,8,8,512]{3,2,1,0:T(8,128)(2,1)S(1)} collective-permute-done((bf16[2,8,8,512]{3,2,1,0:T(8,128)(2,1)S(1)}, bf16[2,8,8,512]{3,2,1,0:T(8,128)(2,1)S(1)}, u32[]{:S(2)}, u32[]{:S(2)}) %collective-permute-start.1) | collective-permute-done | bytes 131104 | tf_op jit(solution)/shard_map/while/body/eval_jaxpr/ppermute | solution.py:40
  286.8 6.7 %all_gather.8 = bf16[2,32,4096]{2,1,0:T(8,128)(2,1)S(1)} all-gather(bf16[2,8,4096]{2,1,0:T(8,128)(2,1)S(1)} %reshape.242), channel_id=1, replica_groups=mesh['groups'=2,'freq'=4,'recv'=4] {'freq'}, dimensions={1}, use_global_device_ids=true | all-gather | bytes 655360 | tf_op jit(solution)/shard_map/while/body/eval_jaxpr/all_gather | solution.py:99
  299.9 3.3 collective-permute-done.3
  303.2 7.1 %collective-permute-done.4 = bf16[2,8,8,512]{3,1,2,0:T(8,128)(2,1)S(1)} collective-permute-done((bf16[2,8,8,512]{3,1,2,0:T(8,128)(2,1)S(1)}, bf16[2,8,8,512]{3,1,2,0:T(8,128)(2,1)S(1)}, u32[]{:S(2)}, u32[]{:S(2)}) %collective-permute-start.4) | collective-permute-done | bytes 131104 | tf_op jit(solution)/shard_map/while/body/eval_jaxpr/ppermute | solution.py:40
  311.3 3.6 %fusion.112 = f32[8,16,128]{2,1,0:T(8,128)S(1)} fusion(bf16[8,128,2048]{2,1,0:T(8,128)(2,1)} %get-tuple-element.303, bf16[8,8,2048]{2,1,0:T(8,128)(2,1)S(1)} %bitcast.168, bf16[8,8,2048]{2,1,0:T(8,128)(2,1)S(1)} %bitcast.170), kind=kOutput, calls=%fused_computation.20.clone.1 | convolution fusion | flops 68157440 | bytes 4784128 | tf_op jit(solution)/shard_map/while/body/eval_jaxpr/fbs,frs->fbr/dot_general | solution.py:109
  323.1 2.0 collective-permute-done.8
  327.2 2.3 collective-permute-done.10
  (326 shorter events, 120.2 us)
Async XLA Ops:
  14.8 9.0 %collective-permute-start = (bf16[2,8,8,512]{3,2,1,0:T(8,128)(2,1)S(1)}, bf16[2,8,8,512]{3,2,1,0:T(8,128)(2,1)S(1)}, u32[]{:S(2)}, u32[]{:S(2)}) collective-permute-start(bf16[2,8,8,512]{3,2,1,0:T(8,128)(2,1)S(1)} %get-tuple-element.253), channel_id=1, source_target_pairs={{0,3},{1,0},{2,1},{3,2},{4,7},{5,4},{6,5},{7,6},{8,11},{9,8},{10,9... | collective-permute-start | bytes 393224 | tf_op jit(solution)/shard_map/while/body/eval_jaxpr/ppermute | solution.py:40
  19.9 11.2 %collective-permute-start.1 = (bf16[2,8,8,512]{3,2,1,0:T(8,128)(2,1)S(1)}, bf16[2,8,8,512]{3,2,1,0:T(8,128)(2,1)S(1)}, u32[]{:S(2)}, u32[]{:S(2)}) collective-permute-start(bf16[2,8,8,512]{3,2,1,0:T(8,128)(2,1)S(1)} %get-tuple-element.254), channel_id=1, source_target_pairs={{0,2},{1,3},{2,0},{3,1},{4,6},{5,7},{6,4},{7,5},{8,10},{9,11},{10,... | collective-permute-start | bytes 393224 | tf_op jit(solution)/shard_map/while/body/eval_jaxpr/ppermute | solution.py:40
  19.9 11.2 %collective-permute-start.2 = (bf16[2,8,8,512]{3,2,1,0:T(8,128)(2,1)S(1)}, bf16[2,8,8,512]{3,2,1,0:T(8,128)(2,1)S(1)}, u32[]{:S(2)}, u32[]{:S(2)}) collective-permute-start(bf16[2,8,8,512]{3,2,1,0:T(8,128)(2,1)S(1)} %get-tuple-element.255), channel_id=1, source_target_pairs={{0,1},{1,2},{2,3},{3,0},{4,5},{5,6},{6,7},{7,4},{8,9},{9,10},{10,1... | collective-permute-start | bytes 393224 | tf_op jit(solution)/shard_map/while/body/eval_jaxpr/ppermute | solution.py:40
  41.5 5.7 %collective-permute-start.3 = (bf16[2,8,8,512]{3,1,2,0:T(8,128)(2,1)S(1)}, bf16[2,8,8,512]{3,1,2,0:T(8,128)(2,1)S(1)}, u32[]{:S(2)}, u32[]{:S(2)}) collective-permute-start(bf16[2,8,8,512]{3,1,2,0:T(8,128)(2,1)S(1)} %bitcast.178), channel_id=1, source_target_pairs={{0,3},{1,0},{2,1},{3,2},{4,7},{5,4},{6,5},{7,6},{8,11},{9,8},{10,9... | collective-permute-start | bytes 393224 | tf_op jit(solution)/shard_map/while/body/eval_jaxpr/ppermute | solution.py:40
  43.1 13.5 %collective-permute-start.4 = (bf16[2,8,8,512]{3,1,2,0:T(8,128)(2,1)S(1)}, bf16[2,8,8,512]{3,1,2,0:T(8,128)(2,1)S(1)}, u32[]{:S(2)}, u32[]{:S(2)}) collective-permute-start(bf16[2,8,8,512]{3,1,2,0:T(8,128)(2,1)S(1)} %bitcast.179), channel_id=1, source_target_pairs={{0,2},{1,3},{2,0},{3,1},{4,6},{5,7},{6,4},{7,5},{8,10},{9,11},{10,... | collective-permute-start | bytes 393224 | tf_op jit(solution)/shard_map/while/body/eval_jaxpr/ppermute | solution.py:40
  44.1 12.4 %collective-permute-start.5 = (bf16[2,8,8,512]{3,1,2,0:T(8,128)(2,1)S(1)}, bf16[2,8,8,512]{3,1,2,0:T(8,128)(2,1)S(1)}, u32[]{:S(2)}, u32[]{:S(2)}) collective-permute-start(bf16[2,8,8,512]{3,1,2,0:T(8,128)(2,1)S(1)} %bitcast.180), channel_id=1, source_target_pairs={{0,1},{1,2},{2,3},{3,0},{4,5},{5,6},{6,7},{7,4},{8,9},{9,10},{10,1... | collective-permute-start | bytes 393224 | tf_op jit(solution)/shard_map/while/body/eval_jaxpr/ppermute | solution.py:40
  64.4 5.0 %collective-permute-start.6 = (f32[1,2]{1,0:T(1,128)S(1)}, f32[1,2]{1,0:T(1,128)S(1)}, u32[]{:S(2)}, u32[]{:S(2)}) collective-permute-start(f32[1,2]{1,0:T(1,128)S(1)} %fusion.115), channel_id=1, source_target_pairs={{0,3},{1,0},{2,1},{3,2},{4,7},{5,4},{6,5},{7,6},{8,11},{9,8},{10,9... | collective-permute-start | bytes 32 | tf_op jit(solution)/shard_map/while/body/eval_jaxpr/ppermute | solution.py:40
  64.4 5.0 %collective-permute-start.7 = (f32[1,2]{1,0:T(1,128)S(1)}, f32[1,2]{1,0:T(1,128)S(1)}, u32[]{:S(2)}, u32[]{:S(2)}) collective-permute-start(f32[1,2]{1,0:T(1,128)S(1)} %fusion.115), channel_id=1, source_target_pairs={{0,2},{1,3},{2,0},{3,1},{4,6},{5,7},{6,4},{7,5},{8,10},{9,11},{10,... | collective-permute-start | bytes 32 | tf_op jit(solution)/shard_map/while/body/eval_jaxpr/ppermute | solution.py:40
  66.1 5.3 %collective-permute-start.8 = (f32[1,2]{1,0:T(1,128)S(1)}, f32[1,2]{1,0:T(1,128)S(1)}, u32[]{:S(2)}, u32[]{:S(2)}) collective-permute-start(f32[1,2]{1,0:T(1,128)S(1)} %fusion.115), channel_id=1, source_target_pairs={{0,1},{1,2},{2,3},{3,0},{4,5},{5,6},{6,7},{7,4},{8,9},{9,10},{10,1... | collective-permute-start | bytes 32 | tf_op jit(solution)/shard_map/while/body/eval_jaxpr/ppermute | solution.py:40
  72.3 3.6 %collective-permute-start.10 = (f32[1,2]{1,0:T(1,128)S(1)}, f32[1,2]{1,0:T(1,128)S(1)}, u32[]{:S(2)}, u32[]{:S(2)}) collective-permute-start(f32[1,2]{1,0:T(1,128)S(1)} %bitcast.188), channel_id=1, source_target_pairs={{0,8},{4,12},{8,0},{12,4},{1,9},{5,13},{9,1},{13,5},{2,10},{6,14},... | collective-permute-start | bytes 32 | tf_op jit(solution)/shard_map/while/body/eval_jaxpr/ppermute | solution.py:40
  83.3 5.3 %collective-permute-start = (bf16[2,8,8,512]{3,2,1,0:T(8,128)(2,1)S(1)}, bf16[2,8,8,512]{3,2,1,0:T(8,128)(2,1)S(1)}, u32[]{:S(2)}, u32[]{:S(2)}) collective-permute-start(bf16[2,8,8,512]{3,2,1,0:T(8,128)(2,1)S(1)} %get-tuple-element.253), channel_id=1, source_target_pairs={{0,3},{1,0},{2,1},{3,2},{4,7},{5,4},{6,5},{7,6},{8,11},{9,8},{10,9... | collective-permute-start | bytes 393224 | tf_op jit(solution)/shard_map/while/body/eval_jaxpr/ppermute | solution.py:40
  84.2 12.1 %collective-permute-start.1 = (bf16[2,8,8,512]{3,2,1,0:T(8,128)(2,1)S(1)}, bf16[2,8,8,512]{3,2,1,0:T(8,128)(2,1)S(1)}, u32[]{:S(2)}, u32[]{:S(2)}) collective-permute-start(bf16[2,8,8,512]{3,2,1,0:T(8,128)(2,1)S(1)} %get-tuple-element.254), channel_id=1, source_target_pairs={{0,2},{1,3},{2,0},{3,1},{4,6},{5,7},{6,4},{7,5},{8,10},{9,11},{10,... | collective-permute-start | bytes 393224 | tf_op jit(solution)/shard_map/while/body/eval_jaxpr/ppermute | solution.py:40
  85.0 11.4 %collective-permute-start.2 = (bf16[2,8,8,512]{3,2,1,0:T(8,128)(2,1)S(1)}, bf16[2,8,8,512]{3,2,1,0:T(8,128)(2,1)S(1)}, u32[]{:S(2)}, u32[]{:S(2)}) collective-permute-start(bf16[2,8,8,512]{3,2,1,0:T(8,128)(2,1)S(1)} %get-tuple-element.255), channel_id=1, source_target_pairs={{0,1},{1,2},{2,3},{3,0},{4,5},{5,6},{6,7},{7,4},{8,9},{9,10},{10,1... | collective-permute-start | bytes 393224 | tf_op jit(solution)/shard_map/while/body/eval_jaxpr/ppermute | solution.py:40
  106.1 6.6 %collective-permute-start.3 = (bf16[2,8,8,512]{3,1,2,0:T(8,128)(2,1)S(1)}, bf16[2,8,8,512]{3,1,2,0:T(8,128)(2,1)S(1)}, u32[]{:S(2)}, u32[]{:S(2)}) collective-permute-start(bf16[2,8,8,512]{3,1,2,0:T(8,128)(2,1)S(1)} %bitcast.178), channel_id=1, source_target_pairs={{0,3},{1,0},{2,1},{3,2},{4,7},{5,4},{6,5},{7,6},{8,11},{9,8},{10,9... | collective-permute-start | bytes 393224 | tf_op jit(solution)/shard_map/while/body/eval_jaxpr/ppermute | solution.py:40
  106.1 13.9 %collective-permute-start.4 = (bf16[2,8,8,512]{3,1,2,0:T(8,128)(2,1)S(1)}, bf16[2,8,8,512]{3,1,2,0:T(8,128)(2,1)S(1)}, u32[]{:S(2)}, u32[]{:S(2)}) collective-permute-start(bf16[2,8,8,512]{3,1,2,0:T(8,128)(2,1)S(1)} %bitcast.179), channel_id=1, source_target_pairs={{0,2},{1,3},{2,0},{3,1},{4,6},{5,7},{6,4},{7,5},{8,10},{9,11},{10,... | collective-permute-start | bytes 393224 | tf_op jit(solution)/shard_map/while/body/eval_jaxpr/ppermute | solution.py:40
  107.6 12.4 %collective-permute-start.5 = (bf16[2,8,8,512]{3,1,2,0:T(8,128)(2,1)S(1)}, bf16[2,8,8,512]{3,1,2,0:T(8,128)(2,1)S(1)}, u32[]{:S(2)}, u32[]{:S(2)}) collective-permute-start(bf16[2,8,8,512]{3,1,2,0:T(8,128)(2,1)S(1)} %bitcast.180), channel_id=1, source_target_pairs={{0,1},{1,2},{2,3},{3,0},{4,5},{5,6},{6,7},{7,4},{8,9},{9,10},{10,1... | collective-permute-start | bytes 393224 | tf_op jit(solution)/shard_map/while/body/eval_jaxpr/ppermute | solution.py:40
  127.8 4.8 %collective-permute-start.6 = (f32[1,2]{1,0:T(1,128)S(1)}, f32[1,2]{1,0:T(1,128)S(1)}, u32[]{:S(2)}, u32[]{:S(2)}) collective-permute-start(f32[1,2]{1,0:T(1,128)S(1)} %fusion.115), channel_id=1, source_target_pairs={{0,3},{1,0},{2,1},{3,2},{4,7},{5,4},{6,5},{7,6},{8,11},{9,8},{10,9... | collective-permute-start | bytes 32 | tf_op jit(solution)/shard_map/while/body/eval_jaxpr/ppermute | solution.py:40
  127.8 4.8 %collective-permute-start.7 = (f32[1,2]{1,0:T(1,128)S(1)}, f32[1,2]{1,0:T(1,128)S(1)}, u32[]{:S(2)}, u32[]{:S(2)}) collective-permute-start(f32[1,2]{1,0:T(1,128)S(1)} %fusion.115), channel_id=1, source_target_pairs={{0,2},{1,3},{2,0},{3,1},{4,6},{5,7},{6,4},{7,5},{8,10},{9,11},{10,... | collective-permute-start | bytes 32 | tf_op jit(solution)/shard_map/while/body/eval_jaxpr/ppermute | solution.py:40
  129.3 5.3 %collective-permute-start.8 = (f32[1,2]{1,0:T(1,128)S(1)}, f32[1,2]{1,0:T(1,128)S(1)}, u32[]{:S(2)}, u32[]{:S(2)}) collective-permute-start(f32[1,2]{1,0:T(1,128)S(1)} %fusion.115), channel_id=1, source_target_pairs={{0,1},{1,2},{2,3},{3,0},{4,5},{5,6},{6,7},{7,4},{8,9},{9,10},{10,1... | collective-permute-start | bytes 32 | tf_op jit(solution)/shard_map/while/body/eval_jaxpr/ppermute | solution.py:40
  135.5 3.6 %collective-permute-start.10 = (f32[1,2]{1,0:T(1,128)S(1)}, f32[1,2]{1,0:T(1,128)S(1)}, u32[]{:S(2)}, u32[]{:S(2)}) collective-permute-start(f32[1,2]{1,0:T(1,128)S(1)} %bitcast.188), channel_id=1, source_target_pairs={{0,8},{4,12},{8,0},{12,4},{1,9},{5,13},{9,1},{13,5},{2,10},{6,14},... | collective-permute-start | bytes 32 | tf_op jit(solution)/shard_map/while/body/eval_jaxpr/ppermute | solution.py:40
  146.9 5.3 %collective-permute-start = (bf16[2,8,8,512]{3,2,1,0:T(8,128)(2,1)S(1)}, bf16[2,8,8,512]{3,2,1,0:T(8,128)(2,1)S(1)}, u32[]{:S(2)}, u32[]{:S(2)}) collective-permute-start(bf16[2,8,8,512]{3,2,1,0:T(8,128)(2,1)S(1)} %get-tuple-element.253), channel_id=1, source_target_pairs={{0,3},{1,0},{2,1},{3,2},{4,7},{5,4},{6,5},{7,6},{8,11},{9,8},{10,9... | collective-permute-start | bytes 393224 | tf_op jit(solution)/shard_map/while/body/eval_jaxpr/ppermute | solution.py:40
  147.9 11.8 %collective-permute-start.1 = (bf16[2,8,8,512]{3,2,1,0:T(8,128)(2,1)S(1)}, bf16[2,8,8,512]{3,2,1,0:T(8,128)(2,1)S(1)}, u32[]{:S(2)}, u32[]{:S(2)}) collective-permute-start(bf16[2,8,8,512]{3,2,1,0:T(8,128)(2,1)S(1)} %get-tuple-element.254), channel_id=1, source_target_pairs={{0,2},{1,3},{2,0},{3,1},{4,6},{5,7},{6,4},{7,5},{8,10},{9,11},{10,... | collective-permute-start | bytes 393224 | tf_op jit(solution)/shard_map/while/body/eval_jaxpr/ppermute | solution.py:40
  148.5 11.2 %collective-permute-start.2 = (bf16[2,8,8,512]{3,2,1,0:T(8,128)(2,1)S(1)}, bf16[2,8,8,512]{3,2,1,0:T(8,128)(2,1)S(1)}, u32[]{:S(2)}, u32[]{:S(2)}) collective-permute-start(bf16[2,8,8,512]{3,2,1,0:T(8,128)(2,1)S(1)} %get-tuple-element.255), channel_id=1, source_target_pairs={{0,1},{1,2},{2,3},{3,0},{4,5},{5,6},{6,7},{7,4},{8,9},{9,10},{10,1... | collective-permute-start | bytes 393224 | tf_op jit(solution)/shard_map/while/body/eval_jaxpr/ppermute | solution.py:40
  169.6 6.7 %collective-permute-start.3 = (bf16[2,8,8,512]{3,1,2,0:T(8,128)(2,1)S(1)}, bf16[2,8,8,512]{3,1,2,0:T(8,128)(2,1)S(1)}, u32[]{:S(2)}, u32[]{:S(2)}) collective-permute-start(bf16[2,8,8,512]{3,1,2,0:T(8,128)(2,1)S(1)} %bitcast.178), channel_id=1, source_target_pairs={{0,3},{1,0},{2,1},{3,2},{4,7},{5,4},{6,5},{7,6},{8,11},{9,8},{10,9... | collective-permute-start | bytes 393224 | tf_op jit(solution)/shard_map/while/body/eval_jaxpr/ppermute | solution.py:40
  169.8 13.7 %collective-permute-start.4 = (bf16[2,8,8,512]{3,1,2,0:T(8,128)(2,1)S(1)}, bf16[2,8,8,512]{3,1,2,0:T(8,128)(2,1)S(1)}, u32[]{:S(2)}, u32[]{:S(2)}) collective-permute-start(bf16[2,8,8,512]{3,1,2,0:T(8,128)(2,1)S(1)} %bitcast.179), channel_id=1, source_target_pairs={{0,2},{1,3},{2,0},{3,1},{4,6},{5,7},{6,4},{7,5},{8,10},{9,11},{10,... | collective-permute-start | bytes 393224 | tf_op jit(solution)/shard_map/while/body/eval_jaxpr/ppermute | solution.py:40
  171.0 12.4 %collective-permute-start.5 = (bf16[2,8,8,512]{3,1,2,0:T(8,128)(2,1)S(1)}, bf16[2,8,8,512]{3,1,2,0:T(8,128)(2,1)S(1)}, u32[]{:S(2)}, u32[]{:S(2)}) collective-permute-start(bf16[2,8,8,512]{3,1,2,0:T(8,128)(2,1)S(1)} %bitcast.180), channel_id=1, source_target_pairs={{0,1},{1,2},{2,3},{3,0},{4,5},{5,6},{6,7},{7,4},{8,9},{9,10},{10,1... | collective-permute-start | bytes 393224 | tf_op jit(solution)/shard_map/while/body/eval_jaxpr/ppermute | solution.py:40
  191.3 4.9 %collective-permute-start.6 = (f32[1,2]{1,0:T(1,128)S(1)}, f32[1,2]{1,0:T(1,128)S(1)}, u32[]{:S(2)}, u32[]{:S(2)}) collective-permute-start(f32[1,2]{1,0:T(1,128)S(1)} %fusion.115), channel_id=1, source_target_pairs={{0,3},{1,0},{2,1},{3,2},{4,7},{5,4},{6,5},{7,6},{8,11},{9,8},{10,9... | collective-permute-start | bytes 32 | tf_op jit(solution)/shard_map/while/body/eval_jaxpr/ppermute | solution.py:40
  191.3 4.9 %collective-permute-start.7 = (f32[1,2]{1,0:T(1,128)S(1)}, f32[1,2]{1,0:T(1,128)S(1)}, u32[]{:S(2)}, u32[]{:S(2)}) collective-permute-start(f32[1,2]{1,0:T(1,128)S(1)} %fusion.115), channel_id=1, source_target_pairs={{0,2},{1,3},{2,0},{3,1},{4,6},{5,7},{6,4},{7,5},{8,10},{9,11},{10,... | collective-permute-start | bytes 32 | tf_op jit(solution)/shard_map/while/body/eval_jaxpr/ppermute | solution.py:40
  192.9 5.3 %collective-permute-start.8 = (f32[1,2]{1,0:T(1,128)S(1)}, f32[1,2]{1,0:T(1,128)S(1)}, u32[]{:S(2)}, u32[]{:S(2)}) collective-permute-start(f32[1,2]{1,0:T(1,128)S(1)} %fusion.115), channel_id=1, source_target_pairs={{0,1},{1,2},{2,3},{3,0},{4,5},{5,6},{6,7},{7,4},{8,9},{9,10},{10,1... | collective-permute-start | bytes 32 | tf_op jit(solution)/shard_map/while/body/eval_jaxpr/ppermute | solution.py:40
  210.3 5.2 %collective-permute-start = (bf16[2,8,8,512]{3,2,1,0:T(8,128)(2,1)S(1)}, bf16[2,8,8,512]{3,2,1,0:T(8,128)(2,1)S(1)}, u32[]{:S(2)}, u32[]{:S(2)}) collective-permute-start(bf16[2,8,8,512]{3,2,1,0:T(8,128)(2,1)S(1)} %get-tuple-element.253), channel_id=1, source_target_pairs={{0,3},{1,0},{2,1},{3,2},{4,7},{5,4},{6,5},{7,6},{8,11},{9,8},{10,9... | collective-permute-start | bytes 393224 | tf_op jit(solution)/shard_map/while/body/eval_jaxpr/ppermute | solution.py:40
  211.1 12.1 %collective-permute-start.1 = (bf16[2,8,8,512]{3,2,1,0:T(8,128)(2,1)S(1)}, bf16[2,8,8,512]{3,2,1,0:T(8,128)(2,1)S(1)}, u32[]{:S(2)}, u32[]{:S(2)}) collective-permute-start(bf16[2,8,8,512]{3,2,1,0:T(8,128)(2,1)S(1)} %get-tuple-element.254), channel_id=1, source_target_pairs={{0,2},{1,3},{2,0},{3,1},{4,6},{5,7},{6,4},{7,5},{8,10},{9,11},{10,... | collective-permute-start | bytes 393224 | tf_op jit(solution)/shard_map/while/body/eval_jaxpr/ppermute | solution.py:40
  211.9 11.3 %collective-permute-start.2 = (bf16[2,8,8,512]{3,2,1,0:T(8,128)(2,1)S(1)}, bf16[2,8,8,512]{3,2,1,0:T(8,128)(2,1)S(1)}, u32[]{:S(2)}, u32[]{:S(2)}) collective-permute-start(bf16[2,8,8,512]{3,2,1,0:T(8,128)(2,1)S(1)} %get-tuple-element.255), channel_id=1, source_target_pairs={{0,1},{1,2},{2,3},{3,0},{4,5},{5,6},{6,7},{7,4},{8,9},{9,10},{10,1... | collective-permute-start | bytes 393224 | tf_op jit(solution)/shard_map/while/body/eval_jaxpr/ppermute | solution.py:40
  232.9 6.6 %collective-permute-start.3 = (bf16[2,8,8,512]{3,1,2,0:T(8,128)(2,1)S(1)}, bf16[2,8,8,512]{3,1,2,0:T(8,128)(2,1)S(1)}, u32[]{:S(2)}, u32[]{:S(2)}) collective-permute-start(bf16[2,8,8,512]{3,1,2,0:T(8,128)(2,1)S(1)} %bitcast.178), channel_id=1, source_target_pairs={{0,3},{1,0},{2,1},{3,2},{4,7},{5,4},{6,5},{7,6},{8,11},{9,8},{10,9... | collective-permute-start | bytes 393224 | tf_op jit(solution)/shard_map/while/body/eval_jaxpr/ppermute | solution.py:40
  232.9 13.9 %collective-permute-start.4 = (bf16[2,8,8,512]{3,1,2,0:T(8,128)(2,1)S(1)}, bf16[2,8,8,512]{3,1,2,0:T(8,128)(2,1)S(1)}, u32[]{:S(2)}, u32[]{:S(2)}) collective-permute-start(bf16[2,8,8,512]{3,1,2,0:T(8,128)(2,1)S(1)} %bitcast.179), channel_id=1, source_target_pairs={{0,2},{1,3},{2,0},{3,1},{4,6},{5,7},{6,4},{7,5},{8,10},{9,11},{10,... | collective-permute-start | bytes 393224 | tf_op jit(solution)/shard_map/while/body/eval_jaxpr/ppermute | solution.py:40
  234.4 12.4 %collective-permute-start.5 = (bf16[2,8,8,512]{3,1,2,0:T(8,128)(2,1)S(1)}, bf16[2,8,8,512]{3,1,2,0:T(8,128)(2,1)S(1)}, u32[]{:S(2)}, u32[]{:S(2)}) collective-permute-start(bf16[2,8,8,512]{3,1,2,0:T(8,128)(2,1)S(1)} %bitcast.180), channel_id=1, source_target_pairs={{0,1},{1,2},{2,3},{3,0},{4,5},{5,6},{6,7},{7,4},{8,9},{9,10},{10,1... | collective-permute-start | bytes 393224 | tf_op jit(solution)/shard_map/while/body/eval_jaxpr/ppermute | solution.py:40
  254.7 4.8 %collective-permute-start.6 = (f32[1,2]{1,0:T(1,128)S(1)}, f32[1,2]{1,0:T(1,128)S(1)}, u32[]{:S(2)}, u32[]{:S(2)}) collective-permute-start(f32[1,2]{1,0:T(1,128)S(1)} %fusion.115), channel_id=1, source_target_pairs={{0,3},{1,0},{2,1},{3,2},{4,7},{5,4},{6,5},{7,6},{8,11},{9,8},{10,9... | collective-permute-start | bytes 32 | tf_op jit(solution)/shard_map/while/body/eval_jaxpr/ppermute | solution.py:40
  254.7 4.8 %collective-permute-start.7 = (f32[1,2]{1,0:T(1,128)S(1)}, f32[1,2]{1,0:T(1,128)S(1)}, u32[]{:S(2)}, u32[]{:S(2)}) collective-permute-start(f32[1,2]{1,0:T(1,128)S(1)} %fusion.115), channel_id=1, source_target_pairs={{0,2},{1,3},{2,0},{3,1},{4,6},{5,7},{6,4},{7,5},{8,10},{9,11},{10,... | collective-permute-start | bytes 32 | tf_op jit(solution)/shard_map/while/body/eval_jaxpr/ppermute | solution.py:40
  256.2 5.3 %collective-permute-start.8 = (f32[1,2]{1,0:T(1,128)S(1)}, f32[1,2]{1,0:T(1,128)S(1)}, u32[]{:S(2)}, u32[]{:S(2)}) collective-permute-start(f32[1,2]{1,0:T(1,128)S(1)} %fusion.115), channel_id=1, source_target_pairs={{0,1},{1,2},{2,3},{3,0},{4,5},{5,6},{6,7},{7,4},{8,9},{9,10},{10,1... | collective-permute-start | bytes 32 | tf_op jit(solution)/shard_map/while/body/eval_jaxpr/ppermute | solution.py:40
  262.4 3.6 %collective-permute-start.10 = (f32[1,2]{1,0:T(1,128)S(1)}, f32[1,2]{1,0:T(1,128)S(1)}, u32[]{:S(2)}, u32[]{:S(2)}) collective-permute-start(f32[1,2]{1,0:T(1,128)S(1)} %bitcast.188), channel_id=1, source_target_pairs={{0,8},{4,12},{8,0},{12,4},{1,9},{5,13},{9,1},{13,5},{2,10},{6,14},... | collective-permute-start | bytes 32 | tf_op jit(solution)/shard_map/while/body/eval_jaxpr/ppermute | solution.py:40
  273.7 5.3 %collective-permute-start = (bf16[2,8,8,512]{3,2,1,0:T(8,128)(2,1)S(1)}, bf16[2,8,8,512]{3,2,1,0:T(8,128)(2,1)S(1)}, u32[]{:S(2)}, u32[]{:S(2)}) collective-permute-start(bf16[2,8,8,512]{3,2,1,0:T(8,128)(2,1)S(1)} %get-tuple-element.253), channel_id=1, source_target_pairs={{0,3},{1,0},{2,1},{3,2},{4,7},{5,4},{6,5},{7,6},{8,11},{9,8},{10,9... | collective-permute-start | bytes 393224 | tf_op jit(solution)/shard_map/while/body/eval_jaxpr/ppermute | solution.py:40
  274.7 11.9 %collective-permute-start.1 = (bf16[2,8,8,512]{3,2,1,0:T(8,128)(2,1)S(1)}, bf16[2,8,8,512]{3,2,1,0:T(8,128)(2,1)S(1)}, u32[]{:S(2)}, u32[]{:S(2)}) collective-permute-start(bf16[2,8,8,512]{3,2,1,0:T(8,128)(2,1)S(1)} %get-tuple-element.254), channel_id=1, source_target_pairs={{0,2},{1,3},{2,0},{3,1},{4,6},{5,7},{6,4},{7,5},{8,10},{9,11},{10,... | collective-permute-start | bytes 393224 | tf_op jit(solution)/shard_map/while/body/eval_jaxpr/ppermute | solution.py:40
  275.4 11.2 %collective-permute-start.2 = (bf16[2,8,8,512]{3,2,1,0:T(8,128)(2,1)S(1)}, bf16[2,8,8,512]{3,2,1,0:T(8,128)(2,1)S(1)}, u32[]{:S(2)}, u32[]{:S(2)}) collective-permute-start(bf16[2,8,8,512]{3,2,1,0:T(8,128)(2,1)S(1)} %get-tuple-element.255), channel_id=1, source_target_pairs={{0,1},{1,2},{2,3},{3,0},{4,5},{5,6},{6,7},{7,4},{8,9},{9,10},{10,1... | collective-permute-start | bytes 393224 | tf_op jit(solution)/shard_map/while/body/eval_jaxpr/ppermute | solution.py:40
  296.5 6.7 %collective-permute-start.3 = (bf16[2,8,8,512]{3,1,2,0:T(8,128)(2,1)S(1)}, bf16[2,8,8,512]{3,1,2,0:T(8,128)(2,1)S(1)}, u32[]{:S(2)}, u32[]{:S(2)}) collective-permute-start(bf16[2,8,8,512]{3,1,2,0:T(8,128)(2,1)S(1)} %bitcast.178), channel_id=1, source_target_pairs={{0,3},{1,0},{2,1},{3,2},{4,7},{5,4},{6,5},{7,6},{8,11},{9,8},{10,9... | collective-permute-start | bytes 393224 | tf_op jit(solution)/shard_map/while/body/eval_jaxpr/ppermute | solution.py:40
  296.5 13.8 %collective-permute-start.4 = (bf16[2,8,8,512]{3,1,2,0:T(8,128)(2,1)S(1)}, bf16[2,8,8,512]{3,1,2,0:T(8,128)(2,1)S(1)}, u32[]{:S(2)}, u32[]{:S(2)}) collective-permute-start(bf16[2,8,8,512]{3,1,2,0:T(8,128)(2,1)S(1)} %bitcast.179), channel_id=1, source_target_pairs={{0,2},{1,3},{2,0},{3,1},{4,6},{5,7},{6,4},{7,5},{8,10},{9,11},{10,... | collective-permute-start | bytes 393224 | tf_op jit(solution)/shard_map/while/body/eval_jaxpr/ppermute | solution.py:40
  297.9 12.4 %collective-permute-start.5 = (bf16[2,8,8,512]{3,1,2,0:T(8,128)(2,1)S(1)}, bf16[2,8,8,512]{3,1,2,0:T(8,128)(2,1)S(1)}, u32[]{:S(2)}, u32[]{:S(2)}) collective-permute-start(bf16[2,8,8,512]{3,1,2,0:T(8,128)(2,1)S(1)} %bitcast.180), channel_id=1, source_target_pairs={{0,1},{1,2},{2,3},{3,0},{4,5},{5,6},{6,7},{7,4},{8,9},{9,10},{10,1... | collective-permute-start | bytes 393224 | tf_op jit(solution)/shard_map/while/body/eval_jaxpr/ppermute | solution.py:40
  318.1 4.9 %collective-permute-start.6 = (f32[1,2]{1,0:T(1,128)S(1)}, f32[1,2]{1,0:T(1,128)S(1)}, u32[]{:S(2)}, u32[]{:S(2)}) collective-permute-start(f32[1,2]{1,0:T(1,128)S(1)} %fusion.115), channel_id=1, source_target_pairs={{0,3},{1,0},{2,1},{3,2},{4,7},{5,4},{6,5},{7,6},{8,11},{9,8},{10,9... | collective-permute-start | bytes 32 | tf_op jit(solution)/shard_map/while/body/eval_jaxpr/ppermute | solution.py:40
  318.1 4.9 %collective-permute-start.7 = (f32[1,2]{1,0:T(1,128)S(1)}, f32[1,2]{1,0:T(1,128)S(1)}, u32[]{:S(2)}, u32[]{:S(2)}) collective-permute-start(f32[1,2]{1,0:T(1,128)S(1)} %fusion.115), channel_id=1, source_target_pairs={{0,2},{1,3},{2,0},{3,1},{4,6},{5,7},{6,4},{7,5},{8,10},{9,11},{10,... | collective-permute-start | bytes 32 | tf_op jit(solution)/shard_map/while/body/eval_jaxpr/ppermute | solution.py:40
  319.7 5.3 %collective-permute-start.8 = (f32[1,2]{1,0:T(1,128)S(1)}, f32[1,2]{1,0:T(1,128)S(1)}, u32[]{:S(2)}, u32[]{:S(2)}) collective-permute-start(f32[1,2]{1,0:T(1,128)S(1)} %fusion.115), channel_id=1, source_target_pairs={{0,1},{1,2},{2,3},{3,0},{4,5},{5,6},{6,7},{7,4},{8,9},{9,10},{10,1... | collective-permute-start | bytes 32 | tf_op jit(solution)/shard_map/while/body/eval_jaxpr/ppermute | solution.py:40
  (26 other events, 89.4 us)

commit v6 on v5

--- a/solution.py
+++ b/solution.py
@@ -3,6 +3,8 @@
 import jax
 import jax.numpy as jnp
 from jax import lax
+from jax.experimental import pallas as pl
+from jax.experimental.pallas import tpu as pltpu
 from jax.sharding import PartitionSpec as P
 
 SBLK = 128
@@ -60,6 +62,65 @@
     return ordered.reshape(block.shape[:dim] + (size * block.shape[dim],) + block.shape[dim + 1 :])
 
 
+def adjoint_kernel(res_ref, op_ref, out_ref):
+    rows = out_ref.shape[2]
+    res = res_ref[0]
+    by_real = jnp.dot(res, op_ref[0, 0], preferred_element_type=jnp.float32)
+    by_imag = jnp.dot(res, op_ref[1, 0], preferred_element_type=jnp.float32)
+    out_ref[0, 0] = (by_real[:rows] + by_imag[rows:]).astype(out_ref.dtype)
+    out_ref[1, 0] = (by_real[rows:] - by_imag[:rows]).astype(out_ref.dtype)
+
+
+def adjoint(stacked, operator):
+    _, freq, receivers, sources = operator.shape
+    rows = stacked.shape[1] // 2
+    return pl.pallas_call(
+        adjoint_kernel,
+        grid=(freq,),
+        in_specs=[
+            pl.BlockSpec((1, 2 * rows, receivers), lambda f: (f, 0, 0)),
+            pl.BlockSpec((2, 1, receivers, sources), lambda f: (0, f, 0, 0)),
+        ],
+        out_specs=pl.BlockSpec((2, 1, rows, sources), lambda f: (0, f, 0, 0)),
+        out_shape=jax.ShapeDtypeStruct((2, freq, rows, sources), jnp.float32),
+        cost_estimate=pl.CostEstimate(
+            flops=8 * freq * rows * receivers * sources,
+            transcendentals=0,
+            bytes_accessed=operator.size * 2 + 2 * freq * rows * sources * 4,
+        ),
+    )(stacked, operator)
+
+
+def forward_kernel(dir_ref, op_ref, out_ref):
+    rows = out_ref.shape[2]
+    direction = dir_ref[0]
+    contract = (((1,), (1,)), ((), ()))
+    by_real = lax.dot_general(direction, op_ref[0, 0], contract, preferred_element_type=jnp.float32)
+    by_imag = lax.dot_general(direction, op_ref[1, 0], contract, preferred_element_type=jnp.float32)
+    out_ref[0, 0] = by_real[:rows] - by_imag[rows:]
+    out_ref[1, 0] = by_imag[:rows] + by_real[rows:]
+
+
+def forward(stacked, operator):
+    _, freq, receivers, sources = operator.shape
+    rows = stacked.shape[1] // 2
+    return pl.pallas_call(
+        forward_kernel,
+        grid=(freq,),
+        in_specs=[
+            pl.BlockSpec((1, 2 * rows, sources), lambda f: (f, 0, 0)),
+            pl.BlockSpec((2, 1, receivers, sources), lambda f: (0, f, 0, 0)),
+        ],
+        out_specs=pl.BlockSpec((2, 1, rows, receivers), lambda f: (0, f, 0, 0)),
+        out_shape=jax.ShapeDtypeStruct((2, freq, rows, receivers), jnp.float32),
+        cost_estimate=pl.CostEstimate(
+            flops=8 * freq * rows * receivers * sources,
+            transcendentals=0,
+            bytes_accessed=operator.size * 2 + stacked.size * 2,
+        ),
+    )(stacked, operator)
+
+
 def on_device(operator, recorded, win_start, win_end):
     freq_local = operator.shape[1]
     sources = operator.shape[3]
@@ -67,8 +128,6 @@
     src_local = sources // lax.axis_size("recv")
     total_freq = freq_local * lax.axis_size("freq")
     columns = right_sides * src_local
-    real_operator = operator[0]
-    imag_operator = operator[1]
 
     cos_part, sin_part = dft_rows(jnp.arange(total_freq, dtype=jnp.int32), total_freq)
     to_time = jnp.block([[cos_part.T, -sin_part.T], [sin_part.T, cos_part.T]])
@@ -84,16 +143,8 @@
         reflect, residual = state
         rounded_residual = residual.astype(jnp.bfloat16)
         stacked_residual = jnp.concatenate([rounded_residual[0], rounded_residual[1]], axis=1)
-        with_real = jnp.einsum(
-            "fbr,frs->fbs", stacked_residual, real_operator, preferred_element_type=jnp.float32
-        )
-        with_imag = jnp.einsum(
-            "fbr,frs->fbs", stacked_residual, imag_operator, preferred_element_type=jnp.float32
-        )
-        partial_real = with_real[:, :right_sides] + with_imag[:, right_sides:]
-        partial_imag = with_real[:, right_sides:] - with_imag[:, :right_sides]
         gradient = sum_scatter(
-            jnp.stack([partial_real, partial_imag]).astype(jnp.bfloat16), "recv", 3
+            adjoint(stacked_residual, operator).astype(jnp.bfloat16), "recv", 3
         )
         flattened = gradient.astype(jnp.bfloat16).reshape(2, freq_local, columns)
         segment = lax.all_gather(flattened, "freq", axis=1, tiled=True).astype(jnp.float32)
@@ -103,15 +154,7 @@
         rounded_direction = direction.astype(jnp.bfloat16)
         add_segment = gather_blocks(rounded_direction, "recv", 3)
         stacked_direction = jnp.concatenate([add_segment[0], add_segment[1]], axis=1)
-        by_real = jnp.einsum(
-            "fbs,frs->fbr", stacked_direction, real_operator, preferred_element_type=jnp.float32
-        )
-        by_imag = jnp.einsum(
-            "fbs,frs->fbr", stacked_direction, imag_operator, preferred_element_type=jnp.float32
-        )
-        image_real = by_real[:, :right_sides] - by_imag[:, right_sides:]
-        image_imag = by_imag[:, :right_sides] + by_real[:, right_sides:]
-        image = jnp.stack([image_real, image_imag])
+        image = forward(stacked_direction, operator)
         sums = jnp.stack([jnp.sum(direction * direction), jnp.sum(image * image)])
         sums = jnp.sum(gather_blocks(sums[None], "recv", 0), axis=0)
         direction_power, image_energy = jnp.sum(gather_blocks(sums[None], "freq", 0), axis=0)

time: 334 us -> 381 us (1.14)
  Pallas kernels: 0 us -> 78.3 us
  matrix products: 57.3 us -> 9.43 us
  other arithmetic: 24.8 us -> 44.2 us
  local copies, waits for them, and re-layouts: 23 us -> 17.3 us
    pallas_call x0 -> x10, Pallas kernels: none -> 78.3 us  [the longest x5 40.1 us: forward(): pl.pallas_call(forward_kernel, grid=(freq,), in_specs=[pl.BlockSpec((1, 2...]
    dot_general x20 -> x0, matrix products: 42 us -> none  [the longest x5 17.8 us: step(): jnp.einsum('fbs,frs->fbr', stacked_direction, imag_operator, preferred_el...]
    concatenate x0 -> x10, other arithmetic: none -> 7.23 us  [the longest x5 4.12 us: step(): jnp.concatenate([add_segment[0], add_segment[1]], axis=1)]
    convert_element_type x0 -> x5, other arithmetic: none -> 6.42 us  [step(): adjoint(stacked_residual, operator).astype(jnp.bfloat16)]
    squeeze x1 -> x5, local copies, waits for them, and re-layouts: 6.08 us -> 0.17 us  [sum_scatter(): lax.dynamic_index_in_dim(blocks, (me + distance) % size, axis=dim, keepdi...]
    dot_general x10, matrix products: 15.2 us -> 9.43 us  [high_dot(): return jnp.dot(left, right, precision=lax.Precision.HIGHEST)]
    sub x5, other arithmetic: 0.08 us -> 4.28 us  [step(): return (reflect + step_length * direction, residual - step_length * image)]
    reduce_sum x5, other arithmetic: 3.33 us -> 7.27 us  [step(): sums = jnp.stack([jnp.sum(direction * direction), jnp.sum(image * image)])]
where the time goes in v6:
time: 381 us; the launch traced here: 378 us
  waiting for transfers between devices  129 us (34%)
  Pallas kernels  78.3 us (21%)
  starting transfers between devices  57.7 us (15%)
  other arithmetic  44.2 us (12%)
  blocking collectives  33.5 us (9%)
  local copies, waits for them, and re-layouts  17.3 us (5%)
  matrix products  9.43 us (2%)
  loops' own time  7.58 us (2%)
    ppermute x60, waiting for transfers between devices, shifted(): lax.ppermute(value, axis, [(i, (i + distance) % size) for i in range(size)])  129 us
    ppermute x60, starting transfers between devices, shifted(): lax.ppermute(value, axis, [(i, (i + distance) % size) for i in range(size)])  57.7 us
    pallas_call x5, Pallas kernels, forward(): pl.pallas_call(forward_kernel, grid=(freq,), in_specs=[pl.BlockSpec((1, 2...  40.1 us
    pallas_call x5, Pallas kernels, adjoint(): pl.pallas_call(adjoint_kernel, grid=(freq,), in_specs=[pl.BlockSpec((1, 2...  38.3 us
    all_gather x5, blocking collectives, step(): lax.all_gather(flattened, 'freq', axis=1, tiled=True).astype(jnp.float32)  33.5 us
    gather x25, local copies, waits for them, and re-layouts, gather_blocks(): ordered = jnp.take(slots, order, axis=dim)  9.43 us
    dot_general x10, matrix products, high_dot(): return jnp.dot(left, right, precision=lax.Precision.HIGHEST)  9.43 us
  transfers between devices with their start and end apart: 60, of which 36 were waited for; matrix products, arithmetic and copies ran while one was open for 2% of the time, Pallas kernels for 0%

profile of v6, /device:TPU:0, one launch (start us, length us, event | category | flops | bytes accessed | tf_op | source)
XLA Modules:
  0.0 378.0 jit_solution(6024420594261782765)
XLA Ops:
  5.5 371.6 %while.15 = (s32[]{:T(128)}, f32[2,8,8,512]{3,1,2,0:T(8,128)S(1)}, f32[2,8,8,128]{3,2,1,0:T(8,128)S(1)}, bf16[2,8,128,2048]{3,2,1,0:T(8,128)(2,1)}, f32[64,64]{1...) while((s32[]{:T(128)}, f32[2,8,8,512]{3,1,2,0:T(8,128)S(1)}, ...), condition=%wide.region_7.9_spmd.clone, body=%wide.region_2.8_spmd.clone.sunk | while | flops 523783552 | bytes 38144084 | solution.py:165
  6.2 7.7 %eval_jaxpr.8 = f32[2,8,8,2048]{3,2,1,0:T(8,128)} custom-call(bf16[8,16,128]{2,1,0:T(8,128)(2,1)} %pad_maximum_fusion.11.res_ref, bf16[2,8,128,2048]{3,2,1,0:T(8,128)(2,1)} %get-tuple-element.264.op_ref), custom_call_target="tpu_custom_call" | custom-call | flops 134217728 | bytes 9437184 | tf_op jit(solution)/shard_map/while/body/eval_jaxpr/pallas_call | solution.py:77
  15.2 5.1 %collective-permute-start = (bf16[2,8,8,512]{3,2,1,0:T(8,128)(2,1)S(1)}, bf16[2,8,8,512]{3,2,1,0:T(8,128)(2,1)S(1)}, u32[]{:S(2)}, u32[]{:S(2)}) collective-permute-start(bf16[2,8,8,512]{3,2,1,0:T(8,128)(2,1)S(1)} %get-tuple-element.219), channel_id=1, source_target_pairs={{0,3},{1,0},{2,1},{3,2},{4,7},{5,4},{6,5},{7,6},{8,11},{9,8},{10,9... | collective-permute-start | bytes 393224 | tf_op jit(solution)/shard_map/while/body/eval_jaxpr/ppermute | solution.py:42
  21.4 2.8 collective-permute-done
  24.2 7.3 %collective-permute-done.1 = bf16[2,8,8,512]{3,2,1,0:T(8,128)(2,1)S(1)} collective-permute-done((bf16[2,8,8,512]{3,2,1,0:T(8,128)(2,1)S(1)}, bf16[2,8,8,512]{3,2,1,0:T(8,128)(2,1)S(1)}, u32[]{:S(2)}, u32[]{:S(2)}) %collective-permute-start.1) | collective-permute-done | bytes 131104 | tf_op jit(solution)/shard_map/while/body/eval_jaxpr/ppermute | solution.py:42
  31.7 7.2 %all_gather.8 = bf16[2,32,4096]{2,1,0:T(8,128)(2,1)S(1)} all-gather(bf16[2,8,4096]{2,1,0:T(8,128)(2,1)S(1)} %reshape.236), channel_id=1, replica_groups=mesh['groups'=2,'freq'=4,'recv'=4] {'freq'}, dimensions={1}, use_global_device_ids=true | all-gather | bytes 655360 | tf_op jit(solution)/shard_map/while/body/eval_jaxpr/all_gather | solution.py:150
  46.6 9.3 %collective-permute-done.4 = bf16[2,8,8,512]{3,2,1,0:T(8,128)(2,1)S(1)} collective-permute-done((bf16[2,8,8,512]{3,2,1,0:T(8,128)(2,1)S(1)}, bf16[2,8,8,512]{3,2,1,0:T(8,128)(2,1)S(1)}, u32[]{:S(2)}, u32[]{:S(2)}) %collective-permute-start.4) | collective-permute-done | bytes 131104 | tf_op jit(solution)/shard_map/while/body/eval_jaxpr/ppermute | solution.py:42
  57.6 8.0 %eval_jaxpr.9 = f32[2,8,8,128]{3,2,1,0:T(8,128)} custom-call(bf16[8,16,2048]{2,1,0:T(8,128)(2,1)} %pad_maximum_fusion.13.dir_ref, bf16[2,8,128,2048]{3,2,1,0:T(8,128)(2,1)} %get-tuple-element.264.op_ref), custom_call_target="tpu_custom_call" | custom-call | flops 134217728 | bytes 8912896 | tf_op jit(solution)/shard_map/while/body/eval_jaxpr/pallas_call | solution.py:107
  73.4 2.1 collective-permute-done.8
  77.6 2.3 collective-permute-done.10
  84.5 7.7 %eval_jaxpr.8 = f32[2,8,8,2048]{3,2,1,0:T(8,128)} custom-call(bf16[8,16,128]{2,1,0:T(8,128)(2,1)} %pad_maximum_fusion.11.res_ref, bf16[2,8,128,2048]{3,2,1,0:T(8,128)(2,1)} %get-tuple-element.264.op_ref), custom_call_target="tpu_custom_call" | custom-call | flops 134217728 | bytes 9437184 | tf_op jit(solution)/shard_map/while/body/eval_jaxpr/pallas_call | solution.py:77
  95.7 3.1 collective-permute-done
  98.8 7.7 %collective-permute-done.1 = bf16[2,8,8,512]{3,2,1,0:T(8,128)(2,1)S(1)} collective-permute-done((bf16[2,8,8,512]{3,2,1,0:T(8,128)(2,1)S(1)}, bf16[2,8,8,512]{3,2,1,0:T(8,128)(2,1)S(1)}, u32[]{:S(2)}, u32[]{:S(2)}) %collective-permute-start.1) | collective-permute-done | bytes 131104 | tf_op jit(solution)/shard_map/while/body/eval_jaxpr/ppermute | solution.py:42
  106.7 6.5 %all_gather.8 = bf16[2,32,4096]{2,1,0:T(8,128)(2,1)S(1)} all-gather(bf16[2,8,4096]{2,1,0:T(8,128)(2,1)S(1)} %reshape.236), channel_id=1, replica_groups=mesh['groups'=2,'freq'=4,'recv'=4] {'freq'}, dimensions={1}, use_global_device_ids=true | all-gather | bytes 655360 | tf_op jit(solution)/shard_map/while/body/eval_jaxpr/all_gather | solution.py:150
  118.9 2.9 collective-permute-done.3
  121.8 7.4 %collective-permute-done.4 = bf16[2,8,8,512]{3,2,1,0:T(8,128)(2,1)S(1)} collective-permute-done((bf16[2,8,8,512]{3,2,1,0:T(8,128)(2,1)S(1)}, bf16[2,8,8,512]{3,2,1,0:T(8,128)(2,1)S(1)}, u32[]{:S(2)}, u32[]{:S(2)}) %collective-permute-start.4) | collective-permute-done | bytes 131104 | tf_op jit(solution)/shard_map/while/body/eval_jaxpr/ppermute | solution.py:42
  130.9 8.0 %eval_jaxpr.9 = f32[2,8,8,128]{3,2,1,0:T(8,128)} custom-call(bf16[8,16,2048]{2,1,0:T(8,128)(2,1)} %pad_maximum_fusion.13.dir_ref, bf16[2,8,128,2048]{3,2,1,0:T(8,128)(2,1)} %get-tuple-element.264.op_ref), custom_call_target="tpu_custom_call" | custom-call | flops 134217728 | bytes 8912896 | tf_op jit(solution)/shard_map/while/body/eval_jaxpr/pallas_call | solution.py:107
  146.4 2.1 collective-permute-done.8
  150.7 2.2 collective-permute-done.10
  157.9 7.7 %eval_jaxpr.8 = f32[2,8,8,2048]{3,2,1,0:T(8,128)} custom-call(bf16[8,16,128]{2,1,0:T(8,128)(2,1)} %pad_maximum_fusion.11.res_ref, bf16[2,8,128,2048]{3,2,1,0:T(8,128)(2,1)} %get-tuple-element.264.op_ref), custom_call_target="tpu_custom_call" | custom-call | flops 134217728 | bytes 9437184 | tf_op jit(solution)/shard_map/while/body/eval_jaxpr/pallas_call | solution.py:77
  169.1 3.1 collective-permute-done
  172.2 7.6 %collective-permute-done.1 = bf16[2,8,8,512]{3,2,1,0:T(8,128)(2,1)S(1)} collective-permute-done((bf16[2,8,8,512]{3,2,1,0:T(8,128)(2,1)S(1)}, bf16[2,8,8,512]{3,2,1,0:T(8,128)(2,1)S(1)}, u32[]{:S(2)}, u32[]{:S(2)}) %collective-permute-start.1) | collective-permute-done | bytes 131104 | tf_op jit(solution)/shard_map/while/body/eval_jaxpr/ppermute | solution.py:42
  180.0 6.6 %all_gather.8 = bf16[2,32,4096]{2,1,0:T(8,128)(2,1)S(1)} all-gather(bf16[2,8,4096]{2,1,0:T(8,128)(2,1)S(1)} %reshape.236), channel_id=1, replica_groups=mesh['groups'=2,'freq'=4,'recv'=4] {'freq'}, dimensions={1}, use_global_device_ids=true | all-gather | bytes 655360 | tf_op jit(solution)/shard_map/while/body/eval_jaxpr/all_gather | solution.py:150
  192.2 3.1 collective-permute-done.3
  195.3 7.2 %collective-permute-done.4 = bf16[2,8,8,512]{3,2,1,0:T(8,128)(2,1)S(1)} collective-permute-done((bf16[2,8,8,512]{3,2,1,0:T(8,128)(2,1)S(1)}, bf16[2,8,8,512]{3,2,1,0:T(8,128)(2,1)S(1)}, u32[]{:S(2)}, u32[]{:S(2)}) %collective-permute-start.4) | collective-permute-done | bytes 131104 | tf_op jit(solution)/shard_map/while/body/eval_jaxpr/ppermute | solution.py:42
  204.2 8.0 %eval_jaxpr.9 = f32[2,8,8,128]{3,2,1,0:T(8,128)} custom-call(bf16[8,16,2048]{2,1,0:T(8,128)(2,1)} %pad_maximum_fusion.13.dir_ref, bf16[2,8,128,2048]{3,2,1,0:T(8,128)(2,1)} %get-tuple-element.264.op_ref), custom_call_target="tpu_custom_call" | custom-call | flops 134217728 | bytes 8912896 | tf_op jit(solution)/shard_map/while/body/eval_jaxpr/pallas_call | solution.py:107
  216.5 2.0 collective-permute-start.8
  219.8 2.1 collective-permute-done.8
  224.0 2.3 collective-permute-done.10
  231.2 7.7 %eval_jaxpr.8 = f32[2,8,8,2048]{3,2,1,0:T(8,128)} custom-call(bf16[8,16,128]{2,1,0:T(8,128)(2,1)} %pad_maximum_fusion.11.res_ref, bf16[2,8,128,2048]{3,2,1,0:T(8,128)(2,1)} %get-tuple-element.264.op_ref), custom_call_target="tpu_custom_call" | custom-call | flops 134217728 | bytes 9437184 | tf_op jit(solution)/shard_map/while/body/eval_jaxpr/pallas_call | solution.py:77
  242.4 3.1 collective-permute-done
  245.5 7.7 %collective-permute-done.1 = bf16[2,8,8,512]{3,2,1,0:T(8,128)(2,1)S(1)} collective-permute-done((bf16[2,8,8,512]{3,2,1,0:T(8,128)(2,1)S(1)}, bf16[2,8,8,512]{3,2,1,0:T(8,128)(2,1)S(1)}, u32[]{:S(2)}, u32[]{:S(2)}) %collective-permute-start.1) | collective-permute-done | bytes 131104 | tf_op jit(solution)/shard_map/while/body/eval_jaxpr/ppermute | solution.py:42
  253.3 6.5 %all_gather.8 = bf16[2,32,4096]{2,1,0:T(8,128)(2,1)S(1)} all-gather(bf16[2,8,4096]{2,1,0:T(8,128)(2,1)S(1)} %reshape.236), channel_id=1, replica_groups=mesh['groups'=2,'freq'=4,'recv'=4] {'freq'}, dimensions={1}, use_global_device_ids=true | all-gather | bytes 655360 | tf_op jit(solution)/shard_map/while/body/eval_jaxpr/all_gather | solution.py:150
  265.4 3.0 collective-permute-done.3
  268.4 7.3 %collective-permute-done.4 = bf16[2,8,8,512]{3,2,1,0:T(8,128)(2,1)S(1)} collective-permute-done((bf16[2,8,8,512]{3,2,1,0:T(8,128)(2,1)S(1)}, bf16[2,8,8,512]{3,2,1,0:T(8,128)(2,1)S(1)}, u32[]{:S(2)}, u32[]{:S(2)}) %collective-permute-start.4) | collective-permute-done | bytes 131104 | tf_op jit(solution)/shard_map/while/body/eval_jaxpr/ppermute | solution.py:42
  277.4 8.0 %eval_jaxpr.9 = f32[2,8,8,128]{3,2,1,0:T(8,128)} custom-call(bf16[8,16,2048]{2,1,0:T(8,128)(2,1)} %pad_maximum_fusion.13.dir_ref, bf16[2,8,128,2048]{3,2,1,0:T(8,128)(2,1)} %get-tuple-element.264.op_ref), custom_call_target="tpu_custom_call" | custom-call | flops 134217728 | bytes 8912896 | tf_op jit(solution)/shard_map/while/body/eval_jaxpr/pallas_call | solution.py:107
  289.7 2.0 collective-permute-start.8
  293.0 2.1 collective-permute-done.8
  297.3 2.2 collective-permute-done.10
  304.5 7.7 %eval_jaxpr.8 = f32[2,8,8,2048]{3,2,1,0:T(8,128)} custom-call(bf16[8,16,128]{2,1,0:T(8,128)(2,1)} %pad_maximum_fusion.11.res_ref, bf16[2,8,128,2048]{3,2,1,0:T(8,128)(2,1)} %get-tuple-element.264.op_ref), custom_call_target="tpu_custom_call" | custom-call | flops 134217728 | bytes 9437184 | tf_op jit(solution)/shard_map/while/body/eval_jaxpr/pallas_call | solution.py:77
  315.7 3.1 collective-permute-done
  318.8 7.6 %collective-permute-done.1 = bf16[2,8,8,512]{3,2,1,0:T(8,128)(2,1)S(1)} collective-permute-done((bf16[2,8,8,512]{3,2,1,0:T(8,128)(2,1)S(1)}, bf16[2,8,8,512]{3,2,1,0:T(8,128)(2,1)S(1)}, u32[]{:S(2)}, u32[]{:S(2)}) %collective-permute-start.1) | collective-permute-done | bytes 131104 | tf_op jit(solution)/shard_map/while/body/eval_jaxpr/ppermute | solution.py:42
  326.6 6.7 %all_gather.8 = bf16[2,32,4096]{2,1,0:T(8,128)(2,1)S(1)} all-gather(bf16[2,8,4096]{2,1,0:T(8,128)(2,1)S(1)} %reshape.236), channel_id=1, replica_groups=mesh['groups'=2,'freq'=4,'recv'=4] {'freq'}, dimensions={1}, use_global_device_ids=true | all-gather | bytes 655360 | tf_op jit(solution)/shard_map/while/body/eval_jaxpr/all_gather | solution.py:150
  338.7 3.2 collective-permute-done.3
  341.9 7.2 %collective-permute-done.4 = bf16[2,8,8,512]{3,2,1,0:T(8,128)(2,1)S(1)} collective-permute-done((bf16[2,8,8,512]{3,2,1,0:T(8,128)(2,1)S(1)}, bf16[2,8,8,512]{3,2,1,0:T(8,128)(2,1)S(1)}, u32[]{:S(2)}, u32[]{:S(2)}) %collective-permute-start.4) | collective-permute-done | bytes 131104 | tf_op jit(solution)/shard_map/while/body/eval_jaxpr/ppermute | solution.py:42
  350.8 8.0 %eval_jaxpr.9 = f32[2,8,8,128]{3,2,1,0:T(8,128)} custom-call(bf16[8,16,2048]{2,1,0:T(8,128)(2,1)} %pad_maximum_fusion.13.dir_ref, bf16[2,8,128,2048]{3,2,1,0:T(8,128)(2,1)} %get-tuple-element.264.op_ref), custom_call_target="tpu_custom_call" | custom-call | flops 134217728 | bytes 8912896 | tf_op jit(solution)/shard_map/while/body/eval_jaxpr/pallas_call | solution.py:107
  366.4 2.1 collective-permute-done.8
  370.6 2.3 collective-permute-done.10
  (305 shorter events, 123.5 us)
Async XLA Ops:
  15.2 9.0 %collective-permute-start = (bf16[2,8,8,512]{3,2,1,0:T(8,128)(2,1)S(1)}, bf16[2,8,8,512]{3,2,1,0:T(8,128)(2,1)S(1)}, u32[]{:S(2)}, u32[]{:S(2)}) collective-permute-start(bf16[2,8,8,512]{3,2,1,0:T(8,128)(2,1)S(1)} %get-tuple-element.219), channel_id=1, source_target_pairs={{0,3},{1,0},{2,1},{3,2},{4,7},{5,4},{6,5},{7,6},{8,11},{9,8},{10,9... | collective-permute-start | bytes 393224 | tf_op jit(solution)/shard_map/while/body/eval_jaxpr/ppermute | solution.py:42
  20.3 11.2 %collective-permute-start.1 = (bf16[2,8,8,512]{3,2,1,0:T(8,128)(2,1)S(1)}, bf16[2,8,8,512]{3,2,1,0:T(8,128)(2,1)S(1)}, u32[]{:S(2)}, u32[]{:S(2)}) collective-permute-start(bf16[2,8,8,512]{3,2,1,0:T(8,128)(2,1)S(1)} %get-tuple-element.220), channel_id=1, source_target_pairs={{0,2},{1,3},{2,0},{3,1},{4,6},{5,7},{6,4},{7,5},{8,10},{9,11},{10,... | collective-permute-start | bytes 393224 | tf_op jit(solution)/shard_map/while/body/eval_jaxpr/ppermute | solution.py:42
  20.3 11.2 %collective-permute-start.2 = (bf16[2,8,8,512]{3,2,1,0:T(8,128)(2,1)S(1)}, bf16[2,8,8,512]{3,2,1,0:T(8,128)(2,1)S(1)}, u32[]{:S(2)}, u32[]{:S(2)}) collective-permute-start(bf16[2,8,8,512]{3,2,1,0:T(8,128)(2,1)S(1)} %get-tuple-element.221), channel_id=1, source_target_pairs={{0,1},{1,2},{2,3},{3,0},{4,5},{5,6},{6,7},{7,4},{8,9},{9,10},{10,1... | collective-permute-start | bytes 393224 | tf_op jit(solution)/shard_map/while/body/eval_jaxpr/ppermute | solution.py:42
  40.8 5.8 %collective-permute-start.3 = (bf16[2,8,8,512]{3,2,1,0:T(8,128)(2,1)S(1)}, bf16[2,8,8,512]{3,2,1,0:T(8,128)(2,1)S(1)}, u32[]{:S(2)}, u32[]{:S(2)}) collective-permute-start(bf16[2,8,8,512]{3,2,1,0:T(8,128)(2,1)S(1)} %copy.47), channel_id=1, source_target_pairs={{0,3},{1,0},{2,1},{3,2},{4,7},{5,4},{6,5},{7,6},{8,11},{9,8},{10,9... | collective-permute-start | bytes 393224 | tf_op jit(solution)/shard_map/while/body/eval_jaxpr/ppermute | solution.py:42
  42.4 13.4 %collective-permute-start.4 = (bf16[2,8,8,512]{3,2,1,0:T(8,128)(2,1)S(1)}, bf16[2,8,8,512]{3,2,1,0:T(8,128)(2,1)S(1)}, u32[]{:S(2)}, u32[]{:S(2)}) collective-permute-start(bf16[2,8,8,512]{3,2,1,0:T(8,128)(2,1)S(1)} %copy.47), channel_id=1, source_target_pairs={{0,2},{1,3},{2,0},{3,1},{4,6},{5,7},{6,4},{7,5},{8,10},{9,11},{10,... | collective-permute-start | bytes 393224 | tf_op jit(solution)/shard_map/while/body/eval_jaxpr/ppermute | solution.py:42
  43.5 12.4 %collective-permute-start.5 = (bf16[2,8,8,512]{3,2,1,0:T(8,128)(2,1)S(1)}, bf16[2,8,8,512]{3,2,1,0:T(8,128)(2,1)S(1)}, u32[]{:S(2)}, u32[]{:S(2)}) collective-permute-start(bf16[2,8,8,512]{3,2,1,0:T(8,128)(2,1)S(1)} %copy.47), channel_id=1, source_target_pairs={{0,1},{1,2},{2,3},{3,0},{4,5},{5,6},{6,7},{7,4},{8,9},{9,10},{10,1... | collective-permute-start | bytes 393224 | tf_op jit(solution)/shard_map/while/body/eval_jaxpr/ppermute | solution.py:42
  68.4 5.0 %collective-permute-start.6 = (f32[1,2]{1,0:T(1,128)S(1)}, f32[1,2]{1,0:T(1,128)S(1)}, u32[]{:S(2)}, u32[]{:S(2)}) collective-permute-start(f32[1,2]{1,0:T(1,128)S(1)} %fusion.69), channel_id=1, source_target_pairs={{0,3},{1,0},{2,1},{3,2},{4,7},{5,4},{6,5},{7,6},{8,11},{9,8},{10,9... | collective-permute-start | bytes 32 | tf_op jit(solution)/shard_map/while/body/eval_jaxpr/ppermute | solution.py:42
  68.4 5.0 %collective-permute-start.7 = (f32[1,2]{1,0:T(1,128)S(1)}, f32[1,2]{1,0:T(1,128)S(1)}, u32[]{:S(2)}, u32[]{:S(2)}) collective-permute-start(f32[1,2]{1,0:T(1,128)S(1)} %fusion.69), channel_id=1, source_target_pairs={{0,2},{1,3},{2,0},{3,1},{4,6},{5,7},{6,4},{7,5},{8,10},{9,11},{10,... | collective-permute-start | bytes 32 | tf_op jit(solution)/shard_map/while/body/eval_jaxpr/ppermute | solution.py:42
  70.1 5.3 %collective-permute-start.8 = (f32[1,2]{1,0:T(1,128)S(1)}, f32[1,2]{1,0:T(1,128)S(1)}, u32[]{:S(2)}, u32[]{:S(2)}) collective-permute-start(f32[1,2]{1,0:T(1,128)S(1)} %fusion.69), channel_id=1, source_target_pairs={{0,1},{1,2},{2,3},{3,0},{4,5},{5,6},{6,7},{7,4},{8,9},{9,10},{10,1... | collective-permute-start | bytes 32 | tf_op jit(solution)/shard_map/while/body/eval_jaxpr/ppermute | solution.py:42
  76.3 3.6 collective-permute-start.10
  93.5 5.3 %collective-permute-start = (bf16[2,8,8,512]{3,2,1,0:T(8,128)(2,1)S(1)}, bf16[2,8,8,512]{3,2,1,0:T(8,128)(2,1)S(1)}, u32[]{:S(2)}, u32[]{:S(2)}) collective-permute-start(bf16[2,8,8,512]{3,2,1,0:T(8,128)(2,1)S(1)} %get-tuple-element.219), channel_id=1, source_target_pairs={{0,3},{1,0},{2,1},{3,2},{4,7},{5,4},{6,5},{7,6},{8,11},{9,8},{10,9... | collective-permute-start | bytes 393224 | tf_op jit(solution)/shard_map/while/body/eval_jaxpr/ppermute | solution.py:42
  94.4 12.1 %collective-permute-start.1 = (bf16[2,8,8,512]{3,2,1,0:T(8,128)(2,1)S(1)}, bf16[2,8,8,512]{3,2,1,0:T(8,128)(2,1)S(1)}, u32[]{:S(2)}, u32[]{:S(2)}) collective-permute-start(bf16[2,8,8,512]{3,2,1,0:T(8,128)(2,1)S(1)} %get-tuple-element.220), channel_id=1, source_target_pairs={{0,2},{1,3},{2,0},{3,1},{4,6},{5,7},{6,4},{7,5},{8,10},{9,11},{10,... | collective-permute-start | bytes 393224 | tf_op jit(solution)/shard_map/while/body/eval_jaxpr/ppermute | solution.py:42
  95.2 11.4 %collective-permute-start.2 = (bf16[2,8,8,512]{3,2,1,0:T(8,128)(2,1)S(1)}, bf16[2,8,8,512]{3,2,1,0:T(8,128)(2,1)S(1)}, u32[]{:S(2)}, u32[]{:S(2)}) collective-permute-start(bf16[2,8,8,512]{3,2,1,0:T(8,128)(2,1)S(1)} %get-tuple-element.221), channel_id=1, source_target_pairs={{0,1},{1,2},{2,3},{3,0},{4,5},{5,6},{6,7},{7,4},{8,9},{9,10},{10,1... | collective-permute-start | bytes 393224 | tf_op jit(solution)/shard_map/while/body/eval_jaxpr/ppermute | solution.py:42
  115.2 6.6 %collective-permute-start.3 = (bf16[2,8,8,512]{3,2,1,0:T(8,128)(2,1)S(1)}, bf16[2,8,8,512]{3,2,1,0:T(8,128)(2,1)S(1)}, u32[]{:S(2)}, u32[]{:S(2)}) collective-permute-start(bf16[2,8,8,512]{3,2,1,0:T(8,128)(2,1)S(1)} %copy.47), channel_id=1, source_target_pairs={{0,3},{1,0},{2,1},{3,2},{4,7},{5,4},{6,5},{7,6},{8,11},{9,8},{10,9... | collective-permute-start | bytes 393224 | tf_op jit(solution)/shard_map/while/body/eval_jaxpr/ppermute | solution.py:42
  115.2 14.0 %collective-permute-start.4 = (bf16[2,8,8,512]{3,2,1,0:T(8,128)(2,1)S(1)}, bf16[2,8,8,512]{3,2,1,0:T(8,128)(2,1)S(1)}, u32[]{:S(2)}, u32[]{:S(2)}) collective-permute-start(bf16[2,8,8,512]{3,2,1,0:T(8,128)(2,1)S(1)} %copy.47), channel_id=1, source_target_pairs={{0,2},{1,3},{2,0},{3,1},{4,6},{5,7},{6,4},{7,5},{8,10},{9,11},{10,... | collective-permute-start | bytes 393224 | tf_op jit(solution)/shard_map/while/body/eval_jaxpr/ppermute | solution.py:42
  116.8 12.4 %collective-permute-start.5 = (bf16[2,8,8,512]{3,2,1,0:T(8,128)(2,1)S(1)}, bf16[2,8,8,512]{3,2,1,0:T(8,128)(2,1)S(1)}, u32[]{:S(2)}, u32[]{:S(2)}) collective-permute-start(bf16[2,8,8,512]{3,2,1,0:T(8,128)(2,1)S(1)} %copy.47), channel_id=1, source_target_pairs={{0,1},{1,2},{2,3},{3,0},{4,5},{5,6},{6,7},{7,4},{8,9},{9,10},{10,1... | collective-permute-start | bytes 393224 | tf_op jit(solution)/shard_map/while/body/eval_jaxpr/ppermute | solution.py:42
  141.7 4.7 %collective-permute-start.6 = (f32[1,2]{1,0:T(1,128)S(1)}, f32[1,2]{1,0:T(1,128)S(1)}, u32[]{:S(2)}, u32[]{:S(2)}) collective-permute-start(f32[1,2]{1,0:T(1,128)S(1)} %fusion.69), channel_id=1, source_target_pairs={{0,3},{1,0},{2,1},{3,2},{4,7},{5,4},{6,5},{7,6},{8,11},{9,8},{10,9... | collective-permute-start | bytes 32 | tf_op jit(solution)/shard_map/while/body/eval_jaxpr/ppermute | solution.py:42
  141.7 4.7 %collective-permute-start.7 = (f32[1,2]{1,0:T(1,128)S(1)}, f32[1,2]{1,0:T(1,128)S(1)}, u32[]{:S(2)}, u32[]{:S(2)}) collective-permute-start(f32[1,2]{1,0:T(1,128)S(1)} %fusion.69), channel_id=1, source_target_pairs={{0,2},{1,3},{2,0},{3,1},{4,6},{5,7},{6,4},{7,5},{8,10},{9,11},{10,... | collective-permute-start | bytes 32 | tf_op jit(solution)/shard_map/while/body/eval_jaxpr/ppermute | solution.py:42
  143.1 5.3 %collective-permute-start.8 = (f32[1,2]{1,0:T(1,128)S(1)}, f32[1,2]{1,0:T(1,128)S(1)}, u32[]{:S(2)}, u32[]{:S(2)}) collective-permute-start(f32[1,2]{1,0:T(1,128)S(1)} %fusion.69), channel_id=1, source_target_pairs={{0,1},{1,2},{2,3},{3,0},{4,5},{5,6},{6,7},{7,4},{8,9},{9,10},{10,1... | collective-permute-start | bytes 32 | tf_op jit(solution)/shard_map/while/body/eval_jaxpr/ppermute | solution.py:42
  149.3 3.6 collective-permute-start.10
  166.9 5.3 %collective-permute-start = (bf16[2,8,8,512]{3,2,1,0:T(8,128)(2,1)S(1)}, bf16[2,8,8,512]{3,2,1,0:T(8,128)(2,1)S(1)}, u32[]{:S(2)}, u32[]{:S(2)}) collective-permute-start(bf16[2,8,8,512]{3,2,1,0:T(8,128)(2,1)S(1)} %get-tuple-element.219), channel_id=1, source_target_pairs={{0,3},{1,0},{2,1},{3,2},{4,7},{5,4},{6,5},{7,6},{8,11},{9,8},{10,9... | collective-permute-start | bytes 393224 | tf_op jit(solution)/shard_map/while/body/eval_jaxpr/ppermute | solution.py:42
  168.0 11.9 %collective-permute-start.1 = (bf16[2,8,8,512]{3,2,1,0:T(8,128)(2,1)S(1)}, bf16[2,8,8,512]{3,2,1,0:T(8,128)(2,1)S(1)}, u32[]{:S(2)}, u32[]{:S(2)}) collective-permute-start(bf16[2,8,8,512]{3,2,1,0:T(8,128)(2,1)S(1)} %get-tuple-element.220), channel_id=1, source_target_pairs={{0,2},{1,3},{2,0},{3,1},{4,6},{5,7},{6,4},{7,5},{8,10},{9,11},{10,... | collective-permute-start | bytes 393224 | tf_op jit(solution)/shard_map/while/body/eval_jaxpr/ppermute | solution.py:42
  168.6 11.3 %collective-permute-start.2 = (bf16[2,8,8,512]{3,2,1,0:T(8,128)(2,1)S(1)}, bf16[2,8,8,512]{3,2,1,0:T(8,128)(2,1)S(1)}, u32[]{:S(2)}, u32[]{:S(2)}) collective-permute-start(bf16[2,8,8,512]{3,2,1,0:T(8,128)(2,1)S(1)} %get-tuple-element.221), channel_id=1, source_target_pairs={{0,1},{1,2},{2,3},{3,0},{4,5},{5,6},{6,7},{7,4},{8,9},{9,10},{10,1... | collective-permute-start | bytes 393224 | tf_op jit(solution)/shard_map/while/body/eval_jaxpr/ppermute | solution.py:42
  188.6 6.7 %collective-permute-start.3 = (bf16[2,8,8,512]{3,2,1,0:T(8,128)(2,1)S(1)}, bf16[2,8,8,512]{3,2,1,0:T(8,128)(2,1)S(1)}, u32[]{:S(2)}, u32[]{:S(2)}) collective-permute-start(bf16[2,8,8,512]{3,2,1,0:T(8,128)(2,1)S(1)} %copy.47), channel_id=1, source_target_pairs={{0,3},{1,0},{2,1},{3,2},{4,7},{5,4},{6,5},{7,6},{8,11},{9,8},{10,9... | collective-permute-start | bytes 393224 | tf_op jit(solution)/shard_map/while/body/eval_jaxpr/ppermute | solution.py:42
  188.8 13.7 %collective-permute-start.4 = (bf16[2,8,8,512]{3,2,1,0:T(8,128)(2,1)S(1)}, bf16[2,8,8,512]{3,2,1,0:T(8,128)(2,1)S(1)}, u32[]{:S(2)}, u32[]{:S(2)}) collective-permute-start(bf16[2,8,8,512]{3,2,1,0:T(8,128)(2,1)S(1)} %copy.47), channel_id=1, source_target_pairs={{0,2},{1,3},{2,0},{3,1},{4,6},{5,7},{6,4},{7,5},{8,10},{9,11},{10,... | collective-permute-start | bytes 393224 | tf_op jit(solution)/shard_map/while/body/eval_jaxpr/ppermute | solution.py:42
  190.1 12.3 %collective-permute-start.5 = (bf16[2,8,8,512]{3,2,1,0:T(8,128)(2,1)S(1)}, bf16[2,8,8,512]{3,2,1,0:T(8,128)(2,1)S(1)}, u32[]{:S(2)}, u32[]{:S(2)}) collective-permute-start(bf16[2,8,8,512]{3,2,1,0:T(8,128)(2,1)S(1)} %copy.47), channel_id=1, source_target_pairs={{0,1},{1,2},{2,3},{3,0},{4,5},{5,6},{6,7},{7,4},{8,9},{9,10},{10,1... | collective-permute-start | bytes 393224 | tf_op jit(solution)/shard_map/while/body/eval_jaxpr/ppermute | solution.py:42
  215.0 4.8 %collective-permute-start.6 = (f32[1,2]{1,0:T(1,128)S(1)}, f32[1,2]{1,0:T(1,128)S(1)}, u32[]{:S(2)}, u32[]{:S(2)}) collective-permute-start(f32[1,2]{1,0:T(1,128)S(1)} %fusion.69), channel_id=1, source_target_pairs={{0,3},{1,0},{2,1},{3,2},{4,7},{5,4},{6,5},{7,6},{8,11},{9,8},{10,9... | collective-permute-start | bytes 32 | tf_op jit(solution)/shard_map/while/body/eval_jaxpr/ppermute | solution.py:42
  215.0 4.8 %collective-permute-start.7 = (f32[1,2]{1,0:T(1,128)S(1)}, f32[1,2]{1,0:T(1,128)S(1)}, u32[]{:S(2)}, u32[]{:S(2)}) collective-permute-start(f32[1,2]{1,0:T(1,128)S(1)} %fusion.69), channel_id=1, source_target_pairs={{0,2},{1,3},{2,0},{3,1},{4,6},{5,7},{6,4},{7,5},{8,10},{9,11},{10,... | collective-permute-start | bytes 32 | tf_op jit(solution)/shard_map/while/body/eval_jaxpr/ppermute | solution.py:42
  216.5 5.3 %collective-permute-start.8 = (f32[1,2]{1,0:T(1,128)S(1)}, f32[1,2]{1,0:T(1,128)S(1)}, u32[]{:S(2)}, u32[]{:S(2)}) collective-permute-start(f32[1,2]{1,0:T(1,128)S(1)} %fusion.69), channel_id=1, source_target_pairs={{0,1},{1,2},{2,3},{3,0},{4,5},{5,6},{6,7},{7,4},{8,9},{9,10},{10,1... | collective-permute-start | bytes 32 | tf_op jit(solution)/shard_map/while/body/eval_jaxpr/ppermute | solution.py:42
  222.7 3.6 collective-permute-start.10
  240.2 5.2 %collective-permute-start = (bf16[2,8,8,512]{3,2,1,0:T(8,128)(2,1)S(1)}, bf16[2,8,8,512]{3,2,1,0:T(8,128)(2,1)S(1)}, u32[]{:S(2)}, u32[]{:S(2)}) collective-permute-start(bf16[2,8,8,512]{3,2,1,0:T(8,128)(2,1)S(1)} %get-tuple-element.219), channel_id=1, source_target_pairs={{0,3},{1,0},{2,1},{3,2},{4,7},{5,4},{6,5},{7,6},{8,11},{9,8},{10,9... | collective-permute-start | bytes 393224 | tf_op jit(solution)/shard_map/while/body/eval_jaxpr/ppermute | solution.py:42
  241.0 12.1 %collective-permute-start.1 = (bf16[2,8,8,512]{3,2,1,0:T(8,128)(2,1)S(1)}, bf16[2,8,8,512]{3,2,1,0:T(8,128)(2,1)S(1)}, u32[]{:S(2)}, u32[]{:S(2)}) collective-permute-start(bf16[2,8,8,512]{3,2,1,0:T(8,128)(2,1)S(1)} %get-tuple-element.220), channel_id=1, source_target_pairs={{0,2},{1,3},{2,0},{3,1},{4,6},{5,7},{6,4},{7,5},{8,10},{9,11},{10,... | collective-permute-start | bytes 393224 | tf_op jit(solution)/shard_map/while/body/eval_jaxpr/ppermute | solution.py:42
  241.9 11.2 %collective-permute-start.2 = (bf16[2,8,8,512]{3,2,1,0:T(8,128)(2,1)S(1)}, bf16[2,8,8,512]{3,2,1,0:T(8,128)(2,1)S(1)}, u32[]{:S(2)}, u32[]{:S(2)}) collective-permute-start(bf16[2,8,8,512]{3,2,1,0:T(8,128)(2,1)S(1)} %get-tuple-element.221), channel_id=1, source_target_pairs={{0,1},{1,2},{2,3},{3,0},{4,5},{5,6},{6,7},{7,4},{8,9},{9,10},{10,1... | collective-permute-start | bytes 393224 | tf_op jit(solution)/shard_map/while/body/eval_jaxpr/ppermute | solution.py:42
  261.7 6.7 %collective-permute-start.3 = (bf16[2,8,8,512]{3,2,1,0:T(8,128)(2,1)S(1)}, bf16[2,8,8,512]{3,2,1,0:T(8,128)(2,1)S(1)}, u32[]{:S(2)}, u32[]{:S(2)}) collective-permute-start(bf16[2,8,8,512]{3,2,1,0:T(8,128)(2,1)S(1)} %copy.47), channel_id=1, source_target_pairs={{0,3},{1,0},{2,1},{3,2},{4,7},{5,4},{6,5},{7,6},{8,11},{9,8},{10,9... | collective-permute-start | bytes 393224 | tf_op jit(solution)/shard_map/while/body/eval_jaxpr/ppermute | solution.py:42
  261.8 13.9 %collective-permute-start.4 = (bf16[2,8,8,512]{3,2,1,0:T(8,128)(2,1)S(1)}, bf16[2,8,8,512]{3,2,1,0:T(8,128)(2,1)S(1)}, u32[]{:S(2)}, u32[]{:S(2)}) collective-permute-start(bf16[2,8,8,512]{3,2,1,0:T(8,128)(2,1)S(1)} %copy.47), channel_id=1, source_target_pairs={{0,2},{1,3},{2,0},{3,1},{4,6},{5,7},{6,4},{7,5},{8,10},{9,11},{10,... | collective-permute-start | bytes 393224 | tf_op jit(solution)/shard_map/while/body/eval_jaxpr/ppermute | solution.py:42
  263.4 12.4 %collective-permute-start.5 = (bf16[2,8,8,512]{3,2,1,0:T(8,128)(2,1)S(1)}, bf16[2,8,8,512]{3,2,1,0:T(8,128)(2,1)S(1)}, u32[]{:S(2)}, u32[]{:S(2)}) collective-permute-start(bf16[2,8,8,512]{3,2,1,0:T(8,128)(2,1)S(1)} %copy.47), channel_id=1, source_target_pairs={{0,1},{1,2},{2,3},{3,0},{4,5},{5,6},{6,7},{7,4},{8,9},{9,10},{10,1... | collective-permute-start | bytes 393224 | tf_op jit(solution)/shard_map/while/body/eval_jaxpr/ppermute | solution.py:42
  288.2 4.8 %collective-permute-start.6 = (f32[1,2]{1,0:T(1,128)S(1)}, f32[1,2]{1,0:T(1,128)S(1)}, u32[]{:S(2)}, u32[]{:S(2)}) collective-permute-start(f32[1,2]{1,0:T(1,128)S(1)} %fusion.69), channel_id=1, source_target_pairs={{0,3},{1,0},{2,1},{3,2},{4,7},{5,4},{6,5},{7,6},{8,11},{9,8},{10,9... | collective-permute-start | bytes 32 | tf_op jit(solution)/shard_map/while/body/eval_jaxpr/ppermute | solution.py:42
  288.2 4.8 %collective-permute-start.7 = (f32[1,2]{1,0:T(1,128)S(1)}, f32[1,2]{1,0:T(1,128)S(1)}, u32[]{:S(2)}, u32[]{:S(2)}) collective-permute-start(f32[1,2]{1,0:T(1,128)S(1)} %fusion.69), channel_id=1, source_target_pairs={{0,2},{1,3},{2,0},{3,1},{4,6},{5,7},{6,4},{7,5},{8,10},{9,11},{10,... | collective-permute-start | bytes 32 | tf_op jit(solution)/shard_map/while/body/eval_jaxpr/ppermute | solution.py:42
  289.7 5.3 %collective-permute-start.8 = (f32[1,2]{1,0:T(1,128)S(1)}, f32[1,2]{1,0:T(1,128)S(1)}, u32[]{:S(2)}, u32[]{:S(2)}) collective-permute-start(f32[1,2]{1,0:T(1,128)S(1)} %fusion.69), channel_id=1, source_target_pairs={{0,1},{1,2},{2,3},{3,0},{4,5},{5,6},{6,7},{7,4},{8,9},{9,10},{10,1... | collective-permute-start | bytes 32 | tf_op jit(solution)/shard_map/while/body/eval_jaxpr/ppermute | solution.py:42
  313.5 5.3 %collective-permute-start = (bf16[2,8,8,512]{3,2,1,0:T(8,128)(2,1)S(1)}, bf16[2,8,8,512]{3,2,1,0:T(8,128)(2,1)S(1)}, u32[]{:S(2)}, u32[]{:S(2)}) collective-permute-start(bf16[2,8,8,512]{3,2,1,0:T(8,128)(2,1)S(1)} %get-tuple-element.219), channel_id=1, source_target_pairs={{0,3},{1,0},{2,1},{3,2},{4,7},{5,4},{6,5},{7,6},{8,11},{9,8},{10,9... | collective-permute-start | bytes 393224 | tf_op jit(solution)/shard_map/while/body/eval_jaxpr/ppermute | solution.py:42
  314.6 11.8 %collective-permute-start.1 = (bf16[2,8,8,512]{3,2,1,0:T(8,128)(2,1)S(1)}, bf16[2,8,8,512]{3,2,1,0:T(8,128)(2,1)S(1)}, u32[]{:S(2)}, u32[]{:S(2)}) collective-permute-start(bf16[2,8,8,512]{3,2,1,0:T(8,128)(2,1)S(1)} %get-tuple-element.220), channel_id=1, source_target_pairs={{0,2},{1,3},{2,0},{3,1},{4,6},{5,7},{6,4},{7,5},{8,10},{9,11},{10,... | collective-permute-start | bytes 393224 | tf_op jit(solution)/shard_map/while/body/eval_jaxpr/ppermute | solution.py:42
  315.2 11.2 %collective-permute-start.2 = (bf16[2,8,8,512]{3,2,1,0:T(8,128)(2,1)S(1)}, bf16[2,8,8,512]{3,2,1,0:T(8,128)(2,1)S(1)}, u32[]{:S(2)}, u32[]{:S(2)}) collective-permute-start(bf16[2,8,8,512]{3,2,1,0:T(8,128)(2,1)S(1)} %get-tuple-element.221), channel_id=1, source_target_pairs={{0,1},{1,2},{2,3},{3,0},{4,5},{5,6},{6,7},{7,4},{8,9},{9,10},{10,1... | collective-permute-start | bytes 393224 | tf_op jit(solution)/shard_map/while/body/eval_jaxpr/ppermute | solution.py:42
  335.2 6.7 %collective-permute-start.3 = (bf16[2,8,8,512]{3,2,1,0:T(8,128)(2,1)S(1)}, bf16[2,8,8,512]{3,2,1,0:T(8,128)(2,1)S(1)}, u32[]{:S(2)}, u32[]{:S(2)}) collective-permute-start(bf16[2,8,8,512]{3,2,1,0:T(8,128)(2,1)S(1)} %copy.47), channel_id=1, source_target_pairs={{0,3},{1,0},{2,1},{3,2},{4,7},{5,4},{6,5},{7,6},{8,11},{9,8},{10,9... | collective-permute-start | bytes 393224 | tf_op jit(solution)/shard_map/while/body/eval_jaxpr/ppermute | solution.py:42
  335.3 13.7 %collective-permute-start.4 = (bf16[2,8,8,512]{3,2,1,0:T(8,128)(2,1)S(1)}, bf16[2,8,8,512]{3,2,1,0:T(8,128)(2,1)S(1)}, u32[]{:S(2)}, u32[]{:S(2)}) collective-permute-start(bf16[2,8,8,512]{3,2,1,0:T(8,128)(2,1)S(1)} %copy.47), channel_id=1, source_target_pairs={{0,2},{1,3},{2,0},{3,1},{4,6},{5,7},{6,4},{7,5},{8,10},{9,11},{10,... | collective-permute-start | bytes 393224 | tf_op jit(solution)/shard_map/while/body/eval_jaxpr/ppermute | solution.py:42
  336.7 12.4 %collective-permute-start.5 = (bf16[2,8,8,512]{3,2,1,0:T(8,128)(2,1)S(1)}, bf16[2,8,8,512]{3,2,1,0:T(8,128)(2,1)S(1)}, u32[]{:S(2)}, u32[]{:S(2)}) collective-permute-start(bf16[2,8,8,512]{3,2,1,0:T(8,128)(2,1)S(1)} %copy.47), channel_id=1, source_target_pairs={{0,1},{1,2},{2,3},{3,0},{4,5},{5,6},{6,7},{7,4},{8,9},{9,10},{10,1... | collective-permute-start | bytes 393224 | tf_op jit(solution)/shard_map/while/body/eval_jaxpr/ppermute | solution.py:42
  361.5 4.8 %collective-permute-start.6 = (f32[1,2]{1,0:T(1,128)S(1)}, f32[1,2]{1,0:T(1,128)S(1)}, u32[]{:S(2)}, u32[]{:S(2)}) collective-permute-start(f32[1,2]{1,0:T(1,128)S(1)} %fusion.69), channel_id=1, source_target_pairs={{0,3},{1,0},{2,1},{3,2},{4,7},{5,4},{6,5},{7,6},{8,11},{9,8},{10,9... | collective-permute-start | bytes 32 | tf_op jit(solution)/shard_map/while/body/eval_jaxpr/ppermute | solution.py:42
  361.5 4.8 %collective-permute-start.7 = (f32[1,2]{1,0:T(1,128)S(1)}, f32[1,2]{1,0:T(1,128)S(1)}, u32[]{:S(2)}, u32[]{:S(2)}) collective-permute-start(f32[1,2]{1,0:T(1,128)S(1)} %fusion.69), channel_id=1, source_target_pairs={{0,2},{1,3},{2,0},{3,1},{4,6},{5,7},{6,4},{7,5},{8,10},{9,11},{10,... | collective-permute-start | bytes 32 | tf_op jit(solution)/shard_map/while/body/eval_jaxpr/ppermute | solution.py:42
  363.1 5.3 %collective-permute-start.8 = (f32[1,2]{1,0:T(1,128)S(1)}, f32[1,2]{1,0:T(1,128)S(1)}, u32[]{:S(2)}, u32[]{:S(2)}) collective-permute-start(f32[1,2]{1,0:T(1,128)S(1)} %fusion.69), channel_id=1, source_target_pairs={{0,1},{1,2},{2,3},{3,0},{4,5},{5,6},{6,7},{7,4},{8,9},{9,10},{10,1... | collective-permute-start | bytes 32 | tf_op jit(solution)/shard_map/while/body/eval_jaxpr/ppermute | solution.py:42
  (13 other events, 30.0 us)

commit v7 on v5

--- a/solution.py
+++ b/solution.py
@@ -10,7 +10,7 @@
 
 
 def high_dot(left, right):
-    return jnp.dot(left, right, precision=lax.Precision.HIGHEST)
+    return jnp.dot(left, right, precision=lax.Precision.HIGH)
 
 
 def dft_rows(row_ids, length):

time: 334 us -> 332 us (level)
  no operation moved by 1% of the time
where the time goes in v7:
time: 332 us; the launch traced here: 331 us
  waiting for transfers between devices  129 us (39%)
  starting transfers between devices  57.3 us (17%)
  matrix products  55.1 us (17%)
  blocking collectives  33.5 us (10%)
  other arithmetic  24.8 us (7%)
  local copies, waits for them, and re-layouts  23 us (7%)
  loops' own time  7.75 us (2%)
    ppermute x60, waiting for transfers between devices, shifted(): lax.ppermute(value, axis, [(i, (i + distance) % size) for i in range(size)])  129 us
    ppermute x60, starting transfers between devices, shifted(): lax.ppermute(value, axis, [(i, (i + distance) % size) for i in range(size)])  57.3 us
    all_gather x5, blocking collectives, step(): lax.all_gather(flattened, 'freq', axis=1, tiled=True).astype(jnp.float32)  33.5 us
    dot_general x5, matrix products, step(): jnp.einsum('fbs,frs->fbr', stacked_direction, imag_operator, preferred_el...  17.8 us
    dot_general x5, matrix products, step(): jnp.einsum('fbr,frs->fbs', stacked_residual, imag_operator, preferred_ele...  15 us
    dot_general x10, matrix products, high_dot(): return jnp.dot(left, right, precision=lax.Precision.HIGH)  13.1 us
    gather x25, local copies, waits for them, and re-layouts, gather_blocks(): ordered = jnp.take(slots, order, axis=dim)  9.43 us
    another operation x1, loops' own time, on_device(): return lax.fori_loop(0, ITERS, step, (reflect, recorded))  7.75 us
  transfers between devices with their start and end apart: 60, of which 36 were waited for; matrix products, arithmetic and copies ran while one was open for 2% of the time, Pallas kernels for 0%

profile of v7, /device:TPU:0, one launch (start us, length us, event | category | flops | bytes accessed | tf_op | source)
XLA Modules:
  0.0 331.5 jit_solution(13860903966466590340)
XLA Ops:
  0.7 6.1 %slice_bitcast_fusion.2 = (bf16[8,128,2048]{2,1,0:T(8,128)(2,1)}, bf16[8,128,2048]{2,1,0:T(8,128)(2,1)}) fusion(bf16[2,8,128,2048]{3,2,1,0:T(8,128)(2,1)} %param.8), kind=kLoop, calls=%fused_computation.83 | loop fusion | bytes 16777216 | tf_op jit(solution)/shard_map/squeeze | solution.py:71
  10.5 320.1 %while.15 = (s32[]{:T(128)}, f32[2,8,8,512]{3,1,2,0:T(8,128)S(1)}, f32[2,8,8,128]{3,2,1,0:T(8,128)S(1)}, bf16[8,128,2048]{2,1,0:T(8,128)(2,1)}, bf16[8,128,2048]...) while((s32[]{:T(128)}, f32[2,8,8,512]{3,1,2,0:T(8,128)S(1)}, ...), condition=%wide.region_7.9_spmd.clone, body=%wide.region_2.8_spmd.clone.sunk | while | flops 399642016 | bytes 73599128 | solution.py:122
  10.6 3.0 fusion.104
  14.8 5.1 %collective-permute-start = (bf16[2,8,8,512]{3,2,1,0:T(8,128)(2,1)S(1)}, bf16[2,8,8,512]{3,2,1,0:T(8,128)(2,1)S(1)}, u32[]{:S(2)}, u32[]{:S(2)}) collective-permute-start(bf16[2,8,8,512]{3,2,1,0:T(8,128)(2,1)S(1)} %get-tuple-element.253), channel_id=1, source_target_pairs={{0,3},{1,0},{2,1},{3,2},{4,7},{5,4},{6,5},{7,6},{8,11},{9,8},{10,9... | collective-permute-start | bytes 393224 | tf_op jit(solution)/shard_map/while/body/eval_jaxpr/ppermute | solution.py:40
  21.0 2.8 collective-permute-done
  23.8 7.3 %collective-permute-done.1 = bf16[2,8,8,512]{3,2,1,0:T(8,128)(2,1)S(1)} collective-permute-done((bf16[2,8,8,512]{3,2,1,0:T(8,128)(2,1)S(1)}, bf16[2,8,8,512]{3,2,1,0:T(8,128)(2,1)S(1)}, u32[]{:S(2)}, u32[]{:S(2)}) %collective-permute-start.1) | collective-permute-done | bytes 131104 | tf_op jit(solution)/shard_map/while/body/eval_jaxpr/ppermute | solution.py:40
  31.3 7.2 %all_gather.8 = bf16[2,32,4096]{2,1,0:T(8,128)(2,1)S(1)} all-gather(bf16[2,8,4096]{2,1,0:T(8,128)(2,1)S(1)} %reshape.242), channel_id=1, replica_groups=mesh['groups'=2,'freq'=4,'recv'=4] {'freq'}, dimensions={1}, use_global_device_ids=true | all-gather | bytes 655360 | tf_op jit(solution)/shard_map/while/body/eval_jaxpr/all_gather | solution.py:99
  43.7 2.0 collective-permute-start.5
  46.8 9.3 %collective-permute-done.4 = bf16[2,8,8,512]{3,1,2,0:T(8,128)(2,1)S(1)} collective-permute-done((bf16[2,8,8,512]{3,1,2,0:T(8,128)(2,1)S(1)}, bf16[2,8,8,512]{3,1,2,0:T(8,128)(2,1)S(1)}, u32[]{:S(2)}, u32[]{:S(2)}) %collective-permute-start.4) | collective-permute-done | bytes 131104 | tf_op jit(solution)/shard_map/while/body/eval_jaxpr/ppermute | solution.py:40
  57.2 3.6 %fusion.112 = f32[8,16,128]{2,1,0:T(8,128)S(1)} fusion(bf16[8,128,2048]{2,1,0:T(8,128)(2,1)} %get-tuple-element.303, bf16[8,8,2048]{2,1,0:T(8,128)(2,1)S(1)} %bitcast.168, bf16[8,8,2048]{2,1,0:T(8,128)(2,1)S(1)} %bitcast.170), kind=kOutput, calls=%fused_computation.20.clone.1 | convolution fusion | flops 68157440 | bytes 4784128 | tf_op jit(solution)/shard_map/while/body/eval_jaxpr/fbs,frs->fbr/dot_general | solution.py:109
  69.0 2.0 collective-permute-done.8
  73.1 2.3 collective-permute-done.10
  78.6 3.0 fusion.104
  85.0 3.1 collective-permute-done
  88.2 7.7 %collective-permute-done.1 = bf16[2,8,8,512]{3,2,1,0:T(8,128)(2,1)S(1)} collective-permute-done((bf16[2,8,8,512]{3,2,1,0:T(8,128)(2,1)S(1)}, bf16[2,8,8,512]{3,2,1,0:T(8,128)(2,1)S(1)}, u32[]{:S(2)}, u32[]{:S(2)}) %collective-permute-start.1) | collective-permute-done | bytes 131104 | tf_op jit(solution)/shard_map/while/body/eval_jaxpr/ppermute | solution.py:40
  96.1 6.5 %all_gather.8 = bf16[2,32,4096]{2,1,0:T(8,128)(2,1)S(1)} all-gather(bf16[2,8,4096]{2,1,0:T(8,128)(2,1)S(1)} %reshape.242), channel_id=1, replica_groups=mesh['groups'=2,'freq'=4,'recv'=4] {'freq'}, dimensions={1}, use_global_device_ids=true | all-gather | bytes 655360 | tf_op jit(solution)/shard_map/while/body/eval_jaxpr/all_gather | solution.py:99
  108.8 3.0 collective-permute-done.3
  111.8 7.3 %collective-permute-done.4 = bf16[2,8,8,512]{3,1,2,0:T(8,128)(2,1)S(1)} collective-permute-done((bf16[2,8,8,512]{3,1,2,0:T(8,128)(2,1)S(1)}, bf16[2,8,8,512]{3,1,2,0:T(8,128)(2,1)S(1)}, u32[]{:S(2)}, u32[]{:S(2)}) %collective-permute-start.4) | collective-permute-done | bytes 131104 | tf_op jit(solution)/shard_map/while/body/eval_jaxpr/ppermute | solution.py:40
  120.1 3.6 %fusion.112 = f32[8,16,128]{2,1,0:T(8,128)S(1)} fusion(bf16[8,128,2048]{2,1,0:T(8,128)(2,1)} %get-tuple-element.303, bf16[8,8,2048]{2,1,0:T(8,128)(2,1)S(1)} %bitcast.168, bf16[8,8,2048]{2,1,0:T(8,128)(2,1)S(1)} %bitcast.170), kind=kOutput, calls=%fused_computation.20.clone.1 | convolution fusion | flops 68157440 | bytes 4784128 | tf_op jit(solution)/shard_map/while/body/eval_jaxpr/fbs,frs->fbr/dot_general | solution.py:109
  131.7 2.0 collective-permute-done.8
  136.0 2.2 collective-permute-done.10
  141.7 3.0 fusion.104
  148.1 3.1 collective-permute-done
  151.3 7.6 %collective-permute-done.1 = bf16[2,8,8,512]{3,2,1,0:T(8,128)(2,1)S(1)} collective-permute-done((bf16[2,8,8,512]{3,2,1,0:T(8,128)(2,1)S(1)}, bf16[2,8,8,512]{3,2,1,0:T(8,128)(2,1)S(1)}, u32[]{:S(2)}, u32[]{:S(2)}) %collective-permute-start.1) | collective-permute-done | bytes 131104 | tf_op jit(solution)/shard_map/while/body/eval_jaxpr/ppermute | solution.py:40
  159.0 6.6 %all_gather.8 = bf16[2,32,4096]{2,1,0:T(8,128)(2,1)S(1)} all-gather(bf16[2,8,4096]{2,1,0:T(8,128)(2,1)S(1)} %reshape.242), channel_id=1, replica_groups=mesh['groups'=2,'freq'=4,'recv'=4] {'freq'}, dimensions={1}, use_global_device_ids=true | all-gather | bytes 655360 | tf_op jit(solution)/shard_map/while/body/eval_jaxpr/all_gather | solution.py:99
  171.8 3.2 collective-permute-done.3
  175.0 7.2 %collective-permute-done.4 = bf16[2,8,8,512]{3,1,2,0:T(8,128)(2,1)S(1)} collective-permute-done((bf16[2,8,8,512]{3,1,2,0:T(8,128)(2,1)S(1)}, bf16[2,8,8,512]{3,1,2,0:T(8,128)(2,1)S(1)}, u32[]{:S(2)}, u32[]{:S(2)}) %collective-permute-start.4) | collective-permute-done | bytes 131104 | tf_op jit(solution)/shard_map/while/body/eval_jaxpr/ppermute | solution.py:40
  183.2 3.6 %fusion.112 = f32[8,16,128]{2,1,0:T(8,128)S(1)} fusion(bf16[8,128,2048]{2,1,0:T(8,128)(2,1)} %get-tuple-element.303, bf16[8,8,2048]{2,1,0:T(8,128)(2,1)S(1)} %bitcast.168, bf16[8,8,2048]{2,1,0:T(8,128)(2,1)S(1)} %bitcast.170), kind=kOutput, calls=%fused_computation.20.clone.1 | convolution fusion | flops 68157440 | bytes 4784128 | tf_op jit(solution)/shard_map/while/body/eval_jaxpr/fbs,frs->fbr/dot_general | solution.py:109
  194.9 2.0 collective-permute-done.8
  199.0 2.3 collective-permute-done.10
  204.7 3.0 fusion.104
  211.1 3.1 collective-permute-done
  214.2 7.7 %collective-permute-done.1 = bf16[2,8,8,512]{3,2,1,0:T(8,128)(2,1)S(1)} collective-permute-done((bf16[2,8,8,512]{3,2,1,0:T(8,128)(2,1)S(1)}, bf16[2,8,8,512]{3,2,1,0:T(8,128)(2,1)S(1)}, u32[]{:S(2)}, u32[]{:S(2)}) %collective-permute-start.1) | collective-permute-done | bytes 131104 | tf_op jit(solution)/shard_map/while/body/eval_jaxpr/ppermute | solution.py:40
  222.1 6.5 %all_gather.8 = bf16[2,32,4096]{2,1,0:T(8,128)(2,1)S(1)} all-gather(bf16[2,8,4096]{2,1,0:T(8,128)(2,1)S(1)} %reshape.242), channel_id=1, replica_groups=mesh['groups'=2,'freq'=4,'recv'=4] {'freq'}, dimensions={1}, use_global_device_ids=true | all-gather | bytes 655360 | tf_op jit(solution)/shard_map/while/body/eval_jaxpr/all_gather | solution.py:99
  234.7 3.1 collective-permute-done.3
  237.8 7.3 %collective-permute-done.4 = bf16[2,8,8,512]{3,1,2,0:T(8,128)(2,1)S(1)} collective-permute-done((bf16[2,8,8,512]{3,1,2,0:T(8,128)(2,1)S(1)}, bf16[2,8,8,512]{3,1,2,0:T(8,128)(2,1)S(1)}, u32[]{:S(2)}, u32[]{:S(2)}) %collective-permute-start.4) | collective-permute-done | bytes 131104 | tf_op jit(solution)/shard_map/while/body/eval_jaxpr/ppermute | solution.py:40
  246.1 3.6 %fusion.112 = f32[8,16,128]{2,1,0:T(8,128)S(1)} fusion(bf16[8,128,2048]{2,1,0:T(8,128)(2,1)} %get-tuple-element.303, bf16[8,8,2048]{2,1,0:T(8,128)(2,1)S(1)} %bitcast.168, bf16[8,8,2048]{2,1,0:T(8,128)(2,1)S(1)} %bitcast.170), kind=kOutput, calls=%fused_computation.20.clone.1 | convolution fusion | flops 68157440 | bytes 4784128 | tf_op jit(solution)/shard_map/while/body/eval_jaxpr/fbs,frs->fbr/dot_general | solution.py:109
  257.8 2.0 collective-permute-done.8
  262.1 2.2 collective-permute-done.10
  267.7 3.0 fusion.104
  274.2 3.1 collective-permute-done
  277.3 7.6 %collective-permute-done.1 = bf16[2,8,8,512]{3,2,1,0:T(8,128)(2,1)S(1)} collective-permute-done((bf16[2,8,8,512]{3,2,1,0:T(8,128)(2,1)S(1)}, bf16[2,8,8,512]{3,2,1,0:T(8,128)(2,1)S(1)}, u32[]{:S(2)}, u32[]{:S(2)}) %collective-permute-start.1) | collective-permute-done | bytes 131104 | tf_op jit(solution)/shard_map/while/body/eval_jaxpr/ppermute | solution.py:40
  285.0 6.7 %all_gather.8 = bf16[2,32,4096]{2,1,0:T(8,128)(2,1)S(1)} all-gather(bf16[2,8,4096]{2,1,0:T(8,128)(2,1)S(1)} %reshape.242), channel_id=1, replica_groups=mesh['groups'=2,'freq'=4,'recv'=4] {'freq'}, dimensions={1}, use_global_device_ids=true | all-gather | bytes 655360 | tf_op jit(solution)/shard_map/while/body/eval_jaxpr/all_gather | solution.py:99
  297.8 3.3 collective-permute-done.3
  301.1 7.1 %collective-permute-done.4 = bf16[2,8,8,512]{3,1,2,0:T(8,128)(2,1)S(1)} collective-permute-done((bf16[2,8,8,512]{3,1,2,0:T(8,128)(2,1)S(1)}, bf16[2,8,8,512]{3,1,2,0:T(8,128)(2,1)S(1)}, u32[]{:S(2)}, u32[]{:S(2)}) %collective-permute-start.4) | collective-permute-done | bytes 131104 | tf_op jit(solution)/shard_map/while/body/eval_jaxpr/ppermute | solution.py:40
  309.2 3.6 %fusion.112 = f32[8,16,128]{2,1,0:T(8,128)S(1)} fusion(bf16[8,128,2048]{2,1,0:T(8,128)(2,1)} %get-tuple-element.303, bf16[8,8,2048]{2,1,0:T(8,128)(2,1)S(1)} %bitcast.168, bf16[8,8,2048]{2,1,0:T(8,128)(2,1)S(1)} %bitcast.170), kind=kOutput, calls=%fused_computation.20.clone.1 | convolution fusion | flops 68157440 | bytes 4784128 | tf_op jit(solution)/shard_map/while/body/eval_jaxpr/fbs,frs->fbr/dot_general | solution.py:109
  320.9 2.0 collective-permute-done.8
  325.0 2.3 collective-permute-done.10
  (326 shorter events, 118.1 us)
Async XLA Ops:
  14.8 9.0 %collective-permute-start = (bf16[2,8,8,512]{3,2,1,0:T(8,128)(2,1)S(1)}, bf16[2,8,8,512]{3,2,1,0:T(8,128)(2,1)S(1)}, u32[]{:S(2)}, u32[]{:S(2)}) collective-permute-start(bf16[2,8,8,512]{3,2,1,0:T(8,128)(2,1)S(1)} %get-tuple-element.253), channel_id=1, source_target_pairs={{0,3},{1,0},{2,1},{3,2},{4,7},{5,4},{6,5},{7,6},{8,11},{9,8},{10,9... | collective-permute-start | bytes 393224 | tf_op jit(solution)/shard_map/while/body/eval_jaxpr/ppermute | solution.py:40
  19.9 11.2 %collective-permute-start.1 = (bf16[2,8,8,512]{3,2,1,0:T(8,128)(2,1)S(1)}, bf16[2,8,8,512]{3,2,1,0:T(8,128)(2,1)S(1)}, u32[]{:S(2)}, u32[]{:S(2)}) collective-permute-start(bf16[2,8,8,512]{3,2,1,0:T(8,128)(2,1)S(1)} %get-tuple-element.254), channel_id=1, source_target_pairs={{0,2},{1,3},{2,0},{3,1},{4,6},{5,7},{6,4},{7,5},{8,10},{9,11},{10,... | collective-permute-start | bytes 393224 | tf_op jit(solution)/shard_map/while/body/eval_jaxpr/ppermute | solution.py:40
  19.9 11.2 %collective-permute-start.2 = (bf16[2,8,8,512]{3,2,1,0:T(8,128)(2,1)S(1)}, bf16[2,8,8,512]{3,2,1,0:T(8,128)(2,1)S(1)}, u32[]{:S(2)}, u32[]{:S(2)}) collective-permute-start(bf16[2,8,8,512]{3,2,1,0:T(8,128)(2,1)S(1)} %get-tuple-element.255), channel_id=1, source_target_pairs={{0,1},{1,2},{2,3},{3,0},{4,5},{5,6},{6,7},{7,4},{8,9},{9,10},{10,1... | collective-permute-start | bytes 393224 | tf_op jit(solution)/shard_map/while/body/eval_jaxpr/ppermute | solution.py:40
  41.1 5.7 %collective-permute-start.3 = (bf16[2,8,8,512]{3,1,2,0:T(8,128)(2,1)S(1)}, bf16[2,8,8,512]{3,1,2,0:T(8,128)(2,1)S(1)}, u32[]{:S(2)}, u32[]{:S(2)}) collective-permute-start(bf16[2,8,8,512]{3,1,2,0:T(8,128)(2,1)S(1)} %bitcast.178), channel_id=1, source_target_pairs={{0,3},{1,0},{2,1},{3,2},{4,7},{5,4},{6,5},{7,6},{8,11},{9,8},{10,9... | collective-permute-start | bytes 393224 | tf_op jit(solution)/shard_map/while/body/eval_jaxpr/ppermute | solution.py:40
  42.7 13.5 %collective-permute-start.4 = (bf16[2,8,8,512]{3,1,2,0:T(8,128)(2,1)S(1)}, bf16[2,8,8,512]{3,1,2,0:T(8,128)(2,1)S(1)}, u32[]{:S(2)}, u32[]{:S(2)}) collective-permute-start(bf16[2,8,8,512]{3,1,2,0:T(8,128)(2,1)S(1)} %bitcast.179), channel_id=1, source_target_pairs={{0,2},{1,3},{2,0},{3,1},{4,6},{5,7},{6,4},{7,5},{8,10},{9,11},{10,... | collective-permute-start | bytes 393224 | tf_op jit(solution)/shard_map/while/body/eval_jaxpr/ppermute | solution.py:40
  43.7 12.4 %collective-permute-start.5 = (bf16[2,8,8,512]{3,1,2,0:T(8,128)(2,1)S(1)}, bf16[2,8,8,512]{3,1,2,0:T(8,128)(2,1)S(1)}, u32[]{:S(2)}, u32[]{:S(2)}) collective-permute-start(bf16[2,8,8,512]{3,1,2,0:T(8,128)(2,1)S(1)} %bitcast.180), channel_id=1, source_target_pairs={{0,1},{1,2},{2,3},{3,0},{4,5},{5,6},{6,7},{7,4},{8,9},{9,10},{10,1... | collective-permute-start | bytes 393224 | tf_op jit(solution)/shard_map/while/body/eval_jaxpr/ppermute | solution.py:40
  64.0 5.0 %collective-permute-start.6 = (f32[1,2]{1,0:T(1,128)S(1)}, f32[1,2]{1,0:T(1,128)S(1)}, u32[]{:S(2)}, u32[]{:S(2)}) collective-permute-start(f32[1,2]{1,0:T(1,128)S(1)} %fusion.115), channel_id=1, source_target_pairs={{0,3},{1,0},{2,1},{3,2},{4,7},{5,4},{6,5},{7,6},{8,11},{9,8},{10,9... | collective-permute-start | bytes 32 | tf_op jit(solution)/shard_map/while/body/eval_jaxpr/ppermute | solution.py:40
  64.0 5.0 %collective-permute-start.7 = (f32[1,2]{1,0:T(1,128)S(1)}, f32[1,2]{1,0:T(1,128)S(1)}, u32[]{:S(2)}, u32[]{:S(2)}) collective-permute-start(f32[1,2]{1,0:T(1,128)S(1)} %fusion.115), channel_id=1, source_target_pairs={{0,2},{1,3},{2,0},{3,1},{4,6},{5,7},{6,4},{7,5},{8,10},{9,11},{10,... | collective-permute-start | bytes 32 | tf_op jit(solution)/shard_map/while/body/eval_jaxpr/ppermute | solution.py:40
  65.7 5.3 %collective-permute-start.8 = (f32[1,2]{1,0:T(1,128)S(1)}, f32[1,2]{1,0:T(1,128)S(1)}, u32[]{:S(2)}, u32[]{:S(2)}) collective-permute-start(f32[1,2]{1,0:T(1,128)S(1)} %fusion.115), channel_id=1, source_target_pairs={{0,1},{1,2},{2,3},{3,0},{4,5},{5,6},{6,7},{7,4},{8,9},{9,10},{10,1... | collective-permute-start | bytes 32 | tf_op jit(solution)/shard_map/while/body/eval_jaxpr/ppermute | solution.py:40
  71.9 3.6 %collective-permute-start.10 = (f32[1,2]{1,0:T(1,128)S(1)}, f32[1,2]{1,0:T(1,128)S(1)}, u32[]{:S(2)}, u32[]{:S(2)}) collective-permute-start(f32[1,2]{1,0:T(1,128)S(1)} %bitcast.188), channel_id=1, source_target_pairs={{0,8},{4,12},{8,0},{12,4},{1,9},{5,13},{9,1},{13,5},{2,10},{6,14},... | collective-permute-start | bytes 32 | tf_op jit(solution)/shard_map/while/body/eval_jaxpr/ppermute | solution.py:40
  82.9 5.3 %collective-permute-start = (bf16[2,8,8,512]{3,2,1,0:T(8,128)(2,1)S(1)}, bf16[2,8,8,512]{3,2,1,0:T(8,128)(2,1)S(1)}, u32[]{:S(2)}, u32[]{:S(2)}) collective-permute-start(bf16[2,8,8,512]{3,2,1,0:T(8,128)(2,1)S(1)} %get-tuple-element.253), channel_id=1, source_target_pairs={{0,3},{1,0},{2,1},{3,2},{4,7},{5,4},{6,5},{7,6},{8,11},{9,8},{10,9... | collective-permute-start | bytes 393224 | tf_op jit(solution)/shard_map/while/body/eval_jaxpr/ppermute | solution.py:40
  83.8 12.1 %collective-permute-start.1 = (bf16[2,8,8,512]{3,2,1,0:T(8,128)(2,1)S(1)}, bf16[2,8,8,512]{3,2,1,0:T(8,128)(2,1)S(1)}, u32[]{:S(2)}, u32[]{:S(2)}) collective-permute-start(bf16[2,8,8,512]{3,2,1,0:T(8,128)(2,1)S(1)} %get-tuple-element.254), channel_id=1, source_target_pairs={{0,2},{1,3},{2,0},{3,1},{4,6},{5,7},{6,4},{7,5},{8,10},{9,11},{10,... | collective-permute-start | bytes 393224 | tf_op jit(solution)/shard_map/while/body/eval_jaxpr/ppermute | solution.py:40
  84.5 11.4 %collective-permute-start.2 = (bf16[2,8,8,512]{3,2,1,0:T(8,128)(2,1)S(1)}, bf16[2,8,8,512]{3,2,1,0:T(8,128)(2,1)S(1)}, u32[]{:S(2)}, u32[]{:S(2)}) collective-permute-start(bf16[2,8,8,512]{3,2,1,0:T(8,128)(2,1)S(1)} %get-tuple-element.255), channel_id=1, source_target_pairs={{0,1},{1,2},{2,3},{3,0},{4,5},{5,6},{6,7},{7,4},{8,9},{9,10},{10,1... | collective-permute-start | bytes 393224 | tf_op jit(solution)/shard_map/while/body/eval_jaxpr/ppermute | solution.py:40
  105.2 6.6 %collective-permute-start.3 = (bf16[2,8,8,512]{3,1,2,0:T(8,128)(2,1)S(1)}, bf16[2,8,8,512]{3,1,2,0:T(8,128)(2,1)S(1)}, u32[]{:S(2)}, u32[]{:S(2)}) collective-permute-start(bf16[2,8,8,512]{3,1,2,0:T(8,128)(2,1)S(1)} %bitcast.178), channel_id=1, source_target_pairs={{0,3},{1,0},{2,1},{3,2},{4,7},{5,4},{6,5},{7,6},{8,11},{9,8},{10,9... | collective-permute-start | bytes 393224 | tf_op jit(solution)/shard_map/while/body/eval_jaxpr/ppermute | solution.py:40
  105.2 13.9 %collective-permute-start.4 = (bf16[2,8,8,512]{3,1,2,0:T(8,128)(2,1)S(1)}, bf16[2,8,8,512]{3,1,2,0:T(8,128)(2,1)S(1)}, u32[]{:S(2)}, u32[]{:S(2)}) collective-permute-start(bf16[2,8,8,512]{3,1,2,0:T(8,128)(2,1)S(1)} %bitcast.179), channel_id=1, source_target_pairs={{0,2},{1,3},{2,0},{3,1},{4,6},{5,7},{6,4},{7,5},{8,10},{9,11},{10,... | collective-permute-start | bytes 393224 | tf_op jit(solution)/shard_map/while/body/eval_jaxpr/ppermute | solution.py:40
  106.7 12.4 %collective-permute-start.5 = (bf16[2,8,8,512]{3,1,2,0:T(8,128)(2,1)S(1)}, bf16[2,8,8,512]{3,1,2,0:T(8,128)(2,1)S(1)}, u32[]{:S(2)}, u32[]{:S(2)}) collective-permute-start(bf16[2,8,8,512]{3,1,2,0:T(8,128)(2,1)S(1)} %bitcast.180), channel_id=1, source_target_pairs={{0,1},{1,2},{2,3},{3,0},{4,5},{5,6},{6,7},{7,4},{8,9},{9,10},{10,1... | collective-permute-start | bytes 393224 | tf_op jit(solution)/shard_map/while/body/eval_jaxpr/ppermute | solution.py:40
  126.9 4.8 %collective-permute-start.6 = (f32[1,2]{1,0:T(1,128)S(1)}, f32[1,2]{1,0:T(1,128)S(1)}, u32[]{:S(2)}, u32[]{:S(2)}) collective-permute-start(f32[1,2]{1,0:T(1,128)S(1)} %fusion.115), channel_id=1, source_target_pairs={{0,3},{1,0},{2,1},{3,2},{4,7},{5,4},{6,5},{7,6},{8,11},{9,8},{10,9... | collective-permute-start | bytes 32 | tf_op jit(solution)/shard_map/while/body/eval_jaxpr/ppermute | solution.py:40
  127.0 4.8 %collective-permute-start.7 = (f32[1,2]{1,0:T(1,128)S(1)}, f32[1,2]{1,0:T(1,128)S(1)}, u32[]{:S(2)}, u32[]{:S(2)}) collective-permute-start(f32[1,2]{1,0:T(1,128)S(1)} %fusion.115), channel_id=1, source_target_pairs={{0,2},{1,3},{2,0},{3,1},{4,6},{5,7},{6,4},{7,5},{8,10},{9,11},{10,... | collective-permute-start | bytes 32 | tf_op jit(solution)/shard_map/while/body/eval_jaxpr/ppermute | solution.py:40
  128.4 5.3 %collective-permute-start.8 = (f32[1,2]{1,0:T(1,128)S(1)}, f32[1,2]{1,0:T(1,128)S(1)}, u32[]{:S(2)}, u32[]{:S(2)}) collective-permute-start(f32[1,2]{1,0:T(1,128)S(1)} %fusion.115), channel_id=1, source_target_pairs={{0,1},{1,2},{2,3},{3,0},{4,5},{5,6},{6,7},{7,4},{8,9},{9,10},{10,1... | collective-permute-start | bytes 32 | tf_op jit(solution)/shard_map/while/body/eval_jaxpr/ppermute | solution.py:40
  146.0 5.3 %collective-permute-start = (bf16[2,8,8,512]{3,2,1,0:T(8,128)(2,1)S(1)}, bf16[2,8,8,512]{3,2,1,0:T(8,128)(2,1)S(1)}, u32[]{:S(2)}, u32[]{:S(2)}) collective-permute-start(bf16[2,8,8,512]{3,2,1,0:T(8,128)(2,1)S(1)} %get-tuple-element.253), channel_id=1, source_target_pairs={{0,3},{1,0},{2,1},{3,2},{4,7},{5,4},{6,5},{7,6},{8,11},{9,8},{10,9... | collective-permute-start | bytes 393224 | tf_op jit(solution)/shard_map/while/body/eval_jaxpr/ppermute | solution.py:40
  147.1 11.8 %collective-permute-start.1 = (bf16[2,8,8,512]{3,2,1,0:T(8,128)(2,1)S(1)}, bf16[2,8,8,512]{3,2,1,0:T(8,128)(2,1)S(1)}, u32[]{:S(2)}, u32[]{:S(2)}) collective-permute-start(bf16[2,8,8,512]{3,2,1,0:T(8,128)(2,1)S(1)} %get-tuple-element.254), channel_id=1, source_target_pairs={{0,2},{1,3},{2,0},{3,1},{4,6},{5,7},{6,4},{7,5},{8,10},{9,11},{10,... | collective-permute-start | bytes 393224 | tf_op jit(solution)/shard_map/while/body/eval_jaxpr/ppermute | solution.py:40
  147.7 11.2 %collective-permute-start.2 = (bf16[2,8,8,512]{3,2,1,0:T(8,128)(2,1)S(1)}, bf16[2,8,8,512]{3,2,1,0:T(8,128)(2,1)S(1)}, u32[]{:S(2)}, u32[]{:S(2)}) collective-permute-start(bf16[2,8,8,512]{3,2,1,0:T(8,128)(2,1)S(1)} %get-tuple-element.255), channel_id=1, source_target_pairs={{0,1},{1,2},{2,3},{3,0},{4,5},{5,6},{6,7},{7,4},{8,9},{9,10},{10,1... | collective-permute-start | bytes 393224 | tf_op jit(solution)/shard_map/while/body/eval_jaxpr/ppermute | solution.py:40
  168.3 6.7 %collective-permute-start.3 = (bf16[2,8,8,512]{3,1,2,0:T(8,128)(2,1)S(1)}, bf16[2,8,8,512]{3,1,2,0:T(8,128)(2,1)S(1)}, u32[]{:S(2)}, u32[]{:S(2)}) collective-permute-start(bf16[2,8,8,512]{3,1,2,0:T(8,128)(2,1)S(1)} %bitcast.178), channel_id=1, source_target_pairs={{0,3},{1,0},{2,1},{3,2},{4,7},{5,4},{6,5},{7,6},{8,11},{9,8},{10,9... | collective-permute-start | bytes 393224 | tf_op jit(solution)/shard_map/while/body/eval_jaxpr/ppermute | solution.py:40
  168.4 13.7 %collective-permute-start.4 = (bf16[2,8,8,512]{3,1,2,0:T(8,128)(2,1)S(1)}, bf16[2,8,8,512]{3,1,2,0:T(8,128)(2,1)S(1)}, u32[]{:S(2)}, u32[]{:S(2)}) collective-permute-start(bf16[2,8,8,512]{3,1,2,0:T(8,128)(2,1)S(1)} %bitcast.179), channel_id=1, source_target_pairs={{0,2},{1,3},{2,0},{3,1},{4,6},{5,7},{6,4},{7,5},{8,10},{9,11},{10,... | collective-permute-start | bytes 393224 | tf_op jit(solution)/shard_map/while/body/eval_jaxpr/ppermute | solution.py:40
  169.7 12.4 %collective-permute-start.5 = (bf16[2,8,8,512]{3,1,2,0:T(8,128)(2,1)S(1)}, bf16[2,8,8,512]{3,1,2,0:T(8,128)(2,1)S(1)}, u32[]{:S(2)}, u32[]{:S(2)}) collective-permute-start(bf16[2,8,8,512]{3,1,2,0:T(8,128)(2,1)S(1)} %bitcast.180), channel_id=1, source_target_pairs={{0,1},{1,2},{2,3},{3,0},{4,5},{5,6},{6,7},{7,4},{8,9},{9,10},{10,1... | collective-permute-start | bytes 393224 | tf_op jit(solution)/shard_map/while/body/eval_jaxpr/ppermute | solution.py:40
  190.0 4.9 %collective-permute-start.6 = (f32[1,2]{1,0:T(1,128)S(1)}, f32[1,2]{1,0:T(1,128)S(1)}, u32[]{:S(2)}, u32[]{:S(2)}) collective-permute-start(f32[1,2]{1,0:T(1,128)S(1)} %fusion.115), channel_id=1, source_target_pairs={{0,3},{1,0},{2,1},{3,2},{4,7},{5,4},{6,5},{7,6},{8,11},{9,8},{10,9... | collective-permute-start | bytes 32 | tf_op jit(solution)/shard_map/while/body/eval_jaxpr/ppermute | solution.py:40
  190.0 4.9 %collective-permute-start.7 = (f32[1,2]{1,0:T(1,128)S(1)}, f32[1,2]{1,0:T(1,128)S(1)}, u32[]{:S(2)}, u32[]{:S(2)}) collective-permute-start(f32[1,2]{1,0:T(1,128)S(1)} %fusion.115), channel_id=1, source_target_pairs={{0,2},{1,3},{2,0},{3,1},{4,6},{5,7},{6,4},{7,5},{8,10},{9,11},{10,... | collective-permute-start | bytes 32 | tf_op jit(solution)/shard_map/while/body/eval_jaxpr/ppermute | solution.py:40
  191.6 5.3 %collective-permute-start.8 = (f32[1,2]{1,0:T(1,128)S(1)}, f32[1,2]{1,0:T(1,128)S(1)}, u32[]{:S(2)}, u32[]{:S(2)}) collective-permute-start(f32[1,2]{1,0:T(1,128)S(1)} %fusion.115), channel_id=1, source_target_pairs={{0,1},{1,2},{2,3},{3,0},{4,5},{5,6},{6,7},{7,4},{8,9},{9,10},{10,1... | collective-permute-start | bytes 32 | tf_op jit(solution)/shard_map/while/body/eval_jaxpr/ppermute | solution.py:40
  197.7 3.6 %collective-permute-start.10 = (f32[1,2]{1,0:T(1,128)S(1)}, f32[1,2]{1,0:T(1,128)S(1)}, u32[]{:S(2)}, u32[]{:S(2)}) collective-permute-start(f32[1,2]{1,0:T(1,128)S(1)} %bitcast.188), channel_id=1, source_target_pairs={{0,8},{4,12},{8,0},{12,4},{1,9},{5,13},{9,1},{13,5},{2,10},{6,14},... | collective-permute-start | bytes 32 | tf_op jit(solution)/shard_map/while/body/eval_jaxpr/ppermute | solution.py:40
  209.0 5.2 %collective-permute-start = (bf16[2,8,8,512]{3,2,1,0:T(8,128)(2,1)S(1)}, bf16[2,8,8,512]{3,2,1,0:T(8,128)(2,1)S(1)}, u32[]{:S(2)}, u32[]{:S(2)}) collective-permute-start(bf16[2,8,8,512]{3,2,1,0:T(8,128)(2,1)S(1)} %get-tuple-element.253), channel_id=1, source_target_pairs={{0,3},{1,0},{2,1},{3,2},{4,7},{5,4},{6,5},{7,6},{8,11},{9,8},{10,9... | collective-permute-start | bytes 393224 | tf_op jit(solution)/shard_map/while/body/eval_jaxpr/ppermute | solution.py:40
  209.8 12.1 %collective-permute-start.1 = (bf16[2,8,8,512]{3,2,1,0:T(8,128)(2,1)S(1)}, bf16[2,8,8,512]{3,2,1,0:T(8,128)(2,1)S(1)}, u32[]{:S(2)}, u32[]{:S(2)}) collective-permute-start(bf16[2,8,8,512]{3,2,1,0:T(8,128)(2,1)S(1)} %get-tuple-element.254), channel_id=1, source_target_pairs={{0,2},{1,3},{2,0},{3,1},{4,6},{5,7},{6,4},{7,5},{8,10},{9,11},{10,... | collective-permute-start | bytes 393224 | tf_op jit(solution)/shard_map/while/body/eval_jaxpr/ppermute | solution.py:40
  210.6 11.3 %collective-permute-start.2 = (bf16[2,8,8,512]{3,2,1,0:T(8,128)(2,1)S(1)}, bf16[2,8,8,512]{3,2,1,0:T(8,128)(2,1)S(1)}, u32[]{:S(2)}, u32[]{:S(2)}) collective-permute-start(bf16[2,8,8,512]{3,2,1,0:T(8,128)(2,1)S(1)} %get-tuple-element.255), channel_id=1, source_target_pairs={{0,1},{1,2},{2,3},{3,0},{4,5},{5,6},{6,7},{7,4},{8,9},{9,10},{10,1... | collective-permute-start | bytes 393224 | tf_op jit(solution)/shard_map/while/body/eval_jaxpr/ppermute | solution.py:40
  231.2 6.6 %collective-permute-start.3 = (bf16[2,8,8,512]{3,1,2,0:T(8,128)(2,1)S(1)}, bf16[2,8,8,512]{3,1,2,0:T(8,128)(2,1)S(1)}, u32[]{:S(2)}, u32[]{:S(2)}) collective-permute-start(bf16[2,8,8,512]{3,1,2,0:T(8,128)(2,1)S(1)} %bitcast.178), channel_id=1, source_target_pairs={{0,3},{1,0},{2,1},{3,2},{4,7},{5,4},{6,5},{7,6},{8,11},{9,8},{10,9... | collective-permute-start | bytes 393224 | tf_op jit(solution)/shard_map/while/body/eval_jaxpr/ppermute | solution.py:40
  231.2 13.9 %collective-permute-start.4 = (bf16[2,8,8,512]{3,1,2,0:T(8,128)(2,1)S(1)}, bf16[2,8,8,512]{3,1,2,0:T(8,128)(2,1)S(1)}, u32[]{:S(2)}, u32[]{:S(2)}) collective-permute-start(bf16[2,8,8,512]{3,1,2,0:T(8,128)(2,1)S(1)} %bitcast.179), channel_id=1, source_target_pairs={{0,2},{1,3},{2,0},{3,1},{4,6},{5,7},{6,4},{7,5},{8,10},{9,11},{10,... | collective-permute-start | bytes 393224 | tf_op jit(solution)/shard_map/while/body/eval_jaxpr/ppermute | solution.py:40
  232.7 12.4 %collective-permute-start.5 = (bf16[2,8,8,512]{3,1,2,0:T(8,128)(2,1)S(1)}, bf16[2,8,8,512]{3,1,2,0:T(8,128)(2,1)S(1)}, u32[]{:S(2)}, u32[]{:S(2)}) collective-permute-start(bf16[2,8,8,512]{3,1,2,0:T(8,128)(2,1)S(1)} %bitcast.180), channel_id=1, source_target_pairs={{0,1},{1,2},{2,3},{3,0},{4,5},{5,6},{6,7},{7,4},{8,9},{9,10},{10,1... | collective-permute-start | bytes 393224 | tf_op jit(solution)/shard_map/while/body/eval_jaxpr/ppermute | solution.py:40
  252.9 4.8 %collective-permute-start.6 = (f32[1,2]{1,0:T(1,128)S(1)}, f32[1,2]{1,0:T(1,128)S(1)}, u32[]{:S(2)}, u32[]{:S(2)}) collective-permute-start(f32[1,2]{1,0:T(1,128)S(1)} %fusion.115), channel_id=1, source_target_pairs={{0,3},{1,0},{2,1},{3,2},{4,7},{5,4},{6,5},{7,6},{8,11},{9,8},{10,9... | collective-permute-start | bytes 32 | tf_op jit(solution)/shard_map/while/body/eval_jaxpr/ppermute | solution.py:40
  252.9 4.8 %collective-permute-start.7 = (f32[1,2]{1,0:T(1,128)S(1)}, f32[1,2]{1,0:T(1,128)S(1)}, u32[]{:S(2)}, u32[]{:S(2)}) collective-permute-start(f32[1,2]{1,0:T(1,128)S(1)} %fusion.115), channel_id=1, source_target_pairs={{0,2},{1,3},{2,0},{3,1},{4,6},{5,7},{6,4},{7,5},{8,10},{9,11},{10,... | collective-permute-start | bytes 32 | tf_op jit(solution)/shard_map/while/body/eval_jaxpr/ppermute | solution.py:40
  254.5 5.3 %collective-permute-start.8 = (f32[1,2]{1,0:T(1,128)S(1)}, f32[1,2]{1,0:T(1,128)S(1)}, u32[]{:S(2)}, u32[]{:S(2)}) collective-permute-start(f32[1,2]{1,0:T(1,128)S(1)} %fusion.115), channel_id=1, source_target_pairs={{0,1},{1,2},{2,3},{3,0},{4,5},{5,6},{6,7},{7,4},{8,9},{9,10},{10,1... | collective-permute-start | bytes 32 | tf_op jit(solution)/shard_map/while/body/eval_jaxpr/ppermute | solution.py:40
  260.6 3.6 %collective-permute-start.10 = (f32[1,2]{1,0:T(1,128)S(1)}, f32[1,2]{1,0:T(1,128)S(1)}, u32[]{:S(2)}, u32[]{:S(2)}) collective-permute-start(f32[1,2]{1,0:T(1,128)S(1)} %bitcast.188), channel_id=1, source_target_pairs={{0,8},{4,12},{8,0},{12,4},{1,9},{5,13},{9,1},{13,5},{2,10},{6,14},... | collective-permute-start | bytes 32 | tf_op jit(solution)/shard_map/while/body/eval_jaxpr/ppermute | solution.py:40
  272.0 5.3 %collective-permute-start = (bf16[2,8,8,512]{3,2,1,0:T(8,128)(2,1)S(1)}, bf16[2,8,8,512]{3,2,1,0:T(8,128)(2,1)S(1)}, u32[]{:S(2)}, u32[]{:S(2)}) collective-permute-start(bf16[2,8,8,512]{3,2,1,0:T(8,128)(2,1)S(1)} %get-tuple-element.253), channel_id=1, source_target_pairs={{0,3},{1,0},{2,1},{3,2},{4,7},{5,4},{6,5},{7,6},{8,11},{9,8},{10,9... | collective-permute-start | bytes 393224 | tf_op jit(solution)/shard_map/while/body/eval_jaxpr/ppermute | solution.py:40
  273.0 11.9 %collective-permute-start.1 = (bf16[2,8,8,512]{3,2,1,0:T(8,128)(2,1)S(1)}, bf16[2,8,8,512]{3,2,1,0:T(8,128)(2,1)S(1)}, u32[]{:S(2)}, u32[]{:S(2)}) collective-permute-start(bf16[2,8,8,512]{3,2,1,0:T(8,128)(2,1)S(1)} %get-tuple-element.254), channel_id=1, source_target_pairs={{0,2},{1,3},{2,0},{3,1},{4,6},{5,7},{6,4},{7,5},{8,10},{9,11},{10,... | collective-permute-start | bytes 393224 | tf_op jit(solution)/shard_map/while/body/eval_jaxpr/ppermute | solution.py:40
  273.7 11.2 %collective-permute-start.2 = (bf16[2,8,8,512]{3,2,1,0:T(8,128)(2,1)S(1)}, bf16[2,8,8,512]{3,2,1,0:T(8,128)(2,1)S(1)}, u32[]{:S(2)}, u32[]{:S(2)}) collective-permute-start(bf16[2,8,8,512]{3,2,1,0:T(8,128)(2,1)S(1)} %get-tuple-element.255), channel_id=1, source_target_pairs={{0,1},{1,2},{2,3},{3,0},{4,5},{5,6},{6,7},{7,4},{8,9},{9,10},{10,1... | collective-permute-start | bytes 393224 | tf_op jit(solution)/shard_map/while/body/eval_jaxpr/ppermute | solution.py:40
  294.3 6.7 %collective-permute-start.3 = (bf16[2,8,8,512]{3,1,2,0:T(8,128)(2,1)S(1)}, bf16[2,8,8,512]{3,1,2,0:T(8,128)(2,1)S(1)}, u32[]{:S(2)}, u32[]{:S(2)}) collective-permute-start(bf16[2,8,8,512]{3,1,2,0:T(8,128)(2,1)S(1)} %bitcast.178), channel_id=1, source_target_pairs={{0,3},{1,0},{2,1},{3,2},{4,7},{5,4},{6,5},{7,6},{8,11},{9,8},{10,9... | collective-permute-start | bytes 393224 | tf_op jit(solution)/shard_map/while/body/eval_jaxpr/ppermute | solution.py:40
  294.3 13.8 %collective-permute-start.4 = (bf16[2,8,8,512]{3,1,2,0:T(8,128)(2,1)S(1)}, bf16[2,8,8,512]{3,1,2,0:T(8,128)(2,1)S(1)}, u32[]{:S(2)}, u32[]{:S(2)}) collective-permute-start(bf16[2,8,8,512]{3,1,2,0:T(8,128)(2,1)S(1)} %bitcast.179), channel_id=1, source_target_pairs={{0,2},{1,3},{2,0},{3,1},{4,6},{5,7},{6,4},{7,5},{8,10},{9,11},{10,... | collective-permute-start | bytes 393224 | tf_op jit(solution)/shard_map/while/body/eval_jaxpr/ppermute | solution.py:40
  295.7 12.4 %collective-permute-start.5 = (bf16[2,8,8,512]{3,1,2,0:T(8,128)(2,1)S(1)}, bf16[2,8,8,512]{3,1,2,0:T(8,128)(2,1)S(1)}, u32[]{:S(2)}, u32[]{:S(2)}) collective-permute-start(bf16[2,8,8,512]{3,1,2,0:T(8,128)(2,1)S(1)} %bitcast.180), channel_id=1, source_target_pairs={{0,1},{1,2},{2,3},{3,0},{4,5},{5,6},{6,7},{7,4},{8,9},{9,10},{10,1... | collective-permute-start | bytes 393224 | tf_op jit(solution)/shard_map/while/body/eval_jaxpr/ppermute | solution.py:40
  316.0 4.9 %collective-permute-start.6 = (f32[1,2]{1,0:T(1,128)S(1)}, f32[1,2]{1,0:T(1,128)S(1)}, u32[]{:S(2)}, u32[]{:S(2)}) collective-permute-start(f32[1,2]{1,0:T(1,128)S(1)} %fusion.115), channel_id=1, source_target_pairs={{0,3},{1,0},{2,1},{3,2},{4,7},{5,4},{6,5},{7,6},{8,11},{9,8},{10,9... | collective-permute-start | bytes 32 | tf_op jit(solution)/shard_map/while/body/eval_jaxpr/ppermute | solution.py:40
  316.0 4.9 %collective-permute-start.7 = (f32[1,2]{1,0:T(1,128)S(1)}, f32[1,2]{1,0:T(1,128)S(1)}, u32[]{:S(2)}, u32[]{:S(2)}) collective-permute-start(f32[1,2]{1,0:T(1,128)S(1)} %fusion.115), channel_id=1, source_target_pairs={{0,2},{1,3},{2,0},{3,1},{4,6},{5,7},{6,4},{7,5},{8,10},{9,11},{10,... | collective-permute-start | bytes 32 | tf_op jit(solution)/shard_map/while/body/eval_jaxpr/ppermute | solution.py:40
  317.6 5.3 %collective-permute-start.8 = (f32[1,2]{1,0:T(1,128)S(1)}, f32[1,2]{1,0:T(1,128)S(1)}, u32[]{:S(2)}, u32[]{:S(2)}) collective-permute-start(f32[1,2]{1,0:T(1,128)S(1)} %fusion.115), channel_id=1, source_target_pairs={{0,1},{1,2},{2,3},{3,0},{4,5},{5,6},{6,7},{7,4},{8,9},{9,10},{10,1... | collective-permute-start | bytes 32 | tf_op jit(solution)/shard_map/while/body/eval_jaxpr/ppermute | solution.py:40
  (26 other events, 89.4 us)

commit v8 on v7

--- a/solution.py
+++ b/solution.py
@@ -60,6 +60,21 @@
     return ordered.reshape(block.shape[:dim] + (size * block.shape[dim],) + block.shape[dim + 1 :])
 
 
+def gather_pairs(block, axis, dim):
+    size = lax.axis_size(axis)
+    me = lax.axis_index(axis)
+    partner = lax.ppermute(block, axis, [(i, i ^ 1) for i in range(size)])
+    first = me % 2 == 0
+    pair = jnp.concatenate(
+        [jnp.where(first, block, partner), jnp.where(first, partner, block)], axis=dim
+    )
+    pairs = size // 2
+    slots = jnp.stack([pair] + [shifted(pair, axis, 2 * d) for d in range(1, pairs)], axis=dim)
+    order = (me // 2 - jnp.arange(pairs, dtype=jnp.int32)) % pairs
+    ordered = jnp.take(slots, order, axis=dim)
+    return ordered.reshape(block.shape[:dim] + (size * block.shape[dim],) + block.shape[dim + 1 :])
+
+
 def on_device(operator, recorded, win_start, win_end):
     freq_local = operator.shape[1]
     sources = operator.shape[3]
@@ -96,7 +111,7 @@
             jnp.stack([partial_real, partial_imag]).astype(jnp.bfloat16), "recv", 3
         )
         flattened = gradient.astype(jnp.bfloat16).reshape(2, freq_local, columns)
-        segment = lax.all_gather(flattened, "freq", axis=1, tiled=True).astype(jnp.float32)
+        segment = gather_pairs(flattened, "freq", 1).astype(jnp.float32)
         timed = high_dot(to_time, segment.reshape(2 * total_freq, columns))
         projected = high_dot(to_freq, timed * window)
         direction = projected.reshape(2, freq_local, right_sides, src_local)

time: 332 us -> 340 us (1.024)
  waiting for transfers between devices: 129 us -> 164 us
  blocking collectives: 33.5 us -> 0 us
  starting transfers between devices: 57.3 us -> 65 us
  matrix products: 55.1 us -> 49 us
  local copies, waits for them, and re-layouts: 23 us -> 26.9 us
    all_gather x5 -> x0, blocking collectives: 33.5 us -> none  [step(): lax.all_gather(flattened, 'freq', axis=1, tiled=True).astype(jnp.float32)]
    ppermute x60 -> x65, waiting for transfers between devices: 129 us -> 158 us  [shifted(): lax.ppermute(value, axis, [(i, (i + distance) % size) for i in range(size)])]
    ppermute x60 -> x65, starting transfers between devices: 57.3 us -> 64.6 us  [shifted(): lax.ppermute(value, axis, [(i, (i + distance) % size) for i in range(size)])]
    ppermute x0 -> x5, waiting for transfers between devices: none -> 6.47 us  [gather_pairs(): partner = lax.ppermute(block, axis, [(i, i ^ 1) for i in range(size)])]
    dot_general x10, matrix products: 13.1 us -> 6.97 us  [high_dot(): return jnp.dot(left, right, precision=lax.Precision.HIGH)]
  transfers between devices with their start and end apart: 60 -> 70, of which waited for: 36 -> 45; matrix products, arithmetic and copies ran while one was open for 2% -> 2% of each run, Pallas kernels for 0% -> 0%
where the time goes in v8:
time: 340 us
  waiting for transfers between devices  164 us (48%)
  starting transfers between devices  65 us (19%)
  matrix products  49 us (14%)
  local copies, waits for them, and re-layouts  26.9 us (8%)
  other arithmetic  25.8 us (8%)
  loops' own time  8.06 us (2%)
    ppermute x65, waiting for transfers between devices, shifted(): lax.ppermute(value, axis, [(i, (i + distance) % size) for i in range(size)])  158 us
    ppermute x65, starting transfers between devices, shifted(): lax.ppermute(value, axis, [(i, (i + distance) % size) for i in range(size)])  64.6 us
    dot_general x5, matrix products, step(): jnp.einsum('fbs,frs->fbr', stacked_direction, imag_operator, preferred_el...  17.8 us
    dot_general x5, matrix products, step(): jnp.einsum('fbr,frs->fbs', stacked_residual, imag_operator, preferred_ele...  15 us
    gather x25, local copies, waits for them, and re-layouts, gather_blocks(): ordered = jnp.take(slots, order, axis=dim)  9.43 us
    another operation x1, loops' own time, on_device(): return lax.fori_loop(0, ITERS, step, (reflect, recorded))  8.06 us
    dot_general x10, matrix products, high_dot(): return jnp.dot(left, right, precision=lax.Precision.HIGH)  6.97 us
  transfers between devices with their start and end apart: 70, of which 45 were waited for; matrix products, arithmetic and copies ran while one was open for 2% of the time, Pallas kernels for 0%

profile of v8, /device:TPU:0, one launch (start us, length us, event | category | flops | bytes accessed | tf_op | source)
XLA Modules:
  0.0 339.8 jit_solution(6370282959182434817)
XLA Ops:
  0.7 6.1 %slice_bitcast_fusion.2 = (bf16[8,128,2048]{2,1,0:T(8,128)(2,1)}, bf16[8,128,2048]{2,1,0:T(8,128)(2,1)}) fusion(bf16[2,8,128,2048]{3,2,1,0:T(8,128)(2,1)} %param.8), kind=kLoop, calls=%fused_computation.103 | loop fusion | bytes 16777216 | tf_op jit(solution)/shard_map/squeeze | solution.py:86
  10.5 328.4 %while.16 = (s32[]{:T(128)}, f32[2,8,8,512]{3,1,2,0:T(8,128)S(1)}, f32[2,8,8,128]{3,2,1,0:T(8,128)S(1)}, bf16[8,128,2048]{2,1,0:T(8,128)(2,1)}, bf16[8,128,2048]...) while((s32[]{:T(128)}, f32[2,8,8,512]{3,1,2,0:T(8,128)S(1)}, ...), condition=%wide.region_7.9_spmd.clone, body=%wide.region_2.8_spmd.clone.sunk | while | flops 400822752 | bytes 84220656 | solution.py:137
  10.5 3.0 fusion.110
  14.8 5.1 %collective-permute-start = (bf16[2,8,8,512]{3,2,1,0:T(8,128)(2,1)S(1)}, bf16[2,8,8,512]{3,2,1,0:T(8,128)(2,1)S(1)}, u32[]{:S(2)}, u32[]{:S(2)}) collective-permute-start(bf16[2,8,8,512]{3,2,1,0:T(8,128)(2,1)S(1)} %get-tuple-element.298), channel_id=1, source_target_pairs={{0,3},{1,0},{2,1},{3,2},{4,7},{5,4},{6,5},{7,6},{8,11},{9,8},{10,9... | collective-permute-start | bytes 393224 | tf_op jit(solution)/shard_map/while/body/eval_jaxpr/ppermute | solution.py:40
  21.0 2.8 collective-permute-done
  23.8 7.3 %collective-permute-done.1 = bf16[2,8,8,512]{3,2,1,0:T(8,128)(2,1)S(1)} collective-permute-done((bf16[2,8,8,512]{3,2,1,0:T(8,128)(2,1)S(1)}, bf16[2,8,8,512]{3,2,1,0:T(8,128)(2,1)S(1)}, u32[]{:S(2)}, u32[]{:S(2)}) %collective-permute-start.1) | collective-permute-done | bytes 131104 | tf_op jit(solution)/shard_map/while/body/eval_jaxpr/ppermute | solution.py:40
  34.5 6.7 %collective-permute-done.4 = bf16[2,16,4096]{2,1,0:T(8,128)(2,1)S(1)} collective-permute-done((bf16[2,16,4096]{2,1,0:T(8,128)(2,1)S(1)}, bf16[2,16,4096]{2,1,0:T(8,128)(2,1)S(1)}, u32[]{:S(2)}, u32[]{:S(2)}) %collective-permute-start.4) | collective-permute-done | bytes 262176 | tf_op jit(solution)/shard_map/while/body/eval_jaxpr/ppermute | solution.py:40
  46.0 2.0 collective-permute-start.7
  49.0 8.4 %collective-permute-done.6 = bf16[2,8,8,512]{3,1,2,0:T(8,128)(2,1)S(1)} collective-permute-done((bf16[2,8,8,512]{3,1,2,0:T(8,128)(2,1)S(1)}, bf16[2,8,8,512]{3,1,2,0:T(8,128)(2,1)S(1)}, u32[]{:S(2)}, u32[]{:S(2)}) %collective-permute-start.6) | collective-permute-done | bytes 131104 | tf_op jit(solution)/shard_map/while/body/eval_jaxpr/ppermute | solution.py:40
  58.5 3.6 %fusion.120 = f32[8,16,128]{2,1,0:T(8,128)S(1)} fusion(bf16[8,128,2048]{2,1,0:T(8,128)(2,1)} %get-tuple-element.354, bf16[8,8,2048]{2,1,0:T(8,128)(2,1)S(1)} %bitcast.185, bf16[8,8,2048]{2,1,0:T(8,128)(2,1)S(1)} %bitcast.187), kind=kOutput, calls=%fused_computation.23.clone.1 | convolution fusion | flops 68157440 | bytes 4784128 | tf_op jit(solution)/shard_map/while/body/eval_jaxpr/fbs,frs->fbr/dot_general | solution.py:124
  70.2 2.0 collective-permute-done.10
  80.5 3.0 fusion.110
  86.9 3.2 collective-permute-done
  90.1 7.0 %collective-permute-done.1 = bf16[2,8,8,512]{3,2,1,0:T(8,128)(2,1)S(1)} collective-permute-done((bf16[2,8,8,512]{3,2,1,0:T(8,128)(2,1)S(1)}, bf16[2,8,8,512]{3,2,1,0:T(8,128)(2,1)S(1)}, u32[]{:S(2)}, u32[]{:S(2)}) %collective-permute-start.1) | collective-permute-done | bytes 131104 | tf_op jit(solution)/shard_map/while/body/eval_jaxpr/ppermute | solution.py:40
  100.3 6.9 %collective-permute-done.4 = bf16[2,16,4096]{2,1,0:T(8,128)(2,1)S(1)} collective-permute-done((bf16[2,16,4096]{2,1,0:T(8,128)(2,1)S(1)}, bf16[2,16,4096]{2,1,0:T(8,128)(2,1)S(1)}, u32[]{:S(2)}, u32[]{:S(2)}) %collective-permute-start.4) | collective-permute-done | bytes 262176 | tf_op jit(solution)/shard_map/while/body/eval_jaxpr/ppermute | solution.py:40
  110.8 2.0 collective-permute-start.7
  112.8 2.2 collective-permute-done.5
  115.0 7.1 %collective-permute-done.6 = bf16[2,8,8,512]{3,1,2,0:T(8,128)(2,1)S(1)} collective-permute-done((bf16[2,8,8,512]{3,1,2,0:T(8,128)(2,1)S(1)}, bf16[2,8,8,512]{3,1,2,0:T(8,128)(2,1)S(1)}, u32[]{:S(2)}, u32[]{:S(2)}) %collective-permute-start.6) | collective-permute-done | bytes 131104 | tf_op jit(solution)/shard_map/while/body/eval_jaxpr/ppermute | solution.py:40
  123.2 3.6 %fusion.120 = f32[8,16,128]{2,1,0:T(8,128)S(1)} fusion(bf16[8,128,2048]{2,1,0:T(8,128)(2,1)} %get-tuple-element.354, bf16[8,8,2048]{2,1,0:T(8,128)(2,1)S(1)} %bitcast.185, bf16[8,8,2048]{2,1,0:T(8,128)(2,1)S(1)} %bitcast.187), kind=kOutput, calls=%fused_computation.23.clone.1 | convolution fusion | flops 68157440 | bytes 4784128 | tf_op jit(solution)/shard_map/while/body/eval_jaxpr/fbs,frs->fbr/dot_general | solution.py:124
  134.9 2.0 collective-permute-done.10
  139.2 2.2 collective-permute-done.12
  144.9 3.0 fusion.110
  151.3 3.3 collective-permute-done
  154.6 7.3 %collective-permute-done.1 = bf16[2,8,8,512]{3,2,1,0:T(8,128)(2,1)S(1)} collective-permute-done((bf16[2,8,8,512]{3,2,1,0:T(8,128)(2,1)S(1)}, bf16[2,8,8,512]{3,2,1,0:T(8,128)(2,1)S(1)}, u32[]{:S(2)}, u32[]{:S(2)}) %collective-permute-start.1) | collective-permute-done | bytes 131104 | tf_op jit(solution)/shard_map/while/body/eval_jaxpr/ppermute | solution.py:40
  164.9 7.0 %collective-permute-done.4 = bf16[2,16,4096]{2,1,0:T(8,128)(2,1)S(1)} collective-permute-done((bf16[2,16,4096]{2,1,0:T(8,128)(2,1)S(1)}, bf16[2,16,4096]{2,1,0:T(8,128)(2,1)S(1)}, u32[]{:S(2)}, u32[]{:S(2)}) %collective-permute-start.4) | collective-permute-done | bytes 262176 | tf_op jit(solution)/shard_map/while/body/eval_jaxpr/ppermute | solution.py:40
  177.5 2.3 collective-permute-done.5
  179.8 7.1 %collective-permute-done.6 = bf16[2,8,8,512]{3,1,2,0:T(8,128)(2,1)S(1)} collective-permute-done((bf16[2,8,8,512]{3,1,2,0:T(8,128)(2,1)S(1)}, bf16[2,8,8,512]{3,1,2,0:T(8,128)(2,1)S(1)}, u32[]{:S(2)}, u32[]{:S(2)}) %collective-permute-start.6) | collective-permute-done | bytes 131104 | tf_op jit(solution)/shard_map/while/body/eval_jaxpr/ppermute | solution.py:40
  187.9 3.6 %fusion.120 = f32[8,16,128]{2,1,0:T(8,128)S(1)} fusion(bf16[8,128,2048]{2,1,0:T(8,128)(2,1)} %get-tuple-element.354, bf16[8,8,2048]{2,1,0:T(8,128)(2,1)S(1)} %bitcast.185, bf16[8,8,2048]{2,1,0:T(8,128)(2,1)S(1)} %bitcast.187), kind=kOutput, calls=%fused_computation.23.clone.1 | convolution fusion | flops 68157440 | bytes 4784128 | tf_op jit(solution)/shard_map/while/body/eval_jaxpr/fbs,frs->fbr/dot_general | solution.py:124
  199.6 2.0 collective-permute-done.10
  203.9 2.2 collective-permute-done.12
  209.6 3.0 fusion.110
  216.0 3.1 collective-permute-done
  219.1 7.5 %collective-permute-done.1 = bf16[2,8,8,512]{3,2,1,0:T(8,128)(2,1)S(1)} collective-permute-done((bf16[2,8,8,512]{3,2,1,0:T(8,128)(2,1)S(1)}, bf16[2,8,8,512]{3,2,1,0:T(8,128)(2,1)S(1)}, u32[]{:S(2)}, u32[]{:S(2)}) %collective-permute-start.1) | collective-permute-done | bytes 131104 | tf_op jit(solution)/shard_map/while/body/eval_jaxpr/ppermute | solution.py:40
  229.7 7.0 %collective-permute-done.4 = bf16[2,16,4096]{2,1,0:T(8,128)(2,1)S(1)} collective-permute-done((bf16[2,16,4096]{2,1,0:T(8,128)(2,1)S(1)}, bf16[2,16,4096]{2,1,0:T(8,128)(2,1)S(1)}, u32[]{:S(2)}, u32[]{:S(2)}) %collective-permute-start.4) | collective-permute-done | bytes 262176 | tf_op jit(solution)/shard_map/while/body/eval_jaxpr/ppermute | solution.py:40
  242.3 2.2 collective-permute-done.5
  244.5 7.1 %collective-permute-done.6 = bf16[2,8,8,512]{3,1,2,0:T(8,128)(2,1)S(1)} collective-permute-done((bf16[2,8,8,512]{3,1,2,0:T(8,128)(2,1)S(1)}, bf16[2,8,8,512]{3,1,2,0:T(8,128)(2,1)S(1)}, u32[]{:S(2)}, u32[]{:S(2)}) %collective-permute-start.6) | collective-permute-done | bytes 131104 | tf_op jit(solution)/shard_map/while/body/eval_jaxpr/ppermute | solution.py:40
  252.6 3.6 %fusion.120 = f32[8,16,128]{2,1,0:T(8,128)S(1)} fusion(bf16[8,128,2048]{2,1,0:T(8,128)(2,1)} %get-tuple-element.354, bf16[8,8,2048]{2,1,0:T(8,128)(2,1)S(1)} %bitcast.185, bf16[8,8,2048]{2,1,0:T(8,128)(2,1)S(1)} %bitcast.187), kind=kOutput, calls=%fused_computation.23.clone.1 | convolution fusion | flops 68157440 | bytes 4784128 | tf_op jit(solution)/shard_map/while/body/eval_jaxpr/fbs,frs->fbr/dot_general | solution.py:124
  264.3 2.0 collective-permute-done.10
  268.6 2.2 collective-permute-done.12
  274.3 3.0 fusion.110
  280.7 3.1 collective-permute-done
  283.8 7.5 %collective-permute-done.1 = bf16[2,8,8,512]{3,2,1,0:T(8,128)(2,1)S(1)} collective-permute-done((bf16[2,8,8,512]{3,2,1,0:T(8,128)(2,1)S(1)}, bf16[2,8,8,512]{3,2,1,0:T(8,128)(2,1)S(1)}, u32[]{:S(2)}, u32[]{:S(2)}) %collective-permute-start.1) | collective-permute-done | bytes 131104 | tf_op jit(solution)/shard_map/while/body/eval_jaxpr/ppermute | solution.py:40
  294.4 7.0 %collective-permute-done.4 = bf16[2,16,4096]{2,1,0:T(8,128)(2,1)S(1)} collective-permute-done((bf16[2,16,4096]{2,1,0:T(8,128)(2,1)S(1)}, bf16[2,16,4096]{2,1,0:T(8,128)(2,1)S(1)}, u32[]{:S(2)}, u32[]{:S(2)}) %collective-permute-start.4) | collective-permute-done | bytes 262176 | tf_op jit(solution)/shard_map/while/body/eval_jaxpr/ppermute | solution.py:40
  307.0 2.3 collective-permute-done.5
  309.2 7.1 %collective-permute-done.6 = bf16[2,8,8,512]{3,1,2,0:T(8,128)(2,1)S(1)} collective-permute-done((bf16[2,8,8,512]{3,1,2,0:T(8,128)(2,1)S(1)}, bf16[2,8,8,512]{3,1,2,0:T(8,128)(2,1)S(1)}, u32[]{:S(2)}, u32[]{:S(2)}) %collective-permute-start.6) | collective-permute-done | bytes 131104 | tf_op jit(solution)/shard_map/while/body/eval_jaxpr/ppermute | solution.py:40
  317.3 3.6 %fusion.120 = f32[8,16,128]{2,1,0:T(8,128)S(1)} fusion(bf16[8,128,2048]{2,1,0:T(8,128)(2,1)} %get-tuple-element.354, bf16[8,8,2048]{2,1,0:T(8,128)(2,1)S(1)} %bitcast.185, bf16[8,8,2048]{2,1,0:T(8,128)(2,1)S(1)} %bitcast.187), kind=kOutput, calls=%fused_computation.23.clone.1 | convolution fusion | flops 68157440 | bytes 4784128 | tf_op jit(solution)/shard_map/while/body/eval_jaxpr/fbs,frs->fbr/dot_general | solution.py:124
  329.1 2.0 collective-permute-done.10
  333.3 2.2 collective-permute-done.12
  (406 shorter events, 131.3 us)
Async XLA Ops:
  14.8 9.0 %collective-permute-start = (bf16[2,8,8,512]{3,2,1,0:T(8,128)(2,1)S(1)}, bf16[2,8,8,512]{3,2,1,0:T(8,128)(2,1)S(1)}, u32[]{:S(2)}, u32[]{:S(2)}) collective-permute-start(bf16[2,8,8,512]{3,2,1,0:T(8,128)(2,1)S(1)} %get-tuple-element.298), channel_id=1, source_target_pairs={{0,3},{1,0},{2,1},{3,2},{4,7},{5,4},{6,5},{7,6},{8,11},{9,8},{10,9... | collective-permute-start | bytes 393224 | tf_op jit(solution)/shard_map/while/body/eval_jaxpr/ppermute | solution.py:40
  19.9 11.2 %collective-permute-start.1 = (bf16[2,8,8,512]{3,2,1,0:T(8,128)(2,1)S(1)}, bf16[2,8,8,512]{3,2,1,0:T(8,128)(2,1)S(1)}, u32[]{:S(2)}, u32[]{:S(2)}) collective-permute-start(bf16[2,8,8,512]{3,2,1,0:T(8,128)(2,1)S(1)} %get-tuple-element.299), channel_id=1, source_target_pairs={{0,2},{1,3},{2,0},{3,1},{4,6},{5,7},{6,4},{7,5},{8,10},{9,11},{10,... | collective-permute-start | bytes 393224 | tf_op jit(solution)/shard_map/while/body/eval_jaxpr/ppermute | solution.py:40
  19.9 11.2 %collective-permute-start.2 = (bf16[2,8,8,512]{3,2,1,0:T(8,128)(2,1)S(1)}, bf16[2,8,8,512]{3,2,1,0:T(8,128)(2,1)S(1)}, u32[]{:S(2)}, u32[]{:S(2)}) collective-permute-start(bf16[2,8,8,512]{3,2,1,0:T(8,128)(2,1)S(1)} %get-tuple-element.300), channel_id=1, source_target_pairs={{0,1},{1,2},{2,3},{3,0},{4,5},{5,6},{6,7},{7,4},{8,9},{9,10},{10,1... | collective-permute-start | bytes 393224 | tf_op jit(solution)/shard_map/while/body/eval_jaxpr/ppermute | solution.py:40
  32.8 8.4 %collective-permute-start.4 = (bf16[2,16,4096]{2,1,0:T(8,128)(2,1)S(1)}, bf16[2,16,4096]{2,1,0:T(8,128)(2,1)S(1)}, u32[]{:S(2)}, u32[]{:S(2)}) collective-permute-start(bf16[2,16,4096]{2,1,0:T(8,128)(2,1)S(1)} %get-tuple-element.303), channel_id=1, source_target_pairs={{0,8},{4,12},{8,0},{12,4},{1,9},{5,13},{9,1},{13,5},{2,10},{6,14},... | collective-permute-start | bytes 786440 | tf_op jit(solution)/shard_map/while/body/eval_jaxpr/ppermute | solution.py:40
  43.4 5.6 %collective-permute-start.5 = (bf16[2,8,8,512]{3,1,2,0:T(8,128)(2,1)S(1)}, bf16[2,8,8,512]{3,1,2,0:T(8,128)(2,1)S(1)}, u32[]{:S(2)}, u32[]{:S(2)}) collective-permute-start(bf16[2,8,8,512]{3,1,2,0:T(8,128)(2,1)S(1)} %bitcast.195), channel_id=1, source_target_pairs={{0,3},{1,0},{2,1},{3,2},{4,7},{5,4},{6,5},{7,6},{8,11},{9,8},{10,9... | collective-permute-start | bytes 393224 | tf_op jit(solution)/shard_map/while/body/eval_jaxpr/ppermute | solution.py:40
  45.0 12.4 %collective-permute-start.6 = (bf16[2,8,8,512]{3,1,2,0:T(8,128)(2,1)S(1)}, bf16[2,8,8,512]{3,1,2,0:T(8,128)(2,1)S(1)}, u32[]{:S(2)}, u32[]{:S(2)}) collective-permute-start(bf16[2,8,8,512]{3,1,2,0:T(8,128)(2,1)S(1)} %bitcast.196), channel_id=1, source_target_pairs={{0,2},{1,3},{2,0},{3,1},{4,6},{5,7},{6,4},{7,5},{8,10},{9,11},{10,... | collective-permute-start | bytes 393224 | tf_op jit(solution)/shard_map/while/body/eval_jaxpr/ppermute | solution.py:40
  46.0 11.4 %collective-permute-start.7 = (bf16[2,8,8,512]{3,1,2,0:T(8,128)(2,1)S(1)}, bf16[2,8,8,512]{3,1,2,0:T(8,128)(2,1)S(1)}, u32[]{:S(2)}, u32[]{:S(2)}) collective-permute-start(bf16[2,8,8,512]{3,1,2,0:T(8,128)(2,1)S(1)} %bitcast.197), channel_id=1, source_target_pairs={{0,1},{1,2},{2,3},{3,0},{4,5},{5,6},{6,7},{7,4},{8,9},{9,10},{10,1... | collective-permute-start | bytes 393224 | tf_op jit(solution)/shard_map/while/body/eval_jaxpr/ppermute | solution.py:40
  65.2 5.0 %collective-permute-start.8 = (f32[1,2]{1,0:T(1,128)S(1)}, f32[1,2]{1,0:T(1,128)S(1)}, u32[]{:S(2)}, u32[]{:S(2)}) collective-permute-start(f32[1,2]{1,0:T(1,128)S(1)} %fusion.123), channel_id=1, source_target_pairs={{0,3},{1,0},{2,1},{3,2},{4,7},{5,4},{6,5},{7,6},{8,11},{9,8},{10,9... | collective-permute-start | bytes 32 | tf_op jit(solution)/shard_map/while/body/eval_jaxpr/ppermute | solution.py:40
  65.2 5.0 %collective-permute-start.9 = (f32[1,2]{1,0:T(1,128)S(1)}, f32[1,2]{1,0:T(1,128)S(1)}, u32[]{:S(2)}, u32[]{:S(2)}) collective-permute-start(f32[1,2]{1,0:T(1,128)S(1)} %fusion.123), channel_id=1, source_target_pairs={{0,2},{1,3},{2,0},{3,1},{4,6},{5,7},{6,4},{7,5},{8,10},{9,11},{10,... | collective-permute-start | bytes 32 | tf_op jit(solution)/shard_map/while/body/eval_jaxpr/ppermute | solution.py:40
  66.9 5.3 %collective-permute-start.10 = (f32[1,2]{1,0:T(1,128)S(1)}, f32[1,2]{1,0:T(1,128)S(1)}, u32[]{:S(2)}, u32[]{:S(2)}) collective-permute-start(f32[1,2]{1,0:T(1,128)S(1)} %fusion.123), channel_id=1, source_target_pairs={{0,1},{1,2},{2,3},{3,0},{4,5},{5,6},{6,7},{7,4},{8,9},{9,10},{10,1... | collective-permute-start | bytes 32 | tf_op jit(solution)/shard_map/while/body/eval_jaxpr/ppermute | solution.py:40
  84.7 5.4 %collective-permute-start = (bf16[2,8,8,512]{3,2,1,0:T(8,128)(2,1)S(1)}, bf16[2,8,8,512]{3,2,1,0:T(8,128)(2,1)S(1)}, u32[]{:S(2)}, u32[]{:S(2)}) collective-permute-start(bf16[2,8,8,512]{3,2,1,0:T(8,128)(2,1)S(1)} %get-tuple-element.298), channel_id=1, source_target_pairs={{0,3},{1,0},{2,1},{3,2},{4,7},{5,4},{6,5},{7,6},{8,11},{9,8},{10,9... | collective-permute-start | bytes 393224 | tf_op jit(solution)/shard_map/while/body/eval_jaxpr/ppermute | solution.py:40
  85.7 11.4 %collective-permute-start.1 = (bf16[2,8,8,512]{3,2,1,0:T(8,128)(2,1)S(1)}, bf16[2,8,8,512]{3,2,1,0:T(8,128)(2,1)S(1)}, u32[]{:S(2)}, u32[]{:S(2)}) collective-permute-start(bf16[2,8,8,512]{3,2,1,0:T(8,128)(2,1)S(1)} %get-tuple-element.299), channel_id=1, source_target_pairs={{0,2},{1,3},{2,0},{3,1},{4,6},{5,7},{6,4},{7,5},{8,10},{9,11},{10,... | collective-permute-start | bytes 393224 | tf_op jit(solution)/shard_map/while/body/eval_jaxpr/ppermute | solution.py:40
  86.4 10.7 %collective-permute-start.2 = (bf16[2,8,8,512]{3,2,1,0:T(8,128)(2,1)S(1)}, bf16[2,8,8,512]{3,2,1,0:T(8,128)(2,1)S(1)}, u32[]{:S(2)}, u32[]{:S(2)}) collective-permute-start(bf16[2,8,8,512]{3,2,1,0:T(8,128)(2,1)S(1)} %get-tuple-element.300), channel_id=1, source_target_pairs={{0,1},{1,2},{2,3},{3,0},{4,5},{5,6},{6,7},{7,4},{8,9},{9,10},{10,1... | collective-permute-start | bytes 393224 | tf_op jit(solution)/shard_map/while/body/eval_jaxpr/ppermute | solution.py:40
  98.8 8.4 %collective-permute-start.4 = (bf16[2,16,4096]{2,1,0:T(8,128)(2,1)S(1)}, bf16[2,16,4096]{2,1,0:T(8,128)(2,1)S(1)}, u32[]{:S(2)}, u32[]{:S(2)}) collective-permute-start(bf16[2,16,4096]{2,1,0:T(8,128)(2,1)S(1)} %get-tuple-element.303), channel_id=1, source_target_pairs={{0,8},{4,12},{8,0},{12,4},{1,9},{5,13},{9,1},{13,5},{2,10},{6,14},... | collective-permute-start | bytes 786440 | tf_op jit(solution)/shard_map/while/body/eval_jaxpr/ppermute | solution.py:40
  109.4 5.6 %collective-permute-start.5 = (bf16[2,8,8,512]{3,1,2,0:T(8,128)(2,1)S(1)}, bf16[2,8,8,512]{3,1,2,0:T(8,128)(2,1)S(1)}, u32[]{:S(2)}, u32[]{:S(2)}) collective-permute-start(bf16[2,8,8,512]{3,1,2,0:T(8,128)(2,1)S(1)} %bitcast.195), channel_id=1, source_target_pairs={{0,3},{1,0},{2,1},{3,2},{4,7},{5,4},{6,5},{7,6},{8,11},{9,8},{10,9... | collective-permute-start | bytes 393224 | tf_op jit(solution)/shard_map/while/body/eval_jaxpr/ppermute | solution.py:40
  109.4 12.7 %collective-permute-start.6 = (bf16[2,8,8,512]{3,1,2,0:T(8,128)(2,1)S(1)}, bf16[2,8,8,512]{3,1,2,0:T(8,128)(2,1)S(1)}, u32[]{:S(2)}, u32[]{:S(2)}) collective-permute-start(bf16[2,8,8,512]{3,1,2,0:T(8,128)(2,1)S(1)} %bitcast.196), channel_id=1, source_target_pairs={{0,2},{1,3},{2,0},{3,1},{4,6},{5,7},{6,4},{7,5},{8,10},{9,11},{10,... | collective-permute-start | bytes 393224 | tf_op jit(solution)/shard_map/while/body/eval_jaxpr/ppermute | solution.py:40
  110.8 11.4 %collective-permute-start.7 = (bf16[2,8,8,512]{3,1,2,0:T(8,128)(2,1)S(1)}, bf16[2,8,8,512]{3,1,2,0:T(8,128)(2,1)S(1)}, u32[]{:S(2)}, u32[]{:S(2)}) collective-permute-start(bf16[2,8,8,512]{3,1,2,0:T(8,128)(2,1)S(1)} %bitcast.197), channel_id=1, source_target_pairs={{0,1},{1,2},{2,3},{3,0},{4,5},{5,6},{6,7},{7,4},{8,9},{9,10},{10,1... | collective-permute-start | bytes 393224 | tf_op jit(solution)/shard_map/while/body/eval_jaxpr/ppermute | solution.py:40
  131.6 5.3 %collective-permute-start.10 = (f32[1,2]{1,0:T(1,128)S(1)}, f32[1,2]{1,0:T(1,128)S(1)}, u32[]{:S(2)}, u32[]{:S(2)}) collective-permute-start(f32[1,2]{1,0:T(1,128)S(1)} %fusion.123), channel_id=1, source_target_pairs={{0,1},{1,2},{2,3},{3,0},{4,5},{5,6},{6,7},{7,4},{8,9},{9,10},{10,1... | collective-permute-start | bytes 32 | tf_op jit(solution)/shard_map/while/body/eval_jaxpr/ppermute | solution.py:40
  149.2 5.4 %collective-permute-start = (bf16[2,8,8,512]{3,2,1,0:T(8,128)(2,1)S(1)}, bf16[2,8,8,512]{3,2,1,0:T(8,128)(2,1)S(1)}, u32[]{:S(2)}, u32[]{:S(2)}) collective-permute-start(bf16[2,8,8,512]{3,2,1,0:T(8,128)(2,1)S(1)} %get-tuple-element.298), channel_id=1, source_target_pairs={{0,3},{1,0},{2,1},{3,2},{4,7},{5,4},{6,5},{7,6},{8,11},{9,8},{10,9... | collective-permute-start | bytes 393224 | tf_op jit(solution)/shard_map/while/body/eval_jaxpr/ppermute | solution.py:40
  150.4 11.4 %collective-permute-start.1 = (bf16[2,8,8,512]{3,2,1,0:T(8,128)(2,1)S(1)}, bf16[2,8,8,512]{3,2,1,0:T(8,128)(2,1)S(1)}, u32[]{:S(2)}, u32[]{:S(2)}) collective-permute-start(bf16[2,8,8,512]{3,2,1,0:T(8,128)(2,1)S(1)} %get-tuple-element.299), channel_id=1, source_target_pairs={{0,2},{1,3},{2,0},{3,1},{4,6},{5,7},{6,4},{7,5},{8,10},{9,11},{10,... | collective-permute-start | bytes 393224 | tf_op jit(solution)/shard_map/while/body/eval_jaxpr/ppermute | solution.py:40
  150.8 11.0 %collective-permute-start.2 = (bf16[2,8,8,512]{3,2,1,0:T(8,128)(2,1)S(1)}, bf16[2,8,8,512]{3,2,1,0:T(8,128)(2,1)S(1)}, u32[]{:S(2)}, u32[]{:S(2)}) collective-permute-start(bf16[2,8,8,512]{3,2,1,0:T(8,128)(2,1)S(1)} %get-tuple-element.300), channel_id=1, source_target_pairs={{0,1},{1,2},{2,3},{3,0},{4,5},{5,6},{6,7},{7,4},{8,9},{9,10},{10,1... | collective-permute-start | bytes 393224 | tf_op jit(solution)/shard_map/while/body/eval_jaxpr/ppermute | solution.py:40
  163.5 8.4 %collective-permute-start.4 = (bf16[2,16,4096]{2,1,0:T(8,128)(2,1)S(1)}, bf16[2,16,4096]{2,1,0:T(8,128)(2,1)S(1)}, u32[]{:S(2)}, u32[]{:S(2)}) collective-permute-start(bf16[2,16,4096]{2,1,0:T(8,128)(2,1)S(1)} %get-tuple-element.303), channel_id=1, source_target_pairs={{0,8},{4,12},{8,0},{12,4},{1,9},{5,13},{9,1},{13,5},{2,10},{6,14},... | collective-permute-start | bytes 786440 | tf_op jit(solution)/shard_map/while/body/eval_jaxpr/ppermute | solution.py:40
  174.2 5.6 %collective-permute-start.5 = (bf16[2,8,8,512]{3,1,2,0:T(8,128)(2,1)S(1)}, bf16[2,8,8,512]{3,1,2,0:T(8,128)(2,1)S(1)}, u32[]{:S(2)}, u32[]{:S(2)}) collective-permute-start(bf16[2,8,8,512]{3,1,2,0:T(8,128)(2,1)S(1)} %bitcast.195), channel_id=1, source_target_pairs={{0,3},{1,0},{2,1},{3,2},{4,7},{5,4},{6,5},{7,6},{8,11},{9,8},{10,9... | collective-permute-start | bytes 393224 | tf_op jit(solution)/shard_map/while/body/eval_jaxpr/ppermute | solution.py:40
  174.2 12.7 %collective-permute-start.6 = (bf16[2,8,8,512]{3,1,2,0:T(8,128)(2,1)S(1)}, bf16[2,8,8,512]{3,1,2,0:T(8,128)(2,1)S(1)}, u32[]{:S(2)}, u32[]{:S(2)}) collective-permute-start(bf16[2,8,8,512]{3,1,2,0:T(8,128)(2,1)S(1)} %bitcast.196), channel_id=1, source_target_pairs={{0,2},{1,3},{2,0},{3,1},{4,6},{5,7},{6,4},{7,5},{8,10},{9,11},{10,... | collective-permute-start | bytes 393224 | tf_op jit(solution)/shard_map/while/body/eval_jaxpr/ppermute | solution.py:40
  175.5 11.4 %collective-permute-start.7 = (bf16[2,8,8,512]{3,1,2,0:T(8,128)(2,1)S(1)}, bf16[2,8,8,512]{3,1,2,0:T(8,128)(2,1)S(1)}, u32[]{:S(2)}, u32[]{:S(2)}) collective-permute-start(bf16[2,8,8,512]{3,1,2,0:T(8,128)(2,1)S(1)} %bitcast.197), channel_id=1, source_target_pairs={{0,1},{1,2},{2,3},{3,0},{4,5},{5,6},{6,7},{7,4},{8,9},{9,10},{10,1... | collective-permute-start | bytes 393224 | tf_op jit(solution)/shard_map/while/body/eval_jaxpr/ppermute | solution.py:40
  194.6 5.0 %collective-permute-start.8 = (f32[1,2]{1,0:T(1,128)S(1)}, f32[1,2]{1,0:T(1,128)S(1)}, u32[]{:S(2)}, u32[]{:S(2)}) collective-permute-start(f32[1,2]{1,0:T(1,128)S(1)} %fusion.123), channel_id=1, source_target_pairs={{0,3},{1,0},{2,1},{3,2},{4,7},{5,4},{6,5},{7,6},{8,11},{9,8},{10,9... | collective-permute-start | bytes 32 | tf_op jit(solution)/shard_map/while/body/eval_jaxpr/ppermute | solution.py:40
  194.7 5.0 %collective-permute-start.9 = (f32[1,2]{1,0:T(1,128)S(1)}, f32[1,2]{1,0:T(1,128)S(1)}, u32[]{:S(2)}, u32[]{:S(2)}) collective-permute-start(f32[1,2]{1,0:T(1,128)S(1)} %fusion.123), channel_id=1, source_target_pairs={{0,2},{1,3},{2,0},{3,1},{4,6},{5,7},{6,4},{7,5},{8,10},{9,11},{10,... | collective-permute-start | bytes 32 | tf_op jit(solution)/shard_map/while/body/eval_jaxpr/ppermute | solution.py:40
  196.3 5.3 %collective-permute-start.10 = (f32[1,2]{1,0:T(1,128)S(1)}, f32[1,2]{1,0:T(1,128)S(1)}, u32[]{:S(2)}, u32[]{:S(2)}) collective-permute-start(f32[1,2]{1,0:T(1,128)S(1)} %fusion.123), channel_id=1, source_target_pairs={{0,1},{1,2},{2,3},{3,0},{4,5},{5,6},{6,7},{7,4},{8,9},{9,10},{10,1... | collective-permute-start | bytes 32 | tf_op jit(solution)/shard_map/while/body/eval_jaxpr/ppermute | solution.py:40
  213.8 5.3 %collective-permute-start = (bf16[2,8,8,512]{3,2,1,0:T(8,128)(2,1)S(1)}, bf16[2,8,8,512]{3,2,1,0:T(8,128)(2,1)S(1)}, u32[]{:S(2)}, u32[]{:S(2)}) collective-permute-start(bf16[2,8,8,512]{3,2,1,0:T(8,128)(2,1)S(1)} %get-tuple-element.298), channel_id=1, source_target_pairs={{0,3},{1,0},{2,1},{3,2},{4,7},{5,4},{6,5},{7,6},{8,11},{9,8},{10,9... | collective-permute-start | bytes 393224 | tf_op jit(solution)/shard_map/while/body/eval_jaxpr/ppermute | solution.py:40
  214.9 11.7 %collective-permute-start.1 = (bf16[2,8,8,512]{3,2,1,0:T(8,128)(2,1)S(1)}, bf16[2,8,8,512]{3,2,1,0:T(8,128)(2,1)S(1)}, u32[]{:S(2)}, u32[]{:S(2)}) collective-permute-start(bf16[2,8,8,512]{3,2,1,0:T(8,128)(2,1)S(1)} %get-tuple-element.299), channel_id=1, source_target_pairs={{0,2},{1,3},{2,0},{3,1},{4,6},{5,7},{6,4},{7,5},{8,10},{9,11},{10,... | collective-permute-start | bytes 393224 | tf_op jit(solution)/shard_map/while/body/eval_jaxpr/ppermute | solution.py:40
  215.5 11.1 %collective-permute-start.2 = (bf16[2,8,8,512]{3,2,1,0:T(8,128)(2,1)S(1)}, bf16[2,8,8,512]{3,2,1,0:T(8,128)(2,1)S(1)}, u32[]{:S(2)}, u32[]{:S(2)}) collective-permute-start(bf16[2,8,8,512]{3,2,1,0:T(8,128)(2,1)S(1)} %get-tuple-element.300), channel_id=1, source_target_pairs={{0,1},{1,2},{2,3},{3,0},{4,5},{5,6},{6,7},{7,4},{8,9},{9,10},{10,1... | collective-permute-start | bytes 393224 | tf_op jit(solution)/shard_map/while/body/eval_jaxpr/ppermute | solution.py:40
  228.2 8.4 %collective-permute-start.4 = (bf16[2,16,4096]{2,1,0:T(8,128)(2,1)S(1)}, bf16[2,16,4096]{2,1,0:T(8,128)(2,1)S(1)}, u32[]{:S(2)}, u32[]{:S(2)}) collective-permute-start(bf16[2,16,4096]{2,1,0:T(8,128)(2,1)S(1)} %get-tuple-element.303), channel_id=1, source_target_pairs={{0,8},{4,12},{8,0},{12,4},{1,9},{5,13},{9,1},{13,5},{2,10},{6,14},... | collective-permute-start | bytes 786440 | tf_op jit(solution)/shard_map/while/body/eval_jaxpr/ppermute | solution.py:40
  238.9 5.6 %collective-permute-start.5 = (bf16[2,8,8,512]{3,1,2,0:T(8,128)(2,1)S(1)}, bf16[2,8,8,512]{3,1,2,0:T(8,128)(2,1)S(1)}, u32[]{:S(2)}, u32[]{:S(2)}) collective-permute-start(bf16[2,8,8,512]{3,1,2,0:T(8,128)(2,1)S(1)} %bitcast.195), channel_id=1, source_target_pairs={{0,3},{1,0},{2,1},{3,2},{4,7},{5,4},{6,5},{7,6},{8,11},{9,8},{10,9... | collective-permute-start | bytes 393224 | tf_op jit(solution)/shard_map/while/body/eval_jaxpr/ppermute | solution.py:40
  238.9 12.7 %collective-permute-start.6 = (bf16[2,8,8,512]{3,1,2,0:T(8,128)(2,1)S(1)}, bf16[2,8,8,512]{3,1,2,0:T(8,128)(2,1)S(1)}, u32[]{:S(2)}, u32[]{:S(2)}) collective-permute-start(bf16[2,8,8,512]{3,1,2,0:T(8,128)(2,1)S(1)} %bitcast.196), channel_id=1, source_target_pairs={{0,2},{1,3},{2,0},{3,1},{4,6},{5,7},{6,4},{7,5},{8,10},{9,11},{10,... | collective-permute-start | bytes 393224 | tf_op jit(solution)/shard_map/while/body/eval_jaxpr/ppermute | solution.py:40
  240.2 11.4 %collective-permute-start.7 = (bf16[2,8,8,512]{3,1,2,0:T(8,128)(2,1)S(1)}, bf16[2,8,8,512]{3,1,2,0:T(8,128)(2,1)S(1)}, u32[]{:S(2)}, u32[]{:S(2)}) collective-permute-start(bf16[2,8,8,512]{3,1,2,0:T(8,128)(2,1)S(1)} %bitcast.197), channel_id=1, source_target_pairs={{0,1},{1,2},{2,3},{3,0},{4,5},{5,6},{6,7},{7,4},{8,9},{9,10},{10,1... | collective-permute-start | bytes 393224 | tf_op jit(solution)/shard_map/while/body/eval_jaxpr/ppermute | solution.py:40
  259.4 5.0 %collective-permute-start.8 = (f32[1,2]{1,0:T(1,128)S(1)}, f32[1,2]{1,0:T(1,128)S(1)}, u32[]{:S(2)}, u32[]{:S(2)}) collective-permute-start(f32[1,2]{1,0:T(1,128)S(1)} %fusion.123), channel_id=1, source_target_pairs={{0,3},{1,0},{2,1},{3,2},{4,7},{5,4},{6,5},{7,6},{8,11},{9,8},{10,9... | collective-permute-start | bytes 32 | tf_op jit(solution)/shard_map/while/body/eval_jaxpr/ppermute | solution.py:40
  259.4 4.9 %collective-permute-start.9 = (f32[1,2]{1,0:T(1,128)S(1)}, f32[1,2]{1,0:T(1,128)S(1)}, u32[]{:S(2)}, u32[]{:S(2)}) collective-permute-start(f32[1,2]{1,0:T(1,128)S(1)} %fusion.123), channel_id=1, source_target_pairs={{0,2},{1,3},{2,0},{3,1},{4,6},{5,7},{6,4},{7,5},{8,10},{9,11},{10,... | collective-permute-start | bytes 32 | tf_op jit(solution)/shard_map/while/body/eval_jaxpr/ppermute | solution.py:40
  261.0 5.3 %collective-permute-start.10 = (f32[1,2]{1,0:T(1,128)S(1)}, f32[1,2]{1,0:T(1,128)S(1)}, u32[]{:S(2)}, u32[]{:S(2)}) collective-permute-start(f32[1,2]{1,0:T(1,128)S(1)} %fusion.123), channel_id=1, source_target_pairs={{0,1},{1,2},{2,3},{3,0},{4,5},{5,6},{6,7},{7,4},{8,9},{9,10},{10,1... | collective-permute-start | bytes 32 | tf_op jit(solution)/shard_map/while/body/eval_jaxpr/ppermute | solution.py:40
  278.6 5.3 %collective-permute-start = (bf16[2,8,8,512]{3,2,1,0:T(8,128)(2,1)S(1)}, bf16[2,8,8,512]{3,2,1,0:T(8,128)(2,1)S(1)}, u32[]{:S(2)}, u32[]{:S(2)}) collective-permute-start(bf16[2,8,8,512]{3,2,1,0:T(8,128)(2,1)S(1)} %get-tuple-element.298), channel_id=1, source_target_pairs={{0,3},{1,0},{2,1},{3,2},{4,7},{5,4},{6,5},{7,6},{8,11},{9,8},{10,9... | collective-permute-start | bytes 393224 | tf_op jit(solution)/shard_map/while/body/eval_jaxpr/ppermute | solution.py:40
  279.6 11.8 %collective-permute-start.1 = (bf16[2,8,8,512]{3,2,1,0:T(8,128)(2,1)S(1)}, bf16[2,8,8,512]{3,2,1,0:T(8,128)(2,1)S(1)}, u32[]{:S(2)}, u32[]{:S(2)}) collective-permute-start(bf16[2,8,8,512]{3,2,1,0:T(8,128)(2,1)S(1)} %get-tuple-element.299), channel_id=1, source_target_pairs={{0,2},{1,3},{2,0},{3,1},{4,6},{5,7},{6,4},{7,5},{8,10},{9,11},{10,... | collective-permute-start | bytes 393224 | tf_op jit(solution)/shard_map/while/body/eval_jaxpr/ppermute | solution.py:40
  280.2 11.1 %collective-permute-start.2 = (bf16[2,8,8,512]{3,2,1,0:T(8,128)(2,1)S(1)}, bf16[2,8,8,512]{3,2,1,0:T(8,128)(2,1)S(1)}, u32[]{:S(2)}, u32[]{:S(2)}) collective-permute-start(bf16[2,8,8,512]{3,2,1,0:T(8,128)(2,1)S(1)} %get-tuple-element.300), channel_id=1, source_target_pairs={{0,1},{1,2},{2,3},{3,0},{4,5},{5,6},{6,7},{7,4},{8,9},{9,10},{10,1... | collective-permute-start | bytes 393224 | tf_op jit(solution)/shard_map/while/body/eval_jaxpr/ppermute | solution.py:40
  293.0 8.4 %collective-permute-start.4 = (bf16[2,16,4096]{2,1,0:T(8,128)(2,1)S(1)}, bf16[2,16,4096]{2,1,0:T(8,128)(2,1)S(1)}, u32[]{:S(2)}, u32[]{:S(2)}) collective-permute-start(bf16[2,16,4096]{2,1,0:T(8,128)(2,1)S(1)} %get-tuple-element.303), channel_id=1, source_target_pairs={{0,8},{4,12},{8,0},{12,4},{1,9},{5,13},{9,1},{13,5},{2,10},{6,14},... | collective-permute-start | bytes 786440 | tf_op jit(solution)/shard_map/while/body/eval_jaxpr/ppermute | solution.py:40
  303.6 5.6 %collective-permute-start.5 = (bf16[2,8,8,512]{3,1,2,0:T(8,128)(2,1)S(1)}, bf16[2,8,8,512]{3,1,2,0:T(8,128)(2,1)S(1)}, u32[]{:S(2)}, u32[]{:S(2)}) collective-permute-start(bf16[2,8,8,512]{3,1,2,0:T(8,128)(2,1)S(1)} %bitcast.195), channel_id=1, source_target_pairs={{0,3},{1,0},{2,1},{3,2},{4,7},{5,4},{6,5},{7,6},{8,11},{9,8},{10,9... | collective-permute-start | bytes 393224 | tf_op jit(solution)/shard_map/while/body/eval_jaxpr/ppermute | solution.py:40
  303.6 12.7 %collective-permute-start.6 = (bf16[2,8,8,512]{3,1,2,0:T(8,128)(2,1)S(1)}, bf16[2,8,8,512]{3,1,2,0:T(8,128)(2,1)S(1)}, u32[]{:S(2)}, u32[]{:S(2)}) collective-permute-start(bf16[2,8,8,512]{3,1,2,0:T(8,128)(2,1)S(1)} %bitcast.196), channel_id=1, source_target_pairs={{0,2},{1,3},{2,0},{3,1},{4,6},{5,7},{6,4},{7,5},{8,10},{9,11},{10,... | collective-permute-start | bytes 393224 | tf_op jit(solution)/shard_map/while/body/eval_jaxpr/ppermute | solution.py:40
  304.9 11.4 %collective-permute-start.7 = (bf16[2,8,8,512]{3,1,2,0:T(8,128)(2,1)S(1)}, bf16[2,8,8,512]{3,1,2,0:T(8,128)(2,1)S(1)}, u32[]{:S(2)}, u32[]{:S(2)}) collective-permute-start(bf16[2,8,8,512]{3,1,2,0:T(8,128)(2,1)S(1)} %bitcast.197), channel_id=1, source_target_pairs={{0,1},{1,2},{2,3},{3,0},{4,5},{5,6},{6,7},{7,4},{8,9},{9,10},{10,1... | collective-permute-start | bytes 393224 | tf_op jit(solution)/shard_map/while/body/eval_jaxpr/ppermute | solution.py:40
  324.1 5.0 %collective-permute-start.8 = (f32[1,2]{1,0:T(1,128)S(1)}, f32[1,2]{1,0:T(1,128)S(1)}, u32[]{:S(2)}, u32[]{:S(2)}) collective-permute-start(f32[1,2]{1,0:T(1,128)S(1)} %fusion.123), channel_id=1, source_target_pairs={{0,3},{1,0},{2,1},{3,2},{4,7},{5,4},{6,5},{7,6},{8,11},{9,8},{10,9... | collective-permute-start | bytes 32 | tf_op jit(solution)/shard_map/while/body/eval_jaxpr/ppermute | solution.py:40
  324.1 5.0 %collective-permute-start.9 = (f32[1,2]{1,0:T(1,128)S(1)}, f32[1,2]{1,0:T(1,128)S(1)}, u32[]{:S(2)}, u32[]{:S(2)}) collective-permute-start(f32[1,2]{1,0:T(1,128)S(1)} %fusion.123), channel_id=1, source_target_pairs={{0,2},{1,3},{2,0},{3,1},{4,6},{5,7},{6,4},{7,5},{8,10},{9,11},{10,... | collective-permute-start | bytes 32 | tf_op jit(solution)/shard_map/while/body/eval_jaxpr/ppermute | solution.py:40
  325.8 5.3 %collective-permute-start.10 = (f32[1,2]{1,0:T(1,128)S(1)}, f32[1,2]{1,0:T(1,128)S(1)}, u32[]{:S(2)}, u32[]{:S(2)}) collective-permute-start(f32[1,2]{1,0:T(1,128)S(1)} %fusion.123), channel_id=1, source_target_pairs={{0,1},{1,2},{2,3},{3,0},{4,5},{5,6},{6,7},{7,4},{8,9},{9,10},{10,1... | collective-permute-start | bytes 32 | tf_op jit(solution)/shard_map/while/body/eval_jaxpr/ppermute | solution.py:40
  (41 other events, 239.5 us)

commit v9 on v7

--- a/solution.py
+++ b/solution.py
@@ -67,8 +67,12 @@
     src_local = sources // lax.axis_size("recv")
     total_freq = freq_local * lax.axis_size("freq")
     columns = right_sides * src_local
-    real_operator = operator[0]
-    imag_operator = operator[1]
+    recv_size = lax.axis_size("recv")
+    me = lax.axis_index("recv")
+    blocks = operator.reshape(operator.shape[:3] + (recv_size, src_local))
+    rolled = jnp.take(blocks, (me + jnp.arange(recv_size, dtype=jnp.int32)) % recv_size, axis=3)
+    real_operator = rolled[0]
+    imag_operator = rolled[1]
 
     cos_part, sin_part = dft_rows(jnp.arange(total_freq, dtype=jnp.int32), total_freq)
     to_time = jnp.block([[cos_part.T, -sin_part.T], [sin_part.T, cos_part.T]])
@@ -84,31 +88,46 @@
         reflect, residual = state
         rounded_residual = residual.astype(jnp.bfloat16)
         stacked_residual = jnp.concatenate([rounded_residual[0], rounded_residual[1]], axis=1)
-        with_real = jnp.einsum(
-            "fbr,frs->fbs", stacked_residual, real_operator, preferred_element_type=jnp.float32
-        )
-        with_imag = jnp.einsum(
-            "fbr,frs->fbs", stacked_residual, imag_operator, preferred_element_type=jnp.float32
-        )
-        partial_real = with_real[:, :right_sides] + with_imag[:, right_sides:]
-        partial_imag = with_real[:, right_sides:] - with_imag[:, :right_sides]
-        gradient = sum_scatter(
-            jnp.stack([partial_real, partial_imag]).astype(jnp.bfloat16), "recv", 3
-        )
+        gradient = None
+        for slot in reversed(range(recv_size)):
+            with_real = jnp.einsum(
+                "fbr,frs->fbs", stacked_residual, real_operator[:, :, slot],
+                preferred_element_type=jnp.float32,
+            )
+            with_imag = jnp.einsum(
+                "fbr,frs->fbs", stacked_residual, imag_operator[:, :, slot],
+                preferred_element_type=jnp.float32,
+            )
+            piece = jnp.stack(
+                [
+                    with_real[:, :right_sides] + with_imag[:, right_sides:],
+                    with_real[:, right_sides:] - with_imag[:, :right_sides],
+                ]
+            ).astype(jnp.bfloat16)
+            if slot:
+                piece = shifted(piece, "recv", slot)
+            piece = piece.astype(jnp.float32)
+            gradient = piece if gradient is None else gradient + piece
         flattened = gradient.astype(jnp.bfloat16).reshape(2, freq_local, columns)
         segment = lax.all_gather(flattened, "freq", axis=1, tiled=True).astype(jnp.float32)
         timed = high_dot(to_time, segment.reshape(2 * total_freq, columns))
         projected = high_dot(to_freq, timed * window)
         direction = projected.reshape(2, freq_local, right_sides, src_local)
         rounded_direction = direction.astype(jnp.bfloat16)
-        add_segment = gather_blocks(rounded_direction, "recv", 3)
-        stacked_direction = jnp.concatenate([add_segment[0], add_segment[1]], axis=1)
-        by_real = jnp.einsum(
-            "fbs,frs->fbr", stacked_direction, real_operator, preferred_element_type=jnp.float32
-        )
-        by_imag = jnp.einsum(
-            "fbs,frs->fbr", stacked_direction, imag_operator, preferred_element_type=jnp.float32
-        )
+        by_real = by_imag = None
+        for slot in range(recv_size):
+            held = rounded_direction if slot == 0 else shifted(rounded_direction, "recv", recv_size - slot)
+            stacked_direction = jnp.concatenate([held[0], held[1]], axis=1)
+            real_part = jnp.einsum(
+                "fbs,frs->fbr", stacked_direction, real_operator[:, :, slot],
+                preferred_element_type=jnp.float32,
+            )
+            imag_part = jnp.einsum(
+                "fbs,frs->fbr", stacked_direction, imag_operator[:, :, slot],
+                preferred_element_type=jnp.float32,
+            )
+            by_real = real_part if by_real is None else by_real + real_part
+            by_imag = imag_part if by_imag is None else by_imag + imag_part
         image_real = by_real[:, :right_sides] - by_imag[:, right_sides:]
         image_imag = by_imag[:, :right_sides] + by_real[:, right_sides:]
         image = jnp.stack([image_real, image_imag])

time: 332 us -> 356 us (1.072)
  local copies, waits for them, and re-layouts: 23 us -> 55.2 us
  waiting for transfers between devices: 129 us -> 103 us
  matrix products: 55.1 us -> 67.1 us
  other arithmetic: 24.8 us -> 28.9 us
    ppermute x60, waiting for transfers between devices: 129 us -> 103 us  [shifted(): lax.ppermute(value, axis, [(i, (i + distance) % size) for i in range(size)])]
    unnamed x9 -> x12, local copies, waits for them, and re-layouts: 0.88 us -> 25 us
    dot_general x20 -> x80, matrix products: 42 us -> 60.2 us  [the longest x20 19.6 us: step(): jnp.einsum('fbs,frs->fbr', stacked_direction, real_operator[:, :, slot],...]
    gather x0 -> x3, local copies, waits for them, and re-layouts: none -> 15.9 us  [on_device(): jnp.take(blocks, (me + jnp.arange(recv_size, dtype=jnp.int32)) % recv_siz...]
    dot_general x10, matrix products: 13.1 us -> 6.94 us  [high_dot(): return jnp.dot(left, right, precision=lax.Precision.HIGH)]
    select_n x0 -> x2, other arithmetic: none -> 5.23 us  [on_device(): jnp.take(blocks, (me + jnp.arange(recv_size, dtype=jnp.int32)) % recv_siz...]
    gather x25 -> x20, local copies, waits for them, and re-layouts: 9.43 us -> 6.53 us  [gather_blocks(): ordered = jnp.take(slots, order, axis=dim)]
  transfers between devices with their start and end apart: 60 -> 60, of which waited for: 36 -> 44; matrix products, arithmetic and copies ran while one was open for 2% -> 11% of each run, Pallas kernels for 0% -> 0%
where the time goes in v9:
time: 356 us; the launch traced here: 354 us
  waiting for transfers between devices  103 us (29%)
  matrix products  67.1 us (19%)
  starting transfers between devices  56.5 us (16%)
  local copies, waits for them, and re-layouts  55.2 us (16%)
  blocking collectives  34.7 us (10%)
  other arithmetic  28.9 us (8%)
  loops' own time  8.14 us (2%)
    ppermute x60, waiting for transfers between devices, shifted(): lax.ppermute(value, axis, [(i, (i + distance) % size) for i in range(size)])  103 us
    ppermute x60, starting transfers between devices, shifted(): lax.ppermute(value, axis, [(i, (i + distance) % size) for i in range(size)])  56.5 us
    all_gather x5, blocking collectives, step(): lax.all_gather(flattened, 'freq', axis=1, tiled=True).astype(jnp.float32)  34.7 us
    unnamed x12, local copies, waits for them, and re-layouts  25 us
    dot_general x20, matrix products, step(): jnp.einsum('fbs,frs->fbr', stacked_direction, real_operator[:, :, slot],...  19.6 us
    dot_general x20, matrix products, step(): jnp.einsum('fbr,frs->fbs', stacked_residual, imag_operator[:, :, slot], p...  17.9 us
    gather x3, local copies, waits for them, and re-layouts, on_device(): jnp.take(blocks, (me + jnp.arange(recv_size, dtype=jnp.int32)) % recv_siz...  15.9 us
    dot_general x20, matrix products, step(): jnp.einsum('fbr,frs->fbs', stacked_residual, real_operator[:, :, slot], p...  14.9 us
  transfers between devices with their start and end apart: 60, of which 44 were waited for; matrix products, arithmetic and copies ran while one was open for 11% of the time, Pallas kernels for 0%

profile of v9, /device:TPU:0, one launch (start us, length us, event | category | flops | bytes accessed | tf_op | source)
XLA Modules:
  0.0 354.5 jit_solution(8533184097369012982)
XLA Ops:
  0.7 11.7 %copy.56 = bf16[2,8,128,2048]{2,3,1,0:T(8,128)(2,1)} copy(bf16[2,8,128,2048]{3,2,1,0:T(8,128)(2,1)} %param.8) | data formatting | bytes 16777216 | tf_op args[0]
  12.4 5.9 %fusion.108 = (bf16[2,8,128,4,256]{2,4,3,1,0:T(8,128)(2,1)}, bf16[2,8,128,4,256]{2,4,3,1,0:T(8,128)(2,1)}) fusion(bf16[2,8,128,4,512]{2,4,3,1,0:T(8,128)(2,1)} %bitcast.242), kind=kLoop, calls=%fused_computation.210 | loop fusion | bytes 16777216 | tf_op jit(solution)/shard_map/jit(_take)/gather | solution.py:73
  18.3 6.2 %copy.62 = bf16[2,8,128,4,256]{4,2,1,0,3:T(8,128)(2,1)} copy(bf16[2,8,128,4,256]{2,4,3,1,0:T(8,128)(2,1)} %get-tuple-element.190) | data formatting | bytes 8388608
  24.5 4.9 %gather_fusion.2 = bf16[4,2,8,128,256]{4,3,2,1,0:T(8,128)(2,1)} fusion(bf16[2,8,128,4,256]{4,2,1,0,3:T(8,128)(2,1)} %copy.62, s32[1024]{0:T(1024)S(1)} %pad_clamp_fusion.2), kind=kCustom, calls=%fused_computation.2 | custom fusion | bytes 8388624 | tf_op jit(solution)/shard_map/jit(_take)/gather | solution.py:73
  29.5 6.2 %copy.63 = bf16[2,8,128,4,256]{4,2,1,0,3:T(8,128)(2,1)} copy(bf16[2,8,128,4,256]{2,4,3,1,0:T(8,128)(2,1)} %get-tuple-element.191) | data formatting | bytes 8388608
  35.7 5.0 %gather_fusion.3 = bf16[4,2,8,128,256]{4,3,2,1,0:T(8,128)(2,1)} fusion(bf16[2,8,128,4,256]{4,2,1,0,3:T(8,128)(2,1)} %copy.63, s32[1024]{0:T(1024)S(1)} %pad_clamp_fusion.2), kind=kCustom, calls=%fused_computation.3 | custom fusion | bytes 8388624 | tf_op jit(solution)/shard_map/jit(_take)/gather | solution.py:73
  40.7 5.2 %maximum_select_fusion = bf16[2,8,128,4,512]{4,2,1,0,3:T(8,128)(2,1)S(1)} fusion(bf16[2,8,128,4,256]{4,2,1,0,3:T(8,128)(2,1)} %bitcast.247, bf16[2,8,128,4,256]{4,2,1,0,3:T(8,128)(2,1)} %bitcast.246, pred[4]{0:T(512)(128)(4,1)S(1)} %compare_and_fusion.2), kind=kLoop, calls=%fused_computation.135 | loop fusion | flops 20971520 | bytes 16777220 | tf_op jit(solution)/shard_map/jit(_take)/select_n | solution.py:73
  45.9 3.5 slice_bitcast_fusion.8
  52.2 301.4 %while.15 = (s32[]{:T(128)}, f32[2,8,8,512]{3,1,2,0:T(8,128)S(1)}, f32[2,8,8,128]{3,2,1,0:T(8,128)S(1)}, bf16[8,128,4,512]{3,1,0,2:T(8,128)(2,1)}, bf16[8,128,4,...) while((s32[]{:T(128)}, f32[2,8,8,512]{3,1,2,0:T(8,128)S(1)}, ...), condition=%wide.region_7.9_spmd.clone, body=%wide.region_2.8_spmd.clone.sunk | while | flops 398559552 | bytes 103937664 | solution.py:141
  53.8 2.2 fusion.188
  56.1 5.1 %collective-permute-start.2 = (bf16[2,8,8,512]{3,2,1,0:T(8,128)(2,1)S(1)}, bf16[2,8,8,512]{3,2,1,0:T(8,128)(2,1)S(1)}, u32[]{:S(2)}, u32[]{:S(2)}) collective-permute-start(bf16[2,8,8,512]{3,2,1,0:T(8,128)(2,1)S(1)} %pad_maximum_fusion.60), channel_id=1, source_target_pairs={{0,3},{1,0},{2,1},{3,2},{4,7},{5,4},{6,5},{7,6},{8,11},{9,8},{10,9... | collective-permute-start | bytes 393224 | tf_op jit(solution)/shard_map/while/body/eval_jaxpr/ppermute | solution.py:40
  65.4 7.9 %collective-permute-done.1 = bf16[2,8,8,512]{3,2,1,0:T(8,128)(2,1)S(1)} collective-permute-done((bf16[2,8,8,512]{3,2,1,0:T(8,128)(2,1)S(1)}, bf16[2,8,8,512]{3,2,1,0:T(8,128)(2,1)S(1)}, u32[]{:S(2)}, u32[]{:S(2)}) %collective-permute-start.1) | collective-permute-done | bytes 131104 | tf_op jit(solution)/shard_map/while/body/eval_jaxpr/ppermute | solution.py:40
  73.5 7.3 %all_gather.8 = bf16[2,32,4096]{2,1,0:T(8,128)(2,1)S(1)} all-gather(bf16[2,8,4096]{2,1,0:T(8,128)(2,1)S(1)} %reshape.220), channel_id=1, replica_groups=mesh['groups'=2,'freq'=4,'recv'=4] {'freq'}, dimensions={1}, use_global_device_ids=true | all-gather | bytes 655360 | tf_op jit(solution)/shard_map/while/body/eval_jaxpr/all_gather | solution.py:112
  84.9 1.9 collective-permute-start.5
  90.9 6.3 %collective-permute-done.4 = bf16[2,8,8,512]{3,2,1,0:T(8,128)(2,1)S(1)} collective-permute-done((bf16[2,8,8,512]{3,2,1,0:T(8,128)(2,1)S(1)}, bf16[2,8,8,512]{3,2,1,0:T(8,128)(2,1)S(1)}, u32[]{:S(2)}, u32[]{:S(2)}) %collective-permute-start.4) | collective-permute-done | bytes 131104 | tf_op jit(solution)/shard_map/while/body/eval_jaxpr/ppermute | solution.py:40
  102.7 2.0 collective-permute-start.8
  110.6 2.1 collective-permute-done.10
  117.9 2.2 fusion.188
  120.2 2.1 collective-permute-start.2
  126.1 7.8 %collective-permute-done.1 = bf16[2,8,8,512]{3,2,1,0:T(8,128)(2,1)S(1)} collective-permute-done((bf16[2,8,8,512]{3,2,1,0:T(8,128)(2,1)S(1)}, bf16[2,8,8,512]{3,2,1,0:T(8,128)(2,1)S(1)}, u32[]{:S(2)}, u32[]{:S(2)}) %collective-permute-start.1) | collective-permute-done | bytes 131104 | tf_op jit(solution)/shard_map/while/body/eval_jaxpr/ppermute | solution.py:40
  134.0 7.1 %all_gather.8 = bf16[2,32,4096]{2,1,0:T(8,128)(2,1)S(1)} all-gather(bf16[2,8,4096]{2,1,0:T(8,128)(2,1)S(1)} %reshape.220), channel_id=1, replica_groups=mesh['groups'=2,'freq'=4,'recv'=4] {'freq'}, dimensions={1}, use_global_device_ids=true | all-gather | bytes 655360 | tf_op jit(solution)/shard_map/while/body/eval_jaxpr/all_gather | solution.py:112
  144.5 1.9 collective-permute-start.5
  150.7 6.2 %collective-permute-done.4 = bf16[2,8,8,512]{3,2,1,0:T(8,128)(2,1)S(1)} collective-permute-done((bf16[2,8,8,512]{3,2,1,0:T(8,128)(2,1)S(1)}, bf16[2,8,8,512]{3,2,1,0:T(8,128)(2,1)S(1)}, u32[]{:S(2)}, u32[]{:S(2)}) %collective-permute-start.4) | collective-permute-done | bytes 131104 | tf_op jit(solution)/shard_map/while/body/eval_jaxpr/ppermute | solution.py:40
  162.4 2.0 collective-permute-start.8
  170.0 2.3 collective-permute-done.10
  177.2 2.2 fusion.188
  179.5 2.1 collective-permute-start.2
  185.4 8.1 %collective-permute-done.1 = bf16[2,8,8,512]{3,2,1,0:T(8,128)(2,1)S(1)} collective-permute-done((bf16[2,8,8,512]{3,2,1,0:T(8,128)(2,1)S(1)}, bf16[2,8,8,512]{3,2,1,0:T(8,128)(2,1)S(1)}, u32[]{:S(2)}, u32[]{:S(2)}) %collective-permute-start.1) | collective-permute-done | bytes 131104 | tf_op jit(solution)/shard_map/while/body/eval_jaxpr/ppermute | solution.py:40
  193.6 6.7 %all_gather.8 = bf16[2,32,4096]{2,1,0:T(8,128)(2,1)S(1)} all-gather(bf16[2,8,4096]{2,1,0:T(8,128)(2,1)S(1)} %reshape.220), channel_id=1, replica_groups=mesh['groups'=2,'freq'=4,'recv'=4] {'freq'}, dimensions={1}, use_global_device_ids=true | all-gather | bytes 655360 | tf_op jit(solution)/shard_map/while/body/eval_jaxpr/all_gather | solution.py:112
  203.7 1.9 collective-permute-start.5
  209.9 6.2 %collective-permute-done.4 = bf16[2,8,8,512]{3,2,1,0:T(8,128)(2,1)S(1)} collective-permute-done((bf16[2,8,8,512]{3,2,1,0:T(8,128)(2,1)S(1)}, bf16[2,8,8,512]{3,2,1,0:T(8,128)(2,1)S(1)}, u32[]{:S(2)}, u32[]{:S(2)}) %collective-permute-start.4) | collective-permute-done | bytes 131104 | tf_op jit(solution)/shard_map/while/body/eval_jaxpr/ppermute | solution.py:40
  221.8 2.0 collective-permute-start.8
  229.3 2.3 collective-permute-done.10
  236.6 2.2 fusion.188
  238.9 2.1 collective-permute-start.2
  244.9 7.9 %collective-permute-done.1 = bf16[2,8,8,512]{3,2,1,0:T(8,128)(2,1)S(1)} collective-permute-done((bf16[2,8,8,512]{3,2,1,0:T(8,128)(2,1)S(1)}, bf16[2,8,8,512]{3,2,1,0:T(8,128)(2,1)S(1)}, u32[]{:S(2)}, u32[]{:S(2)}) %collective-permute-start.1) | collective-permute-done | bytes 131104 | tf_op jit(solution)/shard_map/while/body/eval_jaxpr/ppermute | solution.py:40
  252.9 6.9 %all_gather.8 = bf16[2,32,4096]{2,1,0:T(8,128)(2,1)S(1)} all-gather(bf16[2,8,4096]{2,1,0:T(8,128)(2,1)S(1)} %reshape.220), channel_id=1, replica_groups=mesh['groups'=2,'freq'=4,'recv'=4] {'freq'}, dimensions={1}, use_global_device_ids=true | all-gather | bytes 655360 | tf_op jit(solution)/shard_map/while/body/eval_jaxpr/all_gather | solution.py:112
  263.2 1.9 collective-permute-start.5
  269.3 6.2 %collective-permute-done.4 = bf16[2,8,8,512]{3,2,1,0:T(8,128)(2,1)S(1)} collective-permute-done((bf16[2,8,8,512]{3,2,1,0:T(8,128)(2,1)S(1)}, bf16[2,8,8,512]{3,2,1,0:T(8,128)(2,1)S(1)}, u32[]{:S(2)}, u32[]{:S(2)}) %collective-permute-start.4) | collective-permute-done | bytes 131104 | tf_op jit(solution)/shard_map/while/body/eval_jaxpr/ppermute | solution.py:40
  281.1 2.0 collective-permute-start.8
  288.6 2.3 collective-permute-done.10
  295.8 2.2 fusion.188
  298.1 2.0 collective-permute-start.2
  304.1 8.1 %collective-permute-done.1 = bf16[2,8,8,512]{3,2,1,0:T(8,128)(2,1)S(1)} collective-permute-done((bf16[2,8,8,512]{3,2,1,0:T(8,128)(2,1)S(1)}, bf16[2,8,8,512]{3,2,1,0:T(8,128)(2,1)S(1)}, u32[]{:S(2)}, u32[]{:S(2)}) %collective-permute-start.1) | collective-permute-done | bytes 131104 | tf_op jit(solution)/shard_map/while/body/eval_jaxpr/ppermute | solution.py:40
  312.3 6.7 %all_gather.8 = bf16[2,32,4096]{2,1,0:T(8,128)(2,1)S(1)} all-gather(bf16[2,8,4096]{2,1,0:T(8,128)(2,1)S(1)} %reshape.220), channel_id=1, replica_groups=mesh['groups'=2,'freq'=4,'recv'=4] {'freq'}, dimensions={1}, use_global_device_ids=true | all-gather | bytes 655360 | tf_op jit(solution)/shard_map/while/body/eval_jaxpr/all_gather | solution.py:112
  328.6 6.1 %collective-permute-done.4 = bf16[2,8,8,512]{3,2,1,0:T(8,128)(2,1)S(1)} collective-permute-done((bf16[2,8,8,512]{3,2,1,0:T(8,128)(2,1)S(1)}, bf16[2,8,8,512]{3,2,1,0:T(8,128)(2,1)S(1)}, u32[]{:S(2)}, u32[]{:S(2)}) %collective-permute-start.4) | collective-permute-done | bytes 131104 | tf_op jit(solution)/shard_map/while/body/eval_jaxpr/ppermute | solution.py:40
  340.4 2.0 collective-permute-start.8
  347.9 2.3 collective-permute-done.10
  (436 shorter events, 138.1 us)
Async XLA Ops:
  56.1 9.2 %collective-permute-start.2 = (bf16[2,8,8,512]{3,2,1,0:T(8,128)(2,1)S(1)}, bf16[2,8,8,512]{3,2,1,0:T(8,128)(2,1)S(1)}, u32[]{:S(2)}, u32[]{:S(2)}) collective-permute-start(bf16[2,8,8,512]{3,2,1,0:T(8,128)(2,1)S(1)} %pad_maximum_fusion.60), channel_id=1, source_target_pairs={{0,3},{1,0},{2,1},{3,2},{4,7},{5,4},{6,5},{7,6},{8,11},{9,8},{10,9... | collective-permute-start | bytes 393224 | tf_op jit(solution)/shard_map/while/body/eval_jaxpr/ppermute | solution.py:40
  63.0 10.3 %collective-permute-start.1 = (bf16[2,8,8,512]{3,2,1,0:T(8,128)(2,1)S(1)}, bf16[2,8,8,512]{3,2,1,0:T(8,128)(2,1)S(1)}, u32[]{:S(2)}, u32[]{:S(2)}) collective-permute-start(bf16[2,8,8,512]{3,2,1,0:T(8,128)(2,1)S(1)} %pad_maximum_fusion.59), channel_id=1, source_target_pairs={{0,2},{1,3},{2,0},{3,1},{4,6},{5,7},{6,4},{7,5},{8,10},{9,11},{10,... | collective-permute-start | bytes 393224 | tf_op jit(solution)/shard_map/while/body/eval_jaxpr/ppermute | solution.py:40
  63.7 9.6 %collective-permute-start = (bf16[2,8,8,512]{3,2,1,0:T(8,128)(2,1)S(1)}, bf16[2,8,8,512]{3,2,1,0:T(8,128)(2,1)S(1)}, u32[]{:S(2)}, u32[]{:S(2)}) collective-permute-start(bf16[2,8,8,512]{3,2,1,0:T(8,128)(2,1)S(1)} %pad_maximum_fusion.58), channel_id=1, source_target_pairs={{0,1},{1,2},{2,3},{3,0},{4,5},{5,6},{6,7},{7,4},{8,9},{9,10},{10,1... | collective-permute-start | bytes 393224 | tf_op jit(solution)/shard_map/while/body/eval_jaxpr/ppermute | solution.py:40
  82.3 6.7 %collective-permute-start.3 = (bf16[2,8,8,512]{3,2,1,0:T(8,128)(2,1)S(1)}, bf16[2,8,8,512]{3,2,1,0:T(8,128)(2,1)S(1)}, u32[]{:S(2)}, u32[]{:S(2)}) collective-permute-start(bf16[2,8,8,512]{3,2,1,0:T(8,128)(2,1)S(1)} %copy.73), channel_id=1, source_target_pairs={{0,3},{1,0},{2,1},{3,2},{4,7},{5,4},{6,5},{7,6},{8,11},{9,8},{10,9... | collective-permute-start | bytes 393224 | tf_op jit(solution)/shard_map/while/body/eval_jaxpr/ppermute | solution.py:40
  83.3 14.0 %collective-permute-start.4 = (bf16[2,8,8,512]{3,2,1,0:T(8,128)(2,1)S(1)}, bf16[2,8,8,512]{3,2,1,0:T(8,128)(2,1)S(1)}, u32[]{:S(2)}, u32[]{:S(2)}) collective-permute-start(bf16[2,8,8,512]{3,2,1,0:T(8,128)(2,1)S(1)} %copy.73), channel_id=1, source_target_pairs={{0,2},{1,3},{2,0},{3,1},{4,6},{5,7},{6,4},{7,5},{8,10},{9,11},{10,... | collective-permute-start | bytes 393224 | tf_op jit(solution)/shard_map/while/body/eval_jaxpr/ppermute | solution.py:40
  84.9 13.1 %collective-permute-start.5 = (bf16[2,8,8,512]{3,2,1,0:T(8,128)(2,1)S(1)}, bf16[2,8,8,512]{3,2,1,0:T(8,128)(2,1)S(1)}, u32[]{:S(2)}, u32[]{:S(2)}) collective-permute-start(bf16[2,8,8,512]{3,2,1,0:T(8,128)(2,1)S(1)} %copy.73), channel_id=1, source_target_pairs={{0,1},{1,2},{2,3},{3,0},{4,5},{5,6},{6,7},{7,4},{8,9},{9,10},{10,1... | collective-permute-start | bytes 393224 | tf_op jit(solution)/shard_map/while/body/eval_jaxpr/ppermute | solution.py:40
  102.4 4.5 %collective-permute-start.7 = (f32[1,2]{1,0:T(1,128)S(1)}, f32[1,2]{1,0:T(1,128)S(1)}, u32[]{:S(2)}, u32[]{:S(2)}) collective-permute-start(f32[1,2]{1,0:T(1,128)S(1)} %fusion.198), channel_id=1, source_target_pairs={{0,2},{1,3},{2,0},{3,1},{4,6},{5,7},{6,4},{7,5},{8,10},{9,11},{10,... | collective-permute-start | bytes 32 | tf_op jit(solution)/shard_map/while/body/eval_jaxpr/ppermute | solution.py:40
  102.7 5.5 %collective-permute-start.8 = (f32[1,2]{1,0:T(1,128)S(1)}, f32[1,2]{1,0:T(1,128)S(1)}, u32[]{:S(2)}, u32[]{:S(2)}) collective-permute-start(f32[1,2]{1,0:T(1,128)S(1)} %fusion.198), channel_id=1, source_target_pairs={{0,1},{1,2},{2,3},{3,0},{4,5},{5,6},{6,7},{7,4},{8,9},{9,10},{10,1... | collective-permute-start | bytes 32 | tf_op jit(solution)/shard_map/while/body/eval_jaxpr/ppermute | solution.py:40
  109.1 3.6 %collective-permute-start.10 = (f32[1,2]{1,0:T(1,128)S(1)}, f32[1,2]{1,0:T(1,128)S(1)}, u32[]{:S(2)}, u32[]{:S(2)}) collective-permute-start(f32[1,2]{1,0:T(1,128)S(1)} %bitcast.253), channel_id=1, source_target_pairs={{0,8},{4,12},{8,0},{12,4},{1,9},{5,13},{9,1},{13,5},{2,10},{6,14},... | collective-permute-start | bytes 32 | tf_op jit(solution)/shard_map/while/body/eval_jaxpr/ppermute | solution.py:40
  120.2 5.9 %collective-permute-start.2 = (bf16[2,8,8,512]{3,2,1,0:T(8,128)(2,1)S(1)}, bf16[2,8,8,512]{3,2,1,0:T(8,128)(2,1)S(1)}, u32[]{:S(2)}, u32[]{:S(2)}) collective-permute-start(bf16[2,8,8,512]{3,2,1,0:T(8,128)(2,1)S(1)} %pad_maximum_fusion.60), channel_id=1, source_target_pairs={{0,3},{1,0},{2,1},{3,2},{4,7},{5,4},{6,5},{7,6},{8,11},{9,8},{10,9... | collective-permute-start | bytes 393224 | tf_op jit(solution)/shard_map/while/body/eval_jaxpr/ppermute | solution.py:40
  124.1 9.8 %collective-permute-start.1 = (bf16[2,8,8,512]{3,2,1,0:T(8,128)(2,1)S(1)}, bf16[2,8,8,512]{3,2,1,0:T(8,128)(2,1)S(1)}, u32[]{:S(2)}, u32[]{:S(2)}) collective-permute-start(bf16[2,8,8,512]{3,2,1,0:T(8,128)(2,1)S(1)} %pad_maximum_fusion.59), channel_id=1, source_target_pairs={{0,2},{1,3},{2,0},{3,1},{4,6},{5,7},{6,4},{7,5},{8,10},{9,11},{10,... | collective-permute-start | bytes 393224 | tf_op jit(solution)/shard_map/while/body/eval_jaxpr/ppermute | solution.py:40
  124.8 9.1 %collective-permute-start = (bf16[2,8,8,512]{3,2,1,0:T(8,128)(2,1)S(1)}, bf16[2,8,8,512]{3,2,1,0:T(8,128)(2,1)S(1)}, u32[]{:S(2)}, u32[]{:S(2)}) collective-permute-start(bf16[2,8,8,512]{3,2,1,0:T(8,128)(2,1)S(1)} %pad_maximum_fusion.58), channel_id=1, source_target_pairs={{0,1},{1,2},{2,3},{3,0},{4,5},{5,6},{6,7},{7,4},{8,9},{9,10},{10,1... | collective-permute-start | bytes 393224 | tf_op jit(solution)/shard_map/while/body/eval_jaxpr/ppermute | solution.py:40
  142.6 6.1 %collective-permute-start.3 = (bf16[2,8,8,512]{3,2,1,0:T(8,128)(2,1)S(1)}, bf16[2,8,8,512]{3,2,1,0:T(8,128)(2,1)S(1)}, u32[]{:S(2)}, u32[]{:S(2)}) collective-permute-start(bf16[2,8,8,512]{3,2,1,0:T(8,128)(2,1)S(1)} %copy.73), channel_id=1, source_target_pairs={{0,3},{1,0},{2,1},{3,2},{4,7},{5,4},{6,5},{7,6},{8,11},{9,8},{10,9... | collective-permute-start | bytes 393224 | tf_op jit(solution)/shard_map/while/body/eval_jaxpr/ppermute | solution.py:40
  143.0 13.9 %collective-permute-start.4 = (bf16[2,8,8,512]{3,2,1,0:T(8,128)(2,1)S(1)}, bf16[2,8,8,512]{3,2,1,0:T(8,128)(2,1)S(1)}, u32[]{:S(2)}, u32[]{:S(2)}) collective-permute-start(bf16[2,8,8,512]{3,2,1,0:T(8,128)(2,1)S(1)} %copy.73), channel_id=1, source_target_pairs={{0,2},{1,3},{2,0},{3,1},{4,6},{5,7},{6,4},{7,5},{8,10},{9,11},{10,... | collective-permute-start | bytes 393224 | tf_op jit(solution)/shard_map/while/body/eval_jaxpr/ppermute | solution.py:40
  144.5 13.1 %collective-permute-start.5 = (bf16[2,8,8,512]{3,2,1,0:T(8,128)(2,1)S(1)}, bf16[2,8,8,512]{3,2,1,0:T(8,128)(2,1)S(1)}, u32[]{:S(2)}, u32[]{:S(2)}) collective-permute-start(bf16[2,8,8,512]{3,2,1,0:T(8,128)(2,1)S(1)} %copy.73), channel_id=1, source_target_pairs={{0,1},{1,2},{2,3},{3,0},{4,5},{5,6},{6,7},{7,4},{8,9},{9,10},{10,1... | collective-permute-start | bytes 393224 | tf_op jit(solution)/shard_map/while/body/eval_jaxpr/ppermute | solution.py:40
  162.0 3.5 collective-permute-start.6
  162.0 4.5 %collective-permute-start.7 = (f32[1,2]{1,0:T(1,128)S(1)}, f32[1,2]{1,0:T(1,128)S(1)}, u32[]{:S(2)}, u32[]{:S(2)}) collective-permute-start(f32[1,2]{1,0:T(1,128)S(1)} %fusion.198), channel_id=1, source_target_pairs={{0,2},{1,3},{2,0},{3,1},{4,6},{5,7},{6,4},{7,5},{8,10},{9,11},{10,... | collective-permute-start | bytes 32 | tf_op jit(solution)/shard_map/while/body/eval_jaxpr/ppermute | solution.py:40
  162.4 5.4 %collective-permute-start.8 = (f32[1,2]{1,0:T(1,128)S(1)}, f32[1,2]{1,0:T(1,128)S(1)}, u32[]{:S(2)}, u32[]{:S(2)}) collective-permute-start(f32[1,2]{1,0:T(1,128)S(1)} %fusion.198), channel_id=1, source_target_pairs={{0,1},{1,2},{2,3},{3,0},{4,5},{5,6},{6,7},{7,4},{8,9},{9,10},{10,1... | collective-permute-start | bytes 32 | tf_op jit(solution)/shard_map/while/body/eval_jaxpr/ppermute | solution.py:40
  168.7 3.6 %collective-permute-start.10 = (f32[1,2]{1,0:T(1,128)S(1)}, f32[1,2]{1,0:T(1,128)S(1)}, u32[]{:S(2)}, u32[]{:S(2)}) collective-permute-start(f32[1,2]{1,0:T(1,128)S(1)} %bitcast.253), channel_id=1, source_target_pairs={{0,8},{4,12},{8,0},{12,4},{1,9},{5,13},{9,1},{13,5},{2,10},{6,14},... | collective-permute-start | bytes 32 | tf_op jit(solution)/shard_map/while/body/eval_jaxpr/ppermute | solution.py:40
  179.5 6.0 %collective-permute-start.2 = (bf16[2,8,8,512]{3,2,1,0:T(8,128)(2,1)S(1)}, bf16[2,8,8,512]{3,2,1,0:T(8,128)(2,1)S(1)}, u32[]{:S(2)}, u32[]{:S(2)}) collective-permute-start(bf16[2,8,8,512]{3,2,1,0:T(8,128)(2,1)S(1)} %pad_maximum_fusion.60), channel_id=1, source_target_pairs={{0,3},{1,0},{2,1},{3,2},{4,7},{5,4},{6,5},{7,6},{8,11},{9,8},{10,9... | collective-permute-start | bytes 393224 | tf_op jit(solution)/shard_map/while/body/eval_jaxpr/ppermute | solution.py:40
  183.3 10.1 %collective-permute-start.1 = (bf16[2,8,8,512]{3,2,1,0:T(8,128)(2,1)S(1)}, bf16[2,8,8,512]{3,2,1,0:T(8,128)(2,1)S(1)}, u32[]{:S(2)}, u32[]{:S(2)}) collective-permute-start(bf16[2,8,8,512]{3,2,1,0:T(8,128)(2,1)S(1)} %pad_maximum_fusion.59), channel_id=1, source_target_pairs={{0,2},{1,3},{2,0},{3,1},{4,6},{5,7},{6,4},{7,5},{8,10},{9,11},{10,... | collective-permute-start | bytes 393224 | tf_op jit(solution)/shard_map/while/body/eval_jaxpr/ppermute | solution.py:40
  184.0 9.5 %collective-permute-start = (bf16[2,8,8,512]{3,2,1,0:T(8,128)(2,1)S(1)}, bf16[2,8,8,512]{3,2,1,0:T(8,128)(2,1)S(1)}, u32[]{:S(2)}, u32[]{:S(2)}) collective-permute-start(bf16[2,8,8,512]{3,2,1,0:T(8,128)(2,1)S(1)} %pad_maximum_fusion.58), channel_id=1, source_target_pairs={{0,1},{1,2},{2,3},{3,0},{4,5},{5,6},{6,7},{7,4},{8,9},{9,10},{10,1... | collective-permute-start | bytes 393224 | tf_op jit(solution)/shard_map/while/body/eval_jaxpr/ppermute | solution.py:40
  201.8 6.1 %collective-permute-start.3 = (bf16[2,8,8,512]{3,2,1,0:T(8,128)(2,1)S(1)}, bf16[2,8,8,512]{3,2,1,0:T(8,128)(2,1)S(1)}, u32[]{:S(2)}, u32[]{:S(2)}) collective-permute-start(bf16[2,8,8,512]{3,2,1,0:T(8,128)(2,1)S(1)} %copy.73), channel_id=1, source_target_pairs={{0,3},{1,0},{2,1},{3,2},{4,7},{5,4},{6,5},{7,6},{8,11},{9,8},{10,9... | collective-permute-start | bytes 393224 | tf_op jit(solution)/shard_map/while/body/eval_jaxpr/ppermute | solution.py:40
  202.3 13.7 %collective-permute-start.4 = (bf16[2,8,8,512]{3,2,1,0:T(8,128)(2,1)S(1)}, bf16[2,8,8,512]{3,2,1,0:T(8,128)(2,1)S(1)}, u32[]{:S(2)}, u32[]{:S(2)}) collective-permute-start(bf16[2,8,8,512]{3,2,1,0:T(8,128)(2,1)S(1)} %copy.73), channel_id=1, source_target_pairs={{0,2},{1,3},{2,0},{3,1},{4,6},{5,7},{6,4},{7,5},{8,10},{9,11},{10,... | collective-permute-start | bytes 393224 | tf_op jit(solution)/shard_map/while/body/eval_jaxpr/ppermute | solution.py:40
  203.7 13.1 %collective-permute-start.5 = (bf16[2,8,8,512]{3,2,1,0:T(8,128)(2,1)S(1)}, bf16[2,8,8,512]{3,2,1,0:T(8,128)(2,1)S(1)}, u32[]{:S(2)}, u32[]{:S(2)}) collective-permute-start(bf16[2,8,8,512]{3,2,1,0:T(8,128)(2,1)S(1)} %copy.73), channel_id=1, source_target_pairs={{0,1},{1,2},{2,3},{3,0},{4,5},{5,6},{6,7},{7,4},{8,9},{9,10},{10,1... | collective-permute-start | bytes 393224 | tf_op jit(solution)/shard_map/while/body/eval_jaxpr/ppermute | solution.py:40
  221.2 3.5 collective-permute-start.6
  221.2 4.5 %collective-permute-start.7 = (f32[1,2]{1,0:T(1,128)S(1)}, f32[1,2]{1,0:T(1,128)S(1)}, u32[]{:S(2)}, u32[]{:S(2)}) collective-permute-start(f32[1,2]{1,0:T(1,128)S(1)} %fusion.198), channel_id=1, source_target_pairs={{0,2},{1,3},{2,0},{3,1},{4,6},{5,7},{6,4},{7,5},{8,10},{9,11},{10,... | collective-permute-start | bytes 32 | tf_op jit(solution)/shard_map/while/body/eval_jaxpr/ppermute | solution.py:40
  221.8 5.3 %collective-permute-start.8 = (f32[1,2]{1,0:T(1,128)S(1)}, f32[1,2]{1,0:T(1,128)S(1)}, u32[]{:S(2)}, u32[]{:S(2)}) collective-permute-start(f32[1,2]{1,0:T(1,128)S(1)} %fusion.198), channel_id=1, source_target_pairs={{0,1},{1,2},{2,3},{3,0},{4,5},{5,6},{6,7},{7,4},{8,9},{9,10},{10,1... | collective-permute-start | bytes 32 | tf_op jit(solution)/shard_map/while/body/eval_jaxpr/ppermute | solution.py:40
  227.9 3.6 %collective-permute-start.10 = (f32[1,2]{1,0:T(1,128)S(1)}, f32[1,2]{1,0:T(1,128)S(1)}, u32[]{:S(2)}, u32[]{:S(2)}) collective-permute-start(f32[1,2]{1,0:T(1,128)S(1)} %bitcast.253), channel_id=1, source_target_pairs={{0,8},{4,12},{8,0},{12,4},{1,9},{5,13},{9,1},{13,5},{2,10},{6,14},... | collective-permute-start | bytes 32 | tf_op jit(solution)/shard_map/while/body/eval_jaxpr/ppermute | solution.py:40
  238.9 6.0 %collective-permute-start.2 = (bf16[2,8,8,512]{3,2,1,0:T(8,128)(2,1)S(1)}, bf16[2,8,8,512]{3,2,1,0:T(8,128)(2,1)S(1)}, u32[]{:S(2)}, u32[]{:S(2)}) collective-permute-start(bf16[2,8,8,512]{3,2,1,0:T(8,128)(2,1)S(1)} %pad_maximum_fusion.60), channel_id=1, source_target_pairs={{0,3},{1,0},{2,1},{3,2},{4,7},{5,4},{6,5},{7,6},{8,11},{9,8},{10,9... | collective-permute-start | bytes 393224 | tf_op jit(solution)/shard_map/while/body/eval_jaxpr/ppermute | solution.py:40
  242.8 10.0 %collective-permute-start.1 = (bf16[2,8,8,512]{3,2,1,0:T(8,128)(2,1)S(1)}, bf16[2,8,8,512]{3,2,1,0:T(8,128)(2,1)S(1)}, u32[]{:S(2)}, u32[]{:S(2)}) collective-permute-start(bf16[2,8,8,512]{3,2,1,0:T(8,128)(2,1)S(1)} %pad_maximum_fusion.59), channel_id=1, source_target_pairs={{0,2},{1,3},{2,0},{3,1},{4,6},{5,7},{6,4},{7,5},{8,10},{9,11},{10,... | collective-permute-start | bytes 393224 | tf_op jit(solution)/shard_map/while/body/eval_jaxpr/ppermute | solution.py:40
  243.4 9.3 %collective-permute-start = (bf16[2,8,8,512]{3,2,1,0:T(8,128)(2,1)S(1)}, bf16[2,8,8,512]{3,2,1,0:T(8,128)(2,1)S(1)}, u32[]{:S(2)}, u32[]{:S(2)}) collective-permute-start(bf16[2,8,8,512]{3,2,1,0:T(8,128)(2,1)S(1)} %pad_maximum_fusion.58), channel_id=1, source_target_pairs={{0,1},{1,2},{2,3},{3,0},{4,5},{5,6},{6,7},{7,4},{8,9},{9,10},{10,1... | collective-permute-start | bytes 393224 | tf_op jit(solution)/shard_map/while/body/eval_jaxpr/ppermute | solution.py:40
  261.2 6.1 %collective-permute-start.3 = (bf16[2,8,8,512]{3,2,1,0:T(8,128)(2,1)S(1)}, bf16[2,8,8,512]{3,2,1,0:T(8,128)(2,1)S(1)}, u32[]{:S(2)}, u32[]{:S(2)}) collective-permute-start(bf16[2,8,8,512]{3,2,1,0:T(8,128)(2,1)S(1)} %copy.73), channel_id=1, source_target_pairs={{0,3},{1,0},{2,1},{3,2},{4,7},{5,4},{6,5},{7,6},{8,11},{9,8},{10,9... | collective-permute-start | bytes 393224 | tf_op jit(solution)/shard_map/while/body/eval_jaxpr/ppermute | solution.py:40
  261.7 13.8 %collective-permute-start.4 = (bf16[2,8,8,512]{3,2,1,0:T(8,128)(2,1)S(1)}, bf16[2,8,8,512]{3,2,1,0:T(8,128)(2,1)S(1)}, u32[]{:S(2)}, u32[]{:S(2)}) collective-permute-start(bf16[2,8,8,512]{3,2,1,0:T(8,128)(2,1)S(1)} %copy.73), channel_id=1, source_target_pairs={{0,2},{1,3},{2,0},{3,1},{4,6},{5,7},{6,4},{7,5},{8,10},{9,11},{10,... | collective-permute-start | bytes 393224 | tf_op jit(solution)/shard_map/while/body/eval_jaxpr/ppermute | solution.py:40
  263.2 13.1 %collective-permute-start.5 = (bf16[2,8,8,512]{3,2,1,0:T(8,128)(2,1)S(1)}, bf16[2,8,8,512]{3,2,1,0:T(8,128)(2,1)S(1)}, u32[]{:S(2)}, u32[]{:S(2)}) collective-permute-start(bf16[2,8,8,512]{3,2,1,0:T(8,128)(2,1)S(1)} %copy.73), channel_id=1, source_target_pairs={{0,1},{1,2},{2,3},{3,0},{4,5},{5,6},{6,7},{7,4},{8,9},{9,10},{10,1... | collective-permute-start | bytes 393224 | tf_op jit(solution)/shard_map/while/body/eval_jaxpr/ppermute | solution.py:40
  280.6 3.5 collective-permute-start.6
  280.6 4.5 %collective-permute-start.7 = (f32[1,2]{1,0:T(1,128)S(1)}, f32[1,2]{1,0:T(1,128)S(1)}, u32[]{:S(2)}, u32[]{:S(2)}) collective-permute-start(f32[1,2]{1,0:T(1,128)S(1)} %fusion.198), channel_id=1, source_target_pairs={{0,2},{1,3},{2,0},{3,1},{4,6},{5,7},{6,4},{7,5},{8,10},{9,11},{10,... | collective-permute-start | bytes 32 | tf_op jit(solution)/shard_map/while/body/eval_jaxpr/ppermute | solution.py:40
  281.1 5.4 %collective-permute-start.8 = (f32[1,2]{1,0:T(1,128)S(1)}, f32[1,2]{1,0:T(1,128)S(1)}, u32[]{:S(2)}, u32[]{:S(2)}) collective-permute-start(f32[1,2]{1,0:T(1,128)S(1)} %fusion.198), channel_id=1, source_target_pairs={{0,1},{1,2},{2,3},{3,0},{4,5},{5,6},{6,7},{7,4},{8,9},{9,10},{10,1... | collective-permute-start | bytes 32 | tf_op jit(solution)/shard_map/while/body/eval_jaxpr/ppermute | solution.py:40
  287.4 3.6 %collective-permute-start.10 = (f32[1,2]{1,0:T(1,128)S(1)}, f32[1,2]{1,0:T(1,128)S(1)}, u32[]{:S(2)}, u32[]{:S(2)}) collective-permute-start(f32[1,2]{1,0:T(1,128)S(1)} %bitcast.253), channel_id=1, source_target_pairs={{0,8},{4,12},{8,0},{12,4},{1,9},{5,13},{9,1},{13,5},{2,10},{6,14},... | collective-permute-start | bytes 32 | tf_op jit(solution)/shard_map/while/body/eval_jaxpr/ppermute | solution.py:40
  298.1 5.9 %collective-permute-start.2 = (bf16[2,8,8,512]{3,2,1,0:T(8,128)(2,1)S(1)}, bf16[2,8,8,512]{3,2,1,0:T(8,128)(2,1)S(1)}, u32[]{:S(2)}, u32[]{:S(2)}) collective-permute-start(bf16[2,8,8,512]{3,2,1,0:T(8,128)(2,1)S(1)} %pad_maximum_fusion.60), channel_id=1, source_target_pairs={{0,3},{1,0},{2,1},{3,2},{4,7},{5,4},{6,5},{7,6},{8,11},{9,8},{10,9... | collective-permute-start | bytes 393224 | tf_op jit(solution)/shard_map/while/body/eval_jaxpr/ppermute | solution.py:40
  302.0 10.1 %collective-permute-start.1 = (bf16[2,8,8,512]{3,2,1,0:T(8,128)(2,1)S(1)}, bf16[2,8,8,512]{3,2,1,0:T(8,128)(2,1)S(1)}, u32[]{:S(2)}, u32[]{:S(2)}) collective-permute-start(bf16[2,8,8,512]{3,2,1,0:T(8,128)(2,1)S(1)} %pad_maximum_fusion.59), channel_id=1, source_target_pairs={{0,2},{1,3},{2,0},{3,1},{4,6},{5,7},{6,4},{7,5},{8,10},{9,11},{10,... | collective-permute-start | bytes 393224 | tf_op jit(solution)/shard_map/while/body/eval_jaxpr/ppermute | solution.py:40
  302.6 9.5 %collective-permute-start = (bf16[2,8,8,512]{3,2,1,0:T(8,128)(2,1)S(1)}, bf16[2,8,8,512]{3,2,1,0:T(8,128)(2,1)S(1)}, u32[]{:S(2)}, u32[]{:S(2)}) collective-permute-start(bf16[2,8,8,512]{3,2,1,0:T(8,128)(2,1)S(1)} %pad_maximum_fusion.58), channel_id=1, source_target_pairs={{0,1},{1,2},{2,3},{3,0},{4,5},{5,6},{6,7},{7,4},{8,9},{9,10},{10,1... | collective-permute-start | bytes 393224 | tf_op jit(solution)/shard_map/while/body/eval_jaxpr/ppermute | solution.py:40
  320.5 6.1 %collective-permute-start.3 = (bf16[2,8,8,512]{3,2,1,0:T(8,128)(2,1)S(1)}, bf16[2,8,8,512]{3,2,1,0:T(8,128)(2,1)S(1)}, u32[]{:S(2)}, u32[]{:S(2)}) collective-permute-start(bf16[2,8,8,512]{3,2,1,0:T(8,128)(2,1)S(1)} %copy.73), channel_id=1, source_target_pairs={{0,3},{1,0},{2,1},{3,2},{4,7},{5,4},{6,5},{7,6},{8,11},{9,8},{10,9... | collective-permute-start | bytes 393224 | tf_op jit(solution)/shard_map/while/body/eval_jaxpr/ppermute | solution.py:40
  321.0 13.7 %collective-permute-start.4 = (bf16[2,8,8,512]{3,2,1,0:T(8,128)(2,1)S(1)}, bf16[2,8,8,512]{3,2,1,0:T(8,128)(2,1)S(1)}, u32[]{:S(2)}, u32[]{:S(2)}) collective-permute-start(bf16[2,8,8,512]{3,2,1,0:T(8,128)(2,1)S(1)} %copy.73), channel_id=1, source_target_pairs={{0,2},{1,3},{2,0},{3,1},{4,6},{5,7},{6,4},{7,5},{8,10},{9,11},{10,... | collective-permute-start | bytes 393224 | tf_op jit(solution)/shard_map/while/body/eval_jaxpr/ppermute | solution.py:40
  322.4 13.1 %collective-permute-start.5 = (bf16[2,8,8,512]{3,2,1,0:T(8,128)(2,1)S(1)}, bf16[2,8,8,512]{3,2,1,0:T(8,128)(2,1)S(1)}, u32[]{:S(2)}, u32[]{:S(2)}) collective-permute-start(bf16[2,8,8,512]{3,2,1,0:T(8,128)(2,1)S(1)} %copy.73), channel_id=1, source_target_pairs={{0,1},{1,2},{2,3},{3,0},{4,5},{5,6},{6,7},{7,4},{8,9},{9,10},{10,1... | collective-permute-start | bytes 393224 | tf_op jit(solution)/shard_map/while/body/eval_jaxpr/ppermute | solution.py:40
  339.8 4.5 %collective-permute-start.7 = (f32[1,2]{1,0:T(1,128)S(1)}, f32[1,2]{1,0:T(1,128)S(1)}, u32[]{:S(2)}, u32[]{:S(2)}) collective-permute-start(f32[1,2]{1,0:T(1,128)S(1)} %fusion.198), channel_id=1, source_target_pairs={{0,2},{1,3},{2,0},{3,1},{4,6},{5,7},{6,4},{7,5},{8,10},{9,11},{10,... | collective-permute-start | bytes 32 | tf_op jit(solution)/shard_map/while/body/eval_jaxpr/ppermute | solution.py:40
  340.4 5.3 %collective-permute-start.8 = (f32[1,2]{1,0:T(1,128)S(1)}, f32[1,2]{1,0:T(1,128)S(1)}, u32[]{:S(2)}, u32[]{:S(2)}) collective-permute-start(f32[1,2]{1,0:T(1,128)S(1)} %fusion.198), channel_id=1, source_target_pairs={{0,1},{1,2},{2,3},{3,0},{4,5},{5,6},{6,7},{7,4},{8,9},{9,10},{10,1... | collective-permute-start | bytes 32 | tf_op jit(solution)/shard_map/while/body/eval_jaxpr/ppermute | solution.py:40
  346.6 3.6 %collective-permute-start.10 = (f32[1,2]{1,0:T(1,128)S(1)}, f32[1,2]{1,0:T(1,128)S(1)}, u32[]{:S(2)}, u32[]{:S(2)}) collective-permute-start(f32[1,2]{1,0:T(1,128)S(1)} %bitcast.253), channel_id=1, source_target_pairs={{0,8},{4,12},{8,0},{12,4},{1,9},{5,13},{9,1},{13,5},{2,10},{6,14},... | collective-permute-start | bytes 32 | tf_op jit(solution)/shard_map/while/body/eval_jaxpr/ppermute | solution.py:40
  (36 other events, 275.7 us)

commit v10 on v7

--- a/solution.py
+++ b/solution.py
@@ -80,21 +80,28 @@
     )
     window = jnp.concatenate([window, window])
 
-    def step(iteration, state):
-        reflect, residual = state
-        rounded_residual = residual.astype(jnp.bfloat16)
-        stacked_residual = jnp.concatenate([rounded_residual[0], rounded_residual[1]], axis=1)
+    def adjoint(values):
+        high = lax.reduce_precision(values, exponent_bits=8, mantissa_bits=7)
+        low = values - high
+        stacked = jnp.concatenate(
+            [high[0], high[1], low[0], low[1]], axis=1
+        ).astype(jnp.bfloat16)
         with_real = jnp.einsum(
-            "fbr,frs->fbs", stacked_residual, real_operator, preferred_element_type=jnp.float32
+            "fbr,frs->fbs", stacked, real_operator, preferred_element_type=jnp.float32
         )
         with_imag = jnp.einsum(
-            "fbr,frs->fbs", stacked_residual, imag_operator, preferred_element_type=jnp.float32
+            "fbr,frs->fbs", stacked, imag_operator, preferred_element_type=jnp.float32
         )
-        partial_real = with_real[:, :right_sides] + with_imag[:, right_sides:]
-        partial_imag = with_real[:, right_sides:] - with_imag[:, :right_sides]
-        gradient = sum_scatter(
-            jnp.stack([partial_real, partial_imag]).astype(jnp.bfloat16), "recv", 3
+        rows = right_sides
+        by_real = with_real[:, : 2 * rows] + with_real[:, 2 * rows :]
+        by_imag = with_imag[:, : 2 * rows] + with_imag[:, 2 * rows :]
+        return jnp.stack(
+            [by_real[:, :rows] + by_imag[:, rows:], by_real[:, rows:] - by_imag[:, :rows]]
         )
+
+    def step(iteration, state):
+        reflect, residual, partial = state
+        gradient = sum_scatter(partial.astype(jnp.bfloat16), "recv", 3)
         flattened = gradient.astype(jnp.bfloat16).reshape(2, freq_local, columns)
         segment = lax.all_gather(flattened, "freq", axis=1, tiled=True).astype(jnp.float32)
         timed = high_dot(to_time, segment.reshape(2 * total_freq, columns))
@@ -115,11 +122,17 @@
         sums = jnp.stack([jnp.sum(direction * direction), jnp.sum(image * image)])
         sums = jnp.sum(gather_blocks(sums[None], "recv", 0), axis=0)
         direction_power, image_energy = jnp.sum(gather_blocks(sums[None], "freq", 0), axis=0)
+        normal = adjoint(image)
         step_length = direction_power / (image_energy + 1e-06)
-        return (reflect + step_length * direction, residual - step_length * image)
+        return (
+            reflect + step_length * direction,
+            residual - step_length * image,
+            partial - step_length * normal,
+        )
 
     reflect = jnp.zeros((2, freq_local, right_sides, src_local), jnp.float32)
-    return lax.fori_loop(0, ITERS, step, (reflect, recorded))
+    reflect, residual, _ = lax.fori_loop(0, ITERS, step, (reflect, recorded, adjoint(recorded)))
+    return (reflect, residual)
 
 
 def solution(mesh):

time: 332 us -> 357 us (1.075)
  starting transfers between devices: 57.3 us -> 80.4 us
  waiting for transfers between devices: 129 us -> 121 us
  local copies, waits for them, and re-layouts: 23 us -> 28.9 us
    ppermute x60, starting transfers between devices: 57.3 us -> 80.4 us  [shifted(): lax.ppermute(value, axis, [(i, (i + distance) % size) for i in range(size)])]
    dot_general x5, matrix products: 17.8 us -> 6.01 us  [step(): jnp.einsum('fbs,frs->fbr', stacked_direction, imag_operator, preferred_el...]
    dot_general x5, matrix products: 6.01 us -> 17.8 us  [step(): jnp.einsum('fbs,frs->fbr', stacked_direction, real_operator, preferred_el...]
    ppermute x60, waiting for transfers between devices: 129 us -> 121 us  [shifted(): lax.ppermute(value, axis, [(i, (i + distance) % size) for i in range(size)])]
    dot_general x10, matrix products: 13.1 us -> 6.95 us  [high_dot(): return jnp.dot(left, right, precision=lax.Precision.HIGH)]
    dot_general x10 -> x12, matrix products: 18.3 us -> 21.5 us  [the longest x6 15 us: adjoint(): jnp.einsum('fbr,frs->fbs', stacked, real_operator, preferred_element_type...]
  transfers between devices with their start and end apart: 60 -> 60, of which waited for: 36 -> 45; matrix products, arithmetic and copies ran while one was open for 2% -> 0% of each run, Pallas kernels for 0% -> 0%
where the time goes in v10:
time: 357 us; the launch traced here: 355 us
  waiting for transfers between devices  121 us (34%)
  starting transfers between devices  80.4 us (23%)
  matrix products  52.2 us (15%)
  blocking collectives  35.3 us (10%)
  local copies, waits for them, and re-layouts  28.9 us (8%)
  other arithmetic  26.9 us (8%)
  loops' own time  9.56 us (3%)
    ppermute x60, waiting for transfers between devices, shifted(): lax.ppermute(value, axis, [(i, (i + distance) % size) for i in range(size)])  121 us
    ppermute x60, starting transfers between devices, shifted(): lax.ppermute(value, axis, [(i, (i + distance) % size) for i in range(size)])  80.4 us
    all_gather x5, blocking collectives, step(): lax.all_gather(flattened, 'freq', axis=1, tiled=True).astype(jnp.float32)  35.3 us
    dot_general x5, matrix products, step(): jnp.einsum('fbs,frs->fbr', stacked_direction, real_operator, preferred_el...  17.8 us
    dot_general x6, matrix products, adjoint(): jnp.einsum('fbr,frs->fbs', stacked, real_operator, preferred_element_type...  15 us
    another operation x1, loops' own time, on_device(): lax.fori_loop(0, ITERS, step, (reflect, recorded, adjoint(recorded)))  9.56 us
    gather x25, local copies, waits for them, and re-layouts, gather_blocks(): ordered = jnp.take(slots, order, axis=dim)  9.44 us
  transfers between devices with their start and end apart: 60, of which 45 were waited for; matrix products, arithmetic and copies ran while one was open for 0% of the time, Pallas kernels for 0%

profile of v10, /device:TPU:0, one launch (start us, length us, event | category | flops | bytes accessed | tf_op | source)
XLA Modules:
  0.0 355.0 jit_solution(7595301090119001005)
XLA Ops:
  5.6 3.0 fusion.51
  11.2 3.8 %slice_bitcast_fusion.4 = (bf16[8,128,2048]{2,1,0:T(8,128)(2,1)}, bf16[8,128,2048]{2,1,0:T(8,128)(2,1)}) fusion(bf16[2,8,128,2048]{3,2,1,0:T(8,128)(2,1)S(1)} %copy-done.2), kind=kLoop, calls=%fused_computation.79 | loop fusion | bytes 16777216 | tf_op jit(solution)/shard_map/squeeze | solution.py:71
  15.0 338.2 %while.17 = (s32[]{:T(128)}, f32[2,8,8,512]{3,1,2,0:T(8,128)}, f32[2,8,8,128]{3,2,1,0:T(8,128)S(1)}, f32[2,8,8,2048]{3,2,1,0:T(8,128)S(1)}, f32[64,64]{1,0:T(8,1...) while((s32[]{:T(128)}, f32[2,8,8,512]{3,1,2,0:T(8,128)}, ...), condition=%wide.region_7.9_spmd.clone, body=%wide.region_2.8_spmd.clone.sunk | while | flops 535350720 | bytes 88901840 | solution.py:134
  15.2 5.1 %collective-permute-start = (bf16[2,8,8,512]{3,2,1,0:T(8,128)(2,1)S(1)}, bf16[2,8,8,512]{3,2,1,0:T(8,128)(2,1)S(1)}, u32[]{:S(2)}, u32[]{:S(2)}) collective-permute-start(bf16[2,8,8,512]{3,2,1,0:T(8,128)(2,1)S(1)} %get-tuple-element.292), channel_id=1, source_target_pairs={{0,3},{1,0},{2,1},{3,2},{4,7},{5,4},{6,5},{7,6},{8,11},{9,8},{10,9... | collective-permute-start | bytes 393224 | tf_op jit(solution)/shard_map/while/body/eval_jaxpr/ppermute | solution.py:40
  21.3 2.8 collective-permute-done
  24.2 7.3 %collective-permute-done.1 = bf16[2,8,8,512]{3,2,1,0:T(8,128)(2,1)S(1)} collective-permute-done((bf16[2,8,8,512]{3,2,1,0:T(8,128)(2,1)S(1)}, bf16[2,8,8,512]{3,2,1,0:T(8,128)(2,1)S(1)}, u32[]{:S(2)}, u32[]{:S(2)}) %collective-permute-start.1) | collective-permute-done | bytes 131104 | tf_op jit(solution)/shard_map/while/body/eval_jaxpr/ppermute | solution.py:40
  31.6 7.2 %all_gather.8 = bf16[2,32,4096]{2,1,0:T(8,128)(2,1)S(1)} all-gather(bf16[2,8,4096]{2,1,0:T(8,128)(2,1)S(1)} %reshape.236), channel_id=1, replica_groups=mesh['groups'=2,'freq'=4,'recv'=4] {'freq'}, dimensions={1}, use_global_device_ids=true | all-gather | bytes 655360 | tf_op jit(solution)/shard_map/while/body/eval_jaxpr/all_gather | solution.py:106
  42.8 2.9 collective-permute-start.3
  45.8 2.7 collective-permute-done.5
  48.4 5.0 %collective-permute-done.4 = bf16[2,8,8,512]{3,1,2,0:T(8,128)(2,1)S(1)} collective-permute-done((bf16[2,8,8,512]{3,1,2,0:T(8,128)(2,1)S(1)}, bf16[2,8,8,512]{3,1,2,0:T(8,128)(2,1)S(1)}, u32[]{:S(2)}, u32[]{:S(2)}) %collective-permute-start.4) | collective-permute-done | bytes 131104 | tf_op jit(solution)/shard_map/while/body/eval_jaxpr/ppermute | solution.py:40
  54.5 3.6 %fusion.110 = f32[8,16,128]{2,1,0:T(8,128)S(1)} fusion(bf16[8,128,2048]{2,1,0:T(8,128)(2,1)} %get-tuple-element.356, bf16[8,8,2048]{2,1,0:T(8,128)(2,1)S(1)} %bitcast.189, bf16[8,8,2048]{2,1,0:T(8,128)(2,1)S(1)} %bitcast.191), kind=kOutput, calls=%fused_computation.17.clone.1 | convolution fusion | flops 68157440 | bytes 4784128 | tf_op jit(solution)/shard_map/while/body/eval_jaxpr/fbs,frs->fbr/dot_general | solution.py:113
  62.6 2.8 collective-permute-start.8
  78.7 2.9 fusion.118
  87.3 3.1 collective-permute-done
  90.5 8.8 %collective-permute-done.1 = bf16[2,8,8,512]{3,2,1,0:T(8,128)(2,1)S(1)} collective-permute-done((bf16[2,8,8,512]{3,2,1,0:T(8,128)(2,1)S(1)}, bf16[2,8,8,512]{3,2,1,0:T(8,128)(2,1)S(1)}, u32[]{:S(2)}, u32[]{:S(2)}) %collective-permute-start.1) | collective-permute-done | bytes 131104 | tf_op jit(solution)/shard_map/while/body/eval_jaxpr/ppermute | solution.py:40
  99.4 7.0 %all_gather.8 = bf16[2,32,4096]{2,1,0:T(8,128)(2,1)S(1)} all-gather(bf16[2,8,4096]{2,1,0:T(8,128)(2,1)S(1)} %reshape.236), channel_id=1, replica_groups=mesh['groups'=2,'freq'=4,'recv'=4] {'freq'}, dimensions={1}, use_global_device_ids=true | all-gather | bytes 655360 | tf_op jit(solution)/shard_map/while/body/eval_jaxpr/all_gather | solution.py:106
  110.2 2.9 collective-permute-start.3
  113.1 3.0 collective-permute-done.5
  116.1 5.0 %collective-permute-done.4 = bf16[2,8,8,512]{3,1,2,0:T(8,128)(2,1)S(1)} collective-permute-done((bf16[2,8,8,512]{3,1,2,0:T(8,128)(2,1)S(1)}, bf16[2,8,8,512]{3,1,2,0:T(8,128)(2,1)S(1)}, u32[]{:S(2)}, u32[]{:S(2)}) %collective-permute-start.4) | collective-permute-done | bytes 131104 | tf_op jit(solution)/shard_map/while/body/eval_jaxpr/ppermute | solution.py:40
  122.1 3.6 %fusion.110 = f32[8,16,128]{2,1,0:T(8,128)S(1)} fusion(bf16[8,128,2048]{2,1,0:T(8,128)(2,1)} %get-tuple-element.356, bf16[8,8,2048]{2,1,0:T(8,128)(2,1)S(1)} %bitcast.189, bf16[8,8,2048]{2,1,0:T(8,128)(2,1)S(1)} %bitcast.191), kind=kOutput, calls=%fused_computation.17.clone.1 | convolution fusion | flops 68157440 | bytes 4784128 | tf_op jit(solution)/shard_map/while/body/eval_jaxpr/fbs,frs->fbr/dot_general | solution.py:113
  130.2 2.5 collective-permute-start.8
  146.0 2.9 fusion.118
  154.7 3.1 collective-permute-done
  157.8 8.8 %collective-permute-done.1 = bf16[2,8,8,512]{3,2,1,0:T(8,128)(2,1)S(1)} collective-permute-done((bf16[2,8,8,512]{3,2,1,0:T(8,128)(2,1)S(1)}, bf16[2,8,8,512]{3,2,1,0:T(8,128)(2,1)S(1)}, u32[]{:S(2)}, u32[]{:S(2)}) %collective-permute-start.1) | collective-permute-done | bytes 131104 | tf_op jit(solution)/shard_map/while/body/eval_jaxpr/ppermute | solution.py:40
  166.7 7.0 %all_gather.8 = bf16[2,32,4096]{2,1,0:T(8,128)(2,1)S(1)} all-gather(bf16[2,8,4096]{2,1,0:T(8,128)(2,1)S(1)} %reshape.236), channel_id=1, replica_groups=mesh['groups'=2,'freq'=4,'recv'=4] {'freq'}, dimensions={1}, use_global_device_ids=true | all-gather | bytes 655360 | tf_op jit(solution)/shard_map/while/body/eval_jaxpr/all_gather | solution.py:106
  177.4 2.9 collective-permute-start.3
  180.4 3.0 collective-permute-done.5
  183.4 5.0 %collective-permute-done.4 = bf16[2,8,8,512]{3,1,2,0:T(8,128)(2,1)S(1)} collective-permute-done((bf16[2,8,8,512]{3,1,2,0:T(8,128)(2,1)S(1)}, bf16[2,8,8,512]{3,1,2,0:T(8,128)(2,1)S(1)}, u32[]{:S(2)}, u32[]{:S(2)}) %collective-permute-start.4) | collective-permute-done | bytes 131104 | tf_op jit(solution)/shard_map/while/body/eval_jaxpr/ppermute | solution.py:40
  189.5 3.6 %fusion.110 = f32[8,16,128]{2,1,0:T(8,128)S(1)} fusion(bf16[8,128,2048]{2,1,0:T(8,128)(2,1)} %get-tuple-element.356, bf16[8,8,2048]{2,1,0:T(8,128)(2,1)S(1)} %bitcast.189, bf16[8,8,2048]{2,1,0:T(8,128)(2,1)S(1)} %bitcast.191), kind=kOutput, calls=%fused_computation.17.clone.1 | convolution fusion | flops 68157440 | bytes 4784128 | tf_op jit(solution)/shard_map/while/body/eval_jaxpr/fbs,frs->fbr/dot_general | solution.py:113
  197.6 2.5 collective-permute-start.8
  213.3 2.9 fusion.118
  221.9 3.1 collective-permute-done
  225.1 8.8 %collective-permute-done.1 = bf16[2,8,8,512]{3,2,1,0:T(8,128)(2,1)S(1)} collective-permute-done((bf16[2,8,8,512]{3,2,1,0:T(8,128)(2,1)S(1)}, bf16[2,8,8,512]{3,2,1,0:T(8,128)(2,1)S(1)}, u32[]{:S(2)}, u32[]{:S(2)}) %collective-permute-start.1) | collective-permute-done | bytes 131104 | tf_op jit(solution)/shard_map/while/body/eval_jaxpr/ppermute | solution.py:40
  234.0 7.0 %all_gather.8 = bf16[2,32,4096]{2,1,0:T(8,128)(2,1)S(1)} all-gather(bf16[2,8,4096]{2,1,0:T(8,128)(2,1)S(1)} %reshape.236), channel_id=1, replica_groups=mesh['groups'=2,'freq'=4,'recv'=4] {'freq'}, dimensions={1}, use_global_device_ids=true | all-gather | bytes 655360 | tf_op jit(solution)/shard_map/while/body/eval_jaxpr/all_gather | solution.py:106
  244.7 2.9 collective-permute-start.3
  247.6 3.1 collective-permute-done.5
  250.7 5.0 %collective-permute-done.4 = bf16[2,8,8,512]{3,1,2,0:T(8,128)(2,1)S(1)} collective-permute-done((bf16[2,8,8,512]{3,1,2,0:T(8,128)(2,1)S(1)}, bf16[2,8,8,512]{3,1,2,0:T(8,128)(2,1)S(1)}, u32[]{:S(2)}, u32[]{:S(2)}) %collective-permute-start.4) | collective-permute-done | bytes 131104 | tf_op jit(solution)/shard_map/while/body/eval_jaxpr/ppermute | solution.py:40
  256.7 3.6 %fusion.110 = f32[8,16,128]{2,1,0:T(8,128)S(1)} fusion(bf16[8,128,2048]{2,1,0:T(8,128)(2,1)} %get-tuple-element.356, bf16[8,8,2048]{2,1,0:T(8,128)(2,1)S(1)} %bitcast.189, bf16[8,8,2048]{2,1,0:T(8,128)(2,1)S(1)} %bitcast.191), kind=kOutput, calls=%fused_computation.17.clone.1 | convolution fusion | flops 68157440 | bytes 4784128 | tf_op jit(solution)/shard_map/while/body/eval_jaxpr/fbs,frs->fbr/dot_general | solution.py:113
  264.9 2.6 collective-permute-start.8
  280.5 2.9 fusion.118
  289.2 3.1 collective-permute-done
  292.3 8.9 %collective-permute-done.1 = bf16[2,8,8,512]{3,2,1,0:T(8,128)(2,1)S(1)} collective-permute-done((bf16[2,8,8,512]{3,2,1,0:T(8,128)(2,1)S(1)}, bf16[2,8,8,512]{3,2,1,0:T(8,128)(2,1)S(1)}, u32[]{:S(2)}, u32[]{:S(2)}) %collective-permute-start.1) | collective-permute-done | bytes 131104 | tf_op jit(solution)/shard_map/while/body/eval_jaxpr/ppermute | solution.py:40
  301.3 7.0 %all_gather.8 = bf16[2,32,4096]{2,1,0:T(8,128)(2,1)S(1)} all-gather(bf16[2,8,4096]{2,1,0:T(8,128)(2,1)S(1)} %reshape.236), channel_id=1, replica_groups=mesh['groups'=2,'freq'=4,'recv'=4] {'freq'}, dimensions={1}, use_global_device_ids=true | all-gather | bytes 655360 | tf_op jit(solution)/shard_map/while/body/eval_jaxpr/all_gather | solution.py:106
  311.9 2.9 collective-permute-start.3
  314.8 3.2 collective-permute-done.5
  318.0 5.0 %collective-permute-done.4 = bf16[2,8,8,512]{3,1,2,0:T(8,128)(2,1)S(1)} collective-permute-done((bf16[2,8,8,512]{3,1,2,0:T(8,128)(2,1)S(1)}, bf16[2,8,8,512]{3,1,2,0:T(8,128)(2,1)S(1)}, u32[]{:S(2)}, u32[]{:S(2)}) %collective-permute-start.4) | collective-permute-done | bytes 131104 | tf_op jit(solution)/shard_map/while/body/eval_jaxpr/ppermute | solution.py:40
  324.1 3.6 %fusion.110 = f32[8,16,128]{2,1,0:T(8,128)S(1)} fusion(bf16[8,128,2048]{2,1,0:T(8,128)(2,1)} %get-tuple-element.356, bf16[8,8,2048]{2,1,0:T(8,128)(2,1)S(1)} %bitcast.189, bf16[8,8,2048]{2,1,0:T(8,128)(2,1)S(1)} %bitcast.191), kind=kOutput, calls=%fused_computation.17.clone.1 | convolution fusion | flops 68157440 | bytes 4784128 | tf_op jit(solution)/shard_map/while/body/eval_jaxpr/fbs,frs->fbr/dot_general | solution.py:113
  347.7 2.9 fusion.118
  (371 shorter events, 142.5 us)
Async XLA Ops:
  15.2 9.0 %collective-permute-start = (bf16[2,8,8,512]{3,2,1,0:T(8,128)(2,1)S(1)}, bf16[2,8,8,512]{3,2,1,0:T(8,128)(2,1)S(1)}, u32[]{:S(2)}, u32[]{:S(2)}) collective-permute-start(bf16[2,8,8,512]{3,2,1,0:T(8,128)(2,1)S(1)} %get-tuple-element.292), channel_id=1, source_target_pairs={{0,3},{1,0},{2,1},{3,2},{4,7},{5,4},{6,5},{7,6},{8,11},{9,8},{10,9... | collective-permute-start | bytes 393224 | tf_op jit(solution)/shard_map/while/body/eval_jaxpr/ppermute | solution.py:40
  20.3 11.2 %collective-permute-start.1 = (bf16[2,8,8,512]{3,2,1,0:T(8,128)(2,1)S(1)}, bf16[2,8,8,512]{3,2,1,0:T(8,128)(2,1)S(1)}, u32[]{:S(2)}, u32[]{:S(2)}) collective-permute-start(bf16[2,8,8,512]{3,2,1,0:T(8,128)(2,1)S(1)} %get-tuple-element.293), channel_id=1, source_target_pairs={{0,2},{1,3},{2,0},{3,1},{4,6},{5,7},{6,4},{7,5},{8,10},{9,11},{10,... | collective-permute-start | bytes 393224 | tf_op jit(solution)/shard_map/while/body/eval_jaxpr/ppermute | solution.py:40
  20.3 11.2 %collective-permute-start.2 = (bf16[2,8,8,512]{3,2,1,0:T(8,128)(2,1)S(1)}, bf16[2,8,8,512]{3,2,1,0:T(8,128)(2,1)S(1)}, u32[]{:S(2)}, u32[]{:S(2)}) collective-permute-start(bf16[2,8,8,512]{3,2,1,0:T(8,128)(2,1)S(1)} %get-tuple-element.294), channel_id=1, source_target_pairs={{0,1},{1,2},{2,3},{3,0},{4,5},{5,6},{6,7},{7,4},{8,9},{9,10},{10,1... | collective-permute-start | bytes 393224 | tf_op jit(solution)/shard_map/while/body/eval_jaxpr/ppermute | solution.py:40
  40.2 8.3 %collective-permute-start.5 = (bf16[2,8,8,512]{3,1,2,0:T(8,128)(2,1)S(1)}, bf16[2,8,8,512]{3,1,2,0:T(8,128)(2,1)S(1)}, u32[]{:S(2)}, u32[]{:S(2)}) collective-permute-start(bf16[2,8,8,512]{3,1,2,0:T(8,128)(2,1)S(1)} %bitcast.197), channel_id=1, source_target_pairs={{0,1},{1,2},{2,3},{3,0},{4,5},{5,6},{6,7},{7,4},{8,9},{9,10},{10,1... | collective-permute-start | bytes 393224 | tf_op jit(solution)/shard_map/while/body/eval_jaxpr/ppermute | solution.py:40
  40.9 12.6 %collective-permute-start.4 = (bf16[2,8,8,512]{3,1,2,0:T(8,128)(2,1)S(1)}, bf16[2,8,8,512]{3,1,2,0:T(8,128)(2,1)S(1)}, u32[]{:S(2)}, u32[]{:S(2)}) collective-permute-start(bf16[2,8,8,512]{3,1,2,0:T(8,128)(2,1)S(1)} %bitcast.198), channel_id=1, source_target_pairs={{0,2},{1,3},{2,0},{3,1},{4,6},{5,7},{6,4},{7,5},{8,10},{9,11},{10,... | collective-permute-start | bytes 393224 | tf_op jit(solution)/shard_map/while/body/eval_jaxpr/ppermute | solution.py:40
  42.8 10.7 %collective-permute-start.3 = (bf16[2,8,8,512]{3,1,2,0:T(8,128)(2,1)S(1)}, bf16[2,8,8,512]{3,1,2,0:T(8,128)(2,1)S(1)}, u32[]{:S(2)}, u32[]{:S(2)}) collective-permute-start(bf16[2,8,8,512]{3,1,2,0:T(8,128)(2,1)S(1)} %bitcast.199), channel_id=1, source_target_pairs={{0,3},{1,0},{2,1},{3,2},{4,7},{5,4},{6,5},{7,6},{8,11},{9,8},{10,9... | collective-permute-start | bytes 393224 | tf_op jit(solution)/shard_map/while/body/eval_jaxpr/ppermute | solution.py:40
  62.6 5.9 %collective-permute-start.8 = (f32[1,2]{1,0:T(1,128)S(1)}, f32[1,2]{1,0:T(1,128)S(1)}, u32[]{:S(2)}, u32[]{:S(2)}) collective-permute-start(f32[1,2]{1,0:T(1,128)S(1)} %fusion.112), channel_id=1, source_target_pairs={{0,1},{1,2},{2,3},{3,0},{4,5},{5,6},{6,7},{7,4},{8,9},{9,10},{10,1... | collective-permute-start | bytes 32 | tf_op jit(solution)/shard_map/while/body/eval_jaxpr/ppermute | solution.py:40
  65.4 4.4 %collective-permute-start.7 = (f32[1,2]{1,0:T(1,128)S(1)}, f32[1,2]{1,0:T(1,128)S(1)}, u32[]{:S(2)}, u32[]{:S(2)}) collective-permute-start(f32[1,2]{1,0:T(1,128)S(1)} %fusion.112), channel_id=1, source_target_pairs={{0,2},{1,3},{2,0},{3,1},{4,6},{5,7},{6,4},{7,5},{8,10},{9,11},{10,... | collective-permute-start | bytes 32 | tf_op jit(solution)/shard_map/while/body/eval_jaxpr/ppermute | solution.py:40
  67.6 3.5 collective-permute-start.6
  72.0 3.6 %collective-permute-start.10 = (f32[1,2]{1,0:T(1,128)S(1)}, f32[1,2]{1,0:T(1,128)S(1)}, u32[]{:S(2)}, u32[]{:S(2)}) collective-permute-start(f32[1,2]{1,0:T(1,128)S(1)} %bitcast.207), channel_id=1, source_target_pairs={{0,8},{4,12},{8,0},{12,4},{1,9},{5,13},{9,1},{13,5},{2,10},{6,14},... | collective-permute-start | bytes 32 | tf_op jit(solution)/shard_map/while/body/eval_jaxpr/ppermute | solution.py:40
  84.3 6.2 %collective-permute-start = (bf16[2,8,8,512]{3,2,1,0:T(8,128)(2,1)S(1)}, bf16[2,8,8,512]{3,2,1,0:T(8,128)(2,1)S(1)}, u32[]{:S(2)}, u32[]{:S(2)}) collective-permute-start(bf16[2,8,8,512]{3,2,1,0:T(8,128)(2,1)S(1)} %get-tuple-element.292), channel_id=1, source_target_pairs={{0,3},{1,0},{2,1},{3,2},{4,7},{5,4},{6,5},{7,6},{8,11},{9,8},{10,9... | collective-permute-start | bytes 393224 | tf_op jit(solution)/shard_map/while/body/eval_jaxpr/ppermute | solution.py:40
  86.4 12.8 %collective-permute-start.1 = (bf16[2,8,8,512]{3,2,1,0:T(8,128)(2,1)S(1)}, bf16[2,8,8,512]{3,2,1,0:T(8,128)(2,1)S(1)}, u32[]{:S(2)}, u32[]{:S(2)}) collective-permute-start(bf16[2,8,8,512]{3,2,1,0:T(8,128)(2,1)S(1)} %get-tuple-element.293), channel_id=1, source_target_pairs={{0,2},{1,3},{2,0},{3,1},{4,6},{5,7},{6,4},{7,5},{8,10},{9,11},{10,... | collective-permute-start | bytes 393224 | tf_op jit(solution)/shard_map/while/body/eval_jaxpr/ppermute | solution.py:40
  86.4 12.8 %collective-permute-start.2 = (bf16[2,8,8,512]{3,2,1,0:T(8,128)(2,1)S(1)}, bf16[2,8,8,512]{3,2,1,0:T(8,128)(2,1)S(1)}, u32[]{:S(2)}, u32[]{:S(2)}) collective-permute-start(bf16[2,8,8,512]{3,2,1,0:T(8,128)(2,1)S(1)} %get-tuple-element.294), channel_id=1, source_target_pairs={{0,1},{1,2},{2,3},{3,0},{4,5},{5,6},{6,7},{7,4},{8,9},{9,10},{10,1... | collective-permute-start | bytes 393224 | tf_op jit(solution)/shard_map/while/body/eval_jaxpr/ppermute | solution.py:40
  107.8 8.3 %collective-permute-start.5 = (bf16[2,8,8,512]{3,1,2,0:T(8,128)(2,1)S(1)}, bf16[2,8,8,512]{3,1,2,0:T(8,128)(2,1)S(1)}, u32[]{:S(2)}, u32[]{:S(2)}) collective-permute-start(bf16[2,8,8,512]{3,1,2,0:T(8,128)(2,1)S(1)} %bitcast.197), channel_id=1, source_target_pairs={{0,1},{1,2},{2,3},{3,0},{4,5},{5,6},{6,7},{7,4},{8,9},{9,10},{10,1... | collective-permute-start | bytes 393224 | tf_op jit(solution)/shard_map/while/body/eval_jaxpr/ppermute | solution.py:40
  108.2 12.9 %collective-permute-start.4 = (bf16[2,8,8,512]{3,1,2,0:T(8,128)(2,1)S(1)}, bf16[2,8,8,512]{3,1,2,0:T(8,128)(2,1)S(1)}, u32[]{:S(2)}, u32[]{:S(2)}) collective-permute-start(bf16[2,8,8,512]{3,1,2,0:T(8,128)(2,1)S(1)} %bitcast.198), channel_id=1, source_target_pairs={{0,2},{1,3},{2,0},{3,1},{4,6},{5,7},{6,4},{7,5},{8,10},{9,11},{10,... | collective-permute-start | bytes 393224 | tf_op jit(solution)/shard_map/while/body/eval_jaxpr/ppermute | solution.py:40
  110.2 10.9 %collective-permute-start.3 = (bf16[2,8,8,512]{3,1,2,0:T(8,128)(2,1)S(1)}, bf16[2,8,8,512]{3,1,2,0:T(8,128)(2,1)S(1)}, u32[]{:S(2)}, u32[]{:S(2)}) collective-permute-start(bf16[2,8,8,512]{3,1,2,0:T(8,128)(2,1)S(1)} %bitcast.199), channel_id=1, source_target_pairs={{0,3},{1,0},{2,1},{3,2},{4,7},{5,4},{6,5},{7,6},{8,11},{9,8},{10,9... | collective-permute-start | bytes 393224 | tf_op jit(solution)/shard_map/while/body/eval_jaxpr/ppermute | solution.py:40
  130.2 5.6 %collective-permute-start.8 = (f32[1,2]{1,0:T(1,128)S(1)}, f32[1,2]{1,0:T(1,128)S(1)}, u32[]{:S(2)}, u32[]{:S(2)}) collective-permute-start(f32[1,2]{1,0:T(1,128)S(1)} %fusion.112), channel_id=1, source_target_pairs={{0,1},{1,2},{2,3},{3,0},{4,5},{5,6},{6,7},{7,4},{8,9},{9,10},{10,1... | collective-permute-start | bytes 32 | tf_op jit(solution)/shard_map/while/body/eval_jaxpr/ppermute | solution.py:40
  132.8 4.4 %collective-permute-start.7 = (f32[1,2]{1,0:T(1,128)S(1)}, f32[1,2]{1,0:T(1,128)S(1)}, u32[]{:S(2)}, u32[]{:S(2)}) collective-permute-start(f32[1,2]{1,0:T(1,128)S(1)} %fusion.112), channel_id=1, source_target_pairs={{0,2},{1,3},{2,0},{3,1},{4,6},{5,7},{6,4},{7,5},{8,10},{9,11},{10,... | collective-permute-start | bytes 32 | tf_op jit(solution)/shard_map/while/body/eval_jaxpr/ppermute | solution.py:40
  134.9 3.5 collective-permute-start.6
  139.3 3.6 %collective-permute-start.10 = (f32[1,2]{1,0:T(1,128)S(1)}, f32[1,2]{1,0:T(1,128)S(1)}, u32[]{:S(2)}, u32[]{:S(2)}) collective-permute-start(f32[1,2]{1,0:T(1,128)S(1)} %bitcast.207), channel_id=1, source_target_pairs={{0,8},{4,12},{8,0},{12,4},{1,9},{5,13},{9,1},{13,5},{2,10},{6,14},... | collective-permute-start | bytes 32 | tf_op jit(solution)/shard_map/while/body/eval_jaxpr/ppermute | solution.py:40
  151.6 6.2 %collective-permute-start = (bf16[2,8,8,512]{3,2,1,0:T(8,128)(2,1)S(1)}, bf16[2,8,8,512]{3,2,1,0:T(8,128)(2,1)S(1)}, u32[]{:S(2)}, u32[]{:S(2)}) collective-permute-start(bf16[2,8,8,512]{3,2,1,0:T(8,128)(2,1)S(1)} %get-tuple-element.292), channel_id=1, source_target_pairs={{0,3},{1,0},{2,1},{3,2},{4,7},{5,4},{6,5},{7,6},{8,11},{9,8},{10,9... | collective-permute-start | bytes 393224 | tf_op jit(solution)/shard_map/while/body/eval_jaxpr/ppermute | solution.py:40
  153.7 12.8 %collective-permute-start.1 = (bf16[2,8,8,512]{3,2,1,0:T(8,128)(2,1)S(1)}, bf16[2,8,8,512]{3,2,1,0:T(8,128)(2,1)S(1)}, u32[]{:S(2)}, u32[]{:S(2)}) collective-permute-start(bf16[2,8,8,512]{3,2,1,0:T(8,128)(2,1)S(1)} %get-tuple-element.293), channel_id=1, source_target_pairs={{0,2},{1,3},{2,0},{3,1},{4,6},{5,7},{6,4},{7,5},{8,10},{9,11},{10,... | collective-permute-start | bytes 393224 | tf_op jit(solution)/shard_map/while/body/eval_jaxpr/ppermute | solution.py:40
  153.7 12.8 %collective-permute-start.2 = (bf16[2,8,8,512]{3,2,1,0:T(8,128)(2,1)S(1)}, bf16[2,8,8,512]{3,2,1,0:T(8,128)(2,1)S(1)}, u32[]{:S(2)}, u32[]{:S(2)}) collective-permute-start(bf16[2,8,8,512]{3,2,1,0:T(8,128)(2,1)S(1)} %get-tuple-element.294), channel_id=1, source_target_pairs={{0,1},{1,2},{2,3},{3,0},{4,5},{5,6},{6,7},{7,4},{8,9},{9,10},{10,1... | collective-permute-start | bytes 393224 | tf_op jit(solution)/shard_map/while/body/eval_jaxpr/ppermute | solution.py:40
  175.1 8.3 %collective-permute-start.5 = (bf16[2,8,8,512]{3,1,2,0:T(8,128)(2,1)S(1)}, bf16[2,8,8,512]{3,1,2,0:T(8,128)(2,1)S(1)}, u32[]{:S(2)}, u32[]{:S(2)}) collective-permute-start(bf16[2,8,8,512]{3,1,2,0:T(8,128)(2,1)S(1)} %bitcast.197), channel_id=1, source_target_pairs={{0,1},{1,2},{2,3},{3,0},{4,5},{5,6},{6,7},{7,4},{8,9},{9,10},{10,1... | collective-permute-start | bytes 393224 | tf_op jit(solution)/shard_map/while/body/eval_jaxpr/ppermute | solution.py:40
  175.6 12.9 %collective-permute-start.4 = (bf16[2,8,8,512]{3,1,2,0:T(8,128)(2,1)S(1)}, bf16[2,8,8,512]{3,1,2,0:T(8,128)(2,1)S(1)}, u32[]{:S(2)}, u32[]{:S(2)}) collective-permute-start(bf16[2,8,8,512]{3,1,2,0:T(8,128)(2,1)S(1)} %bitcast.198), channel_id=1, source_target_pairs={{0,2},{1,3},{2,0},{3,1},{4,6},{5,7},{6,4},{7,5},{8,10},{9,11},{10,... | collective-permute-start | bytes 393224 | tf_op jit(solution)/shard_map/while/body/eval_jaxpr/ppermute | solution.py:40
  177.4 11.0 %collective-permute-start.3 = (bf16[2,8,8,512]{3,1,2,0:T(8,128)(2,1)S(1)}, bf16[2,8,8,512]{3,1,2,0:T(8,128)(2,1)S(1)}, u32[]{:S(2)}, u32[]{:S(2)}) collective-permute-start(bf16[2,8,8,512]{3,1,2,0:T(8,128)(2,1)S(1)} %bitcast.199), channel_id=1, source_target_pairs={{0,3},{1,0},{2,1},{3,2},{4,7},{5,4},{6,5},{7,6},{8,11},{9,8},{10,9... | collective-permute-start | bytes 393224 | tf_op jit(solution)/shard_map/while/body/eval_jaxpr/ppermute | solution.py:40
  197.6 5.6 %collective-permute-start.8 = (f32[1,2]{1,0:T(1,128)S(1)}, f32[1,2]{1,0:T(1,128)S(1)}, u32[]{:S(2)}, u32[]{:S(2)}) collective-permute-start(f32[1,2]{1,0:T(1,128)S(1)} %fusion.112), channel_id=1, source_target_pairs={{0,1},{1,2},{2,3},{3,0},{4,5},{5,6},{6,7},{7,4},{8,9},{9,10},{10,1... | collective-permute-start | bytes 32 | tf_op jit(solution)/shard_map/while/body/eval_jaxpr/ppermute | solution.py:40
  200.1 4.4 %collective-permute-start.7 = (f32[1,2]{1,0:T(1,128)S(1)}, f32[1,2]{1,0:T(1,128)S(1)}, u32[]{:S(2)}, u32[]{:S(2)}) collective-permute-start(f32[1,2]{1,0:T(1,128)S(1)} %fusion.112), channel_id=1, source_target_pairs={{0,2},{1,3},{2,0},{3,1},{4,6},{5,7},{6,4},{7,5},{8,10},{9,11},{10,... | collective-permute-start | bytes 32 | tf_op jit(solution)/shard_map/while/body/eval_jaxpr/ppermute | solution.py:40
  202.2 3.5 collective-permute-start.6
  206.6 3.6 %collective-permute-start.10 = (f32[1,2]{1,0:T(1,128)S(1)}, f32[1,2]{1,0:T(1,128)S(1)}, u32[]{:S(2)}, u32[]{:S(2)}) collective-permute-start(f32[1,2]{1,0:T(1,128)S(1)} %bitcast.207), channel_id=1, source_target_pairs={{0,8},{4,12},{8,0},{12,4},{1,9},{5,13},{9,1},{13,5},{2,10},{6,14},... | collective-permute-start | bytes 32 | tf_op jit(solution)/shard_map/while/body/eval_jaxpr/ppermute | solution.py:40
  218.9 6.2 %collective-permute-start = (bf16[2,8,8,512]{3,2,1,0:T(8,128)(2,1)S(1)}, bf16[2,8,8,512]{3,2,1,0:T(8,128)(2,1)S(1)}, u32[]{:S(2)}, u32[]{:S(2)}) collective-permute-start(bf16[2,8,8,512]{3,2,1,0:T(8,128)(2,1)S(1)} %get-tuple-element.292), channel_id=1, source_target_pairs={{0,3},{1,0},{2,1},{3,2},{4,7},{5,4},{6,5},{7,6},{8,11},{9,8},{10,9... | collective-permute-start | bytes 393224 | tf_op jit(solution)/shard_map/while/body/eval_jaxpr/ppermute | solution.py:40
  221.1 12.8 %collective-permute-start.1 = (bf16[2,8,8,512]{3,2,1,0:T(8,128)(2,1)S(1)}, bf16[2,8,8,512]{3,2,1,0:T(8,128)(2,1)S(1)}, u32[]{:S(2)}, u32[]{:S(2)}) collective-permute-start(bf16[2,8,8,512]{3,2,1,0:T(8,128)(2,1)S(1)} %get-tuple-element.293), channel_id=1, source_target_pairs={{0,2},{1,3},{2,0},{3,1},{4,6},{5,7},{6,4},{7,5},{8,10},{9,11},{10,... | collective-permute-start | bytes 393224 | tf_op jit(solution)/shard_map/while/body/eval_jaxpr/ppermute | solution.py:40
  221.1 12.8 %collective-permute-start.2 = (bf16[2,8,8,512]{3,2,1,0:T(8,128)(2,1)S(1)}, bf16[2,8,8,512]{3,2,1,0:T(8,128)(2,1)S(1)}, u32[]{:S(2)}, u32[]{:S(2)}) collective-permute-start(bf16[2,8,8,512]{3,2,1,0:T(8,128)(2,1)S(1)} %get-tuple-element.294), channel_id=1, source_target_pairs={{0,1},{1,2},{2,3},{3,0},{4,5},{5,6},{6,7},{7,4},{8,9},{9,10},{10,1... | collective-permute-start | bytes 393224 | tf_op jit(solution)/shard_map/while/body/eval_jaxpr/ppermute | solution.py:40
  242.4 8.3 %collective-permute-start.5 = (bf16[2,8,8,512]{3,1,2,0:T(8,128)(2,1)S(1)}, bf16[2,8,8,512]{3,1,2,0:T(8,128)(2,1)S(1)}, u32[]{:S(2)}, u32[]{:S(2)}) collective-permute-start(bf16[2,8,8,512]{3,1,2,0:T(8,128)(2,1)S(1)} %bitcast.197), channel_id=1, source_target_pairs={{0,1},{1,2},{2,3},{3,0},{4,5},{5,6},{6,7},{7,4},{8,9},{9,10},{10,1... | collective-permute-start | bytes 393224 | tf_op jit(solution)/shard_map/while/body/eval_jaxpr/ppermute | solution.py:40
  242.9 12.8 %collective-permute-start.4 = (bf16[2,8,8,512]{3,1,2,0:T(8,128)(2,1)S(1)}, bf16[2,8,8,512]{3,1,2,0:T(8,128)(2,1)S(1)}, u32[]{:S(2)}, u32[]{:S(2)}) collective-permute-start(bf16[2,8,8,512]{3,1,2,0:T(8,128)(2,1)S(1)} %bitcast.198), channel_id=1, source_target_pairs={{0,2},{1,3},{2,0},{3,1},{4,6},{5,7},{6,4},{7,5},{8,10},{9,11},{10,... | collective-permute-start | bytes 393224 | tf_op jit(solution)/shard_map/while/body/eval_jaxpr/ppermute | solution.py:40
  244.7 11.1 %collective-permute-start.3 = (bf16[2,8,8,512]{3,1,2,0:T(8,128)(2,1)S(1)}, bf16[2,8,8,512]{3,1,2,0:T(8,128)(2,1)S(1)}, u32[]{:S(2)}, u32[]{:S(2)}) collective-permute-start(bf16[2,8,8,512]{3,1,2,0:T(8,128)(2,1)S(1)} %bitcast.199), channel_id=1, source_target_pairs={{0,3},{1,0},{2,1},{3,2},{4,7},{5,4},{6,5},{7,6},{8,11},{9,8},{10,9... | collective-permute-start | bytes 393224 | tf_op jit(solution)/shard_map/while/body/eval_jaxpr/ppermute | solution.py:40
  264.9 5.5 %collective-permute-start.8 = (f32[1,2]{1,0:T(1,128)S(1)}, f32[1,2]{1,0:T(1,128)S(1)}, u32[]{:S(2)}, u32[]{:S(2)}) collective-permute-start(f32[1,2]{1,0:T(1,128)S(1)} %fusion.112), channel_id=1, source_target_pairs={{0,1},{1,2},{2,3},{3,0},{4,5},{5,6},{6,7},{7,4},{8,9},{9,10},{10,1... | collective-permute-start | bytes 32 | tf_op jit(solution)/shard_map/while/body/eval_jaxpr/ppermute | solution.py:40
  267.5 4.4 %collective-permute-start.7 = (f32[1,2]{1,0:T(1,128)S(1)}, f32[1,2]{1,0:T(1,128)S(1)}, u32[]{:S(2)}, u32[]{:S(2)}) collective-permute-start(f32[1,2]{1,0:T(1,128)S(1)} %fusion.112), channel_id=1, source_target_pairs={{0,2},{1,3},{2,0},{3,1},{4,6},{5,7},{6,4},{7,5},{8,10},{9,11},{10,... | collective-permute-start | bytes 32 | tf_op jit(solution)/shard_map/while/body/eval_jaxpr/ppermute | solution.py:40
  273.8 3.6 %collective-permute-start.10 = (f32[1,2]{1,0:T(1,128)S(1)}, f32[1,2]{1,0:T(1,128)S(1)}, u32[]{:S(2)}, u32[]{:S(2)}) collective-permute-start(f32[1,2]{1,0:T(1,128)S(1)} %bitcast.207), channel_id=1, source_target_pairs={{0,8},{4,12},{8,0},{12,4},{1,9},{5,13},{9,1},{13,5},{2,10},{6,14},... | collective-permute-start | bytes 32 | tf_op jit(solution)/shard_map/while/body/eval_jaxpr/ppermute | solution.py:40
  286.1 6.2 %collective-permute-start = (bf16[2,8,8,512]{3,2,1,0:T(8,128)(2,1)S(1)}, bf16[2,8,8,512]{3,2,1,0:T(8,128)(2,1)S(1)}, u32[]{:S(2)}, u32[]{:S(2)}) collective-permute-start(bf16[2,8,8,512]{3,2,1,0:T(8,128)(2,1)S(1)} %get-tuple-element.292), channel_id=1, source_target_pairs={{0,3},{1,0},{2,1},{3,2},{4,7},{5,4},{6,5},{7,6},{8,11},{9,8},{10,9... | collective-permute-start | bytes 393224 | tf_op jit(solution)/shard_map/while/body/eval_jaxpr/ppermute | solution.py:40
  288.4 12.8 %collective-permute-start.1 = (bf16[2,8,8,512]{3,2,1,0:T(8,128)(2,1)S(1)}, bf16[2,8,8,512]{3,2,1,0:T(8,128)(2,1)S(1)}, u32[]{:S(2)}, u32[]{:S(2)}) collective-permute-start(bf16[2,8,8,512]{3,2,1,0:T(8,128)(2,1)S(1)} %get-tuple-element.293), channel_id=1, source_target_pairs={{0,2},{1,3},{2,0},{3,1},{4,6},{5,7},{6,4},{7,5},{8,10},{9,11},{10,... | collective-permute-start | bytes 393224 | tf_op jit(solution)/shard_map/while/body/eval_jaxpr/ppermute | solution.py:40
  288.4 12.8 %collective-permute-start.2 = (bf16[2,8,8,512]{3,2,1,0:T(8,128)(2,1)S(1)}, bf16[2,8,8,512]{3,2,1,0:T(8,128)(2,1)S(1)}, u32[]{:S(2)}, u32[]{:S(2)}) collective-permute-start(bf16[2,8,8,512]{3,2,1,0:T(8,128)(2,1)S(1)} %get-tuple-element.294), channel_id=1, source_target_pairs={{0,1},{1,2},{2,3},{3,0},{4,5},{5,6},{6,7},{7,4},{8,9},{9,10},{10,1... | collective-permute-start | bytes 393224 | tf_op jit(solution)/shard_map/while/body/eval_jaxpr/ppermute | solution.py:40
  309.8 8.3 %collective-permute-start.5 = (bf16[2,8,8,512]{3,1,2,0:T(8,128)(2,1)S(1)}, bf16[2,8,8,512]{3,1,2,0:T(8,128)(2,1)S(1)}, u32[]{:S(2)}, u32[]{:S(2)}) collective-permute-start(bf16[2,8,8,512]{3,1,2,0:T(8,128)(2,1)S(1)} %bitcast.197), channel_id=1, source_target_pairs={{0,1},{1,2},{2,3},{3,0},{4,5},{5,6},{6,7},{7,4},{8,9},{9,10},{10,1... | collective-permute-start | bytes 393224 | tf_op jit(solution)/shard_map/while/body/eval_jaxpr/ppermute | solution.py:40
  310.2 12.9 %collective-permute-start.4 = (bf16[2,8,8,512]{3,1,2,0:T(8,128)(2,1)S(1)}, bf16[2,8,8,512]{3,1,2,0:T(8,128)(2,1)S(1)}, u32[]{:S(2)}, u32[]{:S(2)}) collective-permute-start(bf16[2,8,8,512]{3,1,2,0:T(8,128)(2,1)S(1)} %bitcast.198), channel_id=1, source_target_pairs={{0,2},{1,3},{2,0},{3,1},{4,6},{5,7},{6,4},{7,5},{8,10},{9,11},{10,... | collective-permute-start | bytes 393224 | tf_op jit(solution)/shard_map/while/body/eval_jaxpr/ppermute | solution.py:40
  311.9 11.2 %collective-permute-start.3 = (bf16[2,8,8,512]{3,1,2,0:T(8,128)(2,1)S(1)}, bf16[2,8,8,512]{3,1,2,0:T(8,128)(2,1)S(1)}, u32[]{:S(2)}, u32[]{:S(2)}) collective-permute-start(bf16[2,8,8,512]{3,1,2,0:T(8,128)(2,1)S(1)} %bitcast.199), channel_id=1, source_target_pairs={{0,3},{1,0},{2,1},{3,2},{4,7},{5,4},{6,5},{7,6},{8,11},{9,8},{10,9... | collective-permute-start | bytes 393224 | tf_op jit(solution)/shard_map/while/body/eval_jaxpr/ppermute | solution.py:40
  332.2 5.4 %collective-permute-start.8 = (f32[1,2]{1,0:T(1,128)S(1)}, f32[1,2]{1,0:T(1,128)S(1)}, u32[]{:S(2)}, u32[]{:S(2)}) collective-permute-start(f32[1,2]{1,0:T(1,128)S(1)} %fusion.112), channel_id=1, source_target_pairs={{0,1},{1,2},{2,3},{3,0},{4,5},{5,6},{6,7},{7,4},{8,9},{9,10},{10,1... | collective-permute-start | bytes 32 | tf_op jit(solution)/shard_map/while/body/eval_jaxpr/ppermute | solution.py:40
  334.7 4.4 %collective-permute-start.7 = (f32[1,2]{1,0:T(1,128)S(1)}, f32[1,2]{1,0:T(1,128)S(1)}, u32[]{:S(2)}, u32[]{:S(2)}) collective-permute-start(f32[1,2]{1,0:T(1,128)S(1)} %fusion.112), channel_id=1, source_target_pairs={{0,2},{1,3},{2,0},{3,1},{4,6},{5,7},{6,4},{7,5},{8,10},{9,11},{10,... | collective-permute-start | bytes 32 | tf_op jit(solution)/shard_map/while/body/eval_jaxpr/ppermute | solution.py:40
  341.0 3.6 %collective-permute-start.10 = (f32[1,2]{1,0:T(1,128)S(1)}, f32[1,2]{1,0:T(1,128)S(1)}, u32[]{:S(2)}, u32[]{:S(2)}) collective-permute-start(f32[1,2]{1,0:T(1,128)S(1)} %bitcast.207), channel_id=1, source_target_pairs={{0,8},{4,12},{8,0},{12,4},{1,9},{5,13},{9,1},{13,5},{2,10},{6,14},... | collective-permute-start | bytes 32 | tf_op jit(solution)/shard_map/while/body/eval_jaxpr/ppermute | solution.py:40
  (34 other events, 97.2 us)

commit v11 on v7

--- a/solution.py
+++ b/solution.py
@@ -72,6 +72,8 @@
 
     cos_part, sin_part = dft_rows(jnp.arange(total_freq, dtype=jnp.int32), total_freq)
     to_time = jnp.block([[cos_part.T, -sin_part.T], [sin_part.T, cos_part.T]])
+    time_high = lax.reduce_precision(to_time, exponent_bits=8, mantissa_bits=7)
+    time_split = jnp.concatenate([time_high, to_time - time_high]).astype(jnp.bfloat16)
     own_rows = lax.axis_index("freq") * freq_local + jnp.arange(freq_local, dtype=jnp.int32)
     cos_rows, sin_rows = dft_rows(own_rows, total_freq)
     to_freq = jnp.block([[cos_rows, sin_rows], [-sin_rows, cos_rows]])
@@ -96,8 +98,11 @@
             jnp.stack([partial_real, partial_imag]).astype(jnp.bfloat16), "recv", 3
         )
         flattened = gradient.astype(jnp.bfloat16).reshape(2, freq_local, columns)
-        segment = lax.all_gather(flattened, "freq", axis=1, tiled=True).astype(jnp.float32)
-        timed = high_dot(to_time, segment.reshape(2 * total_freq, columns))
+        segment = lax.all_gather(flattened, "freq", axis=1, tiled=True)
+        both = jnp.dot(
+            time_split, segment.reshape(2 * total_freq, columns), preferred_element_type=jnp.float32
+        )
+        timed = both[: 2 * total_freq] + both[2 * total_freq :]
         projected = high_dot(to_freq, timed * window)
         direction = projected.reshape(2, freq_local, right_sides, src_local)
         rounded_direction = direction.astype(jnp.bfloat16)

time: 332 us -> 332 us (level)
    dot_general x10 -> x5, matrix products: 13.1 us -> 11.3 us  [high_dot(): return jnp.dot(left, right, precision=lax.Precision.HIGH)]
where the time goes in v11:
time: 332 us
  waiting for transfers between devices  129 us (39%)
  starting transfers between devices  57.4 us (17%)
  matrix products  55.4 us (17%)
  blocking collectives  33.5 us (10%)
  other arithmetic  24.8 us (7%)
  local copies, waits for them, and re-layouts  23 us (7%)
  loops' own time  7.79 us (2%)
    ppermute x60, waiting for transfers between devices, shifted(): lax.ppermute(value, axis, [(i, (i + distance) % size) for i in range(size)])  129 us
    ppermute x60, starting transfers between devices, shifted(): lax.ppermute(value, axis, [(i, (i + distance) % size) for i in range(size)])  57.4 us
    all_gather x5, blocking collectives, step(): segment = lax.all_gather(flattened, 'freq', axis=1, tiled=True)  33.5 us
    dot_general x5, matrix products, step(): jnp.einsum('fbs,frs->fbr', stacked_direction, imag_operator, preferred_el...  17.8 us
    dot_general x5, matrix products, step(): jnp.einsum('fbr,frs->fbs', stacked_residual, imag_operator, preferred_ele...  15 us
    dot_general x5, matrix products, high_dot(): return jnp.dot(left, right, precision=lax.Precision.HIGH)  11.3 us
    gather x25, local copies, waits for them, and re-layouts, gather_blocks(): ordered = jnp.take(slots, order, axis=dim)  9.43 us
    another operation x1, loops' own time, on_device(): return lax.fori_loop(0, ITERS, step, (reflect, recorded))  7.79 us
  transfers between devices with their start and end apart: 60, of which 36 were waited for; matrix products, arithmetic and copies ran while one was open for 2% of the time, Pallas kernels for 0%

profile of v11, /device:TPU:0, one launch (start us, length us, event | category | flops | bytes accessed | tf_op | source)
XLA Modules:
  0.0 331.7 jit_solution(11696247945485866076)
XLA Ops:
  0.7 6.1 %slice_bitcast_fusion.2 = (bf16[8,128,2048]{2,1,0:T(8,128)(2,1)}, bf16[8,128,2048]{2,1,0:T(8,128)(2,1)}) fusion(bf16[2,8,128,2048]{3,2,1,0:T(8,128)(2,1)} %param.8), kind=kLoop, calls=%fused_computation.86 | loop fusion | bytes 16777216 | tf_op jit(solution)/shard_map/squeeze | solution.py:71
  10.5 320.3 %while.15 = (s32[]{:T(128)}, f32[2,8,8,512]{3,1,2,0:T(8,128)S(1)}, f32[2,8,8,128]{3,2,1,0:T(8,128)S(1)}, bf16[8,128,2048]{2,1,0:T(8,128)(2,1)}, bf16[8,128,2048]...) while((s32[]{:T(128)}, f32[2,8,8,512]{3,1,2,0:T(8,128)S(1)}, ...), condition=%wide.region_7.9_spmd.clone, body=%wide.region_2.8_spmd.clone.sunk | while | flops 366349728 | bytes 75696280 | solution.py:127
  10.6 3.0 fusion.104
  14.8 5.1 %collective-permute-start = (bf16[2,8,8,512]{3,2,1,0:T(8,128)(2,1)S(1)}, bf16[2,8,8,512]{3,2,1,0:T(8,128)(2,1)S(1)}, u32[]{:S(2)}, u32[]{:S(2)}) collective-permute-start(bf16[2,8,8,512]{3,2,1,0:T(8,128)(2,1)S(1)} %get-tuple-element.255), channel_id=1, source_target_pairs={{0,3},{1,0},{2,1},{3,2},{4,7},{5,4},{6,5},{7,6},{8,11},{9,8},{10,9... | collective-permute-start | bytes 393224 | tf_op jit(solution)/shard_map/while/body/eval_jaxpr/ppermute | solution.py:40
  21.0 2.8 collective-permute-done
  23.8 7.3 %collective-permute-done.1 = bf16[2,8,8,512]{3,2,1,0:T(8,128)(2,1)S(1)} collective-permute-done((bf16[2,8,8,512]{3,2,1,0:T(8,128)(2,1)S(1)}, bf16[2,8,8,512]{3,2,1,0:T(8,128)(2,1)S(1)}, u32[]{:S(2)}, u32[]{:S(2)}) %collective-permute-start.1) | collective-permute-done | bytes 131104 | tf_op jit(solution)/shard_map/while/body/eval_jaxpr/ppermute | solution.py:40
  31.3 7.2 %all_gather.8 = bf16[2,32,4096]{2,1,0:T(8,128)(2,1)S(1)} all-gather(bf16[2,8,4096]{2,1,0:T(8,128)(2,1)S(1)} %reshape.245), channel_id=1, replica_groups=mesh['groups'=2,'freq'=4,'recv'=4] {'freq'}, dimensions={1}, use_global_device_ids=true | all-gather | bytes 655360 | tf_op jit(solution)/shard_map/while/body/eval_jaxpr/all_gather | solution.py:101
  38.9 2.3 multiply_reduce_fusion.4
  43.8 2.0 collective-permute-start.5
  46.9 9.3 %collective-permute-done.4 = bf16[2,8,8,512]{3,1,2,0:T(8,128)(2,1)S(1)} collective-permute-done((bf16[2,8,8,512]{3,1,2,0:T(8,128)(2,1)S(1)}, bf16[2,8,8,512]{3,1,2,0:T(8,128)(2,1)S(1)}, u32[]{:S(2)}, u32[]{:S(2)}) %collective-permute-start.4) | collective-permute-done | bytes 131104 | tf_op jit(solution)/shard_map/while/body/eval_jaxpr/ppermute | solution.py:40
  57.2 3.6 %fusion.111 = f32[8,16,128]{2,1,0:T(8,128)S(1)} fusion(bf16[8,128,2048]{2,1,0:T(8,128)(2,1)} %get-tuple-element.305, bf16[8,8,2048]{2,1,0:T(8,128)(2,1)S(1)} %bitcast.163, bf16[8,8,2048]{2,1,0:T(8,128)(2,1)S(1)} %bitcast.165), kind=kOutput, calls=%fused_computation.23.clone.1 | convolution fusion | flops 68157440 | bytes 4784128 | tf_op jit(solution)/shard_map/while/body/eval_jaxpr/fbs,frs->fbr/dot_general | solution.py:114
  73.2 2.3 collective-permute-done.10
  78.7 3.0 fusion.104
  85.1 3.1 collective-permute-done
  88.2 7.7 %collective-permute-done.1 = bf16[2,8,8,512]{3,2,1,0:T(8,128)(2,1)S(1)} collective-permute-done((bf16[2,8,8,512]{3,2,1,0:T(8,128)(2,1)S(1)}, bf16[2,8,8,512]{3,2,1,0:T(8,128)(2,1)S(1)}, u32[]{:S(2)}, u32[]{:S(2)}) %collective-permute-start.1) | collective-permute-done | bytes 131104 | tf_op jit(solution)/shard_map/while/body/eval_jaxpr/ppermute | solution.py:40
  96.1 6.5 %all_gather.8 = bf16[2,32,4096]{2,1,0:T(8,128)(2,1)S(1)} all-gather(bf16[2,8,4096]{2,1,0:T(8,128)(2,1)S(1)} %reshape.245), channel_id=1, replica_groups=mesh['groups'=2,'freq'=4,'recv'=4] {'freq'}, dimensions={1}, use_global_device_ids=true | all-gather | bytes 655360 | tf_op jit(solution)/shard_map/while/body/eval_jaxpr/all_gather | solution.py:101
  103.0 2.3 multiply_reduce_fusion.4
  108.9 3.0 collective-permute-done.3
  111.9 7.4 %collective-permute-done.4 = bf16[2,8,8,512]{3,1,2,0:T(8,128)(2,1)S(1)} collective-permute-done((bf16[2,8,8,512]{3,1,2,0:T(8,128)(2,1)S(1)}, bf16[2,8,8,512]{3,1,2,0:T(8,128)(2,1)S(1)}, u32[]{:S(2)}, u32[]{:S(2)}) %collective-permute-start.4) | collective-permute-done | bytes 131104 | tf_op jit(solution)/shard_map/while/body/eval_jaxpr/ppermute | solution.py:40
  120.3 3.6 %fusion.111 = f32[8,16,128]{2,1,0:T(8,128)S(1)} fusion(bf16[8,128,2048]{2,1,0:T(8,128)(2,1)} %get-tuple-element.305, bf16[8,8,2048]{2,1,0:T(8,128)(2,1)S(1)} %bitcast.163, bf16[8,8,2048]{2,1,0:T(8,128)(2,1)S(1)} %bitcast.165), kind=kOutput, calls=%fused_computation.23.clone.1 | convolution fusion | flops 68157440 | bytes 4784128 | tf_op jit(solution)/shard_map/while/body/eval_jaxpr/fbs,frs->fbr/dot_general | solution.py:114
  136.1 2.2 collective-permute-done.10
  141.8 3.0 fusion.104
  148.3 3.1 collective-permute-done
  151.4 7.6 %collective-permute-done.1 = bf16[2,8,8,512]{3,2,1,0:T(8,128)(2,1)S(1)} collective-permute-done((bf16[2,8,8,512]{3,2,1,0:T(8,128)(2,1)S(1)}, bf16[2,8,8,512]{3,2,1,0:T(8,128)(2,1)S(1)}, u32[]{:S(2)}, u32[]{:S(2)}) %collective-permute-start.1) | collective-permute-done | bytes 131104 | tf_op jit(solution)/shard_map/while/body/eval_jaxpr/ppermute | solution.py:40
  159.2 6.6 %all_gather.8 = bf16[2,32,4096]{2,1,0:T(8,128)(2,1)S(1)} all-gather(bf16[2,8,4096]{2,1,0:T(8,128)(2,1)S(1)} %reshape.245), channel_id=1, replica_groups=mesh['groups'=2,'freq'=4,'recv'=4] {'freq'}, dimensions={1}, use_global_device_ids=true | all-gather | bytes 655360 | tf_op jit(solution)/shard_map/while/body/eval_jaxpr/all_gather | solution.py:101
  166.2 2.3 multiply_reduce_fusion.4
  171.9 3.2 collective-permute-done.3
  175.2 7.2 %collective-permute-done.4 = bf16[2,8,8,512]{3,1,2,0:T(8,128)(2,1)S(1)} collective-permute-done((bf16[2,8,8,512]{3,1,2,0:T(8,128)(2,1)S(1)}, bf16[2,8,8,512]{3,1,2,0:T(8,128)(2,1)S(1)}, u32[]{:S(2)}, u32[]{:S(2)}) %collective-permute-start.4) | collective-permute-done | bytes 131104 | tf_op jit(solution)/shard_map/while/body/eval_jaxpr/ppermute | solution.py:40
  183.3 3.6 %fusion.111 = f32[8,16,128]{2,1,0:T(8,128)S(1)} fusion(bf16[8,128,2048]{2,1,0:T(8,128)(2,1)} %get-tuple-element.305, bf16[8,8,2048]{2,1,0:T(8,128)(2,1)S(1)} %bitcast.163, bf16[8,8,2048]{2,1,0:T(8,128)(2,1)S(1)} %bitcast.165), kind=kOutput, calls=%fused_computation.23.clone.1 | convolution fusion | flops 68157440 | bytes 4784128 | tf_op jit(solution)/shard_map/while/body/eval_jaxpr/fbs,frs->fbr/dot_general | solution.py:114
  199.2 2.3 collective-permute-done.10
  204.9 3.0 fusion.104
  211.3 3.1 collective-permute-done
  214.4 7.7 %collective-permute-done.1 = bf16[2,8,8,512]{3,2,1,0:T(8,128)(2,1)S(1)} collective-permute-done((bf16[2,8,8,512]{3,2,1,0:T(8,128)(2,1)S(1)}, bf16[2,8,8,512]{3,2,1,0:T(8,128)(2,1)S(1)}, u32[]{:S(2)}, u32[]{:S(2)}) %collective-permute-start.1) | collective-permute-done | bytes 131104 | tf_op jit(solution)/shard_map/while/body/eval_jaxpr/ppermute | solution.py:40
  222.2 6.5 %all_gather.8 = bf16[2,32,4096]{2,1,0:T(8,128)(2,1)S(1)} all-gather(bf16[2,8,4096]{2,1,0:T(8,128)(2,1)S(1)} %reshape.245), channel_id=1, replica_groups=mesh['groups'=2,'freq'=4,'recv'=4] {'freq'}, dimensions={1}, use_global_device_ids=true | all-gather | bytes 655360 | tf_op jit(solution)/shard_map/while/body/eval_jaxpr/all_gather | solution.py:101
  229.2 2.3 multiply_reduce_fusion.4
  234.9 3.1 collective-permute-done.3
  238.1 7.3 %collective-permute-done.4 = bf16[2,8,8,512]{3,1,2,0:T(8,128)(2,1)S(1)} collective-permute-done((bf16[2,8,8,512]{3,1,2,0:T(8,128)(2,1)S(1)}, bf16[2,8,8,512]{3,1,2,0:T(8,128)(2,1)S(1)}, u32[]{:S(2)}, u32[]{:S(2)}) %collective-permute-start.4) | collective-permute-done | bytes 131104 | tf_op jit(solution)/shard_map/while/body/eval_jaxpr/ppermute | solution.py:40
  246.3 3.6 %fusion.111 = f32[8,16,128]{2,1,0:T(8,128)S(1)} fusion(bf16[8,128,2048]{2,1,0:T(8,128)(2,1)} %get-tuple-element.305, bf16[8,8,2048]{2,1,0:T(8,128)(2,1)S(1)} %bitcast.163, bf16[8,8,2048]{2,1,0:T(8,128)(2,1)S(1)} %bitcast.165), kind=kOutput, calls=%fused_computation.23.clone.1 | convolution fusion | flops 68157440 | bytes 4784128 | tf_op jit(solution)/shard_map/while/body/eval_jaxpr/fbs,frs->fbr/dot_general | solution.py:114
  262.3 2.2 collective-permute-done.10
  268.0 3.0 fusion.104
  274.4 3.1 collective-permute-done
  277.5 7.6 %collective-permute-done.1 = bf16[2,8,8,512]{3,2,1,0:T(8,128)(2,1)S(1)} collective-permute-done((bf16[2,8,8,512]{3,2,1,0:T(8,128)(2,1)S(1)}, bf16[2,8,8,512]{3,2,1,0:T(8,128)(2,1)S(1)}, u32[]{:S(2)}, u32[]{:S(2)}) %collective-permute-start.1) | collective-permute-done | bytes 131104 | tf_op jit(solution)/shard_map/while/body/eval_jaxpr/ppermute | solution.py:40
  285.2 6.7 %all_gather.8 = bf16[2,32,4096]{2,1,0:T(8,128)(2,1)S(1)} all-gather(bf16[2,8,4096]{2,1,0:T(8,128)(2,1)S(1)} %reshape.245), channel_id=1, replica_groups=mesh['groups'=2,'freq'=4,'recv'=4] {'freq'}, dimensions={1}, use_global_device_ids=true | all-gather | bytes 655360 | tf_op jit(solution)/shard_map/while/body/eval_jaxpr/all_gather | solution.py:101
  292.3 2.3 multiply_reduce_fusion.4
  298.0 3.3 collective-permute-done.3
  301.3 7.1 %collective-permute-done.4 = bf16[2,8,8,512]{3,1,2,0:T(8,128)(2,1)S(1)} collective-permute-done((bf16[2,8,8,512]{3,1,2,0:T(8,128)(2,1)S(1)}, bf16[2,8,8,512]{3,1,2,0:T(8,128)(2,1)S(1)}, u32[]{:S(2)}, u32[]{:S(2)}) %collective-permute-start.4) | collective-permute-done | bytes 131104 | tf_op jit(solution)/shard_map/while/body/eval_jaxpr/ppermute | solution.py:40
  309.4 3.6 %fusion.111 = f32[8,16,128]{2,1,0:T(8,128)S(1)} fusion(bf16[8,128,2048]{2,1,0:T(8,128)(2,1)} %get-tuple-element.305, bf16[8,8,2048]{2,1,0:T(8,128)(2,1)S(1)} %bitcast.163, bf16[8,8,2048]{2,1,0:T(8,128)(2,1)S(1)} %bitcast.165), kind=kOutput, calls=%fused_computation.23.clone.1 | convolution fusion | flops 68157440 | bytes 4784128 | tf_op jit(solution)/shard_map/while/body/eval_jaxpr/fbs,frs->fbr/dot_general | solution.py:114
  325.3 2.3 collective-permute-done.10
  (327 shorter events, 117.2 us)
Async XLA Ops:
  14.8 9.0 %collective-permute-start = (bf16[2,8,8,512]{3,2,1,0:T(8,128)(2,1)S(1)}, bf16[2,8,8,512]{3,2,1,0:T(8,128)(2,1)S(1)}, u32[]{:S(2)}, u32[]{:S(2)}) collective-permute-start(bf16[2,8,8,512]{3,2,1,0:T(8,128)(2,1)S(1)} %get-tuple-element.255), channel_id=1, source_target_pairs={{0,3},{1,0},{2,1},{3,2},{4,7},{5,4},{6,5},{7,6},{8,11},{9,8},{10,9... | collective-permute-start | bytes 393224 | tf_op jit(solution)/shard_map/while/body/eval_jaxpr/ppermute | solution.py:40
  19.9 11.2 %collective-permute-start.1 = (bf16[2,8,8,512]{3,2,1,0:T(8,128)(2,1)S(1)}, bf16[2,8,8,512]{3,2,1,0:T(8,128)(2,1)S(1)}, u32[]{:S(2)}, u32[]{:S(2)}) collective-permute-start(bf16[2,8,8,512]{3,2,1,0:T(8,128)(2,1)S(1)} %get-tuple-element.256), channel_id=1, source_target_pairs={{0,2},{1,3},{2,0},{3,1},{4,6},{5,7},{6,4},{7,5},{8,10},{9,11},{10,... | collective-permute-start | bytes 393224 | tf_op jit(solution)/shard_map/while/body/eval_jaxpr/ppermute | solution.py:40
  19.9 11.2 %collective-permute-start.2 = (bf16[2,8,8,512]{3,2,1,0:T(8,128)(2,1)S(1)}, bf16[2,8,8,512]{3,2,1,0:T(8,128)(2,1)S(1)}, u32[]{:S(2)}, u32[]{:S(2)}) collective-permute-start(bf16[2,8,8,512]{3,2,1,0:T(8,128)(2,1)S(1)} %get-tuple-element.257), channel_id=1, source_target_pairs={{0,1},{1,2},{2,3},{3,0},{4,5},{5,6},{6,7},{7,4},{8,9},{9,10},{10,1... | collective-permute-start | bytes 393224 | tf_op jit(solution)/shard_map/while/body/eval_jaxpr/ppermute | solution.py:40
  41.1 5.8 %collective-permute-start.3 = (bf16[2,8,8,512]{3,1,2,0:T(8,128)(2,1)S(1)}, bf16[2,8,8,512]{3,1,2,0:T(8,128)(2,1)S(1)}, u32[]{:S(2)}, u32[]{:S(2)}) collective-permute-start(bf16[2,8,8,512]{3,1,2,0:T(8,128)(2,1)S(1)} %bitcast.173), channel_id=1, source_target_pairs={{0,3},{1,0},{2,1},{3,2},{4,7},{5,4},{6,5},{7,6},{8,11},{9,8},{10,9... | collective-permute-start | bytes 393224 | tf_op jit(solution)/shard_map/while/body/eval_jaxpr/ppermute | solution.py:40
  42.7 13.5 %collective-permute-start.4 = (bf16[2,8,8,512]{3,1,2,0:T(8,128)(2,1)S(1)}, bf16[2,8,8,512]{3,1,2,0:T(8,128)(2,1)S(1)}, u32[]{:S(2)}, u32[]{:S(2)}) collective-permute-start(bf16[2,8,8,512]{3,1,2,0:T(8,128)(2,1)S(1)} %bitcast.174), channel_id=1, source_target_pairs={{0,2},{1,3},{2,0},{3,1},{4,6},{5,7},{6,4},{7,5},{8,10},{9,11},{10,... | collective-permute-start | bytes 393224 | tf_op jit(solution)/shard_map/while/body/eval_jaxpr/ppermute | solution.py:40
  43.8 12.4 %collective-permute-start.5 = (bf16[2,8,8,512]{3,1,2,0:T(8,128)(2,1)S(1)}, bf16[2,8,8,512]{3,1,2,0:T(8,128)(2,1)S(1)}, u32[]{:S(2)}, u32[]{:S(2)}) collective-permute-start(bf16[2,8,8,512]{3,1,2,0:T(8,128)(2,1)S(1)} %bitcast.175), channel_id=1, source_target_pairs={{0,1},{1,2},{2,3},{3,0},{4,5},{5,6},{6,7},{7,4},{8,9},{9,10},{10,1... | collective-permute-start | bytes 393224 | tf_op jit(solution)/shard_map/while/body/eval_jaxpr/ppermute | solution.py:40
  64.0 5.0 %collective-permute-start.6 = (f32[1,2]{1,0:T(1,128)S(1)}, f32[1,2]{1,0:T(1,128)S(1)}, u32[]{:S(2)}, u32[]{:S(2)}) collective-permute-start(f32[1,2]{1,0:T(1,128)S(1)} %fusion.114), channel_id=1, source_target_pairs={{0,3},{1,0},{2,1},{3,2},{4,7},{5,4},{6,5},{7,6},{8,11},{9,8},{10,9... | collective-permute-start | bytes 32 | tf_op jit(solution)/shard_map/while/body/eval_jaxpr/ppermute | solution.py:40
  64.0 5.0 %collective-permute-start.7 = (f32[1,2]{1,0:T(1,128)S(1)}, f32[1,2]{1,0:T(1,128)S(1)}, u32[]{:S(2)}, u32[]{:S(2)}) collective-permute-start(f32[1,2]{1,0:T(1,128)S(1)} %fusion.114), channel_id=1, source_target_pairs={{0,2},{1,3},{2,0},{3,1},{4,6},{5,7},{6,4},{7,5},{8,10},{9,11},{10,... | collective-permute-start | bytes 32 | tf_op jit(solution)/shard_map/while/body/eval_jaxpr/ppermute | solution.py:40
  65.7 5.3 %collective-permute-start.8 = (f32[1,2]{1,0:T(1,128)S(1)}, f32[1,2]{1,0:T(1,128)S(1)}, u32[]{:S(2)}, u32[]{:S(2)}) collective-permute-start(f32[1,2]{1,0:T(1,128)S(1)} %fusion.114), channel_id=1, source_target_pairs={{0,1},{1,2},{2,3},{3,0},{4,5},{5,6},{6,7},{7,4},{8,9},{9,10},{10,1... | collective-permute-start | bytes 32 | tf_op jit(solution)/shard_map/while/body/eval_jaxpr/ppermute | solution.py:40
  82.9 5.3 %collective-permute-start = (bf16[2,8,8,512]{3,2,1,0:T(8,128)(2,1)S(1)}, bf16[2,8,8,512]{3,2,1,0:T(8,128)(2,1)S(1)}, u32[]{:S(2)}, u32[]{:S(2)}) collective-permute-start(bf16[2,8,8,512]{3,2,1,0:T(8,128)(2,1)S(1)} %get-tuple-element.255), channel_id=1, source_target_pairs={{0,3},{1,0},{2,1},{3,2},{4,7},{5,4},{6,5},{7,6},{8,11},{9,8},{10,9... | collective-permute-start | bytes 393224 | tf_op jit(solution)/shard_map/while/body/eval_jaxpr/ppermute | solution.py:40
  83.9 12.1 %collective-permute-start.1 = (bf16[2,8,8,512]{3,2,1,0:T(8,128)(2,1)S(1)}, bf16[2,8,8,512]{3,2,1,0:T(8,128)(2,1)S(1)}, u32[]{:S(2)}, u32[]{:S(2)}) collective-permute-start(bf16[2,8,8,512]{3,2,1,0:T(8,128)(2,1)S(1)} %get-tuple-element.256), channel_id=1, source_target_pairs={{0,2},{1,3},{2,0},{3,1},{4,6},{5,7},{6,4},{7,5},{8,10},{9,11},{10,... | collective-permute-start | bytes 393224 | tf_op jit(solution)/shard_map/while/body/eval_jaxpr/ppermute | solution.py:40
  84.6 11.4 %collective-permute-start.2 = (bf16[2,8,8,512]{3,2,1,0:T(8,128)(2,1)S(1)}, bf16[2,8,8,512]{3,2,1,0:T(8,128)(2,1)S(1)}, u32[]{:S(2)}, u32[]{:S(2)}) collective-permute-start(bf16[2,8,8,512]{3,2,1,0:T(8,128)(2,1)S(1)} %get-tuple-element.257), channel_id=1, source_target_pairs={{0,1},{1,2},{2,3},{3,0},{4,5},{5,6},{6,7},{7,4},{8,9},{9,10},{10,1... | collective-permute-start | bytes 393224 | tf_op jit(solution)/shard_map/while/body/eval_jaxpr/ppermute | solution.py:40
  105.3 6.6 %collective-permute-start.3 = (bf16[2,8,8,512]{3,1,2,0:T(8,128)(2,1)S(1)}, bf16[2,8,8,512]{3,1,2,0:T(8,128)(2,1)S(1)}, u32[]{:S(2)}, u32[]{:S(2)}) collective-permute-start(bf16[2,8,8,512]{3,1,2,0:T(8,128)(2,1)S(1)} %bitcast.173), channel_id=1, source_target_pairs={{0,3},{1,0},{2,1},{3,2},{4,7},{5,4},{6,5},{7,6},{8,11},{9,8},{10,9... | collective-permute-start | bytes 393224 | tf_op jit(solution)/shard_map/while/body/eval_jaxpr/ppermute | solution.py:40
  105.3 13.9 %collective-permute-start.4 = (bf16[2,8,8,512]{3,1,2,0:T(8,128)(2,1)S(1)}, bf16[2,8,8,512]{3,1,2,0:T(8,128)(2,1)S(1)}, u32[]{:S(2)}, u32[]{:S(2)}) collective-permute-start(bf16[2,8,8,512]{3,1,2,0:T(8,128)(2,1)S(1)} %bitcast.174), channel_id=1, source_target_pairs={{0,2},{1,3},{2,0},{3,1},{4,6},{5,7},{6,4},{7,5},{8,10},{9,11},{10,... | collective-permute-start | bytes 393224 | tf_op jit(solution)/shard_map/while/body/eval_jaxpr/ppermute | solution.py:40
  106.8 12.4 %collective-permute-start.5 = (bf16[2,8,8,512]{3,1,2,0:T(8,128)(2,1)S(1)}, bf16[2,8,8,512]{3,1,2,0:T(8,128)(2,1)S(1)}, u32[]{:S(2)}, u32[]{:S(2)}) collective-permute-start(bf16[2,8,8,512]{3,1,2,0:T(8,128)(2,1)S(1)} %bitcast.175), channel_id=1, source_target_pairs={{0,1},{1,2},{2,3},{3,0},{4,5},{5,6},{6,7},{7,4},{8,9},{9,10},{10,1... | collective-permute-start | bytes 393224 | tf_op jit(solution)/shard_map/while/body/eval_jaxpr/ppermute | solution.py:40
  127.0 4.8 %collective-permute-start.6 = (f32[1,2]{1,0:T(1,128)S(1)}, f32[1,2]{1,0:T(1,128)S(1)}, u32[]{:S(2)}, u32[]{:S(2)}) collective-permute-start(f32[1,2]{1,0:T(1,128)S(1)} %fusion.114), channel_id=1, source_target_pairs={{0,3},{1,0},{2,1},{3,2},{4,7},{5,4},{6,5},{7,6},{8,11},{9,8},{10,9... | collective-permute-start | bytes 32 | tf_op jit(solution)/shard_map/while/body/eval_jaxpr/ppermute | solution.py:40
  127.1 4.8 %collective-permute-start.7 = (f32[1,2]{1,0:T(1,128)S(1)}, f32[1,2]{1,0:T(1,128)S(1)}, u32[]{:S(2)}, u32[]{:S(2)}) collective-permute-start(f32[1,2]{1,0:T(1,128)S(1)} %fusion.114), channel_id=1, source_target_pairs={{0,2},{1,3},{2,0},{3,1},{4,6},{5,7},{6,4},{7,5},{8,10},{9,11},{10,... | collective-permute-start | bytes 32 | tf_op jit(solution)/shard_map/while/body/eval_jaxpr/ppermute | solution.py:40
  128.5 5.3 %collective-permute-start.8 = (f32[1,2]{1,0:T(1,128)S(1)}, f32[1,2]{1,0:T(1,128)S(1)}, u32[]{:S(2)}, u32[]{:S(2)}) collective-permute-start(f32[1,2]{1,0:T(1,128)S(1)} %fusion.114), channel_id=1, source_target_pairs={{0,1},{1,2},{2,3},{3,0},{4,5},{5,6},{6,7},{7,4},{8,9},{9,10},{10,1... | collective-permute-start | bytes 32 | tf_op jit(solution)/shard_map/while/body/eval_jaxpr/ppermute | solution.py:40
  134.7 3.6 %collective-permute-start.10 = (f32[1,2]{1,0:T(1,128)S(1)}, f32[1,2]{1,0:T(1,128)S(1)}, u32[]{:S(2)}, u32[]{:S(2)}) collective-permute-start(f32[1,2]{1,0:T(1,128)S(1)} %bitcast.183), channel_id=1, source_target_pairs={{0,8},{4,12},{8,0},{12,4},{1,9},{5,13},{9,1},{13,5},{2,10},{6,14},... | collective-permute-start | bytes 32 | tf_op jit(solution)/shard_map/while/body/eval_jaxpr/ppermute | solution.py:40
  146.1 5.3 %collective-permute-start = (bf16[2,8,8,512]{3,2,1,0:T(8,128)(2,1)S(1)}, bf16[2,8,8,512]{3,2,1,0:T(8,128)(2,1)S(1)}, u32[]{:S(2)}, u32[]{:S(2)}) collective-permute-start(bf16[2,8,8,512]{3,2,1,0:T(8,128)(2,1)S(1)} %get-tuple-element.255), channel_id=1, source_target_pairs={{0,3},{1,0},{2,1},{3,2},{4,7},{5,4},{6,5},{7,6},{8,11},{9,8},{10,9... | collective-permute-start | bytes 393224 | tf_op jit(solution)/shard_map/while/body/eval_jaxpr/ppermute | solution.py:40
  147.2 11.8 %collective-permute-start.1 = (bf16[2,8,8,512]{3,2,1,0:T(8,128)(2,1)S(1)}, bf16[2,8,8,512]{3,2,1,0:T(8,128)(2,1)S(1)}, u32[]{:S(2)}, u32[]{:S(2)}) collective-permute-start(bf16[2,8,8,512]{3,2,1,0:T(8,128)(2,1)S(1)} %get-tuple-element.256), channel_id=1, source_target_pairs={{0,2},{1,3},{2,0},{3,1},{4,6},{5,7},{6,4},{7,5},{8,10},{9,11},{10,... | collective-permute-start | bytes 393224 | tf_op jit(solution)/shard_map/while/body/eval_jaxpr/ppermute | solution.py:40
  147.8 11.2 %collective-permute-start.2 = (bf16[2,8,8,512]{3,2,1,0:T(8,128)(2,1)S(1)}, bf16[2,8,8,512]{3,2,1,0:T(8,128)(2,1)S(1)}, u32[]{:S(2)}, u32[]{:S(2)}) collective-permute-start(bf16[2,8,8,512]{3,2,1,0:T(8,128)(2,1)S(1)} %get-tuple-element.257), channel_id=1, source_target_pairs={{0,1},{1,2},{2,3},{3,0},{4,5},{5,6},{6,7},{7,4},{8,9},{9,10},{10,1... | collective-permute-start | bytes 393224 | tf_op jit(solution)/shard_map/while/body/eval_jaxpr/ppermute | solution.py:40
  168.5 6.7 %collective-permute-start.3 = (bf16[2,8,8,512]{3,1,2,0:T(8,128)(2,1)S(1)}, bf16[2,8,8,512]{3,1,2,0:T(8,128)(2,1)S(1)}, u32[]{:S(2)}, u32[]{:S(2)}) collective-permute-start(bf16[2,8,8,512]{3,1,2,0:T(8,128)(2,1)S(1)} %bitcast.173), channel_id=1, source_target_pairs={{0,3},{1,0},{2,1},{3,2},{4,7},{5,4},{6,5},{7,6},{8,11},{9,8},{10,9... | collective-permute-start | bytes 393224 | tf_op jit(solution)/shard_map/while/body/eval_jaxpr/ppermute | solution.py:40
  168.6 13.7 %collective-permute-start.4 = (bf16[2,8,8,512]{3,1,2,0:T(8,128)(2,1)S(1)}, bf16[2,8,8,512]{3,1,2,0:T(8,128)(2,1)S(1)}, u32[]{:S(2)}, u32[]{:S(2)}) collective-permute-start(bf16[2,8,8,512]{3,1,2,0:T(8,128)(2,1)S(1)} %bitcast.174), channel_id=1, source_target_pairs={{0,2},{1,3},{2,0},{3,1},{4,6},{5,7},{6,4},{7,5},{8,10},{9,11},{10,... | collective-permute-start | bytes 393224 | tf_op jit(solution)/shard_map/while/body/eval_jaxpr/ppermute | solution.py:40
  169.9 12.4 %collective-permute-start.5 = (bf16[2,8,8,512]{3,1,2,0:T(8,128)(2,1)S(1)}, bf16[2,8,8,512]{3,1,2,0:T(8,128)(2,1)S(1)}, u32[]{:S(2)}, u32[]{:S(2)}) collective-permute-start(bf16[2,8,8,512]{3,1,2,0:T(8,128)(2,1)S(1)} %bitcast.175), channel_id=1, source_target_pairs={{0,1},{1,2},{2,3},{3,0},{4,5},{5,6},{6,7},{7,4},{8,9},{9,10},{10,1... | collective-permute-start | bytes 393224 | tf_op jit(solution)/shard_map/while/body/eval_jaxpr/ppermute | solution.py:40
  190.1 4.9 %collective-permute-start.6 = (f32[1,2]{1,0:T(1,128)S(1)}, f32[1,2]{1,0:T(1,128)S(1)}, u32[]{:S(2)}, u32[]{:S(2)}) collective-permute-start(f32[1,2]{1,0:T(1,128)S(1)} %fusion.114), channel_id=1, source_target_pairs={{0,3},{1,0},{2,1},{3,2},{4,7},{5,4},{6,5},{7,6},{8,11},{9,8},{10,9... | collective-permute-start | bytes 32 | tf_op jit(solution)/shard_map/while/body/eval_jaxpr/ppermute | solution.py:40
  190.1 4.9 %collective-permute-start.7 = (f32[1,2]{1,0:T(1,128)S(1)}, f32[1,2]{1,0:T(1,128)S(1)}, u32[]{:S(2)}, u32[]{:S(2)}) collective-permute-start(f32[1,2]{1,0:T(1,128)S(1)} %fusion.114), channel_id=1, source_target_pairs={{0,2},{1,3},{2,0},{3,1},{4,6},{5,7},{6,4},{7,5},{8,10},{9,11},{10,... | collective-permute-start | bytes 32 | tf_op jit(solution)/shard_map/while/body/eval_jaxpr/ppermute | solution.py:40
  191.7 5.3 %collective-permute-start.8 = (f32[1,2]{1,0:T(1,128)S(1)}, f32[1,2]{1,0:T(1,128)S(1)}, u32[]{:S(2)}, u32[]{:S(2)}) collective-permute-start(f32[1,2]{1,0:T(1,128)S(1)} %fusion.114), channel_id=1, source_target_pairs={{0,1},{1,2},{2,3},{3,0},{4,5},{5,6},{6,7},{7,4},{8,9},{9,10},{10,1... | collective-permute-start | bytes 32 | tf_op jit(solution)/shard_map/while/body/eval_jaxpr/ppermute | solution.py:40
  209.1 5.2 %collective-permute-start = (bf16[2,8,8,512]{3,2,1,0:T(8,128)(2,1)S(1)}, bf16[2,8,8,512]{3,2,1,0:T(8,128)(2,1)S(1)}, u32[]{:S(2)}, u32[]{:S(2)}) collective-permute-start(bf16[2,8,8,512]{3,2,1,0:T(8,128)(2,1)S(1)} %get-tuple-element.255), channel_id=1, source_target_pairs={{0,3},{1,0},{2,1},{3,2},{4,7},{5,4},{6,5},{7,6},{8,11},{9,8},{10,9... | collective-permute-start | bytes 393224 | tf_op jit(solution)/shard_map/while/body/eval_jaxpr/ppermute | solution.py:40
  210.0 12.1 %collective-permute-start.1 = (bf16[2,8,8,512]{3,2,1,0:T(8,128)(2,1)S(1)}, bf16[2,8,8,512]{3,2,1,0:T(8,128)(2,1)S(1)}, u32[]{:S(2)}, u32[]{:S(2)}) collective-permute-start(bf16[2,8,8,512]{3,2,1,0:T(8,128)(2,1)S(1)} %get-tuple-element.256), channel_id=1, source_target_pairs={{0,2},{1,3},{2,0},{3,1},{4,6},{5,7},{6,4},{7,5},{8,10},{9,11},{10,... | collective-permute-start | bytes 393224 | tf_op jit(solution)/shard_map/while/body/eval_jaxpr/ppermute | solution.py:40
  210.8 11.3 %collective-permute-start.2 = (bf16[2,8,8,512]{3,2,1,0:T(8,128)(2,1)S(1)}, bf16[2,8,8,512]{3,2,1,0:T(8,128)(2,1)S(1)}, u32[]{:S(2)}, u32[]{:S(2)}) collective-permute-start(bf16[2,8,8,512]{3,2,1,0:T(8,128)(2,1)S(1)} %get-tuple-element.257), channel_id=1, source_target_pairs={{0,1},{1,2},{2,3},{3,0},{4,5},{5,6},{6,7},{7,4},{8,9},{9,10},{10,1... | collective-permute-start | bytes 393224 | tf_op jit(solution)/shard_map/while/body/eval_jaxpr/ppermute | solution.py:40
  231.4 6.6 %collective-permute-start.3 = (bf16[2,8,8,512]{3,1,2,0:T(8,128)(2,1)S(1)}, bf16[2,8,8,512]{3,1,2,0:T(8,128)(2,1)S(1)}, u32[]{:S(2)}, u32[]{:S(2)}) collective-permute-start(bf16[2,8,8,512]{3,1,2,0:T(8,128)(2,1)S(1)} %bitcast.173), channel_id=1, source_target_pairs={{0,3},{1,0},{2,1},{3,2},{4,7},{5,4},{6,5},{7,6},{8,11},{9,8},{10,9... | collective-permute-start | bytes 393224 | tf_op jit(solution)/shard_map/while/body/eval_jaxpr/ppermute | solution.py:40
  231.4 13.9 %collective-permute-start.4 = (bf16[2,8,8,512]{3,1,2,0:T(8,128)(2,1)S(1)}, bf16[2,8,8,512]{3,1,2,0:T(8,128)(2,1)S(1)}, u32[]{:S(2)}, u32[]{:S(2)}) collective-permute-start(bf16[2,8,8,512]{3,1,2,0:T(8,128)(2,1)S(1)} %bitcast.174), channel_id=1, source_target_pairs={{0,2},{1,3},{2,0},{3,1},{4,6},{5,7},{6,4},{7,5},{8,10},{9,11},{10,... | collective-permute-start | bytes 393224 | tf_op jit(solution)/shard_map/while/body/eval_jaxpr/ppermute | solution.py:40
  232.9 12.4 %collective-permute-start.5 = (bf16[2,8,8,512]{3,1,2,0:T(8,128)(2,1)S(1)}, bf16[2,8,8,512]{3,1,2,0:T(8,128)(2,1)S(1)}, u32[]{:S(2)}, u32[]{:S(2)}) collective-permute-start(bf16[2,8,8,512]{3,1,2,0:T(8,128)(2,1)S(1)} %bitcast.175), channel_id=1, source_target_pairs={{0,1},{1,2},{2,3},{3,0},{4,5},{5,6},{6,7},{7,4},{8,9},{9,10},{10,1... | collective-permute-start | bytes 393224 | tf_op jit(solution)/shard_map/while/body/eval_jaxpr/ppermute | solution.py:40
  253.1 4.8 %collective-permute-start.6 = (f32[1,2]{1,0:T(1,128)S(1)}, f32[1,2]{1,0:T(1,128)S(1)}, u32[]{:S(2)}, u32[]{:S(2)}) collective-permute-start(f32[1,2]{1,0:T(1,128)S(1)} %fusion.114), channel_id=1, source_target_pairs={{0,3},{1,0},{2,1},{3,2},{4,7},{5,4},{6,5},{7,6},{8,11},{9,8},{10,9... | collective-permute-start | bytes 32 | tf_op jit(solution)/shard_map/while/body/eval_jaxpr/ppermute | solution.py:40
  253.1 4.8 %collective-permute-start.7 = (f32[1,2]{1,0:T(1,128)S(1)}, f32[1,2]{1,0:T(1,128)S(1)}, u32[]{:S(2)}, u32[]{:S(2)}) collective-permute-start(f32[1,2]{1,0:T(1,128)S(1)} %fusion.114), channel_id=1, source_target_pairs={{0,2},{1,3},{2,0},{3,1},{4,6},{5,7},{6,4},{7,5},{8,10},{9,11},{10,... | collective-permute-start | bytes 32 | tf_op jit(solution)/shard_map/while/body/eval_jaxpr/ppermute | solution.py:40
  254.6 5.3 %collective-permute-start.8 = (f32[1,2]{1,0:T(1,128)S(1)}, f32[1,2]{1,0:T(1,128)S(1)}, u32[]{:S(2)}, u32[]{:S(2)}) collective-permute-start(f32[1,2]{1,0:T(1,128)S(1)} %fusion.114), channel_id=1, source_target_pairs={{0,1},{1,2},{2,3},{3,0},{4,5},{5,6},{6,7},{7,4},{8,9},{9,10},{10,1... | collective-permute-start | bytes 32 | tf_op jit(solution)/shard_map/while/body/eval_jaxpr/ppermute | solution.py:40
  260.8 3.6 %collective-permute-start.10 = (f32[1,2]{1,0:T(1,128)S(1)}, f32[1,2]{1,0:T(1,128)S(1)}, u32[]{:S(2)}, u32[]{:S(2)}) collective-permute-start(f32[1,2]{1,0:T(1,128)S(1)} %bitcast.183), channel_id=1, source_target_pairs={{0,8},{4,12},{8,0},{12,4},{1,9},{5,13},{9,1},{13,5},{2,10},{6,14},... | collective-permute-start | bytes 32 | tf_op jit(solution)/shard_map/while/body/eval_jaxpr/ppermute | solution.py:40
  272.2 5.3 %collective-permute-start = (bf16[2,8,8,512]{3,2,1,0:T(8,128)(2,1)S(1)}, bf16[2,8,8,512]{3,2,1,0:T(8,128)(2,1)S(1)}, u32[]{:S(2)}, u32[]{:S(2)}) collective-permute-start(bf16[2,8,8,512]{3,2,1,0:T(8,128)(2,1)S(1)} %get-tuple-element.255), channel_id=1, source_target_pairs={{0,3},{1,0},{2,1},{3,2},{4,7},{5,4},{6,5},{7,6},{8,11},{9,8},{10,9... | collective-permute-start | bytes 393224 | tf_op jit(solution)/shard_map/while/body/eval_jaxpr/ppermute | solution.py:40
  273.2 11.9 %collective-permute-start.1 = (bf16[2,8,8,512]{3,2,1,0:T(8,128)(2,1)S(1)}, bf16[2,8,8,512]{3,2,1,0:T(8,128)(2,1)S(1)}, u32[]{:S(2)}, u32[]{:S(2)}) collective-permute-start(bf16[2,8,8,512]{3,2,1,0:T(8,128)(2,1)S(1)} %get-tuple-element.256), channel_id=1, source_target_pairs={{0,2},{1,3},{2,0},{3,1},{4,6},{5,7},{6,4},{7,5},{8,10},{9,11},{10,... | collective-permute-start | bytes 393224 | tf_op jit(solution)/shard_map/while/body/eval_jaxpr/ppermute | solution.py:40
  273.9 11.2 %collective-permute-start.2 = (bf16[2,8,8,512]{3,2,1,0:T(8,128)(2,1)S(1)}, bf16[2,8,8,512]{3,2,1,0:T(8,128)(2,1)S(1)}, u32[]{:S(2)}, u32[]{:S(2)}) collective-permute-start(bf16[2,8,8,512]{3,2,1,0:T(8,128)(2,1)S(1)} %get-tuple-element.257), channel_id=1, source_target_pairs={{0,1},{1,2},{2,3},{3,0},{4,5},{5,6},{6,7},{7,4},{8,9},{9,10},{10,1... | collective-permute-start | bytes 393224 | tf_op jit(solution)/shard_map/while/body/eval_jaxpr/ppermute | solution.py:40
  294.6 6.7 %collective-permute-start.3 = (bf16[2,8,8,512]{3,1,2,0:T(8,128)(2,1)S(1)}, bf16[2,8,8,512]{3,1,2,0:T(8,128)(2,1)S(1)}, u32[]{:S(2)}, u32[]{:S(2)}) collective-permute-start(bf16[2,8,8,512]{3,1,2,0:T(8,128)(2,1)S(1)} %bitcast.173), channel_id=1, source_target_pairs={{0,3},{1,0},{2,1},{3,2},{4,7},{5,4},{6,5},{7,6},{8,11},{9,8},{10,9... | collective-permute-start | bytes 393224 | tf_op jit(solution)/shard_map/while/body/eval_jaxpr/ppermute | solution.py:40
  294.6 13.8 %collective-permute-start.4 = (bf16[2,8,8,512]{3,1,2,0:T(8,128)(2,1)S(1)}, bf16[2,8,8,512]{3,1,2,0:T(8,128)(2,1)S(1)}, u32[]{:S(2)}, u32[]{:S(2)}) collective-permute-start(bf16[2,8,8,512]{3,1,2,0:T(8,128)(2,1)S(1)} %bitcast.174), channel_id=1, source_target_pairs={{0,2},{1,3},{2,0},{3,1},{4,6},{5,7},{6,4},{7,5},{8,10},{9,11},{10,... | collective-permute-start | bytes 393224 | tf_op jit(solution)/shard_map/while/body/eval_jaxpr/ppermute | solution.py:40
  296.0 12.4 %collective-permute-start.5 = (bf16[2,8,8,512]{3,1,2,0:T(8,128)(2,1)S(1)}, bf16[2,8,8,512]{3,1,2,0:T(8,128)(2,1)S(1)}, u32[]{:S(2)}, u32[]{:S(2)}) collective-permute-start(bf16[2,8,8,512]{3,1,2,0:T(8,128)(2,1)S(1)} %bitcast.175), channel_id=1, source_target_pairs={{0,1},{1,2},{2,3},{3,0},{4,5},{5,6},{6,7},{7,4},{8,9},{9,10},{10,1... | collective-permute-start | bytes 393224 | tf_op jit(solution)/shard_map/while/body/eval_jaxpr/ppermute | solution.py:40
  316.2 4.9 %collective-permute-start.6 = (f32[1,2]{1,0:T(1,128)S(1)}, f32[1,2]{1,0:T(1,128)S(1)}, u32[]{:S(2)}, u32[]{:S(2)}) collective-permute-start(f32[1,2]{1,0:T(1,128)S(1)} %fusion.114), channel_id=1, source_target_pairs={{0,3},{1,0},{2,1},{3,2},{4,7},{5,4},{6,5},{7,6},{8,11},{9,8},{10,9... | collective-permute-start | bytes 32 | tf_op jit(solution)/shard_map/while/body/eval_jaxpr/ppermute | solution.py:40
  316.2 4.9 %collective-permute-start.7 = (f32[1,2]{1,0:T(1,128)S(1)}, f32[1,2]{1,0:T(1,128)S(1)}, u32[]{:S(2)}, u32[]{:S(2)}) collective-permute-start(f32[1,2]{1,0:T(1,128)S(1)} %fusion.114), channel_id=1, source_target_pairs={{0,2},{1,3},{2,0},{3,1},{4,6},{5,7},{6,4},{7,5},{8,10},{9,11},{10,... | collective-permute-start | bytes 32 | tf_op jit(solution)/shard_map/while/body/eval_jaxpr/ppermute | solution.py:40
  317.8 5.3 %collective-permute-start.8 = (f32[1,2]{1,0:T(1,128)S(1)}, f32[1,2]{1,0:T(1,128)S(1)}, u32[]{:S(2)}, u32[]{:S(2)}) collective-permute-start(f32[1,2]{1,0:T(1,128)S(1)} %fusion.114), channel_id=1, source_target_pairs={{0,1},{1,2},{2,3},{3,0},{4,5},{5,6},{6,7},{7,4},{8,9},{9,10},{10,1... | collective-permute-start | bytes 32 | tf_op jit(solution)/shard_map/while/body/eval_jaxpr/ppermute | solution.py:40
  324.0 3.6 %collective-permute-start.10 = (f32[1,2]{1,0:T(1,128)S(1)}, f32[1,2]{1,0:T(1,128)S(1)}, u32[]{:S(2)}, u32[]{:S(2)}) collective-permute-start(f32[1,2]{1,0:T(1,128)S(1)} %bitcast.183), channel_id=1, source_target_pairs={{0,8},{4,12},{8,0},{12,4},{1,9},{5,13},{9,1},{13,5},{2,10},{6,14},... | collective-permute-start | bytes 32 | tf_op jit(solution)/shard_map/while/body/eval_jaxpr/ppermute | solution.py:40
  (26 other events, 89.5 us)
